TPU v7x, 32 devices: a whole 2x2x4 slice. The times are simulated.
32 devices in a mesh: layer: 2 (over x), row: 4 (over y, core), col: 4 (over z).
Axes of the slice: x: 2, y: 2, z: 4, core: 2. Of those that a mesh axis runs over, the one named last changes fastest.
Arguments:
- left_matrix: bfloat16 [8192, 1024], P('row', ('layer', 'col')), may hold values from -6 to 6
- square_term: bfloat16 [1024, 1024], P(('layer', 'row'), 'col'), may hold values from -0.5 to 0.5
- block_pattern: int32 [64, 8], replicated, may hold values from 0 to 1, as said below
- keep_mask: int32 [64, 8], replicated, may hold values 0 or 1
Outputs:
- product: bfloat16 [8192, 1024], P('row', 'col')
Inputs may be any that keep to these rules, and one draw needn't show every extreme that they name: `block_pattern`: in each aligned group of 16 block rows, every block column holds 1 to 8 stored blocks; some group holds exactly 8.
All inputs are finite; a program needn't handle non-finite values.
Results may differ from a plain program's by a relative error of at most 0.0038.
Values may be sent and summed in bfloat16 or wider, within the bound.
No kernel may reach another device: no remote copies, remote signals or barrier semaphores. Data moves between devices by JAX's collectives and lax.ppermute only.
A program may use at most 64 MiB of HBM per device.

v0:
```python
import jax
import jax.numpy as jnp
from jax import lax
from jax.sharding import PartitionSpec as P

BLK = 128


def expand(mask_blocks):
    return jnp.repeat(jnp.repeat(mask_blocks, BLK, axis=0), BLK, axis=1)


def per_device(left_matrix, square_term, block_pattern, keep_mask):
    row_idx = lax.axis_index("row")
    col_idx = lax.axis_index("col")
    layer_idx = lax.axis_index("layer")
    row_count = lax.axis_size("row")
    col_count = lax.axis_size("col")
    rows_local = left_matrix.shape[0]
    row_blocks = rows_local // BLK
    inner_blocks = left_matrix.shape[1] // BLK
    inner_local = square_term.shape[0]
    cols_local = square_term.shape[1]
    col_blocks = cols_local // BLK
    inner_start = (layer_idx * col_count + col_idx) * inner_blocks
    pattern_patch = lax.dynamic_slice(
        block_pattern, (row_idx * row_blocks, inner_start), (row_blocks, inner_blocks)
    )
    first_inner = (layer_idx * row_count + row_idx) * inner_local
    first_col = col_idx * cols_local
    inner_pos = first_inner + lax.broadcasted_iota(jnp.int32, (inner_local, cols_local), 0)
    col_pos = first_col + lax.broadcasted_iota(jnp.int32, (inner_local, cols_local), 1)
    unit = jnp.where(inner_pos == col_pos, jnp.float32(1.5), jnp.float32(0.0))
    right_factor = (unit - 0.5 * square_term.astype(jnp.float32)).astype(jnp.bfloat16)
    right_half = lax.all_gather(right_factor, "row", axis=0, tiled=True)
    sparse_left = jnp.where(expand(pattern_patch) > 0, left_matrix, jnp.zeros_like(left_matrix))
    partial_sum = jnp.dot(
        lax.all_gather(sparse_left, "col", axis=1, tiled=True),
        right_half,
        preferred_element_type=jnp.float32,
    )
    keep_patch = lax.dynamic_slice(
        keep_mask, (row_idx * row_blocks, col_idx * col_blocks), (row_blocks, col_blocks)
    )
    keep_full = expand(keep_patch)
    full_sum = lax.psum(partial_sum, "layer")
    kept = jnp.where(keep_full > 0, full_sum, jnp.zeros_like(full_sum))
    return kept.astype(jnp.bfloat16)


def solution(mesh):
    return jax.shard_map(
        per_device,
        mesh=mesh,
        in_specs=(P("row", ("layer", "col")), P(("layer", "row"), "col"), P(), P()),
        out_specs=P("row", "col"),
        check_vma=False,
    )
```

profile of v0, /device:TPU:0, one launch (start us, length us, event | category | flops | bytes accessed | tf_op | source)
XLA Modules:
  0.0 123.4 jit_solution(1267802918335464349)
XLA Ops:
  6.5 0.0 copy-start
  6.5 0.0 all-gather.2.cloned.1.call-start
  6.5 0.8 compare_bitcast_fusion
  7.3 0.1 broadcast_bitcast_fusion.1
  7.4 2.2 %broadcast_select_fusion = bf16[2048,128]{1,0:T(8,128)(2,1)} fusion(bf16[2048,128]{1,0:T(8,128)(2,1)} %param.4, pred[2048]{0:T(1024)(128)(4,1)S(1)} %broadcast_bitcast_fusion.1), kind=kLoop, calls=%fused_computation.1 | loop fusion | flops 262144 | bytes 1050624 | tf_op jit(solution)/shard_map/jit(_where)/select_n | solution.py:36
  9.6 0.0 all-gather.2.cloned.1.call-update
  9.6 0.8 dynamic-slice_compare_fusion
  10.4 0.1 broadcast_bitcast_fusion
  10.5 0.2 broadcast_in_dim.25
  10.7 1.5 %copy.6 = pred[2048,256]{1,0:T(8,128)(4,1)} copy(pred[2048,256]{0,1:T(8,128)(4,1)S(1)} %bitcast.14) | data formatting | bytes 1048576 | tf_op jit(solution)/shard_map/gt | solution.py:47
  12.2 0.0 copy-done
  12.2 0.1 subtract_convert_fusion
  12.3 7.2 %all_gather.7 = bf16[512,256]{1,0:T(8,128)(2,1)S(1)} all-gather(bf16[128,256]{1,0:T(8,128)(2,1)S(1)} %subtract_convert_fusion), channel_id=1, replica_groups=mesh['layer'=2,'row'=4,'col'=4] {'row'}, dimensions={0}, use_global_device_ids=true | all-gather | bytes 327680 | tf_op jit(solution)/shard_map/all_gather | solution.py:35
  19.5 39.2 %all-gather.2.cloned.1.call-done = bf16[2048,512]{1,0:T(8,128)(2,1)} async-done(((bf16[2048,128]{1,0:T(8,128)(2,1)}), bf16[2048,512]{1,0:T(8,128)(2,1)}) %all-gather.2.cloned.1.call-update) | async-done | bytes 2097168 | tf_op jit(solution)/shard_map/all_gather | solution.py:38
  58.7 2.3 %fusion = f32[2048,256]{1,0:T(8,128)S(1)} fusion(bf16[2048,512]{1,0:T(8,128)(2,1)} %all-gather.2.cloned.1.call-done, bf16[512,256]{1,0:T(8,128)(2,1)S(1)} %all_gather.7), kind=kOutput, calls=%fused_computation.10 | convolution fusion | flops 536870912 | bytes 4456448 | tf_op jit(solution)/shard_map/dot_general | solution.py:37
  61.0 53.2 %all-reduce.1 = bf16[2048,256]{1,0:T(8,128)(2,1)S(1)} all-reduce(f32[2048,256]{1,0:T(8,128)S(1)} %fusion), channel_id=1, replica_groups=mesh['layer'=2,'row'=4,'col'=4] {'layer'}, use_global_device_ids=true, to_apply=%region_0.1 | all-reduce | flops 524288 | bytes 3145728 | tf_op jit(solution)/shard_map/psum | solution.py:46
  114.2 2.3 %select_convert_fusion = bf16[2048,256]{1,0:T(8,128)(2,1)} fusion(pred[2048,256]{1,0:T(8,128)(4,1)} %copy.6, bf16[2048,256]{1,0:T(8,128)(2,1)S(1)} %all-reduce.1), kind=kLoop, calls=%fused_computation | loop fusion | flops 524288 | bytes 2621440 | tf_op jit(solution)/shard_map/convert_element_type | solution.py:48
  (3 shorter events, 0.0 us)
Async XLA Ops:
  6.5 5.6 %copy-start = (bf16[128,256]{1,0:T(8,128)(2,1)S(1)}, bf16[128,256]{1,0:T(8,128)(2,1)}, u32[]{:S(2)}) copy-start(bf16[128,256]{1,0:T(8,128)(2,1)} %param.5) | copy-start | bytes 196612
  6.5 52.2 %all-gather.2.cloned.1.call-start = ((), (), s32[]{:S(2)}) async-start(), calls=%async_computation | async-start | bytes 2621440 | tf_op jit(solution)/shard_map/all_gather | solution.py:38
Sparse Core Ops, SparseCore 0:
  9.7 48.9 all-gather.1
where the time goes:
time: 124 us; the launch traced here: 123 us
  blocking collectives  60.4 us (49%)
  waiting for transfers between devices  39.2 us (32%)
  between operations  13.4 us (11%)
  other arithmetic  6.15 us (5%)
  matrix products  2.29 us (2%)
  local copies, waits for them, and re-layouts  1.83 us (1%)
    psum x1, blocking collectives, per_device(): full_sum = lax.psum(partial_sum, 'layer')  53.2 us
    all_gather x1, waiting for transfers between devices, per_device(): lax.all_gather(sparse_left, 'col', axis=1, tiled=True)  39.2 us
    all_gather x1, blocking collectives, per_device(): right_half = lax.all_gather(right_factor, 'row', axis=0, tiled=True)  7.22 us
  transfers between devices with their start and end apart: 1, of which 1 were waited for; matrix products, arithmetic and copies ran while one was open for 2% of the time, Pallas kernels for 0%

commit v1 on v0

v1 whole, which is shorter than its diff:
```python
import jax
import jax.numpy as jnp
from jax import lax
from jax.sharding import PartitionSpec as P

BLK = 128
GROUP = 16
CAP = 8


def slot_table(pattern):
    stored = (pattern > 0).astype(jnp.int32)
    rows = pattern.shape[0]
    groups = rows // GROUP
    grouped = stored.reshape(groups, GROUP, -1)
    slot = jnp.cumsum(grouped, axis=1) - 1
    group_base = (jnp.arange(groups, dtype=jnp.int32) * CAP)[:, None, None]
    slot = (slot + group_base).reshape(rows, -1)
    return stored, slot


def per_device(left_matrix, square_term, block_pattern, keep_mask):
    row_idx = lax.axis_index("row")
    col_idx = lax.axis_index("col")
    layer_idx = lax.axis_index("layer")
    row_count = lax.axis_size("row")
    col_count = lax.axis_size("col")
    rows_local = left_matrix.shape[0]
    row_blocks = rows_local // BLK
    inner_blocks = left_matrix.shape[1] // BLK
    inner_local = square_term.shape[0]
    cols_local = square_term.shape[1]
    col_blocks = cols_local // BLK
    slots = (row_blocks // GROUP) * CAP
    total_inner_blocks = block_pattern.shape[1]

    inner_start = (layer_idx * col_count + col_idx) * inner_blocks
    pattern_patch = lax.dynamic_slice(
        block_pattern, (row_idx * row_blocks, inner_start), (row_blocks, inner_blocks)
    )
    stored, slot = slot_table(pattern_patch)
    slot_ids = jnp.arange(slots, dtype=jnp.int32)
    hit = (stored[:, :, None] > 0) & (slot[:, :, None] == slot_ids[None, None, :])
    source_row = jnp.sum(
        jnp.where(hit, jnp.arange(row_blocks, dtype=jnp.int32)[:, None, None], 0), axis=0
    )
    blocks = left_matrix.reshape(row_blocks, BLK, inner_blocks, BLK).transpose(2, 0, 1, 3)
    flat_blocks = blocks.reshape(inner_blocks * row_blocks, BLK, BLK)
    take_idx = source_row + (jnp.arange(inner_blocks, dtype=jnp.int32) * row_blocks)[:, None]
    packed = jnp.take(flat_blocks, take_idx.reshape(-1), axis=0)
    packed = packed.reshape(inner_blocks, slots, BLK, BLK)

    gathered = lax.all_gather(packed, ("layer", "col"), axis=0, tiled=True)

    first_inner = (layer_idx * row_count + row_idx) * inner_local
    first_col = col_idx * cols_local
    inner_pos = first_inner + lax.broadcasted_iota(jnp.int32, (inner_local, cols_local), 0)
    col_pos = first_col + lax.broadcasted_iota(jnp.int32, (inner_local, cols_local), 1)
    unit = jnp.where(inner_pos == col_pos, jnp.float32(1.5), jnp.float32(0.0))
    right_factor = (unit - 0.5 * square_term.astype(jnp.float32)).astype(jnp.bfloat16)
    right_full = lax.all_gather(right_factor, ("layer", "row"), axis=0, tiled=True)

    panel_pattern = lax.dynamic_slice(
        block_pattern, (row_idx * row_blocks, 0), (row_blocks, total_inner_blocks)
    )
    p_stored, p_slot = slot_table(panel_pattern)
    gather_idx = (
        jnp.arange(total_inner_blocks, dtype=jnp.int32)[None, :] * slots
        + jnp.clip(p_slot, 0, slots - 1)
    )
    flat_packed = gathered.reshape(total_inner_blocks * slots, BLK, BLK)
    right_blocks = right_full.reshape(total_inner_blocks, BLK, cols_local)

    def chunk_sum(first, count):
        idx = lax.dynamic_slice_in_dim(gather_idx, first, count, axis=1)
        keep = lax.dynamic_slice_in_dim(p_stored, first, count, axis=1)
        dense = jnp.take(flat_packed, idx.reshape(-1), axis=0)
        dense = dense.reshape(row_blocks, count, BLK, BLK)
        dense = jnp.where(keep[:, :, None, None] > 0, dense, jnp.zeros_like(dense))
        rhs = lax.dynamic_slice_in_dim(right_blocks, first, count, axis=0)
        return jnp.einsum("ijab,jbc->iac", dense, rhs, preferred_element_type=jnp.float32)

    dense_bytes = row_blocks * total_inner_blocks * BLK * BLK * 2
    chunks = max(1, dense_bytes // (4 << 20))
    while total_inner_blocks % chunks:
        chunks += 1
    if chunks == 1:
        full_sum = chunk_sum(0, total_inner_blocks)
    else:
        per_chunk = total_inner_blocks // chunks

        def body(c, acc):
            return acc + chunk_sum(c * per_chunk, per_chunk)

        full_sum = lax.fori_loop(
            0, chunks, body, jnp.zeros((row_blocks, BLK, cols_local), jnp.float32)
        )
    full_sum = full_sum.reshape(rows_local, cols_local)

    keep_patch = lax.dynamic_slice(
        keep_mask, (row_idx * row_blocks, col_idx * col_blocks), (row_blocks, col_blocks)
    )
    keep_full = jnp.repeat(jnp.repeat(keep_patch, BLK, axis=0), BLK, axis=1)
    kept = jnp.where(keep_full > 0, full_sum, jnp.zeros_like(full_sum))
    return kept.astype(jnp.bfloat16)


def solution(mesh):
    return jax.shard_map(
        per_device,
        mesh=mesh,
        in_specs=(P("row", ("layer", "col")), P(("layer", "row"), "col"), P(), P()),
        out_specs=P("row", "col"),
        check_vma=False,
    )
```

time: 124 us -> 82.1 us (0.66)
  blocking collectives: 60.4 us -> 12.6 us
  local copies, waits for them, and re-layouts: 1.83 us -> 10.2 us
  waiting for transfers between devices: 39.2 us -> 36.2 us
    psum x1 -> x0, blocking collectives: 53.2 us -> none  [per_device(): full_sum = lax.psum(partial_sum, 'layer')]
    all_gather x1, blocking collectives: 7.22 us -> 12.6 us  [per_device(): lax.all_gather(right_factor, ('layer', 'row'), axis=0, tiled=True)]
    gather x0 -> x2, local copies, waits for them, and re-layouts: none -> 5.2 us  [the longest x1 4.6 us: chunk_sum(): dense = jnp.take(flat_packed, idx.reshape(-1), axis=0)]
    dot_general x0 -> x1, local copies, waits for them, and re-layouts: none -> 3.54 us  [chunk_sum(): jnp.einsum('ijab,jbc->iac', dense, rhs, preferred_element_type=jnp.float32)]
    all_gather x1, waiting for transfers between devices: 39.2 us -> 36.2 us  [per_device(): gathered = lax.all_gather(packed, ('layer', 'col'), axis=0, tiled=True)]
    dot_general x0 -> x1, other arithmetic: none -> 2.56 us  [chunk_sum(): jnp.einsum('ijab,jbc->iac', dense, rhs, preferred_element_type=jnp.float32)]
    convert_element_type x1 -> x0, other arithmetic: 2.32 us -> none  [per_device(): return kept.astype(jnp.bfloat16)]
    select_n x1 -> x3, other arithmetic: 2.17 us -> 0.81 us  [the longest x2 0.8 us: per_device(): packed = jnp.take(flat_blocks, take_idx.reshape(-1), axis=0)]
  transfers between devices with their start and end apart: 1 -> 1, of which waited for: 1 -> 1; matrix products, arithmetic and copies ran while one was open for 2% -> 5% of each run, Pallas kernels for 0% -> 0%
where the time goes in v1:
time: 82.1 us; the launch traced here: 81.9 us
  waiting for transfers between devices  36.2 us (44%)
  between operations  13.5 us (16%)
  blocking collectives  12.6 us (15%)
  local copies, waits for them, and re-layouts  10.2 us (12%)
  other arithmetic  7.08 us (9%)
  matrix products  2.27 us (3%)
    all_gather x1, waiting for transfers between devices, per_device(): gathered = lax.all_gather(packed, ('layer', 'col'), axis=0, tiled=True)  36.2 us
    all_gather x1, blocking collectives, per_device(): lax.all_gather(right_factor, ('layer', 'row'), axis=0, tiled=True)  12.6 us
    gather x1, local copies, waits for them, and re-layouts, chunk_sum(): dense = jnp.take(flat_packed, idx.reshape(-1), axis=0)  4.6 us
    dot_general x1, local copies, waits for them, and re-layouts, chunk_sum(): jnp.einsum('ijab,jbc->iac', dense, rhs, preferred_element_type=jnp.float32)  3.54 us
    dot_general x1, other arithmetic, chunk_sum(): jnp.einsum('ijab,jbc->iac', dense, rhs, preferred_element_type=jnp.float32)  2.56 us
    dot_general x1, matrix products, chunk_sum(): jnp.einsum('ijab,jbc->iac', dense, rhs, preferred_element_type=jnp.float32)  2.27 us
  transfers between devices with their start and end apart: 1, of which 1 were waited for; matrix products, arithmetic and copies ran while one was open for 5% of the time, Pallas kernels for 0%

profile of v1, /device:TPU:0, one launch (start us, length us, event | category | flops | bytes accessed | tf_op | source)
XLA Modules:
  0.0 81.9 jit_solution(10551937533751118428)
XLA Ops:
  6.5 0.0 copy-start
  6.5 0.0 all-gather.2.cloned.1.call-start
  6.5 0.8 %compare_bitcast_fusion = (pred[16]{0:T(512)(128)(4,1)S(1)}, s32[16,1]{0,1:T(1,128)S(1)}) fusion(s32[64,8]{0,1:T(8,128)} %param.6, s32[]{:T(128)S(6)} %select_n.84, s32[]{:T(128)S(6)} %select_n.87), kind=kLoop, calls=%fused_computation.29 | loop fusion | flops 48 | bytes 152 | tf_op jit(solution)/shard_map/gt | solution.py:43
  7.4 0.1 copy.39
  7.5 0.1 add_reduce_fusion
  7.6 0.1 select_reduce_fusion
  7.8 0.0 copy-done
  7.8 0.6 gather_fusion
  8.4 0.8 bitcast_select_fusion
  9.2 0.0 all-gather.2.cloned.1.call-update
  9.2 0.8 convert_compare_fusion
  10.0 0.1 copy.36
  10.1 0.1 min.15
  10.2 0.1 copy.37
  10.3 0.1 add.128
  10.3 0.1 compare_and_fusion
  10.4 0.1 copy.38
  10.5 0.1 copy.35
  10.6 0.8 dynamic-slice_compare_fusion.1
  11.4 0.1 broadcast_bitcast_fusion
  11.5 0.1 broadcast_in_dim.66
  11.6 0.6 copy.43
  12.3 0.9 %subtract_convert_fusion = bf16[128,256]{1,0:T(8,128)(2,1)S(1)} fusion(bf16[128,256]{1,0:T(8,128)(2,1)} %param.5, s32[256]{0:T(256)S(1)} %iota_add_fusion, s32[128]{0:T(128)S(1)} %iota_add_fusion.1), kind=kLoop, calls=%fused_computation.9 | loop fusion | flops 196608 | bytes 132608 | tf_op jit(solution)/shard_map/convert_element_type | solution.py:60
  13.2 12.6 %all_gather.7 = bf16[1024,256]{1,0:T(8,128)(2,1)S(1)} all-gather(bf16[128,256]{1,0:T(8,128)(2,1)S(1)} %subtract_convert_fusion), channel_id=1, replica_groups=mesh['layer'=2,'row'=4,'col'=4] {'layer','row'}, dimensions={0}, use_global_device_ids=true | all-gather | bytes 589824 | tf_op jit(solution)/shard_map/all_gather | solution.py:61
  25.8 36.2 %all-gather.2.cloned.1.call-done = bf16[8,8,128,128]{3,2,1,0:T(8,128)(2,1)} async-done(((bf16[1,8,128,128]{3,2,1,0:T(8,128)(2,1)}), bf16[8,8,128,128]{3,2,1,0:T(8,128)(2,1)}) %all-gather.2.cloned.1.call-update) | async-done | bytes 2097168 | tf_op jit(solution)/shard_map/all_gather | solution.py:53
  62.0 4.6 %gather_fusion.1 = bf16[128,128,128]{2,1,0:T(8,128)(2,1)} fusion(bf16[64,128,128]{2,1,0:T(8,128)(2,1)} %bitcast.42, s32[1024]{0:T(1024)S(1)} %pad_clamp_fusion), kind=kCustom, calls=%fused_computation.1 | custom fusion | bytes 8389120 | tf_op jit(solution)/shard_map/jit(_take)/gather | solution.py:77
  66.6 2.6 %select_bitcast_fusion = bf16[16,128,128,8]{2,1,3,0:T(8,128)(2,1)S(1)} fusion(bf16[16,8,128,128]{3,2,1,0:T(8,128)(2,1)} %bitcast.41, pred[16,8]{1,0:T(8,128)(4,1)S(1)} %copy.38, pred[16,8]{1,0:T(8,128)(4,1)S(1)} %copy.35), kind=kLoop, calls=%fused_computation.4 | loop fusion | flops 4194304 | bytes 8388864 | tf_op jit(solution)/shard_map/ijab,jbc->iac/dot_general | solution.py:81
  69.2 3.5 %copy.41 = bf16[16,128,128,8]{2,3,1,0:T(8,128)(2,1)S(1)} copy(bf16[16,128,128,8]{2,1,3,0:T(8,128)(2,1)S(1)} %select_bitcast_fusion) | data formatting | bytes 8388608 | tf_op jit(solution)/shard_map/ijab,jbc->iac/dot_general | solution.py:81
  72.7 2.3 %fusion.8 = bf16[2048,256]{1,0:T(8,128)(2,1)} fusion(pred[2048,256]{1,0:T(32,128)(4,1)S(1)} %copy.43, bf16[8,128,256]{2,1,0:T(8,128)(2,1)S(1)} %bitcast.45, bf16[2048,128,8]{1,2,0:T(8,128)(2,1)S(1)} %bitcast.43), kind=kOutput, calls=%fused_computation.7 | convolution fusion | flops 1074790400 | bytes 6291456 | tf_op jit(solution)/shard_map/ijab,jbc->iac/dot_general | solution.py:81
  (14 shorter events, 0.2 us)
Async XLA Ops:
  6.5 1.2 %copy-start = (bf16[2048,128]{1,0:T(8,128)(2,1)S(1)}, bf16[2048,128]{1,0:T(8,128)(2,1)}, u32[]{:S(2)}) copy-start(bf16[2048,128]{1,0:T(8,128)(2,1)} %param.4) | copy-start | bytes 1572868
  6.5 55.5 %all-gather.2.cloned.1.call-start = ((), (), s32[]{:S(2)}) async-start(), calls=%async_computation | async-start | bytes 2359296 | tf_op jit(solution)/shard_map/all_gather | solution.py:53
Sparse Core Ops, SparseCore 0:
  9.5 52.4 all-gather.1

commit v2 on v1

--- a/solution.py
+++ b/solution.py
@@ -17,6 +17,24 @@
     group_base = (jnp.arange(groups, dtype=jnp.int32) * CAP)[:, None, None]
     slot = (slot + group_base).reshape(rows, -1)
     return stored, slot
+
+
+def ring_gather(x, axis, index, count):
+    pieces = [x]
+    for k in range(1, count):
+        perm = [(s, (s + k) % count) for s in range(count)]
+        pieces.append(lax.ppermute(x, axis, perm))
+    sources = [(index - k) % count for k in range(count)]
+    return pieces, sources
+
+
+def ring_gather_list(xs, axis, index, count):
+    out, sources = [], []
+    for x in xs:
+        got, src = ring_gather(x, axis, index, count)
+        out.extend(got)
+        sources.extend(src)
+    return out, sources
 
 
 def per_device(left_matrix, square_term, block_pattern, keep_mask):
@@ -50,7 +68,19 @@
     packed = jnp.take(flat_blocks, take_idx.reshape(-1), axis=0)
     packed = packed.reshape(inner_blocks, slots, BLK, BLK)
 
-    gathered = lax.all_gather(packed, ("layer", "col"), axis=0, tiled=True)
+    layer_count = lax.axis_size("layer")
+    use_permutes = inner_blocks == 1 and col_count <= 4 and row_count <= 4 and layer_count <= 2
+    if use_permutes:
+        pieces, piece_col = ring_gather(packed, "col", col_idx, col_count)
+        pieces, piece_layer = ring_gather_list(pieces, "layer", layer_idx, layer_count)
+        piece_col = [piece_col[k] for k in range(col_count) for m in range(layer_count)]
+        piece_j = jnp.stack(
+            [pl_ * col_count + pc for pl_, pc in zip(piece_layer, piece_col)]
+        ).astype(jnp.int32)
+        gathered = jnp.concatenate(pieces, axis=0)
+    else:
+        gathered = lax.all_gather(packed, ("layer", "col"), axis=0, tiled=True)
+        piece_j = jnp.arange(total_inner_blocks, dtype=jnp.int32)
 
     first_inner = (layer_idx * row_count + row_idx) * inner_local
     first_col = col_idx * cols_local
@@ -58,18 +88,30 @@
     col_pos = first_col + lax.broadcasted_iota(jnp.int32, (inner_local, cols_local), 1)
     unit = jnp.where(inner_pos == col_pos, jnp.float32(1.5), jnp.float32(0.0))
     right_factor = (unit - 0.5 * square_term.astype(jnp.float32)).astype(jnp.bfloat16)
-    right_full = lax.all_gather(right_factor, ("layer", "row"), axis=0, tiled=True)
+    if use_permutes:
+        rf_pieces, rf_row = ring_gather(right_factor[None], "row", row_idx, row_count)
+        rf_pieces, rf_layer = ring_gather_list(rf_pieces, "layer", layer_idx, layer_count)
+        rf_stack = jnp.concatenate(rf_pieces, axis=0)
+        q = jnp.arange(layer_count * row_count, dtype=jnp.int32)
+        shift_r = (row_idx - q % row_count) % row_count
+        shift_l = (layer_idx - q // row_count) % layer_count
+        right_full = jnp.take(rf_stack, shift_r * layer_count + shift_l, axis=0)
+        right_full = right_full.reshape(layer_count * row_count * inner_local, cols_local)
+    else:
+        right_full = lax.all_gather(right_factor, ("layer", "row"), axis=0, tiled=True)
 
     panel_pattern = lax.dynamic_slice(
         block_pattern, (row_idx * row_blocks, 0), (row_blocks, total_inner_blocks)
     )
     p_stored, p_slot = slot_table(panel_pattern)
+    p_stored = jnp.take(p_stored, piece_j, axis=1)
+    p_slot = jnp.take(p_slot, piece_j, axis=1)
     gather_idx = (
         jnp.arange(total_inner_blocks, dtype=jnp.int32)[None, :] * slots
         + jnp.clip(p_slot, 0, slots - 1)
     )
     flat_packed = gathered.reshape(total_inner_blocks * slots, BLK, BLK)
-    right_blocks = right_full.reshape(total_inner_blocks, BLK, cols_local)
+    right_blocks = jnp.take(right_full.reshape(total_inner_blocks, BLK, cols_local), piece_j, axis=0)
 
     def chunk_sum(first, count):
         idx = lax.dynamic_slice_in_dim(gather_idx, first, count, axis=1)

time: 82.1 us -> 64.5 us (0.79)
  waiting for transfers between devices: 36.2 us -> 10.5 us
  starting transfers between devices: 0.01 us -> 20 us
  between operations: 13.5 us -> 0.2 us
  blocking collectives: 12.6 us -> 0 us
  local copies, waits for them, and re-layouts: 10.2 us -> 22.3 us
  other arithmetic: 7.08 us -> 8.67 us
    all_gather x1 -> x0, waiting for transfers between devices: 36.2 us -> none  [per_device(): gathered = lax.all_gather(packed, ('layer', 'col'), axis=0, tiled=True)]
    ppermute x0 -> x14, starting transfers between devices: none -> 20 us  [ring_gather(): pieces.append(lax.ppermute(x, axis, perm))]
    all_gather x1 -> x0, blocking collectives: 12.6 us -> none  [per_device(): lax.all_gather(right_factor, ('layer', 'row'), axis=0, tiled=True)]
    ppermute x0 -> x14, waiting for transfers between devices: none -> 10.5 us  [ring_gather(): pieces.append(lax.ppermute(x, axis, perm))]
    unnamed x4 -> x18, local copies, waits for them, and re-layouts: 0.1 us -> 7.89 us
    gather x0 -> x4, local copies, waits for them, and re-layouts: none -> 4.35 us  [the longest x1 1.62 us: per_device(): right_full = jnp.take(rf_stack, shift_r * layer_count + shift_l, axis=0)]
    unnamed x0 -> x2, other arithmetic: none -> 2.38 us
    gather x1, local copies, waits for them, and re-layouts: 4.6 us -> 3.03 us  [chunk_sum(): dense = jnp.take(flat_packed, idx.reshape(-1), axis=0)]
  transfers between devices with their start and end apart: 1 -> 14, of which waited for: 1 -> 7; matrix products, arithmetic and copies ran while one was open for 5% -> 30% of each run, Pallas kernels for 0% -> 0%
where the time goes in v2:
time: 64.5 us; the launch traced here: 64 us
  local copies, waits for them, and re-layouts  22.3 us (35%)
  starting transfers between devices  20 us (31%)
  waiting for transfers between devices  10.5 us (16%)
  other arithmetic  8.67 us (13%)
  matrix products  2.35 us (4%)
    ppermute x14, starting transfers between devices, ring_gather(): pieces.append(lax.ppermute(x, axis, perm))  20 us
    ppermute x14, waiting for transfers between devices, ring_gather(): pieces.append(lax.ppermute(x, axis, perm))  10.5 us
    unnamed x18, local copies, waits for them, and re-layouts  7.89 us
    dot_general x1, local copies, waits for them, and re-layouts, chunk_sum(): jnp.einsum('ijab,jbc->iac', dense, rhs, preferred_element_type=jnp.float32)  3.55 us
    gather x1, local copies, waits for them, and re-layouts, chunk_sum(): dense = jnp.take(flat_packed, idx.reshape(-1), axis=0)  3.03 us
    dot_general x1, other arithmetic, chunk_sum(): jnp.einsum('ijab,jbc->iac', dense, rhs, preferred_element_type=jnp.float32)  2.56 us
    unnamed x2, other arithmetic  2.38 us
    dot_general x1, matrix products, chunk_sum(): jnp.einsum('ijab,jbc->iac', dense, rhs, preferred_element_type=jnp.float32)  2.35 us
  transfers between devices with their start and end apart: 14, of which 7 were waited for; matrix products, arithmetic and copies ran while one was open for 30% of the time, Pallas kernels for 0%

profile of v2, /device:TPU:0, one launch (start us, length us, event | category | flops | bytes accessed | tf_op | source)
XLA Modules:
  0.0 64.0 jit_solution(15408584252672124979)
XLA Ops:
  0.0 0.8 %compare_bitcast_fusion = (pred[16]{0:T(512)(128)(4,1)S(1)}, s32[16,1]{0,1:T(1,128)S(1)}) fusion(s32[64,8]{0,1:T(8,128)} %param.10, s32[]{:T(128)S(6)} %select_n.153, s32[]{:T(128)S(6)} %select_n.162), kind=kLoop, calls=%fused_computation.69 | loop fusion | flops 48 | bytes 152 | tf_op jit(solution)/shard_map/gt | solution.py:61
  1.9 0.8 %constant_dynamic-update-slice_fusion.7 = (bf16[8,8,128,128]{3,2,1,0:T(8,128)(2,1)S(1)}, bf16[1,8,128,128]{3,2,1,0:T(8,128)(2,1)}) fusion(bf16[8,128,128]{2,1,0:T(8,128)(2,1)S(1)} %gather_fusion, pred[8]{0:T(512)(128)(4,1)S(1)} %compare_and_fusion.3), kind=kLoop, calls=%fused_computation.26 | loop fusion | flops 131071 | bytes 786440
  2.8 2.9 %collective-permute-start = (bf16[1,8,128,128]{3,2,1,0:T(8,128)(2,1)}, bf16[1,8,128,128]{3,2,1,0:T(8,128)(2,1)}, u32[]{:S(2)}, u32[]{:S(2)}) collective-permute-start(bf16[1,8,128,128]{3,2,1,0:T(8,128)(2,1)} %get-tuple-element.14), channel_id=1, source_target_pairs={{0,16},{16,0},{1,17},{17,1},{2,18},{18,2},{3,19},{19,3},{4,20},{20... | collective-permute-start | bytes 786440 | tf_op jit(solution)/shard_map/ppermute | solution.py:26
  5.7 1.6 %collective-permute-start.1 = (bf16[1,8,128,128]{3,2,1,0:T(8,128)(2,1)}, bf16[1,8,128,128]{3,2,1,0:T(8,128)(2,1)}, u32[]{:S(2)}, u32[]{:S(2)}) collective-permute-start(bf16[1,8,128,128]{3,2,1,0:T(8,128)(2,1)} %get-tuple-element.14), channel_id=1, source_target_pairs={{0,1},{1,2},{2,3},{3,0},{4,5},{5,6},{6,7},{7,4},{8,9},{9,10},{10,1... | collective-permute-start | bytes 786440 | tf_op jit(solution)/shard_map/ppermute | solution.py:26
  7.3 2.6 %collective-permute-start.3 = (bf16[1,8,128,128]{3,2,1,0:T(8,128)(2,1)}, bf16[1,8,128,128]{3,2,1,0:T(8,128)(2,1)S(1)}, u32[]{:S(2)}, u32[]{:S(2)}) collective-permute-start(bf16[1,8,128,128]{3,2,1,0:T(8,128)(2,1)} %get-tuple-element.14), channel_id=1, source_target_pairs={{0,2},{1,3},{2,0},{3,1},{4,6},{5,7},{6,4},{7,5},{8,10},{9,11},{10,... | collective-permute-start | bytes 786440 | tf_op jit(solution)/shard_map/ppermute | solution.py:26
  9.9 1.6 %constant_dynamic-update-slice_fusion.15 = (bf16[8,128,256]{2,1,0:T(8,128)(2,1)}, bf16[1,128,256]{2,1,0:T(8,128)(2,1)S(1)}) fusion(bf16[128,256]{1,0:T(8,128)(2,1)} %param.9, s32[256]{0:T(256)S(1)} %iota_add_fusion, s32[128]{0:T(128)S(1)} %iota_add_fusion.1), kind=kLoop, calls=%fused_computation.34 | loop fusion | flops 196607 | bytes 198144
  12.0 0.8 %fusion.16 = s32[16,8]{0,1:T(8,128)S(1)} fusion(s32[64,8]{0,1:T(8,128)} %param.10, s32[]{:T(128)S(6)} %select_n.153), kind=kLoop, calls=%fused_computation.50 | loop fusion | flops 256 | bytes 1028 | tf_op jit(solution)/shard_map/convert_element_type | solution.py:12
  14.5 0.8 %dynamic-slice_compare_fusion.1 = pred[16,2]{0,1:T(4,128)(4,1)S(1)} fusion(s32[64,8]{0,1:T(8,128)} %param.11, s32[]{:T(128)S(6)} %select_n.153, s32[]{:T(128)S(6)} %select_n.154), kind=kLoop, calls=%fused_computation.72 | loop fusion | flops 32 | bytes 168 | tf_op jit(solution)/shard_map/gt | solution.py:146
  15.5 1.4 %copy.34 = pred[2048,256]{1,0:T(32,128)(4,1)} copy(pred[2048,256]{0,1:T(32,128)(4,1)S(1)} %bitcast.53) | data formatting | bytes 1048576 | tf_op jit(solution)/shard_map/gt | solution.py:146
  17.0 1.6 %collective-permute-start.10 = (bf16[1,128,256]{2,1,0:T(8,128)(2,1)S(1)}, bf16[1,128,256]{2,1,0:T(8,128)(2,1)S(1)}, u32[]{:S(2)}, u32[]{:S(2)}) collective-permute-start(bf16[1,128,256]{2,1,0:T(8,128)(2,1)S(1)} %get-tuple-element.10), channel_id=1, source_target_pairs={{0,8},{4,12},{8,0},{12,4},{1,9},{5,13},{9,1},{13,5},{2,10},{6,14},... | collective-permute-start | bytes 196616 | tf_op jit(solution)/shard_map/ppermute | solution.py:26
  18.5 1.5 %collective-permute-start.9 = (bf16[1,128,256]{2,1,0:T(8,128)(2,1)S(1)}, bf16[1,128,256]{2,1,0:T(8,128)(2,1)S(1)}, u32[]{:S(2)}, u32[]{:S(2)}) collective-permute-start(bf16[1,128,256]{2,1,0:T(8,128)(2,1)S(1)} %collective-permute-done.8), channel_id=1, source_target_pairs={{0,16},{16,0},{1,17},{17,1},{2,18},{18,2},{3,19},{19,3},{4,20},{20... | collective-permute-start | bytes 196616 | tf_op jit(solution)/shard_map/ppermute | solution.py:26
  21.4 1.2 %collective-permute-start.12 = (bf16[1,128,256]{2,1,0:T(8,128)(2,1)S(1)}, bf16[1,128,256]{2,1,0:T(8,128)(2,1)S(1)}, u32[]{:S(2)}, u32[]{:S(2)}) collective-permute-start(bf16[1,128,256]{2,1,0:T(8,128)(2,1)S(1)} %get-tuple-element.10), channel_id=1, source_target_pairs={{0,12},{4,0},{8,4},{12,8},{1,13},{5,1},{9,5},{13,9},{2,14},{6,2},{... | collective-permute-start | bytes 196616 | tf_op jit(solution)/shard_map/ppermute | solution.py:26
  22.9 1.5 %collective-permute-start.11 = (bf16[1,128,256]{2,1,0:T(8,128)(2,1)S(1)}, bf16[1,128,256]{2,1,0:T(8,128)(2,1)S(1)}, u32[]{:S(2)}, u32[]{:S(2)}) collective-permute-start(bf16[1,128,256]{2,1,0:T(8,128)(2,1)S(1)} %collective-permute-done.10), channel_id=1, source_target_pairs={{0,16},{16,0},{1,17},{17,1},{2,18},{18,2},{3,19},{19,3},{4,20},{20... | collective-permute-start | bytes 196616 | tf_op jit(solution)/shard_map/ppermute | solution.py:26
  25.6 1.3 %collective-permute-start.5 = (bf16[1,8,128,128]{3,2,1,0:T(8,128)(2,1)}, bf16[1,8,128,128]{3,2,1,0:T(8,128)(2,1)}, u32[]{:S(2)}, u32[]{:S(2)}) collective-permute-start(bf16[1,8,128,128]{3,2,1,0:T(8,128)(2,1)} %get-tuple-element.14), channel_id=1, source_target_pairs={{0,3},{1,0},{2,1},{3,2},{4,7},{5,4},{6,5},{7,6},{8,11},{9,8},{10,9... | collective-permute-start | bytes 786440 | tf_op jit(solution)/shard_map/ppermute | solution.py:26
  27.1 1.5 %collective-permute-start.13 = (bf16[1,128,256]{2,1,0:T(8,128)(2,1)S(1)}, bf16[1,128,256]{2,1,0:T(8,128)(2,1)S(1)}, u32[]{:S(2)}, u32[]{:S(2)}) collective-permute-start(bf16[1,128,256]{2,1,0:T(8,128)(2,1)S(1)} %collective-permute-done.12), channel_id=1, source_target_pairs={{0,16},{16,0},{1,17},{17,1},{2,18},{18,2},{3,19},{19,3},{4,20},{20... | collective-permute-start | bytes 196616 | tf_op jit(solution)/shard_map/ppermute | solution.py:26
  29.9 1.5 %collective-permute-done.13 = bf16[1,128,256]{2,1,0:T(8,128)(2,1)S(1)} collective-permute-done((bf16[1,128,256]{2,1,0:T(8,128)(2,1)S(1)}, bf16[1,128,256]{2,1,0:T(8,128)(2,1)S(1)}, u32[]{:S(2)}, u32[]{:S(2)}) %collective-permute-start.13) | collective-permute-done | bytes 65568 | tf_op jit(solution)/shard_map/ppermute | solution.py:26
  32.0 1.6 %gather_fusion.4 = bf16[8,128,256]{2,1,0:T(8,128)(2,1)S(1)} fusion(bf16[8,128,256]{2,1,0:T(8,128)(2,1)} %constant_dynamic-update-slice_fusion.8, s32[1024]{0:T(1024)S(1)} %pad_clamp_fusion), kind=kCustom, calls=%fused_computation.1.clone | custom fusion | bytes 1048608 | tf_op jit(solution)/shard_map/jit(_take)/gather | solution.py:98
  33.7 1.6 %collective-permute-start.2 = (bf16[1,8,128,128]{3,2,1,0:T(8,128)(2,1)}, bf16[1,8,128,128]{3,2,1,0:T(8,128)(2,1)}, u32[]{:S(2)}, u32[]{:S(2)}) collective-permute-start(bf16[1,8,128,128]{3,2,1,0:T(8,128)(2,1)} %collective-permute-done.1), channel_id=1, source_target_pairs={{0,16},{16,0},{1,17},{17,1},{2,18},{18,2},{3,19},{19,3},{4,20},{20... | collective-permute-start | bytes 786440 | tf_op jit(solution)/shard_map/ppermute | solution.py:26
  35.2 0.9 %broadcast_select_fusion = bf16[8,128,256]{2,1,0:T(8,128)(2,1)} fusion(bf16[8,128,256]{2,1,0:T(8,128)(2,1)S(1)} %gather_fusion.4, pred[8]{0:T(512)(128)(4,1)S(1)} %get-tuple-element.6), kind=kLoop, calls=%fused_computation.14 | loop fusion | flops 262144 | bytes 1048584 | tf_op jit(solution)/shard_map/jit(_take)/select_n | solution.py:98
  36.1 1.6 %gather_fusion.5 = bf16[8,128,256]{2,1,0:T(8,128)(2,1)S(1)} fusion(bf16[8,128,256]{2,1,0:T(8,128)(2,1)} %broadcast_select_fusion, s32[1024]{0:T(1024)S(1)} %get-tuple-element.19), kind=kCustom, calls=%fused_computation.3.clone | custom fusion | bytes 1048608 | tf_op jit(solution)/shard_map/jit(_take)/gather | solution.py:114
  38.4 1.0 %constant_dynamic-update-slice_fusion.6 = bf16[8,8,128,128]{3,2,1,0:T(8,128)(2,1)S(1)} fusion(bf16[8,8,128,128]{3,2,1,0:T(8,128)(2,1)S(1)} %get-tuple-element.13, bf16[1,8,128,128]{3,2,1,0:T(8,128)(2,1)} %collective-permute-done), kind=kLoop, calls=%fused_computation.25 | loop fusion | bytes 524288
  39.4 1.0 %constant_dynamic-update-slice_fusion.5 = bf16[8,8,128,128]{3,2,1,0:T(8,128)(2,1)S(1)} fusion(bf16[8,8,128,128]{3,2,1,0:T(8,128)(2,1)S(1)} %constant_dynamic-update-slice_fusion.6, bf16[1,8,128,128]{3,2,1,0:T(8,128)(2,1)} %collective-permute-done.1), kind=kLoop, calls=%fused_computation.24 | loop fusion | bytes 524288
  40.4 1.6 %collective-permute-start.6 = (bf16[1,8,128,128]{3,2,1,0:T(8,128)(2,1)}, bf16[1,8,128,128]{3,2,1,0:T(8,128)(2,1)S(1)}, u32[]{:S(2)}, u32[]{:S(2)}) collective-permute-start(bf16[1,8,128,128]{3,2,1,0:T(8,128)(2,1)} %collective-permute-done.5), channel_id=1, source_target_pairs={{0,16},{16,0},{1,17},{17,1},{2,18},{18,2},{3,19},{19,3},{4,20},{20... | collective-permute-start | bytes 786440 | tf_op jit(solution)/shard_map/ppermute | solution.py:26
  41.9 1.0 %collective-permute-done.2 = bf16[1,8,128,128]{3,2,1,0:T(8,128)(2,1)} collective-permute-done((bf16[1,8,128,128]{3,2,1,0:T(8,128)(2,1)}, bf16[1,8,128,128]{3,2,1,0:T(8,128)(2,1)}, u32[]{:S(2)}, u32[]{:S(2)}) %collective-permute-start.2) | collective-permute-done | bytes 262176 | tf_op jit(solution)/shard_map/ppermute | solution.py:26
  43.0 1.0 %constant_dynamic-update-slice_fusion.4 = bf16[8,8,128,128]{3,2,1,0:T(8,128)(2,1)S(1)} fusion(bf16[8,8,128,128]{3,2,1,0:T(8,128)(2,1)S(1)} %constant_dynamic-update-slice_fusion.5, bf16[1,8,128,128]{3,2,1,0:T(8,128)(2,1)} %collective-permute-done.2), kind=kLoop, calls=%fused_computation.23 | loop fusion | bytes 524288
  44.0 4.5 %collective-permute-done.4 = bf16[1,8,128,128]{3,2,1,0:T(8,128)(2,1)S(1)} collective-permute-done((bf16[1,8,128,128]{3,2,1,0:T(8,128)(2,1)S(1)}, bf16[1,8,128,128]{3,2,1,0:T(8,128)(2,1)S(1)}, u32[]{:S(2)}, u32[]{:S(2)}) %collective-permute-start.4) | collective-permute-done | bytes 262176 | tf_op jit(solution)/shard_map/ppermute | solution.py:26
  48.5 1.0 %constant_dynamic-update-slice_fusion.1 = bf16[8,8,128,128]{3,2,1,0:T(8,128)(2,1)S(1)} fusion(bf16[8,8,128,128]{3,2,1,0:T(8,128)(2,1)S(1)} %constant_dynamic-update-slice_fusion.2, bf16[1,8,128,128]{3,2,1,0:T(8,128)(2,1)} %collective-permute-done.5), kind=kLoop, calls=%fused_computation.20 | loop fusion | bytes 524288
  49.5 2.9 %collective-permute-done.6 = bf16[1,8,128,128]{3,2,1,0:T(8,128)(2,1)S(1)} collective-permute-done((bf16[1,8,128,128]{3,2,1,0:T(8,128)(2,1)}, bf16[1,8,128,128]{3,2,1,0:T(8,128)(2,1)S(1)}, u32[]{:S(2)}, u32[]{:S(2)}) %collective-permute-start.6) | collective-permute-done | bytes 262176 | tf_op jit(solution)/shard_map/ppermute | solution.py:26
  52.5 3.0 %gather_fusion.1 = bf16[128,128,128]{2,1,0:T(8,128)(2,1)} fusion(bf16[64,128,128]{2,1,0:T(8,128)(2,1)S(1)} %bitcast.51, s32[1024]{0:T(1024)S(1)} %pad_clamp_fusion.1), kind=kCustom, calls=%fused_computation.5 | custom fusion | bytes 8389120 | tf_op jit(solution)/shard_map/jit(_take)/gather | solution.py:119
  55.5 2.6 %select_bitcast_fusion = bf16[16,128,128,8]{2,1,3,0:T(8,128)(2,1)S(1)} fusion(bf16[16,8,128,128]{3,2,1,0:T(8,128)(2,1)} %bitcast.50, pred[16,8]{1,0:T(8,128)(4,1)S(1)} %copy.29, pred[16,8]{1,0:T(8,128)(4,1)S(1)} %copy.26), kind=kLoop, calls=%fused_computation.8 | loop fusion | flops 4194304 | bytes 8388864 | tf_op jit(solution)/shard_map/ijab,jbc->iac/dot_general | solution.py:123
  58.1 3.5 %copy.32 = bf16[16,128,128,8]{2,3,1,0:T(8,128)(2,1)S(1)} copy(bf16[16,128,128,8]{2,1,3,0:T(8,128)(2,1)S(1)} %select_bitcast_fusion) | data formatting | bytes 8388608 | tf_op jit(solution)/shard_map/ijab,jbc->iac/dot_general | solution.py:123
  61.6 2.4 %fusion.8 = bf16[2048,256]{1,0:T(8,128)(2,1)} fusion(pred[2048,256]{1,0:T(32,128)(4,1)S(1)} %copy-done.1, bf16[2048,128,8]{1,2,0:T(8,128)(2,1)S(1)} %bitcast.52, bf16[8,128,256]{2,1,0:T(8,128)(2,1)S(1)} %gather_fusion.5, pred[8]{0:T(512)(128)(4,1)S(1)} %compare_and_fusion.2), kind=kOutput, calls=%fused_computation.11 | convolution fusion | flops 1075052544 | bytes 6291464 | tf_op jit(solution)/shard_map/ijab,jbc->iac/dot_general | solution.py:123
  (59 shorter events, 9.3 us)
Async XLA Ops:
  0.0 1.3 %copy-start = (bf16[2048,128]{1,0:T(8,128)(2,1)S(1)}, bf16[2048,128]{1,0:T(8,128)(2,1)}, u32[]{:S(2)}) copy-start(bf16[2048,128]{1,0:T(8,128)(2,1)} %param.8) | copy-start | bytes 1572868
  2.8 35.6 %collective-permute-start = (bf16[1,8,128,128]{3,2,1,0:T(8,128)(2,1)}, bf16[1,8,128,128]{3,2,1,0:T(8,128)(2,1)}, u32[]{:S(2)}, u32[]{:S(2)}) collective-permute-start(bf16[1,8,128,128]{3,2,1,0:T(8,128)(2,1)} %get-tuple-element.14), channel_id=1, source_target_pairs={{0,16},{16,0},{1,17},{17,1},{2,18},{18,2},{3,19},{19,3},{4,20},{20... | collective-permute-start | bytes 786440 | tf_op jit(solution)/shard_map/ppermute | solution.py:26
  5.7 28.0 %collective-permute-start.1 = (bf16[1,8,128,128]{3,2,1,0:T(8,128)(2,1)}, bf16[1,8,128,128]{3,2,1,0:T(8,128)(2,1)}, u32[]{:S(2)}, u32[]{:S(2)}) collective-permute-start(bf16[1,8,128,128]{3,2,1,0:T(8,128)(2,1)} %get-tuple-element.14), channel_id=1, source_target_pairs={{0,1},{1,2},{2,3},{3,0},{4,5},{5,6},{6,7},{7,4},{8,9},{9,10},{10,1... | collective-permute-start | bytes 786440 | tf_op jit(solution)/shard_map/ppermute | solution.py:26
  7.3 30.5 %collective-permute-start.3 = (bf16[1,8,128,128]{3,2,1,0:T(8,128)(2,1)}, bf16[1,8,128,128]{3,2,1,0:T(8,128)(2,1)S(1)}, u32[]{:S(2)}, u32[]{:S(2)}) collective-permute-start(bf16[1,8,128,128]{3,2,1,0:T(8,128)(2,1)} %get-tuple-element.14), channel_id=1, source_target_pairs={{0,2},{1,3},{2,0},{3,1},{4,6},{5,7},{6,4},{7,5},{8,10},{9,11},{10,... | collective-permute-start | bytes 786440 | tf_op jit(solution)/shard_map/ppermute | solution.py:26
  11.4 5.5 %collective-permute-start.7 = (bf16[1,128,256]{2,1,0:T(8,128)(2,1)S(1)}, bf16[1,128,256]{2,1,0:T(8,128)(2,1)S(1)}, u32[]{:S(2)}, u32[]{:S(2)}) collective-permute-start(bf16[1,128,256]{2,1,0:T(8,128)(2,1)S(1)} %get-tuple-element.10), channel_id=1, source_target_pairs={{0,16},{16,0},{1,17},{17,1},{2,18},{18,2},{3,19},{19,3},{4,20},{20... | collective-permute-start | bytes 196616 | tf_op jit(solution)/shard_map/ppermute | solution.py:26
  12.0 6.6 %collective-permute-start.8 = (bf16[1,128,256]{2,1,0:T(8,128)(2,1)S(1)}, bf16[1,128,256]{2,1,0:T(8,128)(2,1)S(1)}, u32[]{:S(2)}, u32[]{:S(2)}) collective-permute-start(bf16[1,128,256]{2,1,0:T(8,128)(2,1)S(1)} %get-tuple-element.10), channel_id=1, source_target_pairs={{0,4},{4,8},{8,12},{12,0},{1,5},{5,9},{9,13},{13,1},{2,6},{6,10},{... | collective-permute-start | bytes 196616 | tf_op jit(solution)/shard_map/ppermute | solution.py:26
  17.0 4.4 %collective-permute-start.10 = (bf16[1,128,256]{2,1,0:T(8,128)(2,1)S(1)}, bf16[1,128,256]{2,1,0:T(8,128)(2,1)S(1)}, u32[]{:S(2)}, u32[]{:S(2)}) collective-permute-start(bf16[1,128,256]{2,1,0:T(8,128)(2,1)S(1)} %get-tuple-element.10), channel_id=1, source_target_pairs={{0,8},{4,12},{8,0},{12,4},{1,9},{5,13},{9,1},{13,5},{2,10},{6,14},... | collective-permute-start | bytes 196616 | tf_op jit(solution)/shard_map/ppermute | solution.py:26
  18.5 4.3 %collective-permute-start.9 = (bf16[1,128,256]{2,1,0:T(8,128)(2,1)S(1)}, bf16[1,128,256]{2,1,0:T(8,128)(2,1)S(1)}, u32[]{:S(2)}, u32[]{:S(2)}) collective-permute-start(bf16[1,128,256]{2,1,0:T(8,128)(2,1)S(1)} %collective-permute-done.8), channel_id=1, source_target_pairs={{0,16},{16,0},{1,17},{17,1},{2,18},{18,2},{3,19},{19,3},{4,20},{20... | collective-permute-start | bytes 196616 | tf_op jit(solution)/shard_map/ppermute | solution.py:26
  21.4 4.3 %collective-permute-start.12 = (bf16[1,128,256]{2,1,0:T(8,128)(2,1)S(1)}, bf16[1,128,256]{2,1,0:T(8,128)(2,1)S(1)}, u32[]{:S(2)}, u32[]{:S(2)}) collective-permute-start(bf16[1,128,256]{2,1,0:T(8,128)(2,1)S(1)} %get-tuple-element.10), channel_id=1, source_target_pairs={{0,12},{4,0},{8,4},{12,8},{1,13},{5,1},{9,5},{13,9},{2,14},{6,2},{... | collective-permute-start | bytes 196616 | tf_op jit(solution)/shard_map/ppermute | solution.py:26
  22.9 4.3 %collective-permute-start.11 = (bf16[1,128,256]{2,1,0:T(8,128)(2,1)S(1)}, bf16[1,128,256]{2,1,0:T(8,128)(2,1)S(1)}, u32[]{:S(2)}, u32[]{:S(2)}) collective-permute-start(bf16[1,128,256]{2,1,0:T(8,128)(2,1)S(1)} %collective-permute-done.10), channel_id=1, source_target_pairs={{0,16},{16,0},{1,17},{17,1},{2,18},{18,2},{3,19},{19,3},{4,20},{20... | collective-permute-start | bytes 196616 | tf_op jit(solution)/shard_map/ppermute | solution.py:26
  25.6 14.7 %collective-permute-start.5 = (bf16[1,8,128,128]{3,2,1,0:T(8,128)(2,1)}, bf16[1,8,128,128]{3,2,1,0:T(8,128)(2,1)}, u32[]{:S(2)}, u32[]{:S(2)}) collective-permute-start(bf16[1,8,128,128]{3,2,1,0:T(8,128)(2,1)} %get-tuple-element.14), channel_id=1, source_target_pairs={{0,3},{1,0},{2,1},{3,2},{4,7},{5,4},{6,5},{7,6},{8,11},{9,8},{10,9... | collective-permute-start | bytes 786440 | tf_op jit(solution)/shard_map/ppermute | solution.py:26
  27.1 4.3 %collective-permute-start.13 = (bf16[1,128,256]{2,1,0:T(8,128)(2,1)S(1)}, bf16[1,128,256]{2,1,0:T(8,128)(2,1)S(1)}, u32[]{:S(2)}, u32[]{:S(2)}) collective-permute-start(bf16[1,128,256]{2,1,0:T(8,128)(2,1)S(1)} %collective-permute-done.12), channel_id=1, source_target_pairs={{0,16},{16,0},{1,17},{17,1},{2,18},{18,2},{3,19},{19,3},{4,20},{20... | collective-permute-start | bytes 196616 | tf_op jit(solution)/shard_map/ppermute | solution.py:26
  33.7 9.3 %collective-permute-start.2 = (bf16[1,8,128,128]{3,2,1,0:T(8,128)(2,1)}, bf16[1,8,128,128]{3,2,1,0:T(8,128)(2,1)}, u32[]{:S(2)}, u32[]{:S(2)}) collective-permute-start(bf16[1,8,128,128]{3,2,1,0:T(8,128)(2,1)} %collective-permute-done.1), channel_id=1, source_target_pairs={{0,16},{16,0},{1,17},{17,1},{2,18},{18,2},{3,19},{19,3},{4,20},{20... | collective-permute-start | bytes 786440 | tf_op jit(solution)/shard_map/ppermute | solution.py:26
  37.8 10.7 %collective-permute-start.4 = (bf16[1,8,128,128]{3,2,1,0:T(8,128)(2,1)S(1)}, bf16[1,8,128,128]{3,2,1,0:T(8,128)(2,1)S(1)}, u32[]{:S(2)}, u32[]{:S(2)}) collective-permute-start(bf16[1,8,128,128]{3,2,1,0:T(8,128)(2,1)S(1)} %collective-permute-done.3), channel_id=1, source_target_pairs={{0,16},{16,0},{1,17},{17,1},{2,18},{18,2},{3,19},{19,3},{4,20},{20... | collective-permute-start | bytes 786440 | tf_op jit(solution)/shard_map/ppermute | solution.py:26
  40.4 12.0 %collective-permute-start.6 = (bf16[1,8,128,128]{3,2,1,0:T(8,128)(2,1)}, bf16[1,8,128,128]{3,2,1,0:T(8,128)(2,1)S(1)}, u32[]{:S(2)}, u32[]{:S(2)}) collective-permute-start(bf16[1,8,128,128]{3,2,1,0:T(8,128)(2,1)} %collective-permute-done.5), channel_id=1, source_target_pairs={{0,16},{16,0},{1,17},{17,1},{2,18},{18,2},{3,19},{19,3},{4,20},{20... | collective-permute-start | bytes 786440 | tf_op jit(solution)/shard_map/ppermute | solution.py:26
  58.1 3.6 %copy-start.1 = (pred[2048,256]{1,0:T(32,128)(4,1)S(1)}, pred[2048,256]{1,0:T(32,128)(4,1)}, u32[]{:S(2)}) copy-start(pred[2048,256]{1,0:T(32,128)(4,1)} %copy.34) | copy-start | bytes 1572868

commit v3 on v2

--- a/solution.py
+++ b/solution.py
@@ -1,6 +1,10 @@
+import functools
+
 import jax
 import jax.numpy as jnp
 from jax import lax
+from jax.experimental import pallas as pl
+from jax.experimental.pallas import tpu as pltpu
 from jax.sharding import PartitionSpec as P
 
 BLK = 128
@@ -35,6 +39,54 @@
         out.extend(got)
         sources.extend(src)
     return out, sources
+
+
+def product_kernel(slot_ref, rf_pos_ref, keep_ref, *refs, pieces, row_blocks, cols):
+    left_refs = refs[:pieces]
+    rf_refs = refs[pieces:2 * pieces]
+    out_ref = refs[2 * pieces]
+    lhs_scr, rf_scr = refs[2 * pieces + 1:]
+    for q in range(pieces):
+        at = pl.multiple_of(rf_pos_ref[q] * BLK, BLK)
+        rf_scr[pl.ds(at, BLK), :] = rf_refs[q][...]
+    for p in range(pieces):
+        for i in range(row_blocks):
+            s = slot_ref[p, i]
+            blk = left_refs[p][jnp.maximum(s, 0)]
+            blk = jnp.where(s >= 0, blk, jnp.zeros_like(blk))
+            lhs_scr[i * BLK:(i + 1) * BLK, p * BLK:(p + 1) * BLK] = blk
+    tile = 2 * BLK
+    for t in range(row_blocks * BLK // tile):
+        res = jnp.dot(
+            lhs_scr[t * tile:(t + 1) * tile, :], rf_scr[...], preferred_element_type=jnp.float32
+        )
+        for a in range(tile // BLK):
+            i = t * (tile // BLK) + a
+            for b in range(cols // BLK):
+                sub = res[a * BLK:(a + 1) * BLK, b * BLK:(b + 1) * BLK]
+                sub = jnp.where(keep_ref[i, b] > 0, sub, jnp.zeros_like(sub))
+                out_ref[i * BLK:(i + 1) * BLK, b * BLK:(b + 1) * BLK] = sub.astype(out_ref.dtype)
+
+
+def product_call(slot_tbl, rf_pos, keep_patch, left_pieces, rf_pieces):
+    pieces = len(left_pieces)
+    row_blocks = slot_tbl.shape[1]
+    cols = rf_pieces[0].shape[1]
+    smem = pl.BlockSpec(memory_space=pltpu.SMEM)
+    vmem = pl.BlockSpec(memory_space=pltpu.VMEM)
+    flops = 2 * row_blocks * BLK * pieces * BLK * cols
+    bytes_accessed = pieces * (left_pieces[0].size + rf_pieces[0].size) * 2 + row_blocks * BLK * cols * 2
+    return pl.pallas_call(
+        functools.partial(product_kernel, pieces=pieces, row_blocks=row_blocks, cols=cols),
+        out_shape=jax.ShapeDtypeStruct((row_blocks * BLK, cols), jnp.bfloat16),
+        in_specs=[smem, smem, smem] + [vmem] * (2 * pieces),
+        out_specs=vmem,
+        scratch_shapes=[
+            pltpu.VMEM((row_blocks * BLK, pieces * BLK), jnp.bfloat16),
+            pltpu.VMEM((pieces * BLK, cols), jnp.bfloat16),
+        ],
+        cost_estimate=pl.CostEstimate(flops=flops, bytes_accessed=bytes_accessed, transcendentals=0),
+    )(slot_tbl, rf_pos, keep_patch, *left_pieces, *rf_pieces)
 
 
 def per_device(left_matrix, square_term, block_pattern, keep_mask):
@@ -69,18 +121,12 @@
     packed = packed.reshape(inner_blocks, slots, BLK, BLK)
 
     layer_count = lax.axis_size("layer")
-    use_permutes = inner_blocks == 1 and col_count <= 4 and row_count <= 4 and layer_count <= 2
-    if use_permutes:
-        pieces, piece_col = ring_gather(packed, "col", col_idx, col_count)
-        pieces, piece_layer = ring_gather_list(pieces, "layer", layer_idx, layer_count)
-        piece_col = [piece_col[k] for k in range(col_count) for m in range(layer_count)]
-        piece_j = jnp.stack(
-            [pl_ * col_count + pc for pl_, pc in zip(piece_layer, piece_col)]
-        ).astype(jnp.int32)
-        gathered = jnp.concatenate(pieces, axis=0)
-    else:
-        gathered = lax.all_gather(packed, ("layer", "col"), axis=0, tiled=True)
-        piece_j = jnp.arange(total_inner_blocks, dtype=jnp.int32)
+    keep_patch = lax.dynamic_slice(
+        keep_mask, (row_idx * row_blocks, col_idx * col_blocks), (row_blocks, col_blocks)
+    ).astype(jnp.int32)
+    panel_pattern = lax.dynamic_slice(
+        block_pattern, (row_idx * row_blocks, 0), (row_blocks, total_inner_blocks)
+    )
 
     first_inner = (layer_idx * row_count + row_idx) * inner_local
     first_col = col_idx * cols_local
@@ -88,21 +134,39 @@
     col_pos = first_col + lax.broadcasted_iota(jnp.int32, (inner_local, cols_local), 1)
     unit = jnp.where(inner_pos == col_pos, jnp.float32(1.5), jnp.float32(0.0))
     right_factor = (unit - 0.5 * square_term.astype(jnp.float32)).astype(jnp.bfloat16)
+
+    use_permutes = (
+        inner_blocks == 1
+        and inner_local == BLK
+        and col_count == row_count
+        and col_count <= 4
+        and layer_count <= 2
+    )
     if use_permutes:
-        rf_pieces, rf_row = ring_gather(right_factor[None], "row", row_idx, row_count)
+        pieces, piece_col = ring_gather(packed[0], "col", col_idx, col_count)
+        pieces, piece_layer = ring_gather_list(pieces, "layer", layer_idx, layer_count)
+        piece_col = [piece_col[k] for k in range(col_count) for m in range(layer_count)]
+        piece_j = jnp.stack(
+            [src_l * col_count + src_c for src_l, src_c in zip(piece_layer, piece_col)]
+        ).astype(jnp.int32)
+        rf_pieces, rf_row = ring_gather(right_factor, "row", row_idx, row_count)
         rf_pieces, rf_layer = ring_gather_list(rf_pieces, "layer", layer_idx, layer_count)
-        rf_stack = jnp.concatenate(rf_pieces, axis=0)
-        q = jnp.arange(layer_count * row_count, dtype=jnp.int32)
-        shift_r = (row_idx - q % row_count) % row_count
-        shift_l = (layer_idx - q // row_count) % layer_count
-        right_full = jnp.take(rf_stack, shift_r * layer_count + shift_l, axis=0)
-        right_full = right_full.reshape(layer_count * row_count * inner_local, cols_local)
-    else:
-        right_full = lax.all_gather(right_factor, ("layer", "row"), axis=0, tiled=True)
-
-    panel_pattern = lax.dynamic_slice(
-        block_pattern, (row_idx * row_blocks, 0), (row_blocks, total_inner_blocks)
-    )
+        rf_row = [rf_row[k] for k in range(row_count) for m in range(layer_count)]
+        rf_q = jnp.stack(
+            [src_l * row_count + src_r for src_l, src_r in zip(rf_layer, rf_row)]
+        ).astype(jnp.int32)
+        rf_pos = ((col_idx - rf_q % col_count) % col_count) * layer_count + (
+            (layer_idx - rf_q // col_count) % layer_count
+        )
+        p_stored, p_slot = slot_table(panel_pattern)
+        slot_tbl = jnp.where(p_stored > 0, p_slot, -1)
+        slot_tbl = jnp.take(slot_tbl, piece_j, axis=1).T.astype(jnp.int32)
+        return product_call(slot_tbl, rf_pos.astype(jnp.int32), keep_patch, pieces, rf_pieces)
+
+    gathered = lax.all_gather(packed, ("layer", "col"), axis=0, tiled=True)
+    piece_j = jnp.arange(total_inner_blocks, dtype=jnp.int32)
+    right_full = lax.all_gather(right_factor, ("layer", "row"), axis=0, tiled=True)
+
     p_stored, p_slot = slot_table(panel_pattern)
     p_stored = jnp.take(p_stored, piece_j, axis=1)
     p_slot = jnp.take(p_slot, piece_j, axis=1)
@@ -139,9 +203,6 @@
         )
     full_sum = full_sum.reshape(rows_local, cols_local)
 
-    keep_patch = lax.dynamic_slice(
-        keep_mask, (row_idx * row_blocks, col_idx * col_blocks), (row_blocks, col_blocks)
-    )
     keep_full = jnp.repeat(jnp.repeat(keep_patch, BLK, axis=0), BLK, axis=1)
     kept = jnp.where(keep_full > 0, full_sum, jnp.zeros_like(full_sum))
     return kept.astype(jnp.bfloat16)

time: 64.5 us -> 54.3 us (0.84)
  local copies, waits for them, and re-layouts: 22.3 us -> 5.38 us
  waiting for transfers between devices: 10.5 us -> 24.2 us
  other arithmetic: 8.67 us -> 2.76 us
  Pallas kernels: 0 us -> 4.15 us
  starting transfers between devices: 20 us -> 17.4 us
  matrix products: 2.35 us -> 0 us
    ppermute x14, waiting for transfers between devices: 10.5 us -> 24.2 us  [ring_gather(): pieces.append(lax.ppermute(x, axis, perm))]
    gather x5 -> x1, local copies, waits for them, and re-layouts: 7.38 us -> 0.55 us  [per_device(): slot_tbl = jnp.take(slot_tbl, piece_j, axis=1).T.astype(jnp.int32)]
    unnamed x18 -> x38, local copies, waits for them, and re-layouts: 7.89 us -> 2.98 us
    pallas_call x0 -> x1, Pallas kernels: none -> 4.15 us  [product_call(): pl.pallas_call(functools.partial(product_kernel, pieces=pieces, row_block...]
    dot_general x1 -> x0, local copies, waits for them, and re-layouts: 3.55 us -> none  [chunk_sum(): jnp.einsum('ijab,jbc->iac', dense, rhs, preferred_element_type=jnp.float32)]
    ppermute x14, starting transfers between devices: 20 us -> 17.4 us  [ring_gather(): pieces.append(lax.ppermute(x, axis, perm))]
    dot_general x1 -> x0, other arithmetic: 2.56 us -> none  [chunk_sum(): jnp.einsum('ijab,jbc->iac', dense, rhs, preferred_element_type=jnp.float32)]
    unnamed x2 -> x0, other arithmetic: 2.38 us -> none
  transfers between devices with their start and end apart: 14 -> 14, of which waited for: 7 -> 3; matrix products, arithmetic and copies ran while one was open for 30% -> 9% of each run, Pallas kernels for 0% -> 0%
where the time goes in v3:
time: 54.3 us; the launch traced here: 54.1 us
  waiting for transfers between devices  24.2 us (45%)
  starting transfers between devices  17.4 us (32%)
  local copies, waits for them, and re-layouts  5.38 us (10%)
  Pallas kernels  4.15 us (8%)
  other arithmetic  2.76 us (5%)
    ppermute x14, waiting for transfers between devices, ring_gather(): pieces.append(lax.ppermute(x, axis, perm))  24.2 us
    ppermute x14, starting transfers between devices, ring_gather(): pieces.append(lax.ppermute(x, axis, perm))  17.4 us
    pallas_call x1, Pallas kernels, product_call(): pl.pallas_call(functools.partial(product_kernel, pieces=pieces, row_block...  4.15 us
    unnamed x38, local copies, waits for them, and re-layouts  2.98 us
  transfers between devices with their start and end apart: 14, of which 3 were waited for; matrix products, arithmetic and copies ran while one was open for 9% of the time, Pallas kernels for 0%

profile of v3, /device:TPU:0, one launch (start us, length us, event | category | flops | bytes accessed | tf_op | source)
XLA Modules:
  0.0 54.1 jit_solution(6870541067074422259)
XLA Ops:
  0.0 1.0 %subtract_convert_fusion.refs_8_ = bf16[128,256]{1,0:T(8,128)(2,1)S(1)} fusion(bf16[128,256]{1,0:T(8,128)(2,1)} %param.5, s32[256]{0:T(256)S(1)} %iota_add_fusion, s32[128]{0:T(128)S(1)} %iota_add_fusion.1), kind=kLoop, calls=%fused_computation.3 | loop fusion | flops 196608 | bytes 132608 | tf_op jit(solution)/shard_map/convert_element_type | solution.py:136
  1.0 2.5 %collective-permute-start.12 = (bf16[128,256]{1,0:T(8,128)(2,1)S(1)}, bf16[128,256]{1,0:T(8,128)(2,1)S(1)}, u32[]{:S(2)}, u32[]{:S(2)}) collective-permute-start(bf16[128,256]{1,0:T(8,128)(2,1)S(1)} %subtract_convert_fusion.refs_8_), channel_id=1, source_target_pairs={{0,12},{4,0},{8,4},{12,8},{1,13},{5,1},{9,5},{13,9},{2,14},{6,2},{... | collective-permute-start | bytes 196616 | tf_op jit(solution)/shard_map/ppermute | solution.py:30
  3.5 0.6 %collective-permute-start.10 = (bf16[128,256]{1,0:T(8,128)(2,1)S(1)}, bf16[128,256]{1,0:T(8,128)(2,1)S(1)}, u32[]{:S(2)}, u32[]{:S(2)}) collective-permute-start(bf16[128,256]{1,0:T(8,128)(2,1)S(1)} %subtract_convert_fusion.refs_8_), channel_id=1, source_target_pairs={{0,8},{4,12},{8,0},{12,4},{1,9},{5,13},{9,1},{13,5},{2,10},{6,14},... | collective-permute-start | bytes 196616 | tf_op jit(solution)/shard_map/ppermute | solution.py:30
  4.1 0.2 collective-permute-start.8
  4.3 0.7 %copy-done.3 = s32[64,8]{0,1:T(8,128)S(1)} copy-done((s32[64,8]{0,1:T(8,128)S(1)}, s32[64,8]{0,1:T(8,128)}, u32[]{:S(2)}) %copy-start.3) | copy-done | bytes 2072
  5.2 0.1 add_reduce_fusion
  5.3 0.1 select_reduce_fusion
  5.5 0.6 %gather_fusion.1 = bf16[8,128,128]{2,1,0:T(8,128)(2,1)S(1)} fusion(bf16[16,128,128]{2,1,0:T(8,128)(2,1)S(1)} %bitcast.33, s32[1024]{0:T(1024)S(1)} %pad_clamp_fusion), kind=kCustom, calls=%fused_computation.1 | custom fusion | bytes 524320 | tf_op jit(solution)/shard_map/jit(_take)/gather | solution.py:120
  6.2 3.7 %collective-permute-start.5 = (bf16[8,128,128]{2,1,0:T(8,128)(2,1)S(1)}, bf16[8,128,128]{2,1,0:T(8,128)(2,1)S(1)}, u32[]{:S(2)}, u32[]{:S(2)}) collective-permute-start(bf16[8,128,128]{2,1,0:T(8,128)(2,1)S(1)} %broadcast_select_fusion.refs_0_), channel_id=1, source_target_pairs={{0,3},{1,0},{2,1},{3,2},{4,7},{5,4},{6,5},{7,6},{8,11},{9,8},{10,9... | collective-permute-start | bytes 786440 | tf_op jit(solution)/shard_map/ppermute | solution.py:30
  10.1 0.1 stack.89
  10.2 1.1 %collective-permute-start.1 = (bf16[8,128,128]{2,1,0:T(8,128)(2,1)S(1)}, bf16[8,128,128]{2,1,0:T(8,128)(2,1)S(1)}, u32[]{:S(2)}, u32[]{:S(2)}) collective-permute-start(bf16[8,128,128]{2,1,0:T(8,128)(2,1)S(1)} %broadcast_select_fusion.refs_0_), channel_id=1, source_target_pairs={{0,1},{1,2},{2,3},{3,0},{4,5},{5,6},{6,7},{7,4},{8,9},{9,10},{10,1... | collective-permute-start | bytes 786440 | tf_op jit(solution)/shard_map/ppermute | solution.py:30
  11.4 1.5 %collective-permute-start.7 = (bf16[128,256]{1,0:T(8,128)(2,1)S(1)}, bf16[128,256]{1,0:T(8,128)(2,1)S(1)}, u32[]{:S(2)}, u32[]{:S(2)}) collective-permute-start(bf16[128,256]{1,0:T(8,128)(2,1)S(1)} %subtract_convert_fusion.refs_8_), channel_id=1, source_target_pairs={{0,16},{16,0},{1,17},{17,1},{2,18},{18,2},{3,19},{19,3},{4,20},{20... | collective-permute-start | bytes 196616 | tf_op jit(solution)/shard_map/ppermute | solution.py:30
  12.9 0.5 collective-permute-start.13
  13.5 0.6 %gather_fusion = s32[8,16]{1,0:T(8,128)S(1)} fusion(s32[16,8]{0,1:T(8,128)S(1)} %copy.14, s32[1024]{0:T(1024)S(1)} %pad_clamp_fusion.1), kind=kCustom, calls=%fused_computation | custom fusion | bytes 1056 | tf_op jit(solution)/shard_map/jit(_take)/gather | solution.py:163
  14.0 2.1 %collective-permute-done.7.refs_9_ = bf16[128,256]{1,0:T(8,128)(2,1)S(1)} collective-permute-done((bf16[128,256]{1,0:T(8,128)(2,1)S(1)}, bf16[128,256]{1,0:T(8,128)(2,1)S(1)}, u32[]{:S(2)}, u32[]{:S(2)}) %collective-permute-start.7) | collective-permute-done | bytes 65568 | tf_op jit(solution)/shard_map/ppermute | solution.py:30
  16.1 1.7 %collective-permute-start = (bf16[8,128,128]{2,1,0:T(8,128)(2,1)S(1)}, bf16[8,128,128]{2,1,0:T(8,128)(2,1)S(1)}, u32[]{:S(2)}, u32[]{:S(2)}) collective-permute-start(bf16[8,128,128]{2,1,0:T(8,128)(2,1)S(1)} %broadcast_select_fusion.refs_0_), channel_id=1, source_target_pairs={{0,16},{16,0},{1,17},{17,1},{2,18},{18,2},{3,19},{19,3},{4,20},{20... | collective-permute-start | bytes 786440 | tf_op jit(solution)/shard_map/ppermute | solution.py:30
  17.8 1.0 %collective-permute-start.11 = (bf16[128,256]{1,0:T(8,128)(2,1)S(1)}, bf16[128,256]{1,0:T(8,128)(2,1)S(1)}, u32[]{:S(2)}, u32[]{:S(2)}) collective-permute-start(bf16[128,256]{1,0:T(8,128)(2,1)S(1)} %collective-permute-done.10.refs_12_), channel_id=1, source_target_pairs={{0,16},{16,0},{1,17},{17,1},{2,18},{18,2},{3,19},{19,3},{4,20},{20... | collective-permute-start | bytes 196616 | tf_op jit(solution)/shard_map/ppermute | solution.py:30
  18.8 1.0 %collective-permute-start.6 = (bf16[8,128,128]{2,1,0:T(8,128)(2,1)S(1)}, bf16[8,128,128]{2,1,0:T(8,128)(2,1)S(1)}, u32[]{:S(2)}, u32[]{:S(2)}) collective-permute-start(bf16[8,128,128]{2,1,0:T(8,128)(2,1)S(1)} %collective-permute-done.5.refs_6_), channel_id=1, source_target_pairs={{0,16},{16,0},{1,17},{17,1},{2,18},{18,2},{3,19},{19,3},{4,20},{20... | collective-permute-start | bytes 786440 | tf_op jit(solution)/shard_map/ppermute | solution.py:30
  19.8 13.1 %collective-permute-done.3.refs_4_ = bf16[8,128,128]{2,1,0:T(8,128)(2,1)S(1)} collective-permute-done((bf16[8,128,128]{2,1,0:T(8,128)(2,1)S(1)}, bf16[8,128,128]{2,1,0:T(8,128)(2,1)S(1)}, u32[]{:S(2)}, u32[]{:S(2)}) %collective-permute-start.3) | collective-permute-done | bytes 262176 | tf_op jit(solution)/shard_map/ppermute | solution.py:30
  33.0 1.5 %collective-permute-start.4 = (bf16[8,128,128]{2,1,0:T(8,128)(2,1)S(1)}, bf16[8,128,128]{2,1,0:T(8,128)(2,1)S(1)}, u32[]{:S(2)}, u32[]{:S(2)}) collective-permute-start(bf16[8,128,128]{2,1,0:T(8,128)(2,1)S(1)} %collective-permute-done.3.refs_4_), channel_id=1, source_target_pairs={{0,16},{16,0},{1,17},{17,1},{2,18},{18,2},{3,19},{19,3},{4,20},{20... | collective-permute-start | bytes 786440 | tf_op jit(solution)/shard_map/ppermute | solution.py:30
  34.5 0.5 collective-permute-start.2
  35.0 0.7 %broadcast_select_fusion.1.slot_ref = s32[8,16]{1,0:T(8,128)} fusion(s32[8,16]{1,0:T(8,128)S(1)} %gather_fusion, pred[8]{0:T(512)(128)(4,1)S(1)} %compare_and_fusion.1), kind=kLoop, calls=%fused_computation.20 | loop fusion | flops 128 | bytes 1032 | tf_op jit(solution)/shard_map/jit(_take)/select_n | solution.py:163
  35.8 1.6 %collective-permute-start.9 = (bf16[128,256]{1,0:T(8,128)(2,1)S(1)}, bf16[128,256]{1,0:T(8,128)(2,1)S(1)}, u32[]{:S(2)}, u32[]{:S(2)}) collective-permute-start(bf16[128,256]{1,0:T(8,128)(2,1)S(1)} %collective-permute-done.8.refs_10_), channel_id=1, source_target_pairs={{0,16},{16,0},{1,17},{17,1},{2,18},{18,2},{3,19},{19,3},{4,20},{20... | collective-permute-start | bytes 196616 | tf_op jit(solution)/shard_map/ppermute | solution.py:30
  37.4 0.6 %fusion.1.rf_pos_ref = s32[8]{0:T(128)} fusion(s32[8]{0:T(128)S(1)} %stack.98, s32[]{:T(128)S(6)} %axis_index.33, s32[]{:T(128)S(6)} %axis_index.35), kind=kLoop, calls=%fused_computation.33 | loop fusion | flops 360 | bytes 72 | tf_op jit(solution)/shard_map/add | solution.py:158
  38.0 0.8 %dynamic_slice.10 = s32[16,2]{0,1:T(2,128)S(1)} dynamic-slice(s32[64,8]{0,1:T(8,128)} %param.7, s32[]{:T(128)S(6)} %select_n.170, s32[]{:T(128)S(6)} %select_n.183), dynamic_slice_sizes={16,2} | dynamic-slice | bytes 260 | tf_op jit(solution)/shard_map/dynamic_slice | solution.py:124
  38.7 0.7 %copy.18.keep_ref = s32[16,2]{1,0:T(8,128)} copy(s32[16,2]{0,1:T(2,128)S(1)} %dynamic_slice.10) | data formatting | bytes 256
  39.4 8.9 %collective-permute-done.9.refs_11_ = bf16[128,256]{1,0:T(8,128)(2,1)S(1)} collective-permute-done((bf16[128,256]{1,0:T(8,128)(2,1)S(1)}, bf16[128,256]{1,0:T(8,128)(2,1)S(1)}, u32[]{:S(2)}, u32[]{:S(2)}) %collective-permute-start.9) | collective-permute-done | bytes 65568 | tf_op jit(solution)/shard_map/ppermute | solution.py:30
  48.5 0.5 copy-done.17
  49.0 0.1 copy-done.7
  49.1 0.1 copy-done.8
  49.2 0.7 %copy-done.10 = bf16[8,128,128]{2,1,0:T(8,128)(2,1)} copy-done((bf16[8,128,128]{2,1,0:T(8,128)(2,1)}, bf16[8,128,128]{2,1,0:T(8,128)(2,1)S(1)}, u32[]{:S(2)}) %copy-start.10) | copy-done | bytes 262168
  49.9 4.1 %shard_map.46 = bf16[2048,256]{1,0:T(8,128)(2,1)} custom-call(s32[8,16]{1,0:T(8,128)} %broadcast_select_fusion.1.slot_ref, s32[8]{0:T(128)} %fusion.1.rf_pos_ref, s32[16,2]{1,0:T(8,128)} %copy.18.keep_ref, bf16[8,128,128]{2,1,0:T(8,128)(2,1)} %copy-done.1, bf16[8,128,128]{2,1,0:T(8,128)(2,1)} %copy-done.7, bf16[8,128,128]{2,1,0:T(8,128)(2,1)} %copy-done.6, ...), custom_call_target="tpu_custom_call" | custom-call | flops 1073741824 | bytes 3670016 | tf_op jit(solution)/shard_map/pallas_call | solution.py:79
  (63 shorter events, 0.9 us)
Async XLA Ops:
  0.0 5.4 %copy-start = (bf16[2048,128]{1,0:T(8,128)(2,1)S(1)}, bf16[2048,128]{1,0:T(8,128)(2,1)}, u32[]{:S(2)}) copy-start(bf16[2048,128]{1,0:T(8,128)(2,1)} %param.4) | copy-start | bytes 1572868
  1.0 10.4 %copy-start.2 = (bf16[128,256]{1,0:T(8,128)(2,1)}, bf16[128,256]{1,0:T(8,128)(2,1)S(1)}, u32[]{:S(2)}) copy-start(bf16[128,256]{1,0:T(8,128)(2,1)S(1)} %subtract_convert_fusion.refs_8_) | copy-start | bytes 196612
  1.0 9.2 %collective-permute-start.12 = (bf16[128,256]{1,0:T(8,128)(2,1)S(1)}, bf16[128,256]{1,0:T(8,128)(2,1)S(1)}, u32[]{:S(2)}, u32[]{:S(2)}) collective-permute-start(bf16[128,256]{1,0:T(8,128)(2,1)S(1)} %subtract_convert_fusion.refs_8_), channel_id=1, source_target_pairs={{0,12},{4,0},{8,4},{12,8},{1,13},{5,1},{9,5},{13,9},{2,14},{6,2},{... | collective-permute-start | bytes 196616 | tf_op jit(solution)/shard_map/ppermute | solution.py:30
  3.5 7.9 %collective-permute-start.10 = (bf16[128,256]{1,0:T(8,128)(2,1)S(1)}, bf16[128,256]{1,0:T(8,128)(2,1)S(1)}, u32[]{:S(2)}, u32[]{:S(2)}) collective-permute-start(bf16[128,256]{1,0:T(8,128)(2,1)S(1)} %subtract_convert_fusion.refs_8_), channel_id=1, source_target_pairs={{0,8},{4,12},{8,0},{12,4},{1,9},{5,13},{9,1},{13,5},{2,10},{6,14},... | collective-permute-start | bytes 196616 | tf_op jit(solution)/shard_map/ppermute | solution.py:30
  4.1 8.8 %collective-permute-start.8 = (bf16[128,256]{1,0:T(8,128)(2,1)S(1)}, bf16[128,256]{1,0:T(8,128)(2,1)S(1)}, u32[]{:S(2)}, u32[]{:S(2)}) collective-permute-start(bf16[128,256]{1,0:T(8,128)(2,1)S(1)} %subtract_convert_fusion.refs_8_), channel_id=1, source_target_pairs={{0,4},{4,8},{8,12},{12,0},{1,5},{5,9},{9,13},{13,1},{2,6},{6,10},{... | collective-permute-start | bytes 196616 | tf_op jit(solution)/shard_map/ppermute | solution.py:30
  4.3 0.7 %copy-start.3 = (s32[64,8]{0,1:T(8,128)S(1)}, s32[64,8]{0,1:T(8,128)}, u32[]{:S(2)}) copy-start(s32[64,8]{0,1:T(8,128)} %param.6) | copy-start | bytes 6148
  6.2 33.2 %copy-start.1 = (bf16[8,128,128]{2,1,0:T(8,128)(2,1)}, bf16[8,128,128]{2,1,0:T(8,128)(2,1)S(1)}, u32[]{:S(2)}) copy-start(bf16[8,128,128]{2,1,0:T(8,128)(2,1)S(1)} %broadcast_select_fusion.refs_0_) | copy-start | bytes 786436
  6.2 12.7 %collective-permute-start.5 = (bf16[8,128,128]{2,1,0:T(8,128)(2,1)S(1)}, bf16[8,128,128]{2,1,0:T(8,128)(2,1)S(1)}, u32[]{:S(2)}, u32[]{:S(2)}) collective-permute-start(bf16[8,128,128]{2,1,0:T(8,128)(2,1)S(1)} %broadcast_select_fusion.refs_0_), channel_id=1, source_target_pairs={{0,3},{1,0},{2,1},{3,2},{4,7},{5,4},{6,5},{7,6},{8,11},{9,8},{10,9... | collective-permute-start | bytes 786440 | tf_op jit(solution)/shard_map/ppermute | solution.py:30
  9.8 23.2 %collective-permute-start.3 = (bf16[8,128,128]{2,1,0:T(8,128)(2,1)S(1)}, bf16[8,128,128]{2,1,0:T(8,128)(2,1)S(1)}, u32[]{:S(2)}, u32[]{:S(2)}) collective-permute-start(bf16[8,128,128]{2,1,0:T(8,128)(2,1)S(1)} %broadcast_select_fusion.refs_0_), channel_id=1, source_target_pairs={{0,2},{1,3},{2,0},{3,1},{4,6},{5,7},{6,4},{7,5},{8,10},{9,11},{10,... | collective-permute-start | bytes 786440 | tf_op jit(solution)/shard_map/ppermute | solution.py:30
  10.2 25.5 %copy-start.11 = (bf16[128,256]{1,0:T(8,128)(2,1)}, bf16[128,256]{1,0:T(8,128)(2,1)S(1)}, u32[]{:S(2)}) copy-start(bf16[128,256]{1,0:T(8,128)(2,1)S(1)} %collective-permute-done.12.refs_14_) | copy-start | bytes 196612
  10.2 24.3 %collective-permute-start.1 = (bf16[8,128,128]{2,1,0:T(8,128)(2,1)S(1)}, bf16[8,128,128]{2,1,0:T(8,128)(2,1)S(1)}, u32[]{:S(2)}, u32[]{:S(2)}) collective-permute-start(bf16[8,128,128]{2,1,0:T(8,128)(2,1)S(1)} %broadcast_select_fusion.refs_0_), channel_id=1, source_target_pairs={{0,1},{1,2},{2,3},{3,0},{4,5},{5,6},{6,7},{7,4},{8,9},{9,10},{10,1... | collective-permute-start | bytes 786440 | tf_op jit(solution)/shard_map/ppermute | solution.py:30
  11.4 24.3 %copy-start.12 = (bf16[128,256]{1,0:T(8,128)(2,1)}, bf16[128,256]{1,0:T(8,128)(2,1)S(1)}, u32[]{:S(2)}) copy-start(bf16[128,256]{1,0:T(8,128)(2,1)S(1)} %collective-permute-done.10.refs_12_) | copy-start | bytes 196612
  11.4 4.8 %collective-permute-start.7 = (bf16[128,256]{1,0:T(8,128)(2,1)S(1)}, bf16[128,256]{1,0:T(8,128)(2,1)S(1)}, u32[]{:S(2)}, u32[]{:S(2)}) collective-permute-start(bf16[128,256]{1,0:T(8,128)(2,1)S(1)} %subtract_convert_fusion.refs_8_), channel_id=1, source_target_pairs={{0,16},{16,0},{1,17},{17,1},{2,18},{18,2},{3,19},{19,3},{4,20},{20... | collective-permute-start | bytes 196616 | tf_op jit(solution)/shard_map/ppermute | solution.py:30
  12.9 22.9 %copy-start.13 = (bf16[128,256]{1,0:T(8,128)(2,1)}, bf16[128,256]{1,0:T(8,128)(2,1)S(1)}, u32[]{:S(2)}) copy-start(bf16[128,256]{1,0:T(8,128)(2,1)S(1)} %collective-permute-done.8.refs_10_) | copy-start | bytes 196612
  12.9 4.9 %collective-permute-start.13 = (bf16[128,256]{1,0:T(8,128)(2,1)S(1)}, bf16[128,256]{1,0:T(8,128)(2,1)S(1)}, u32[]{:S(2)}, u32[]{:S(2)}) collective-permute-start(bf16[128,256]{1,0:T(8,128)(2,1)S(1)} %collective-permute-done.12.refs_14_), channel_id=1, source_target_pairs={{0,16},{16,0},{1,17},{17,1},{2,18},{18,2},{3,19},{19,3},{4,20},{20... | collective-permute-start | bytes 196616 | tf_op jit(solution)/shard_map/ppermute | solution.py:30
  16.1 32.3 %copy-start.14 = (bf16[128,256]{1,0:T(8,128)(2,1)}, bf16[128,256]{1,0:T(8,128)(2,1)S(1)}, u32[]{:S(2)}) copy-start(bf16[128,256]{1,0:T(8,128)(2,1)S(1)} %collective-permute-done.7.refs_9_) | copy-start | bytes 196612
  16.1 32.2 %collective-permute-start = (bf16[8,128,128]{2,1,0:T(8,128)(2,1)S(1)}, bf16[8,128,128]{2,1,0:T(8,128)(2,1)S(1)}, u32[]{:S(2)}, u32[]{:S(2)}) collective-permute-start(bf16[8,128,128]{2,1,0:T(8,128)(2,1)S(1)} %broadcast_select_fusion.refs_0_), channel_id=1, source_target_pairs={{0,16},{16,0},{1,17},{17,1},{2,18},{18,2},{3,19},{19,3},{4,20},{20... | collective-permute-start | bytes 786440 | tf_op jit(solution)/shard_map/ppermute | solution.py:30
  17.8 30.6 %copy-start.15 = (bf16[128,256]{1,0:T(8,128)(2,1)}, bf16[128,256]{1,0:T(8,128)(2,1)S(1)}, u32[]{:S(2)}) copy-start(bf16[128,256]{1,0:T(8,128)(2,1)S(1)} %collective-permute-done.13.refs_15_) | copy-start | bytes 196612
  17.8 18.0 %collective-permute-start.11 = (bf16[128,256]{1,0:T(8,128)(2,1)S(1)}, bf16[128,256]{1,0:T(8,128)(2,1)S(1)}, u32[]{:S(2)}, u32[]{:S(2)}) collective-permute-start(bf16[128,256]{1,0:T(8,128)(2,1)S(1)} %collective-permute-done.10.refs_12_), channel_id=1, source_target_pairs={{0,16},{16,0},{1,17},{17,1},{2,18},{18,2},{3,19},{19,3},{4,20},{20... | collective-permute-start | bytes 196616 | tf_op jit(solution)/shard_map/ppermute | solution.py:30
  18.8 29.6 %copy-start.4 = (bf16[8,128,128]{2,1,0:T(8,128)(2,1)}, bf16[8,128,128]{2,1,0:T(8,128)(2,1)S(1)}, u32[]{:S(2)}) copy-start(bf16[8,128,128]{2,1,0:T(8,128)(2,1)S(1)} %collective-permute-done.5.refs_6_) | copy-start | bytes 786436
  18.8 29.5 %collective-permute-start.6 = (bf16[8,128,128]{2,1,0:T(8,128)(2,1)S(1)}, bf16[8,128,128]{2,1,0:T(8,128)(2,1)S(1)}, u32[]{:S(2)}, u32[]{:S(2)}) collective-permute-start(bf16[8,128,128]{2,1,0:T(8,128)(2,1)S(1)} %collective-permute-done.5.refs_6_), channel_id=1, source_target_pairs={{0,16},{16,0},{1,17},{17,1},{2,18},{18,2},{3,19},{19,3},{4,20},{20... | collective-permute-start | bytes 786440 | tf_op jit(solution)/shard_map/ppermute | solution.py:30
  33.0 15.4 %copy-start.5 = (bf16[8,128,128]{2,1,0:T(8,128)(2,1)}, bf16[8,128,128]{2,1,0:T(8,128)(2,1)S(1)}, u32[]{:S(2)}) copy-start(bf16[8,128,128]{2,1,0:T(8,128)(2,1)S(1)} %collective-permute-done.3.refs_4_) | copy-start | bytes 786436
  33.0 15.4 %collective-permute-start.4 = (bf16[8,128,128]{2,1,0:T(8,128)(2,1)S(1)}, bf16[8,128,128]{2,1,0:T(8,128)(2,1)S(1)}, u32[]{:S(2)}, u32[]{:S(2)}) collective-permute-start(bf16[8,128,128]{2,1,0:T(8,128)(2,1)S(1)} %collective-permute-done.3.refs_4_), channel_id=1, source_target_pairs={{0,16},{16,0},{1,17},{17,1},{2,18},{18,2},{3,19},{19,3},{4,20},{20... | collective-permute-start | bytes 786440 | tf_op jit(solution)/shard_map/ppermute | solution.py:30
  34.5 13.9 %copy-start.6 = (bf16[8,128,128]{2,1,0:T(8,128)(2,1)}, bf16[8,128,128]{2,1,0:T(8,128)(2,1)S(1)}, u32[]{:S(2)}) copy-start(bf16[8,128,128]{2,1,0:T(8,128)(2,1)S(1)} %collective-permute-done.1.refs_2_) | copy-start | bytes 786436
  34.5 13.9 %collective-permute-start.2 = (bf16[8,128,128]{2,1,0:T(8,128)(2,1)S(1)}, bf16[8,128,128]{2,1,0:T(8,128)(2,1)S(1)}, u32[]{:S(2)}, u32[]{:S(2)}) collective-permute-start(bf16[8,128,128]{2,1,0:T(8,128)(2,1)S(1)} %collective-permute-done.1.refs_2_), channel_id=1, source_target_pairs={{0,16},{16,0},{1,17},{17,1},{2,18},{18,2},{3,19},{19,3},{4,20},{20... | collective-permute-start | bytes 786440 | tf_op jit(solution)/shard_map/ppermute | solution.py:30
  35.8 12.7 %copy-start.16 = (bf16[128,256]{1,0:T(8,128)(2,1)}, bf16[128,256]{1,0:T(8,128)(2,1)S(1)}, u32[]{:S(2)}) copy-start(bf16[128,256]{1,0:T(8,128)(2,1)S(1)} %collective-permute-done.11.refs_13_) | copy-start | bytes 196612
  35.8 12.5 %collective-permute-start.9 = (bf16[128,256]{1,0:T(8,128)(2,1)S(1)}, bf16[128,256]{1,0:T(8,128)(2,1)S(1)}, u32[]{:S(2)}, u32[]{:S(2)}) collective-permute-start(bf16[128,256]{1,0:T(8,128)(2,1)S(1)} %collective-permute-done.8.refs_10_), channel_id=1, source_target_pairs={{0,16},{16,0},{1,17},{17,1},{2,18},{18,2},{3,19},{19,3},{4,20},{20... | collective-permute-start | bytes 196616 | tf_op jit(solution)/shard_map/ppermute | solution.py:30
  48.3 0.6 %copy-start.17 = (bf16[128,256]{1,0:T(8,128)(2,1)}, bf16[128,256]{1,0:T(8,128)(2,1)S(1)}, u32[]{:S(2)}) copy-start(bf16[128,256]{1,0:T(8,128)(2,1)S(1)} %collective-permute-done.9.refs_11_) | copy-start | bytes 196612
  48.3 0.7 %copy-start.7 = (bf16[8,128,128]{2,1,0:T(8,128)(2,1)}, bf16[8,128,128]{2,1,0:T(8,128)(2,1)S(1)}, u32[]{:S(2)}) copy-start(bf16[8,128,128]{2,1,0:T(8,128)(2,1)S(1)} %collective-permute-done.refs_1_) | copy-start | bytes 786436
  48.4 0.8 %copy-start.8 = (bf16[8,128,128]{2,1,0:T(8,128)(2,1)}, bf16[8,128,128]{2,1,0:T(8,128)(2,1)S(1)}, u32[]{:S(2)}) copy-start(bf16[8,128,128]{2,1,0:T(8,128)(2,1)S(1)} %collective-permute-done.6.refs_7_) | copy-start | bytes 786436
  48.4 0.9 %copy-start.9 = (bf16[8,128,128]{2,1,0:T(8,128)(2,1)}, bf16[8,128,128]{2,1,0:T(8,128)(2,1)S(1)}, u32[]{:S(2)}) copy-start(bf16[8,128,128]{2,1,0:T(8,128)(2,1)S(1)} %collective-permute-done.4.refs_5_) | copy-start | bytes 786436
  49.2 0.7 %copy-start.10 = (bf16[8,128,128]{2,1,0:T(8,128)(2,1)}, bf16[8,128,128]{2,1,0:T(8,128)(2,1)S(1)}, u32[]{:S(2)}) copy-start(bf16[8,128,128]{2,1,0:T(8,128)(2,1)S(1)} %collective-permute-done.2.refs_3_) | copy-start | bytes 786436

commit v4 on v3

--- a/solution.py
+++ b/solution.py
@@ -41,14 +41,15 @@
     return out, sources
 
 
-def product_kernel(slot_ref, rf_pos_ref, keep_ref, *refs, pieces, row_blocks, cols):
+def product_kernel(slot_ref, rf_pos_ref, keep_ref, *refs, pieces, rf_groups, row_blocks, cols):
     left_refs = refs[:pieces]
-    rf_refs = refs[pieces:2 * pieces]
-    out_ref = refs[2 * pieces]
-    lhs_scr, rf_scr = refs[2 * pieces + 1:]
+    rf_refs = refs[pieces:pieces + rf_groups]
+    out_ref = refs[pieces + rf_groups]
+    lhs_scr, rf_scr = refs[pieces + rf_groups + 1:]
+    per_group = pieces // rf_groups
     for q in range(pieces):
         at = pl.multiple_of(rf_pos_ref[q] * BLK, BLK)
-        rf_scr[pl.ds(at, BLK), :] = rf_refs[q][...]
+        rf_scr[pl.ds(at, BLK), :] = rf_refs[q // per_group][q % per_group]
     for p in range(pieces):
         for i in range(row_blocks):
             s = slot_ref[p, i]
@@ -70,16 +71,21 @@
 
 def product_call(slot_tbl, rf_pos, keep_patch, left_pieces, rf_pieces):
     pieces = len(left_pieces)
+    rf_groups = len(rf_pieces)
     row_blocks = slot_tbl.shape[1]
-    cols = rf_pieces[0].shape[1]
+    cols = rf_pieces[0].shape[-1]
     smem = pl.BlockSpec(memory_space=pltpu.SMEM)
     vmem = pl.BlockSpec(memory_space=pltpu.VMEM)
     flops = 2 * row_blocks * BLK * pieces * BLK * cols
-    bytes_accessed = pieces * (left_pieces[0].size + rf_pieces[0].size) * 2 + row_blocks * BLK * cols * 2
+    bytes_accessed = (
+        pieces * left_pieces[0].size * 2 + rf_groups * rf_pieces[0].size * 2 + row_blocks * BLK * cols * 2
+    )
     return pl.pallas_call(
-        functools.partial(product_kernel, pieces=pieces, row_blocks=row_blocks, cols=cols),
+        functools.partial(
+            product_kernel, pieces=pieces, rf_groups=rf_groups, row_blocks=row_blocks, cols=cols
+        ),
         out_shape=jax.ShapeDtypeStruct((row_blocks * BLK, cols), jnp.bfloat16),
-        in_specs=[smem, smem, smem] + [vmem] * (2 * pieces),
+        in_specs=[smem, smem, smem] + [vmem] * (pieces + rf_groups),
         out_specs=vmem,
         scratch_shapes=[
             pltpu.VMEM((row_blocks * BLK, pieces * BLK), jnp.bfloat16),
@@ -143,14 +149,24 @@
         and layer_count <= 2
     )
     if use_permutes:
-        pieces, piece_col = ring_gather(packed[0], "col", col_idx, col_count)
-        pieces, piece_layer = ring_gather_list(pieces, "layer", layer_idx, layer_count)
+        own_over_layer = [
+            lax.ppermute(packed[0], "layer", [(s, (s + m) % layer_count) for s in range(layer_count)])
+            for m in range(1, layer_count)
+        ]
+        rf_pair, rf_layer_src = ring_gather(right_factor, "layer", layer_idx, layer_count)
+        rf_pair = jnp.stack(rf_pair)
+        col_pieces, piece_col = ring_gather(packed[0], "col", col_idx, col_count)
+        pieces = [packed[0]] + own_over_layer
+        for k in range(1, col_count):
+            got, _ = ring_gather(col_pieces[k], "layer", layer_idx, layer_count)
+            pieces.extend(got)
+        piece_layer = [(layer_idx - m) % layer_count for k in range(col_count) for m in range(layer_count)]
         piece_col = [piece_col[k] for k in range(col_count) for m in range(layer_count)]
         piece_j = jnp.stack(
             [src_l * col_count + src_c for src_l, src_c in zip(piece_layer, piece_col)]
         ).astype(jnp.int32)
-        rf_pieces, rf_row = ring_gather(right_factor, "row", row_idx, row_count)
-        rf_pieces, rf_layer = ring_gather_list(rf_pieces, "layer", layer_idx, layer_count)
+        rf_pieces, rf_row = ring_gather(rf_pair, "row", row_idx, row_count)
+        rf_layer = [(layer_idx - m) % layer_count for k in range(row_count) for m in range(layer_count)]
         rf_row = [rf_row[k] for k in range(row_count) for m in range(layer_count)]
         rf_q = jnp.stack(
             [src_l * row_count + src_r for src_l, src_r in zip(rf_layer, rf_row)]

time: 54.3 us -> 47.3 us (0.87)
  starting transfers between devices: 17.4 us -> 13.4 us
  waiting for transfers between devices: 24.2 us -> 22.7 us
  other arithmetic: 2.76 us -> 1.97 us
  local copies, waits for them, and re-layouts: 5.38 us -> 4.66 us
    ppermute x14 -> x10, starting transfers between devices: 17.4 us -> 11.9 us  [ring_gather(): pieces.append(lax.ppermute(x, axis, perm))]
    ppermute x14 -> x10, waiting for transfers between devices: 24.2 us -> 22.7 us  [ring_gather(): pieces.append(lax.ppermute(x, axis, perm))]
    ppermute x0 -> x1, starting transfers between devices: none -> 1.49 us  [per_device(): lax.ppermute(packed[0], 'layer', [(s, (s + m) % layer_count) for s in ran...]
    convert_element_type x1, other arithmetic: 0.98 us -> 0.09 us  [per_device(): (unit - 0.5 * square_term.astype(jnp.float32)).astype(jnp.bfloat16)]
    unnamed x38 -> x32, local copies, waits for them, and re-layouts: 2.98 us -> 2.24 us
  transfers between devices with their start and end apart: 14 -> 11, of which waited for: 3 -> 6; matrix products, arithmetic and copies ran while one was open for 9% -> 8% of each run, Pallas kernels for 0% -> 0%
where the time goes in v4:
time: 47.3 us; the launch traced here: 47.1 us
  waiting for transfers between devices  22.7 us (48%)
  starting transfers between devices  13.4 us (28%)
  local copies, waits for them, and re-layouts  4.66 us (10%)
  Pallas kernels  4.19 us (9%)
  other arithmetic  1.97 us (4%)
    ppermute x10, waiting for transfers between devices, ring_gather(): pieces.append(lax.ppermute(x, axis, perm))  22.7 us
    ppermute x10, starting transfers between devices, ring_gather(): pieces.append(lax.ppermute(x, axis, perm))  11.9 us
    pallas_call x1, Pallas kernels, product_call(): pl.pallas_call(functools.partial(product_kernel, pieces=pieces, rf_groups...  4.19 us
    unnamed x32, local copies, waits for them, and re-layouts  2.24 us
    ppermute x1, starting transfers between devices, per_device(): lax.ppermute(packed[0], 'layer', [(s, (s + m) % layer_count) for s in ran...  1.49 us
  transfers between devices with their start and end apart: 11, of which 6 were waited for; matrix products, arithmetic and copies ran while one was open for 8% of the time, Pallas kernels for 0%

profile of v4, /device:TPU:0, one launch (start us, length us, event | category | flops | bytes accessed | tf_op | source)
XLA Modules:
  0.0 47.1 jit_solution(15893766533808966302)
XLA Ops:
  0.0 0.7 %copy-done.4 = s32[64,8]{0,1:T(8,128)S(1)} copy-done((s32[64,8]{0,1:T(8,128)S(1)}, s32[64,8]{0,1:T(8,128)}, u32[]{:S(2)}) %copy-start.4) | copy-done | bytes 2072
  0.8 0.1 copy.16
  0.9 0.1 add_reduce_fusion
  1.1 0.1 select_reduce_fusion
  1.2 0.6 %gather_fusion.1 = bf16[8,128,128]{2,1,0:T(8,128)(2,1)S(1)} fusion(bf16[16,128,128]{2,1,0:T(8,128)(2,1)S(1)} %bitcast.36, s32[1024]{0:T(1024)S(1)} %pad_clamp_fusion), kind=kCustom, calls=%fused_computation.1 | custom fusion | bytes 524320 | tf_op jit(solution)/shard_map/jit(_take)/gather | solution.py:126
  1.8 0.1 broadcast_select_fusion.refs_0_
  2.0 5.1 %collective-permute-start.5 = (bf16[8,128,128]{2,1,0:T(8,128)(2,1)S(1)}, bf16[8,128,128]{2,1,0:T(8,128)(2,1)S(1)}, u32[]{:S(2)}, u32[]{:S(2)}) collective-permute-start(bf16[8,128,128]{2,1,0:T(8,128)(2,1)S(1)} %broadcast_select_fusion.refs_0_), channel_id=1, source_target_pairs={{0,3},{1,0},{2,1},{3,2},{4,7},{5,4},{6,5},{7,6},{8,11},{9,8},{10,9... | collective-permute-start | bytes 786440 | tf_op jit(solution)/shard_map/ppermute | solution.py:30
  7.1 1.0 %collective-permute-start.1 = (bf16[8,128,128]{2,1,0:T(8,128)(2,1)S(1)}, bf16[8,128,128]{2,1,0:T(8,128)(2,1)S(1)}, u32[]{:S(2)}, u32[]{:S(2)}) collective-permute-start(bf16[8,128,128]{2,1,0:T(8,128)(2,1)S(1)} %broadcast_select_fusion.refs_0_), channel_id=1, source_target_pairs={{0,1},{1,2},{2,3},{3,0},{4,5},{5,6},{6,7},{7,4},{8,9},{9,10},{10,1... | collective-permute-start | bytes 786440 | tf_op jit(solution)/shard_map/ppermute | solution.py:30
  8.1 1.5 %collective-permute-start = (bf16[8,128,128]{2,1,0:T(8,128)(2,1)S(1)}, bf16[8,128,128]{2,1,0:T(8,128)(2,1)S(1)}, u32[]{:S(2)}, u32[]{:S(2)}) collective-permute-start(bf16[8,128,128]{2,1,0:T(8,128)(2,1)S(1)} %broadcast_select_fusion.refs_0_), channel_id=1, source_target_pairs={{0,16},{16,0},{1,17},{17,1},{2,18},{18,2},{3,19},{19,3},{4,20},{20... | collective-permute-start | bytes 786440 | tf_op jit(solution)/shard_map/ppermute | solution.py:153
  9.6 0.1 subtract_convert_fusion
  9.7 0.6 %collective-permute-start.7 = (bf16[128,256]{1,0:T(8,128)(2,1)S(1)}, bf16[128,256]{1,0:T(8,128)(2,1)S(1)}, u32[]{:S(2)}, u32[]{:S(2)}) collective-permute-start(bf16[128,256]{1,0:T(8,128)(2,1)S(1)} %subtract_convert_fusion), channel_id=1, source_target_pairs={{0,16},{16,0},{1,17},{17,1},{2,18},{18,2},{3,19},{19,3},{4,20},{20... | collective-permute-start | bytes 196616 | tf_op jit(solution)/shard_map/ppermute | solution.py:30
  10.4 0.1 fusion.8
  10.4 0.1 stack.98
  10.8 0.6 %gather_fusion = s32[8,16]{1,0:T(8,128)S(1)} fusion(s32[16,8]{0,1:T(8,128)S(1)} %copy.14, s32[1024]{0:T(1024)S(1)} %pad_clamp_fusion.1), kind=kCustom, calls=%fused_computation | custom fusion | bytes 1056 | tf_op jit(solution)/shard_map/jit(_take)/gather | solution.py:179
  11.3 0.1 stack.89
  11.4 5.3 %collective-permute-done.7 = bf16[128,256]{1,0:T(8,128)(2,1)S(1)} collective-permute-done((bf16[128,256]{1,0:T(8,128)(2,1)S(1)}, bf16[128,256]{1,0:T(8,128)(2,1)S(1)}, u32[]{:S(2)}, u32[]{:S(2)}) %collective-permute-start.7) | collective-permute-done | bytes 65568 | tf_op jit(solution)/shard_map/ppermute | solution.py:30
  16.8 2.5 %collective-permute-done.10.refs_11_ = bf16[2,128,256]{2,1,0:T(8,128)(2,1)S(1)} collective-permute-done((bf16[2,128,256]{2,1,0:T(8,128)(2,1)S(1)}, bf16[2,128,256]{2,1,0:T(8,128)(2,1)S(1)}, u32[]{:S(2)}, u32[]{:S(2)}) %collective-permute-start.10) | collective-permute-done | bytes 131104 | tf_op jit(solution)/shard_map/ppermute | solution.py:30
  19.3 1.5 %collective-permute-start.9 = (bf16[2,128,256]{2,1,0:T(8,128)(2,1)S(1)}, bf16[2,128,256]{2,1,0:T(8,128)(2,1)S(1)}, u32[]{:S(2)}, u32[]{:S(2)}) collective-permute-start(bf16[2,128,256]{2,1,0:T(8,128)(2,1)S(1)} %pad_maximum_fusion.refs_8_), channel_id=1, source_target_pairs={{0,8},{4,12},{8,0},{12,4},{1,9},{5,13},{9,1},{13,5},{2,10},{6,14},... | collective-permute-start | bytes 393224 | tf_op jit(solution)/shard_map/ppermute | solution.py:30
  20.8 1.5 %collective-permute-start.6 = (bf16[8,128,128]{2,1,0:T(8,128)(2,1)S(1)}, bf16[8,128,128]{2,1,0:T(8,128)(2,1)S(1)}, u32[]{:S(2)}, u32[]{:S(2)}) collective-permute-start(bf16[8,128,128]{2,1,0:T(8,128)(2,1)S(1)} %collective-permute-done.5.refs_6_), channel_id=1, source_target_pairs={{0,16},{16,0},{1,17},{17,1},{2,18},{18,2},{3,19},{19,3},{4,20},{20... | collective-permute-start | bytes 786440 | tf_op jit(solution)/shard_map/ppermute | solution.py:30
  22.3 7.1 %collective-permute-done.3.refs_4_ = bf16[8,128,128]{2,1,0:T(8,128)(2,1)S(1)} collective-permute-done((bf16[8,128,128]{2,1,0:T(8,128)(2,1)S(1)}, bf16[8,128,128]{2,1,0:T(8,128)(2,1)S(1)}, u32[]{:S(2)}, u32[]{:S(2)}) %collective-permute-start.3) | collective-permute-done | bytes 262176 | tf_op jit(solution)/shard_map/ppermute | solution.py:30
  29.4 1.5 %collective-permute-start.4 = (bf16[8,128,128]{2,1,0:T(8,128)(2,1)S(1)}, bf16[8,128,128]{2,1,0:T(8,128)(2,1)S(1)}, u32[]{:S(2)}, u32[]{:S(2)}) collective-permute-start(bf16[8,128,128]{2,1,0:T(8,128)(2,1)S(1)} %collective-permute-done.3.refs_4_), channel_id=1, source_target_pairs={{0,16},{16,0},{1,17},{17,1},{2,18},{18,2},{3,19},{19,3},{4,20},{20... | collective-permute-start | bytes 786440 | tf_op jit(solution)/shard_map/ppermute | solution.py:30
  30.9 0.5 %collective-permute-start.2 = (bf16[8,128,128]{2,1,0:T(8,128)(2,1)S(1)}, bf16[8,128,128]{2,1,0:T(8,128)(2,1)S(1)}, u32[]{:S(2)}, u32[]{:S(2)}) collective-permute-start(bf16[8,128,128]{2,1,0:T(8,128)(2,1)S(1)} %collective-permute-done.1.refs_2_), channel_id=1, source_target_pairs={{0,16},{16,0},{1,17},{17,1},{2,18},{18,2},{3,19},{19,3},{4,20},{20... | collective-permute-start | bytes 786440 | tf_op jit(solution)/shard_map/ppermute | solution.py:30
  31.4 0.7 %broadcast_select_fusion.1.slot_ref = s32[8,16]{1,0:T(8,128)} fusion(s32[8,16]{1,0:T(8,128)S(1)} %gather_fusion, pred[8]{0:T(512)(128)(4,1)S(1)} %compare_and_fusion.1), kind=kLoop, calls=%fused_computation.21 | loop fusion | flops 128 | bytes 1032 | tf_op jit(solution)/shard_map/jit(_take)/select_n | solution.py:179
  32.1 0.8 %dynamic_slice.10 = s32[16,2]{0,1:T(2,128)S(1)} dynamic-slice(s32[64,8]{0,1:T(8,128)} %param.7, s32[]{:T(128)S(6)} %select_n.170, s32[]{:T(128)S(6)} %select_n.183), dynamic_slice_sizes={16,2} | dynamic-slice | bytes 260 | tf_op jit(solution)/shard_map/dynamic_slice | solution.py:130
  32.8 0.7 %copy.18.keep_ref = s32[16,2]{1,0:T(8,128)} copy(s32[16,2]{0,1:T(2,128)S(1)} %dynamic_slice.10) | data formatting | bytes 256
  33.5 0.1 stack.107
  33.7 0.6 %fusion.1.rf_pos_ref = s32[8]{0:T(128)} fusion(s32[8]{0:T(128)S(1)} %stack.107, s32[]{:T(128)S(6)} %axis_index.33, s32[]{:T(128)S(6)} %axis_index.35), kind=kLoop, calls=%fused_computation.34 | loop fusion | flops 360 | bytes 72 | tf_op jit(solution)/shard_map/add | solution.py:174
  34.3 3.8 %collective-permute-done.8.refs_9_ = bf16[2,128,256]{2,1,0:T(8,128)(2,1)S(1)} collective-permute-done((bf16[2,128,256]{2,1,0:T(8,128)(2,1)S(1)}, bf16[2,128,256]{2,1,0:T(8,128)(2,1)S(1)}, u32[]{:S(2)}, u32[]{:S(2)}) %collective-permute-start.8) | collective-permute-done | bytes 131104 | tf_op jit(solution)/shard_map/ppermute | solution.py:30
  38.1 0.5 %collective-permute-done.4.refs_5_ = bf16[8,128,128]{2,1,0:T(8,128)(2,1)S(1)} collective-permute-done((bf16[8,128,128]{2,1,0:T(8,128)(2,1)S(1)}, bf16[8,128,128]{2,1,0:T(8,128)(2,1)S(1)}, u32[]{:S(2)}, u32[]{:S(2)}) %collective-permute-start.4) | collective-permute-done | bytes 262176 | tf_op jit(solution)/shard_map/ppermute | solution.py:30
  38.6 3.5 %collective-permute-done.2.refs_3_ = bf16[8,128,128]{2,1,0:T(8,128)(2,1)S(1)} collective-permute-done((bf16[8,128,128]{2,1,0:T(8,128)(2,1)S(1)}, bf16[8,128,128]{2,1,0:T(8,128)(2,1)S(1)}, u32[]{:S(2)}, u32[]{:S(2)}) %collective-permute-start.2) | collective-permute-done | bytes 262176 | tf_op jit(solution)/shard_map/ppermute | solution.py:30
  42.3 0.7 %copy-done.11 = bf16[8,128,128]{2,1,0:T(8,128)(2,1)} copy-done((bf16[8,128,128]{2,1,0:T(8,128)(2,1)}, bf16[8,128,128]{2,1,0:T(8,128)(2,1)S(1)}, u32[]{:S(2)}) %copy-start.11) | copy-done | bytes 262168
  42.9 4.2 %shard_map.46 = bf16[2048,256]{1,0:T(8,128)(2,1)} custom-call(s32[8,16]{1,0:T(8,128)} %broadcast_select_fusion.1.slot_ref, s32[8]{0:T(128)} %fusion.1.rf_pos_ref, s32[16,2]{1,0:T(8,128)} %copy.18.keep_ref, bf16[8,128,128]{2,1,0:T(8,128)(2,1)} %copy-done.1, bf16[8,128,128]{2,1,0:T(8,128)(2,1)} %copy-done.8, bf16[8,128,128]{2,1,0:T(8,128)(2,1)} %copy-done.7, ...), custom_call_target="tpu_custom_call" | custom-call | flops 1073741824 | bytes 3670016 | tf_op jit(solution)/shard_map/pallas_call | solution.py:83
  (53 shorter events, 0.6 us)
Async XLA Ops:
  0.0 1.2 %copy-start = (bf16[2048,128]{1,0:T(8,128)(2,1)S(1)}, bf16[2048,128]{1,0:T(8,128)(2,1)}, u32[]{:S(2)}) copy-start(bf16[2048,128]{1,0:T(8,128)(2,1)} %param.4) | copy-start | bytes 1572868
  0.0 0.7 %copy-start.4 = (s32[64,8]{0,1:T(8,128)S(1)}, s32[64,8]{0,1:T(8,128)}, u32[]{:S(2)}) copy-start(s32[64,8]{0,1:T(8,128)} %param.6) | copy-start | bytes 6148
  1.8 7.7 %copy-start.2 = (bf16[128,256]{1,0:T(8,128)(2,1)S(1)}, bf16[128,256]{1,0:T(8,128)(2,1)}, u32[]{:S(2)}) copy-start(bf16[128,256]{1,0:T(8,128)(2,1)} %param.5) | copy-start | bytes 196612
  1.9 8.7 %copy-start.1 = (bf16[8,128,128]{2,1,0:T(8,128)(2,1)}, bf16[8,128,128]{2,1,0:T(8,128)(2,1)S(1)}, u32[]{:S(2)}) copy-start(bf16[8,128,128]{2,1,0:T(8,128)(2,1)S(1)} %broadcast_select_fusion.refs_0_) | copy-start | bytes 786436
  2.0 18.9 %collective-permute-start.5 = (bf16[8,128,128]{2,1,0:T(8,128)(2,1)S(1)}, bf16[8,128,128]{2,1,0:T(8,128)(2,1)S(1)}, u32[]{:S(2)}, u32[]{:S(2)}) collective-permute-start(bf16[8,128,128]{2,1,0:T(8,128)(2,1)S(1)} %broadcast_select_fusion.refs_0_), channel_id=1, source_target_pairs={{0,3},{1,0},{2,1},{3,2},{4,7},{5,4},{6,5},{7,6},{8,11},{9,8},{10,9... | collective-permute-start | bytes 786440 | tf_op jit(solution)/shard_map/ppermute | solution.py:30
  7.1 22.3 %collective-permute-start.3 = (bf16[8,128,128]{2,1,0:T(8,128)(2,1)S(1)}, bf16[8,128,128]{2,1,0:T(8,128)(2,1)S(1)}, u32[]{:S(2)}, u32[]{:S(2)}) collective-permute-start(bf16[8,128,128]{2,1,0:T(8,128)(2,1)S(1)} %broadcast_select_fusion.refs_0_), channel_id=1, source_target_pairs={{0,2},{1,3},{2,0},{3,1},{4,6},{5,7},{6,4},{7,5},{8,10},{9,11},{10,... | collective-permute-start | bytes 786440 | tf_op jit(solution)/shard_map/ppermute | solution.py:30
  7.1 23.8 %collective-permute-start.1 = (bf16[8,128,128]{2,1,0:T(8,128)(2,1)S(1)}, bf16[8,128,128]{2,1,0:T(8,128)(2,1)S(1)}, u32[]{:S(2)}, u32[]{:S(2)}) collective-permute-start(bf16[8,128,128]{2,1,0:T(8,128)(2,1)S(1)} %broadcast_select_fusion.refs_0_), channel_id=1, source_target_pairs={{0,1},{1,2},{2,3},{3,0},{4,5},{5,6},{6,7},{7,4},{8,9},{9,10},{10,1... | collective-permute-start | bytes 786440 | tf_op jit(solution)/shard_map/ppermute | solution.py:30
  8.1 30.0 %collective-permute-start = (bf16[8,128,128]{2,1,0:T(8,128)(2,1)S(1)}, bf16[8,128,128]{2,1,0:T(8,128)(2,1)S(1)}, u32[]{:S(2)}, u32[]{:S(2)}) collective-permute-start(bf16[8,128,128]{2,1,0:T(8,128)(2,1)S(1)} %broadcast_select_fusion.refs_0_), channel_id=1, source_target_pairs={{0,16},{16,0},{1,17},{17,1},{2,18},{18,2},{3,19},{19,3},{4,20},{20... | collective-permute-start | bytes 786440 | tf_op jit(solution)/shard_map/ppermute | solution.py:153
  9.7 7.0 %collective-permute-start.7 = (bf16[128,256]{1,0:T(8,128)(2,1)S(1)}, bf16[128,256]{1,0:T(8,128)(2,1)S(1)}, u32[]{:S(2)}, u32[]{:S(2)}) collective-permute-start(bf16[128,256]{1,0:T(8,128)(2,1)S(1)} %subtract_convert_fusion), channel_id=1, source_target_pairs={{0,16},{16,0},{1,17},{17,1},{2,18},{18,2},{3,19},{19,3},{4,20},{20... | collective-permute-start | bytes 196616 | tf_op jit(solution)/shard_map/ppermute | solution.py:30
  16.7 25.5 %copy-start.3 = (bf16[2,128,256]{2,1,0:T(8,128)(2,1)}, bf16[2,128,256]{2,1,0:T(8,128)(2,1)S(1)}, u32[]{:S(2)}) copy-start(bf16[2,128,256]{2,1,0:T(8,128)(2,1)S(1)} %pad_maximum_fusion.refs_8_) | copy-start | bytes 393220
  16.7 2.6 %collective-permute-start.10 = (bf16[2,128,256]{2,1,0:T(8,128)(2,1)S(1)}, bf16[2,128,256]{2,1,0:T(8,128)(2,1)S(1)}, u32[]{:S(2)}, u32[]{:S(2)}) collective-permute-start(bf16[2,128,256]{2,1,0:T(8,128)(2,1)S(1)} %pad_maximum_fusion.refs_8_), channel_id=1, source_target_pairs={{0,12},{4,0},{8,4},{12,8},{1,13},{5,1},{9,5},{13,9},{2,14},{6,2},{... | collective-permute-start | bytes 393224 | tf_op jit(solution)/shard_map/ppermute | solution.py:30
  19.3 22.9 %copy-start.12 = (bf16[2,128,256]{2,1,0:T(8,128)(2,1)}, bf16[2,128,256]{2,1,0:T(8,128)(2,1)S(1)}, u32[]{:S(2)}) copy-start(bf16[2,128,256]{2,1,0:T(8,128)(2,1)S(1)} %collective-permute-done.10.refs_11_) | copy-start | bytes 393220
  19.3 14.3 %collective-permute-start.9 = (bf16[2,128,256]{2,1,0:T(8,128)(2,1)S(1)}, bf16[2,128,256]{2,1,0:T(8,128)(2,1)S(1)}, u32[]{:S(2)}, u32[]{:S(2)}) collective-permute-start(bf16[2,128,256]{2,1,0:T(8,128)(2,1)S(1)} %pad_maximum_fusion.refs_8_), channel_id=1, source_target_pairs={{0,8},{4,12},{8,0},{12,4},{1,9},{5,13},{9,1},{13,5},{2,10},{6,14},... | collective-permute-start | bytes 393224 | tf_op jit(solution)/shard_map/ppermute | solution.py:30
  20.8 21.4 %copy-start.5 = (bf16[8,128,128]{2,1,0:T(8,128)(2,1)}, bf16[8,128,128]{2,1,0:T(8,128)(2,1)S(1)}, u32[]{:S(2)}) copy-start(bf16[8,128,128]{2,1,0:T(8,128)(2,1)S(1)} %collective-permute-done.5.refs_6_) | copy-start | bytes 786436
  20.8 17.2 %collective-permute-start.6 = (bf16[8,128,128]{2,1,0:T(8,128)(2,1)S(1)}, bf16[8,128,128]{2,1,0:T(8,128)(2,1)S(1)}, u32[]{:S(2)}, u32[]{:S(2)}) collective-permute-start(bf16[8,128,128]{2,1,0:T(8,128)(2,1)S(1)} %collective-permute-done.5.refs_6_), channel_id=1, source_target_pairs={{0,16},{16,0},{1,17},{17,1},{2,18},{18,2},{3,19},{19,3},{4,20},{20... | collective-permute-start | bytes 786440 | tf_op jit(solution)/shard_map/ppermute | solution.py:30
  29.4 12.8 %copy-start.6 = (bf16[8,128,128]{2,1,0:T(8,128)(2,1)}, bf16[8,128,128]{2,1,0:T(8,128)(2,1)S(1)}, u32[]{:S(2)}) copy-start(bf16[8,128,128]{2,1,0:T(8,128)(2,1)S(1)} %collective-permute-done.3.refs_4_) | copy-start | bytes 786436
  29.4 9.2 %collective-permute-start.4 = (bf16[8,128,128]{2,1,0:T(8,128)(2,1)S(1)}, bf16[8,128,128]{2,1,0:T(8,128)(2,1)S(1)}, u32[]{:S(2)}, u32[]{:S(2)}) collective-permute-start(bf16[8,128,128]{2,1,0:T(8,128)(2,1)S(1)} %collective-permute-done.3.refs_4_), channel_id=1, source_target_pairs={{0,16},{16,0},{1,17},{17,1},{2,18},{18,2},{3,19},{19,3},{4,20},{20... | collective-permute-start | bytes 786440 | tf_op jit(solution)/shard_map/ppermute | solution.py:30
  30.9 11.3 %copy-start.7 = (bf16[8,128,128]{2,1,0:T(8,128)(2,1)}, bf16[8,128,128]{2,1,0:T(8,128)(2,1)S(1)}, u32[]{:S(2)}) copy-start(bf16[8,128,128]{2,1,0:T(8,128)(2,1)S(1)} %collective-permute-done.1.refs_2_) | copy-start | bytes 786436
  30.9 11.3 %collective-permute-start.2 = (bf16[8,128,128]{2,1,0:T(8,128)(2,1)S(1)}, bf16[8,128,128]{2,1,0:T(8,128)(2,1)S(1)}, u32[]{:S(2)}, u32[]{:S(2)}) collective-permute-start(bf16[8,128,128]{2,1,0:T(8,128)(2,1)S(1)} %collective-permute-done.1.refs_2_), channel_id=1, source_target_pairs={{0,16},{16,0},{1,17},{17,1},{2,18},{18,2},{3,19},{19,3},{4,20},{20... | collective-permute-start | bytes 786440 | tf_op jit(solution)/shard_map/ppermute | solution.py:30
  33.6 8.6 %copy-start.13 = (bf16[2,128,256]{2,1,0:T(8,128)(2,1)}, bf16[2,128,256]{2,1,0:T(8,128)(2,1)S(1)}, u32[]{:S(2)}) copy-start(bf16[2,128,256]{2,1,0:T(8,128)(2,1)S(1)} %collective-permute-done.9.refs_10_) | copy-start | bytes 393220
  33.6 4.4 %collective-permute-start.8 = (bf16[2,128,256]{2,1,0:T(8,128)(2,1)S(1)}, bf16[2,128,256]{2,1,0:T(8,128)(2,1)S(1)}, u32[]{:S(2)}, u32[]{:S(2)}) collective-permute-start(bf16[2,128,256]{2,1,0:T(8,128)(2,1)S(1)} %pad_maximum_fusion.refs_8_), channel_id=1, source_target_pairs={{0,4},{4,8},{8,12},{12,0},{1,5},{5,9},{9,13},{13,1},{2,6},{6,10},{... | collective-permute-start | bytes 393224 | tf_op jit(solution)/shard_map/ppermute | solution.py:30
  38.0 4.2 %copy-start.14 = (bf16[2,128,256]{2,1,0:T(8,128)(2,1)}, bf16[2,128,256]{2,1,0:T(8,128)(2,1)S(1)}, u32[]{:S(2)}) copy-start(bf16[2,128,256]{2,1,0:T(8,128)(2,1)S(1)} %collective-permute-done.8.refs_9_) | copy-start | bytes 393220
  38.1 4.2 %copy-start.8 = (bf16[8,128,128]{2,1,0:T(8,128)(2,1)}, bf16[8,128,128]{2,1,0:T(8,128)(2,1)S(1)}, u32[]{:S(2)}) copy-start(bf16[8,128,128]{2,1,0:T(8,128)(2,1)S(1)} %collective-permute-done.refs_1_) | copy-start | bytes 786436
  38.1 4.2 %copy-start.9 = (bf16[8,128,128]{2,1,0:T(8,128)(2,1)}, bf16[8,128,128]{2,1,0:T(8,128)(2,1)S(1)}, u32[]{:S(2)}) copy-start(bf16[8,128,128]{2,1,0:T(8,128)(2,1)S(1)} %collective-permute-done.6.refs_7_) | copy-start | bytes 786436
  38.6 3.6 %copy-start.10 = (bf16[8,128,128]{2,1,0:T(8,128)(2,1)}, bf16[8,128,128]{2,1,0:T(8,128)(2,1)S(1)}, u32[]{:S(2)}) copy-start(bf16[8,128,128]{2,1,0:T(8,128)(2,1)S(1)} %collective-permute-done.4.refs_5_) | copy-start | bytes 786436
  42.2 0.7 %copy-start.11 = (bf16[8,128,128]{2,1,0:T(8,128)(2,1)}, bf16[8,128,128]{2,1,0:T(8,128)(2,1)S(1)}, u32[]{:S(2)}) copy-start(bf16[8,128,128]{2,1,0:T(8,128)(2,1)S(1)} %collective-permute-done.2.refs_3_) | copy-start | bytes 786436

commit v5 on v4

--- a/solution.py
+++ b/solution.py
@@ -149,13 +149,20 @@
         and layer_count <= 2
     )
     if use_permutes:
+        rf_pair, rf_layer_src = ring_gather(right_factor, "layer", layer_idx, layer_count)
+        rf_pair = jnp.stack(rf_pair)
         own_over_layer = [
             lax.ppermute(packed[0], "layer", [(s, (s + m) % layer_count) for s in range(layer_count)])
             for m in range(1, layer_count)
         ]
-        rf_pair, rf_layer_src = ring_gather(right_factor, "layer", layer_idx, layer_count)
-        rf_pair = jnp.stack(rf_pair)
-        col_pieces, piece_col = ring_gather(packed[0], "col", col_idx, col_count)
+        def col_shift(x, k):
+            return lax.ppermute(x, "col", [(s, (s + k) % col_count) for s in range(col_count)])
+
+        col_pieces = {1: col_shift(packed[0], 1)}
+        later, col_pieces[1] = lax.optimization_barrier((packed[0], col_pieces[1]))
+        for k in range(2, col_count):
+            col_pieces[k] = col_shift(later, k)
+        piece_col = [(col_idx - k) % col_count for k in range(col_count)]
         pieces = [packed[0]] + own_over_layer
         for k in range(1, col_count):
             got, _ = ring_gather(col_pieces[k], "layer", layer_idx, layer_count)

time: 47.3 us -> 45.1 us (0.953)
  waiting for transfers between devices: 22.7 us -> 20.3 us
  local copies, waits for them, and re-layouts: 4.66 us -> 5.51 us
  starting transfers between devices: 13.4 us -> 12.8 us
    ppermute x10 -> x7, waiting for transfers between devices: 22.7 us -> 5 us  [ring_gather(): pieces.append(lax.ppermute(x, axis, perm))]
    ppermute x0 -> x3, waiting for transfers between devices: none -> 15.3 us  [col_shift(): lax.ppermute(x, 'col', [(s, (s + k) % col_count) for s in range(col_count)])]
    ppermute x10 -> x7, starting transfers between devices: 11.9 us -> 6.44 us  [ring_gather(): pieces.append(lax.ppermute(x, axis, perm))]
    ppermute x0 -> x3, starting transfers between devices: none -> 4.82 us  [col_shift(): lax.ppermute(x, 'col', [(s, (s + k) % col_count) for s in range(col_count)])]
    unnamed x32, local copies, waits for them, and re-layouts: 2.24 us -> 3.1 us
  transfers between devices with their start and end apart: 11 -> 11, of which waited for: 6 -> 5; matrix products, arithmetic and copies ran while one was open for 8% -> 9% of each run, Pallas kernels for 0% -> 0%
where the time goes in v5:
time: 45.1 us; the launch traced here: 44.9 us
  waiting for transfers between devices  20.3 us (45%)
  starting transfers between devices  12.8 us (28%)
  local copies, waits for them, and re-layouts  5.51 us (12%)
  Pallas kernels  4.19 us (9%)
  other arithmetic  1.97 us (4%)
    ppermute x3, waiting for transfers between devices, col_shift(): lax.ppermute(x, 'col', [(s, (s + k) % col_count) for s in range(col_count)])  15.3 us
    ppermute x7, starting transfers between devices, ring_gather(): pieces.append(lax.ppermute(x, axis, perm))  6.44 us
    ppermute x7, waiting for transfers between devices, ring_gather(): pieces.append(lax.ppermute(x, axis, perm))  5 us
    ppermute x3, starting transfers between devices, col_shift(): lax.ppermute(x, 'col', [(s, (s + k) % col_count) for s in range(col_count)])  4.82 us
    pallas_call x1, Pallas kernels, product_call(): pl.pallas_call(functools.partial(product_kernel, pieces=pieces, rf_groups...  4.19 us
    unnamed x32, local copies, waits for them, and re-layouts  3.1 us
    ppermute x1, starting transfers between devices, per_device(): lax.ppermute(packed[0], 'layer', [(s, (s + m) % layer_count) for s in ran...  1.49 us
  transfers between devices with their start and end apart: 11, of which 5 were waited for; matrix products, arithmetic and copies ran while one was open for 9% of the time, Pallas kernels for 0%

profile of v5, /device:TPU:0, one launch (start us, length us, event | category | flops | bytes accessed | tf_op | source)
XLA Modules:
  0.0 44.9 jit_solution(16679946386540272500)
XLA Ops:
  0.0 0.7 %copy-done.4 = s32[64,8]{0,1:T(8,128)S(1)} copy-done((s32[64,8]{0,1:T(8,128)S(1)}, s32[64,8]{0,1:T(8,128)}, u32[]{:S(2)}) %copy-start.4) | copy-done | bytes 2072
  0.8 0.1 copy.16
  0.9 0.1 add_reduce_fusion
  1.1 0.1 select_reduce_fusion
  1.2 0.6 %gather_fusion.1 = bf16[8,128,128]{2,1,0:T(8,128)(2,1)S(1)} fusion(bf16[16,128,128]{2,1,0:T(8,128)(2,1)S(1)} %bitcast.36, s32[1024]{0:T(1024)S(1)} %pad_clamp_fusion), kind=kCustom, calls=%fused_computation.1 | custom fusion | bytes 524320 | tf_op jit(solution)/shard_map/jit(_take)/gather | solution.py:126
  1.8 0.1 broadcast_select_fusion.refs_0_
  2.0 3.1 %collective-permute-start.1 = (bf16[8,128,128]{2,1,0:T(8,128)(2,1)S(1)}, bf16[8,128,128]{2,1,0:T(8,128)(2,1)S(1)}, u32[]{:S(2)}, u32[]{:S(2)}) collective-permute-start(bf16[8,128,128]{2,1,0:T(8,128)(2,1)S(1)} %broadcast_select_fusion.refs_0_), channel_id=1, source_target_pairs={{0,1},{1,2},{2,3},{3,0},{4,5},{5,6},{6,7},{7,4},{8,9},{9,10},{10,1... | collective-permute-start | bytes 786440 | tf_op jit(solution)/shard_map/ppermute | solution.py:159
  5.0 1.5 %collective-permute-start = (bf16[8,128,128]{2,1,0:T(8,128)(2,1)S(1)}, bf16[8,128,128]{2,1,0:T(8,128)(2,1)S(1)}, u32[]{:S(2)}, u32[]{:S(2)}) collective-permute-start(bf16[8,128,128]{2,1,0:T(8,128)(2,1)S(1)} %broadcast_select_fusion.refs_0_), channel_id=1, source_target_pairs={{0,16},{16,0},{1,17},{17,1},{2,18},{18,2},{3,19},{19,3},{4,20},{20... | collective-permute-start | bytes 786440 | tf_op jit(solution)/shard_map/ppermute | solution.py:155
  6.5 0.1 subtract_convert_fusion
  6.6 0.6 %collective-permute-start.7 = (bf16[128,256]{1,0:T(8,128)(2,1)S(1)}, bf16[128,256]{1,0:T(8,128)(2,1)S(1)}, u32[]{:S(2)}, u32[]{:S(2)}) collective-permute-start(bf16[128,256]{1,0:T(8,128)(2,1)S(1)} %subtract_convert_fusion), channel_id=1, source_target_pairs={{0,16},{16,0},{1,17},{17,1},{2,18},{18,2},{3,19},{19,3},{4,20},{20... | collective-permute-start | bytes 196616 | tf_op jit(solution)/shard_map/ppermute | solution.py:30
  7.6 0.1 stack.98
  7.7 0.6 %gather_fusion = s32[8,16]{1,0:T(8,128)S(1)} fusion(s32[16,8]{0,1:T(8,128)S(1)} %copy.14, s32[1024]{0:T(1024)S(1)} %pad_clamp_fusion.1), kind=kCustom, calls=%fused_computation | custom fusion | bytes 1056 | tf_op jit(solution)/shard_map/jit(_take)/gather | solution.py:186
  8.3 0.1 stack.89
  8.4 5.0 %collective-permute-done.1.refs_2_ = bf16[8,128,128]{2,1,0:T(8,128)(2,1)S(1)} collective-permute-done((bf16[8,128,128]{2,1,0:T(8,128)(2,1)S(1)}, bf16[8,128,128]{2,1,0:T(8,128)(2,1)S(1)}, u32[]{:S(2)}, u32[]{:S(2)}) %collective-permute-start.1) | collective-permute-done | bytes 262176 | tf_op jit(solution)/shard_map/ppermute | solution.py:159
  13.4 1.7 %collective-permute-start.5 = (bf16[8,128,128]{2,1,0:T(8,128)(2,1)S(1)}, bf16[8,128,128]{2,1,0:T(8,128)(2,1)S(1)}, u32[]{:S(2)}, u32[]{:S(2)}) collective-permute-start(bf16[8,128,128]{2,1,0:T(8,128)(2,1)S(1)} %broadcast_select_fusion.refs_0_), channel_id=1, source_target_pairs={{0,3},{1,0},{2,1},{3,2},{4,7},{5,4},{6,5},{7,6},{8,11},{9,8},{10,9... | collective-permute-start | bytes 786440 | tf_op jit(solution)/shard_map/ppermute | solution.py:159
  15.2 1.6 %collective-permute-start.9 = (bf16[2,128,256]{2,1,0:T(8,128)(2,1)S(1)}, bf16[2,128,256]{2,1,0:T(8,128)(2,1)S(1)}, u32[]{:S(2)}, u32[]{:S(2)}) collective-permute-start(bf16[2,128,256]{2,1,0:T(8,128)(2,1)S(1)} %pad_maximum_fusion.refs_8_), channel_id=1, source_target_pairs={{0,8},{4,12},{8,0},{12,4},{1,9},{5,13},{9,1},{13,5},{2,10},{6,14},... | collective-permute-start | bytes 393224 | tf_op jit(solution)/shard_map/ppermute | solution.py:30
  16.8 1.2 %collective-permute-done.10.refs_11_ = bf16[2,128,256]{2,1,0:T(8,128)(2,1)S(1)} collective-permute-done((bf16[2,128,256]{2,1,0:T(8,128)(2,1)S(1)}, bf16[2,128,256]{2,1,0:T(8,128)(2,1)S(1)}, u32[]{:S(2)}, u32[]{:S(2)}) %collective-permute-start.10) | collective-permute-done | bytes 131104 | tf_op jit(solution)/shard_map/ppermute | solution.py:30
  18.0 1.5 %collective-permute-start.2 = (bf16[8,128,128]{2,1,0:T(8,128)(2,1)S(1)}, bf16[8,128,128]{2,1,0:T(8,128)(2,1)S(1)}, u32[]{:S(2)}, u32[]{:S(2)}) collective-permute-start(bf16[8,128,128]{2,1,0:T(8,128)(2,1)S(1)} %collective-permute-done.1.refs_2_), channel_id=1, source_target_pairs={{0,16},{16,0},{1,17},{17,1},{2,18},{18,2},{3,19},{19,3},{4,20},{20... | collective-permute-start | bytes 786440 | tf_op jit(solution)/shard_map/ppermute | solution.py:30
  19.5 2.8 %collective-permute-done.5.refs_6_ = bf16[8,128,128]{2,1,0:T(8,128)(2,1)S(1)} collective-permute-done((bf16[8,128,128]{2,1,0:T(8,128)(2,1)S(1)}, bf16[8,128,128]{2,1,0:T(8,128)(2,1)S(1)}, u32[]{:S(2)}, u32[]{:S(2)}) %collective-permute-start.5) | collective-permute-done | bytes 262176 | tf_op jit(solution)/shard_map/ppermute | solution.py:159
  22.3 1.2 %collective-permute-start.6 = (bf16[8,128,128]{2,1,0:T(8,128)(2,1)S(1)}, bf16[8,128,128]{2,1,0:T(8,128)(2,1)S(1)}, u32[]{:S(2)}, u32[]{:S(2)}) collective-permute-start(bf16[8,128,128]{2,1,0:T(8,128)(2,1)S(1)} %collective-permute-done.5.refs_6_), channel_id=1, source_target_pairs={{0,16},{16,0},{1,17},{17,1},{2,18},{18,2},{3,19},{19,3},{4,20},{20... | collective-permute-start | bytes 786440 | tf_op jit(solution)/shard_map/ppermute | solution.py:30
  23.4 7.5 %collective-permute-done.3.refs_4_ = bf16[8,128,128]{2,1,0:T(8,128)(2,1)S(1)} collective-permute-done((bf16[8,128,128]{2,1,0:T(8,128)(2,1)S(1)}, bf16[8,128,128]{2,1,0:T(8,128)(2,1)S(1)}, u32[]{:S(2)}, u32[]{:S(2)}) %collective-permute-start.3) | collective-permute-done | bytes 262176 | tf_op jit(solution)/shard_map/ppermute | solution.py:159
  30.9 1.5 %collective-permute-start.4 = (bf16[8,128,128]{2,1,0:T(8,128)(2,1)S(1)}, bf16[8,128,128]{2,1,0:T(8,128)(2,1)S(1)}, u32[]{:S(2)}, u32[]{:S(2)}) collective-permute-start(bf16[8,128,128]{2,1,0:T(8,128)(2,1)S(1)} %collective-permute-done.3.refs_4_), channel_id=1, source_target_pairs={{0,16},{16,0},{1,17},{17,1},{2,18},{18,2},{3,19},{19,3},{4,20},{20... | collective-permute-start | bytes 786440 | tf_op jit(solution)/shard_map/ppermute | solution.py:30
  32.4 0.7 %broadcast_select_fusion.1.slot_ref = s32[8,16]{1,0:T(8,128)} fusion(s32[8,16]{1,0:T(8,128)S(1)} %gather_fusion, pred[8]{0:T(512)(128)(4,1)S(1)} %compare_and_fusion.1), kind=kLoop, calls=%fused_computation.21 | loop fusion | flops 128 | bytes 1032 | tf_op jit(solution)/shard_map/jit(_take)/select_n | solution.py:186
  33.1 0.8 %dynamic_slice.10 = s32[16,2]{0,1:T(2,128)S(1)} dynamic-slice(s32[64,8]{0,1:T(8,128)} %param.7, s32[]{:T(128)S(6)} %select_n.170, s32[]{:T(128)S(6)} %select_n.183), dynamic_slice_sizes={16,2} | dynamic-slice | bytes 260 | tf_op jit(solution)/shard_map/dynamic_slice | solution.py:130
  33.8 0.7 %copy.18.keep_ref = s32[16,2]{1,0:T(8,128)} copy(s32[16,2]{0,1:T(2,128)S(1)} %dynamic_slice.10) | data formatting | bytes 256
  34.7 0.6 %fusion.1.rf_pos_ref = s32[8]{0:T(128)} fusion(s32[8]{0:T(128)S(1)} %stack.107, s32[]{:T(128)S(6)} %axis_index.33, s32[]{:T(128)S(6)} %axis_index.35), kind=kLoop, calls=%fused_computation.34 | loop fusion | flops 360 | bytes 72 | tf_op jit(solution)/shard_map/add | solution.py:181
  35.3 3.8 %collective-permute-done.8.refs_9_ = bf16[2,128,256]{2,1,0:T(8,128)(2,1)S(1)} collective-permute-done((bf16[2,128,256]{2,1,0:T(8,128)(2,1)S(1)}, bf16[2,128,256]{2,1,0:T(8,128)(2,1)S(1)}, u32[]{:S(2)}, u32[]{:S(2)}) %collective-permute-start.8) | collective-permute-done | bytes 131104 | tf_op jit(solution)/shard_map/ppermute | solution.py:30
  39.2 0.5 %copy-done.14 = bf16[2,128,256]{2,1,0:T(8,128)(2,1)} copy-done((bf16[2,128,256]{2,1,0:T(8,128)(2,1)}, bf16[2,128,256]{2,1,0:T(8,128)(2,1)S(1)}, u32[]{:S(2)}) %copy-start.14) | copy-done | bytes 131096
  39.7 0.1 copy-done.6
  39.8 0.1 copy-done.9
  40.0 0.7 %copy-done.11 = bf16[8,128,128]{2,1,0:T(8,128)(2,1)} copy-done((bf16[8,128,128]{2,1,0:T(8,128)(2,1)}, bf16[8,128,128]{2,1,0:T(8,128)(2,1)S(1)}, u32[]{:S(2)}) %copy-start.11) | copy-done | bytes 262168
  40.7 4.2 %shard_map.46 = bf16[2048,256]{1,0:T(8,128)(2,1)} custom-call(s32[8,16]{1,0:T(8,128)} %broadcast_select_fusion.1.slot_ref, s32[8]{0:T(128)} %fusion.1.rf_pos_ref, s32[16,2]{1,0:T(8,128)} %copy.18.keep_ref, bf16[8,128,128]{2,1,0:T(8,128)(2,1)} %copy-done.1, bf16[8,128,128]{2,1,0:T(8,128)(2,1)} %copy-done.6, bf16[8,128,128]{2,1,0:T(8,128)(2,1)} %copy-done.5, ...), custom_call_target="tpu_custom_call" | custom-call | flops 1073741824 | bytes 3670016 | tf_op jit(solution)/shard_map/pallas_call | solution.py:83
  (53 shorter events, 0.9 us)
Async XLA Ops:
  0.0 1.2 %copy-start = (bf16[2048,128]{1,0:T(8,128)(2,1)S(1)}, bf16[2048,128]{1,0:T(8,128)(2,1)}, u32[]{:S(2)}) copy-start(bf16[2048,128]{1,0:T(8,128)(2,1)} %param.4) | copy-start | bytes 1572868
  0.0 0.7 %copy-start.4 = (s32[64,8]{0,1:T(8,128)S(1)}, s32[64,8]{0,1:T(8,128)}, u32[]{:S(2)}) copy-start(s32[64,8]{0,1:T(8,128)} %param.6) | copy-start | bytes 6148
  1.8 4.7 %copy-start.2 = (bf16[128,256]{1,0:T(8,128)(2,1)S(1)}, bf16[128,256]{1,0:T(8,128)(2,1)}, u32[]{:S(2)}) copy-start(bf16[128,256]{1,0:T(8,128)(2,1)} %param.5) | copy-start | bytes 196612
  1.9 13.2 %copy-start.1 = (bf16[8,128,128]{2,1,0:T(8,128)(2,1)}, bf16[8,128,128]{2,1,0:T(8,128)(2,1)S(1)}, u32[]{:S(2)}) copy-start(bf16[8,128,128]{2,1,0:T(8,128)(2,1)S(1)} %broadcast_select_fusion.refs_0_) | copy-start | bytes 786436
  2.0 11.4 %collective-permute-start.1 = (bf16[8,128,128]{2,1,0:T(8,128)(2,1)S(1)}, bf16[8,128,128]{2,1,0:T(8,128)(2,1)S(1)}, u32[]{:S(2)}, u32[]{:S(2)}) collective-permute-start(bf16[8,128,128]{2,1,0:T(8,128)(2,1)S(1)} %broadcast_select_fusion.refs_0_), channel_id=1, source_target_pairs={{0,1},{1,2},{2,3},{3,0},{4,5},{5,6},{6,7},{7,4},{8,9},{9,10},{10,1... | collective-permute-start | bytes 786440 | tf_op jit(solution)/shard_map/ppermute | solution.py:159
  5.0 34.0 %collective-permute-start = (bf16[8,128,128]{2,1,0:T(8,128)(2,1)S(1)}, bf16[8,128,128]{2,1,0:T(8,128)(2,1)S(1)}, u32[]{:S(2)}, u32[]{:S(2)}) collective-permute-start(bf16[8,128,128]{2,1,0:T(8,128)(2,1)S(1)} %broadcast_select_fusion.refs_0_), channel_id=1, source_target_pairs={{0,16},{16,0},{1,17},{17,1},{2,18},{18,2},{3,19},{19,3},{4,20},{20... | collective-permute-start | bytes 786440 | tf_op jit(solution)/shard_map/ppermute | solution.py:155
  6.6 8.5 %collective-permute-start.7 = (bf16[128,256]{1,0:T(8,128)(2,1)S(1)}, bf16[128,256]{1,0:T(8,128)(2,1)S(1)}, u32[]{:S(2)}, u32[]{:S(2)}) collective-permute-start(bf16[128,256]{1,0:T(8,128)(2,1)S(1)} %subtract_convert_fusion), channel_id=1, source_target_pairs={{0,16},{16,0},{1,17},{17,1},{2,18},{18,2},{3,19},{19,3},{4,20},{20... | collective-permute-start | bytes 196616 | tf_op jit(solution)/shard_map/ppermute | solution.py:30
  13.4 25.8 %copy-start.5 = (bf16[8,128,128]{2,1,0:T(8,128)(2,1)}, bf16[8,128,128]{2,1,0:T(8,128)(2,1)S(1)}, u32[]{:S(2)}) copy-start(bf16[8,128,128]{2,1,0:T(8,128)(2,1)S(1)} %collective-permute-done.1.refs_2_) | copy-start | bytes 786436
  13.4 8.9 %collective-permute-start.5 = (bf16[8,128,128]{2,1,0:T(8,128)(2,1)S(1)}, bf16[8,128,128]{2,1,0:T(8,128)(2,1)S(1)}, u32[]{:S(2)}, u32[]{:S(2)}) collective-permute-start(bf16[8,128,128]{2,1,0:T(8,128)(2,1)S(1)} %broadcast_select_fusion.refs_0_), channel_id=1, source_target_pairs={{0,3},{1,0},{2,1},{3,2},{4,7},{5,4},{6,5},{7,6},{8,11},{9,8},{10,9... | collective-permute-start | bytes 786440 | tf_op jit(solution)/shard_map/ppermute | solution.py:159
  15.1 15.8 %collective-permute-start.3 = (bf16[8,128,128]{2,1,0:T(8,128)(2,1)S(1)}, bf16[8,128,128]{2,1,0:T(8,128)(2,1)S(1)}, u32[]{:S(2)}, u32[]{:S(2)}) collective-permute-start(bf16[8,128,128]{2,1,0:T(8,128)(2,1)S(1)} %broadcast_select_fusion.refs_0_), channel_id=1, source_target_pairs={{0,2},{1,3},{2,0},{3,1},{4,6},{5,7},{6,4},{7,5},{8,10},{9,11},{10,... | collective-permute-start | bytes 786440 | tf_op jit(solution)/shard_map/ppermute | solution.py:159
  15.1 24.0 %copy-start.3 = (bf16[2,128,256]{2,1,0:T(8,128)(2,1)}, bf16[2,128,256]{2,1,0:T(8,128)(2,1)S(1)}, u32[]{:S(2)}) copy-start(bf16[2,128,256]{2,1,0:T(8,128)(2,1)S(1)} %pad_maximum_fusion.refs_8_) | copy-start | bytes 393220
  15.1 2.9 %collective-permute-start.10 = (bf16[2,128,256]{2,1,0:T(8,128)(2,1)S(1)}, bf16[2,128,256]{2,1,0:T(8,128)(2,1)S(1)}, u32[]{:S(2)}, u32[]{:S(2)}) collective-permute-start(bf16[2,128,256]{2,1,0:T(8,128)(2,1)S(1)} %pad_maximum_fusion.refs_8_), channel_id=1, source_target_pairs={{0,12},{4,0},{8,4},{12,8},{1,13},{5,1},{9,5},{13,9},{2,14},{6,2},{... | collective-permute-start | bytes 393224 | tf_op jit(solution)/shard_map/ppermute | solution.py:30
  15.2 19.4 %collective-permute-start.9 = (bf16[2,128,256]{2,1,0:T(8,128)(2,1)S(1)}, bf16[2,128,256]{2,1,0:T(8,128)(2,1)S(1)}, u32[]{:S(2)}, u32[]{:S(2)}) collective-permute-start(bf16[2,128,256]{2,1,0:T(8,128)(2,1)S(1)} %pad_maximum_fusion.refs_8_), channel_id=1, source_target_pairs={{0,8},{4,12},{8,0},{12,4},{1,9},{5,13},{9,1},{13,5},{2,10},{6,14},... | collective-permute-start | bytes 393224 | tf_op jit(solution)/shard_map/ppermute | solution.py:30
  18.0 21.1 %copy-start.12 = (bf16[2,128,256]{2,1,0:T(8,128)(2,1)}, bf16[2,128,256]{2,1,0:T(8,128)(2,1)S(1)}, u32[]{:S(2)}) copy-start(bf16[2,128,256]{2,1,0:T(8,128)(2,1)S(1)} %collective-permute-done.10.refs_11_) | copy-start | bytes 393220
  18.0 21.1 %collective-permute-start.2 = (bf16[8,128,128]{2,1,0:T(8,128)(2,1)S(1)}, bf16[8,128,128]{2,1,0:T(8,128)(2,1)S(1)}, u32[]{:S(2)}, u32[]{:S(2)}) collective-permute-start(bf16[8,128,128]{2,1,0:T(8,128)(2,1)S(1)} %collective-permute-done.1.refs_2_), channel_id=1, source_target_pairs={{0,16},{16,0},{1,17},{17,1},{2,18},{18,2},{3,19},{19,3},{4,20},{20... | collective-permute-start | bytes 786440 | tf_op jit(solution)/shard_map/ppermute | solution.py:30
  22.3 16.9 %copy-start.7 = (bf16[8,128,128]{2,1,0:T(8,128)(2,1)}, bf16[8,128,128]{2,1,0:T(8,128)(2,1)S(1)}, u32[]{:S(2)}) copy-start(bf16[8,128,128]{2,1,0:T(8,128)(2,1)S(1)} %collective-permute-done.5.refs_6_) | copy-start | bytes 786436
  22.3 16.8 %collective-permute-start.6 = (bf16[8,128,128]{2,1,0:T(8,128)(2,1)S(1)}, bf16[8,128,128]{2,1,0:T(8,128)(2,1)S(1)}, u32[]{:S(2)}, u32[]{:S(2)}) collective-permute-start(bf16[8,128,128]{2,1,0:T(8,128)(2,1)S(1)} %collective-permute-done.5.refs_6_), channel_id=1, source_target_pairs={{0,16},{16,0},{1,17},{17,1},{2,18},{18,2},{3,19},{19,3},{4,20},{20... | collective-permute-start | bytes 786440 | tf_op jit(solution)/shard_map/ppermute | solution.py:30
  30.9 8.2 %copy-start.8 = (bf16[8,128,128]{2,1,0:T(8,128)(2,1)}, bf16[8,128,128]{2,1,0:T(8,128)(2,1)S(1)}, u32[]{:S(2)}) copy-start(bf16[8,128,128]{2,1,0:T(8,128)(2,1)S(1)} %collective-permute-done.3.refs_4_) | copy-start | bytes 786436
  30.9 8.2 %collective-permute-start.4 = (bf16[8,128,128]{2,1,0:T(8,128)(2,1)S(1)}, bf16[8,128,128]{2,1,0:T(8,128)(2,1)S(1)}, u32[]{:S(2)}, u32[]{:S(2)}) collective-permute-start(bf16[8,128,128]{2,1,0:T(8,128)(2,1)S(1)} %collective-permute-done.3.refs_4_), channel_id=1, source_target_pairs={{0,16},{16,0},{1,17},{17,1},{2,18},{18,2},{3,19},{19,3},{4,20},{20... | collective-permute-start | bytes 786440 | tf_op jit(solution)/shard_map/ppermute | solution.py:30
  34.6 4.6 %copy-start.13 = (bf16[2,128,256]{2,1,0:T(8,128)(2,1)}, bf16[2,128,256]{2,1,0:T(8,128)(2,1)S(1)}, u32[]{:S(2)}) copy-start(bf16[2,128,256]{2,1,0:T(8,128)(2,1)S(1)} %collective-permute-done.9.refs_10_) | copy-start | bytes 393220
  34.6 4.4 %collective-permute-start.8 = (bf16[2,128,256]{2,1,0:T(8,128)(2,1)S(1)}, bf16[2,128,256]{2,1,0:T(8,128)(2,1)S(1)}, u32[]{:S(2)}, u32[]{:S(2)}) collective-permute-start(bf16[2,128,256]{2,1,0:T(8,128)(2,1)S(1)} %pad_maximum_fusion.refs_8_), channel_id=1, source_target_pairs={{0,4},{4,8},{8,12},{12,0},{1,5},{5,9},{9,13},{13,1},{2,6},{6,10},{... | collective-permute-start | bytes 393224 | tf_op jit(solution)/shard_map/ppermute | solution.py:30
  39.1 0.6 %copy-start.14 = (bf16[2,128,256]{2,1,0:T(8,128)(2,1)}, bf16[2,128,256]{2,1,0:T(8,128)(2,1)S(1)}, u32[]{:S(2)}) copy-start(bf16[2,128,256]{2,1,0:T(8,128)(2,1)S(1)} %collective-permute-done.8.refs_9_) | copy-start | bytes 393220
  39.1 0.8 %copy-start.6 = (bf16[8,128,128]{2,1,0:T(8,128)(2,1)}, bf16[8,128,128]{2,1,0:T(8,128)(2,1)S(1)}, u32[]{:S(2)}) copy-start(bf16[8,128,128]{2,1,0:T(8,128)(2,1)S(1)} %collective-permute-done.refs_1_) | copy-start | bytes 786436
  39.1 0.9 %copy-start.9 = (bf16[8,128,128]{2,1,0:T(8,128)(2,1)}, bf16[8,128,128]{2,1,0:T(8,128)(2,1)S(1)}, u32[]{:S(2)}) copy-start(bf16[8,128,128]{2,1,0:T(8,128)(2,1)S(1)} %collective-permute-done.2.refs_3_) | copy-start | bytes 786436
  39.1 0.9 %copy-start.10 = (bf16[8,128,128]{2,1,0:T(8,128)(2,1)}, bf16[8,128,128]{2,1,0:T(8,128)(2,1)S(1)}, u32[]{:S(2)}) copy-start(bf16[8,128,128]{2,1,0:T(8,128)(2,1)S(1)} %collective-permute-done.6.refs_7_) | copy-start | bytes 786436
  40.0 0.7 %copy-start.11 = (bf16[8,128,128]{2,1,0:T(8,128)(2,1)}, bf16[8,128,128]{2,1,0:T(8,128)(2,1)S(1)}, u32[]{:S(2)}) copy-start(bf16[8,128,128]{2,1,0:T(8,128)(2,1)S(1)} %collective-permute-done.4.refs_5_) | copy-start | bytes 786436

commit v6 on v5

--- a/solution.py
+++ b/solution.py
@@ -41,15 +41,18 @@
     return out, sources
 
 
-def product_kernel(slot_ref, rf_pos_ref, keep_ref, *refs, pieces, rf_groups, row_blocks, cols):
+def product_kernel(slot_ref, rf_src_ref, keep_ref, rf_ref, *refs, pieces, row_blocks, with_acc, final):
     left_refs = refs[:pieces]
-    rf_refs = refs[pieces:pieces + rf_groups]
-    out_ref = refs[pieces + rf_groups]
-    lhs_scr, rf_scr = refs[pieces + rf_groups + 1:]
-    per_group = pieces // rf_groups
-    for q in range(pieces):
-        at = pl.multiple_of(rf_pos_ref[q] * BLK, BLK)
-        rf_scr[pl.ds(at, BLK), :] = rf_refs[q // per_group][q % per_group]
+    at = pieces
+    acc_ref = None
+    if with_acc:
+        acc_ref = refs[at]
+        at += 1
+    out_ref = refs[at]
+    lhs_scr, rf_scr = refs[at + 1:]
+    cols = rf_ref.shape[-1]
+    for p in range(pieces):
+        rf_scr[p * BLK:(p + 1) * BLK, :] = rf_ref[rf_src_ref[p]]
     for p in range(pieces):
         for i in range(row_blocks):
             s = slot_ref[p, i]
@@ -58,9 +61,13 @@
             lhs_scr[i * BLK:(i + 1) * BLK, p * BLK:(p + 1) * BLK] = blk
     tile = 2 * BLK
     for t in range(row_blocks * BLK // tile):
-        res = jnp.dot(
-            lhs_scr[t * tile:(t + 1) * tile, :], rf_scr[...], preferred_element_type=jnp.float32
-        )
+        rows = slice(t * tile, (t + 1) * tile)
+        res = jnp.dot(lhs_scr[rows, :], rf_scr[...], preferred_element_type=jnp.float32)
+        if with_acc:
+            res = res + acc_ref[rows, :]
+        if not final:
+            out_ref[rows, :] = res
+            continue
         for a in range(tile // BLK):
             i = t * (tile // BLK) + a
             for b in range(cols // BLK):
@@ -69,30 +76,39 @@
                 out_ref[i * BLK:(i + 1) * BLK, b * BLK:(b + 1) * BLK] = sub.astype(out_ref.dtype)
 
 
-def product_call(slot_tbl, rf_pos, keep_patch, left_pieces, rf_pieces):
+def product_call(slot_tbl, rf_src, keep_patch, rf_all, left_pieces, acc=None, final=True):
     pieces = len(left_pieces)
-    rf_groups = len(rf_pieces)
     row_blocks = slot_tbl.shape[1]
-    cols = rf_pieces[0].shape[-1]
+    cols = rf_all.shape[-1]
     smem = pl.BlockSpec(memory_space=pltpu.SMEM)
     vmem = pl.BlockSpec(memory_space=pltpu.VMEM)
+    operands = [slot_tbl, rf_src, keep_patch, rf_all, *left_pieces]
+    if acc is not None:
+        operands.append(acc)
+    out_dtype = jnp.bfloat16 if final else jnp.float32
     flops = 2 * row_blocks * BLK * pieces * BLK * cols
     bytes_accessed = (
-        pieces * left_pieces[0].size * 2 + rf_groups * rf_pieces[0].size * 2 + row_blocks * BLK * cols * 2
+        pieces * (left_pieces[0].size + BLK * cols) * 2
+        + row_blocks * BLK * cols * (2 if final else 4)
+        + (0 if acc is None else acc.size * 4)
     )
     return pl.pallas_call(
         functools.partial(
-            product_kernel, pieces=pieces, rf_groups=rf_groups, row_blocks=row_blocks, cols=cols
+            product_kernel,
+            pieces=pieces,
+            row_blocks=row_blocks,
+            with_acc=acc is not None,
+            final=final,
         ),
-        out_shape=jax.ShapeDtypeStruct((row_blocks * BLK, cols), jnp.bfloat16),
-        in_specs=[smem, smem, smem] + [vmem] * (pieces + rf_groups),
+        out_shape=jax.ShapeDtypeStruct((row_blocks * BLK, cols), out_dtype),
+        in_specs=[smem, smem, smem] + [vmem] * (len(operands) - 3),
         out_specs=vmem,
         scratch_shapes=[
             pltpu.VMEM((row_blocks * BLK, pieces * BLK), jnp.bfloat16),
             pltpu.VMEM((pieces * BLK, cols), jnp.bfloat16),
         ],
         cost_estimate=pl.CostEstimate(flops=flops, bytes_accessed=bytes_accessed, transcendentals=0),
-    )(slot_tbl, rf_pos, keep_patch, *left_pieces, *rf_pieces)
+    )(*operands)
 
 
 def per_device(left_matrix, square_term, block_pattern, keep_mask):
@@ -149,42 +165,48 @@
         and layer_count <= 2
     )
     if use_permutes:
-        rf_pair, rf_layer_src = ring_gather(right_factor, "layer", layer_idx, layer_count)
+        rf_pair, _ = ring_gather(right_factor, "layer", layer_idx, layer_count)
         rf_pair = jnp.stack(rf_pair)
         own_over_layer = [
             lax.ppermute(packed[0], "layer", [(s, (s + m) % layer_count) for s in range(layer_count)])
             for m in range(1, layer_count)
         ]
+
         def col_shift(x, k):
             return lax.ppermute(x, "col", [(s, (s + k) % col_count) for s in range(col_count)])
 
         col_pieces = {1: col_shift(packed[0], 1)}
-        later, col_pieces[1] = lax.optimization_barrier((packed[0], col_pieces[1]))
+        rf_pieces, _ = ring_gather(rf_pair, "row", row_idx, row_count)
+        rf_all = jnp.concatenate(rf_pieces, axis=0)
+        later, col_pieces[1], rf_all = lax.optimization_barrier((packed[0], col_pieces[1], rf_all))
         for k in range(2, col_count):
             col_pieces[k] = col_shift(later, k)
-        piece_col = [(col_idx - k) % col_count for k in range(col_count)]
         pieces = [packed[0]] + own_over_layer
         for k in range(1, col_count):
             got, _ = ring_gather(col_pieces[k], "layer", layer_idx, layer_count)
             pieces.extend(got)
         piece_layer = [(layer_idx - m) % layer_count for k in range(col_count) for m in range(layer_count)]
-        piece_col = [piece_col[k] for k in range(col_count) for m in range(layer_count)]
+        piece_col = [(col_idx - k) % col_count for k in range(col_count) for m in range(layer_count)]
         piece_j = jnp.stack(
             [src_l * col_count + src_c for src_l, src_c in zip(piece_layer, piece_col)]
         ).astype(jnp.int32)
-        rf_pieces, rf_row = ring_gather(rf_pair, "row", row_idx, row_count)
-        rf_layer = [(layer_idx - m) % layer_count for k in range(row_count) for m in range(layer_count)]
-        rf_row = [rf_row[k] for k in range(row_count) for m in range(layer_count)]
-        rf_q = jnp.stack(
-            [src_l * row_count + src_r for src_l, src_r in zip(rf_layer, rf_row)]
-        ).astype(jnp.int32)
-        rf_pos = ((col_idx - rf_q % col_count) % col_count) * layer_count + (
-            (layer_idx - rf_q // col_count) % layer_count
-        )
+        rf_src = ((row_idx - piece_j % row_count) % row_count) * layer_count + (
+            (layer_idx - piece_j // row_count) % layer_count
+        )
+        rf_src = rf_src.astype(jnp.int32)
         p_stored, p_slot = slot_table(panel_pattern)
         slot_tbl = jnp.where(p_stored > 0, p_slot, -1)
         slot_tbl = jnp.take(slot_tbl, piece_j, axis=1).T.astype(jnp.int32)
-        return product_call(slot_tbl, rf_pos.astype(jnp.int32), keep_patch, pieces, rf_pieces)
+        last = [k * layer_count + m for k in range(2, col_count) for m in range(1, layer_count)]
+        first = [p for p in range(len(pieces)) if p not in last]
+        partial = product_call(
+            slot_tbl[jnp.array(first)], rf_src[jnp.array(first)], keep_patch, rf_all,
+            [pieces[p] for p in first], final=False,
+        )
+        return product_call(
+            slot_tbl[jnp.array(last)], rf_src[jnp.array(last)], keep_patch, rf_all,
+            [pieces[p] for p in last], acc=partial, final=True,
+        )
 
     gathered = lax.all_gather(packed, ("layer", "col"), axis=0, tiled=True)
     piece_j = jnp.arange(total_inner_blocks, dtype=jnp.int32)

time: 45.1 us -> 59.6 us (1.32)
  the two profiles are of different devices: /device:TPU:0 before, /device:TPU:26 now
where the time goes in v6:
time: 59.6 us; the launch traced here: 59.3 us
  waiting for transfers between devices  27.9 us (47%)
  local copies, waits for them, and re-layouts  11.1 us (19%)
  starting transfers between devices  10 us (17%)
  Pallas kernels  7.6 us (13%)
  other arithmetic  2.34 us (4%)
    ppermute x3, waiting for transfers between devices, col_shift(): lax.ppermute(x, 'col', [(s, (s + k) % col_count) for s in range(col_count)])  18.5 us
    ppermute x7, waiting for transfers between devices, ring_gather(): pieces.append(lax.ppermute(x, axis, perm))  9.44 us
    pallas_call x2, Pallas kernels, product_call(): pl.pallas_call(functools.partial(product_kernel, pieces=pieces, row_block...  7.6 us
    ppermute x7, starting transfers between devices, ring_gather(): pieces.append(lax.ppermute(x, axis, perm))  7.29 us
    unnamed x29, local copies, waits for them, and re-layouts  3.47 us
    ppermute x3, starting transfers between devices, col_shift(): lax.ppermute(x, 'col', [(s, (s + k) % col_count) for s in range(col_count)])  2.34 us
    gather x1, local copies, waits for them, and re-layouts, per_device(): rf_src[jnp.array(last)]  1.22 us
  transfers between devices with their start and end apart: 11, of which 6 were waited for; matrix products, arithmetic and copies ran while one was open for 15% of the time, Pallas kernels for 7%

profile of v6, /device:TPU:26, one launch (start us, length us, event | category | flops | bytes accessed | tf_op | source)
XLA Modules:
  0.0 59.3 jit_solution(8064705453143382033)
XLA Ops:
  0.1 0.8 %compare_bitcast_fusion = (pred[16]{0:T(512)(128)(4,1)S(1)}, s32[16,1]{0,1:T(1,128)S(1)}) fusion(s32[64,8]{0,1:T(8,128)} %param.10, s32[]{:T(128)S(6)} %select_n.158, s32[]{:T(128)S(6)} %select_n.170), kind=kLoop, calls=%fused_computation.33 | loop fusion | flops 48 | bytes 152 | tf_op jit(solution)/shard_map/gt | solution.py:135
  1.5 0.6 %gather_fusion.3 = bf16[8,128,128]{2,1,0:T(8,128)(2,1)S(1)} fusion(bf16[16,128,128]{2,1,0:T(8,128)(2,1)S(1)} %bitcast.29, s32[1024]{0:T(1024)S(1)} %get-tuple-element.15), kind=kCustom, calls=%fused_computation.3 | custom fusion | bytes 524320 | tf_op jit(solution)/shard_map/jit(_take)/gather | solution.py:142
  2.2 0.3 collective-permute-start
  2.5 0.4 collective-permute-start.9
  2.9 0.9 %constant_dynamic-update-slice_fusion.4 = (bf16[8,128,256]{2,1,0:T(8,128)(2,1)S(1)}, bf16[128,256]{1,0:T(8,128)(2,1)S(1)}) fusion(bf16[128,256]{1,0:T(8,128)(2,1)} %param.9, s32[256]{0:T(256)S(1)} %iota_add_fusion, s32[128]{0:T(128)S(1)} %iota_add_fusion.1), kind=kLoop, calls=%fused_computation.13 | loop fusion | flops 196607 | bytes 198144
  3.8 1.7 %collective-permute-start.1 = (bf16[128,256]{1,0:T(8,128)(2,1)S(1)}, bf16[128,256]{1,0:T(8,128)(2,1)S(1)}, u32[]{:S(2)}, u32[]{:S(2)}) collective-permute-start(bf16[128,256]{1,0:T(8,128)(2,1)S(1)} %get-tuple-element.12), channel_id=1, source_target_pairs={{0,16},{16,0},{1,17},{17,1},{2,18},{18,2},{3,19},{19,3},{4,20},{20... | collective-permute-start | bytes 196616 | tf_op jit(solution)/shard_map/ppermute | solution.py:30
  5.5 0.8 %constant_dynamic-slice_fusion = s32[16,8]{0,1:T(8,128)S(1)} fusion(s32[64,8]{0,1:T(8,128)} %param.10, s32[]{:T(128)S(6)} %select_n.158), kind=kLoop, calls=%fused_computation.53 | loop fusion | bytes 1028 | tf_op jit(solution)/shard_map/dynamic_slice | solution.py:149
  6.5 0.6 gather_fusion
  7.1 4.7 %collective-permute-done.1 = bf16[128,256]{1,0:T(8,128)(2,1)S(1)} collective-permute-done((bf16[128,256]{1,0:T(8,128)(2,1)S(1)}, bf16[128,256]{1,0:T(8,128)(2,1)S(1)}, u32[]{:S(2)}, u32[]{:S(2)}) %collective-permute-start.1) | collective-permute-done | bytes 65568 | tf_op jit(solution)/shard_map/ppermute | solution.py:30
  11.8 1.6 %collective-permute-start.3 = (bf16[2,128,256]{2,1,0:T(8,128)(2,1)S(1)}, bf16[2,128,256]{2,1,0:T(8,128)(2,1)S(1)}, u32[]{:S(2)}, u32[]{:S(2)}) collective-permute-start(bf16[2,128,256]{2,1,0:T(8,128)(2,1)S(1)} %pad_maximum_fusion), channel_id=1, source_target_pairs={{0,8},{4,12},{8,0},{12,4},{1,9},{5,13},{9,1},{13,5},{2,10},{6,14},... | collective-permute-start | bytes 393224 | tf_op jit(solution)/shard_map/ppermute | solution.py:30
  13.4 1.4 %collective-permute-start.4 = (bf16[2,128,256]{2,1,0:T(8,128)(2,1)S(1)}, bf16[2,128,256]{2,1,0:T(8,128)(2,1)S(1)}, u32[]{:S(2)}, u32[]{:S(2)}) collective-permute-start(bf16[2,128,256]{2,1,0:T(8,128)(2,1)S(1)} %pad_maximum_fusion), channel_id=1, source_target_pairs={{0,12},{4,0},{8,4},{12,8},{1,13},{5,1},{9,5},{13,9},{2,14},{6,2},{... | collective-permute-start | bytes 393224 | tf_op jit(solution)/shard_map/ppermute | solution.py:30
  14.8 2.2 %collective-permute-done.2 = bf16[2,128,256]{2,1,0:T(8,128)(2,1)S(1)} collective-permute-done((bf16[2,128,256]{2,1,0:T(8,128)(2,1)S(1)}, bf16[2,128,256]{2,1,0:T(8,128)(2,1)S(1)}, u32[]{:S(2)}, u32[]{:S(2)}) %collective-permute-start.2) | collective-permute-done | bytes 131104 | tf_op jit(solution)/shard_map/ppermute | solution.py:30
  17.0 1.2 %collective-permute-done.3 = bf16[2,128,256]{2,1,0:T(8,128)(2,1)S(1)} collective-permute-done((bf16[2,128,256]{2,1,0:T(8,128)(2,1)S(1)}, bf16[2,128,256]{2,1,0:T(8,128)(2,1)S(1)}, u32[]{:S(2)}, u32[]{:S(2)}) %collective-permute-start.3) | collective-permute-done | bytes 131104 | tf_op jit(solution)/shard_map/ppermute | solution.py:30
  18.2 1.2 %collective-permute-done.4 = bf16[2,128,256]{2,1,0:T(8,128)(2,1)S(1)} collective-permute-done((bf16[2,128,256]{2,1,0:T(8,128)(2,1)S(1)}, bf16[2,128,256]{2,1,0:T(8,128)(2,1)S(1)}, u32[]{:S(2)}, u32[]{:S(2)}) %collective-permute-start.4) | collective-permute-done | bytes 131104 | tf_op jit(solution)/shard_map/ppermute | solution.py:30
  19.5 1.6 %collective-permute-start.5 = (bf16[8,128,128]{2,1,0:T(8,128)(2,1)S(1)}, bf16[8,128,128]{2,1,0:T(8,128)(2,1)S(1)}, u32[]{:S(2)}, u32[]{:S(2)}) collective-permute-start(bf16[8,128,128]{2,1,0:T(8,128)(2,1)S(1)} %broadcast_select_fusion.refs_0_), channel_id=1, source_target_pairs={{0,2},{1,3},{2,0},{3,1},{4,6},{5,7},{6,4},{7,5},{8,10},{9,11},{10,... | collective-permute-start | bytes 786440 | tf_op jit(solution)/shard_map/ppermute | solution.py:176
  21.1 0.4 collective-permute-start.7
  21.7 0.5 collective-permute-start.10
  22.2 18.5 %collective-permute-done.5.refs_4_ = bf16[8,128,128]{2,1,0:T(8,128)(2,1)S(1)} collective-permute-done((bf16[8,128,128]{2,1,0:T(8,128)(2,1)S(1)}, bf16[8,128,128]{2,1,0:T(8,128)(2,1)S(1)}, u32[]{:S(2)}, u32[]{:S(2)}) %collective-permute-start.5) | collective-permute-done | bytes 262176 | tf_op jit(solution)/shard_map/ppermute | solution.py:176
  40.7 0.5 collective-permute-start.6
  41.3 1.5 %collective-permute-start.8 = (bf16[8,128,128]{2,1,0:T(8,128)(2,1)S(1)}, bf16[8,128,128]{2,1,0:T(8,128)(2,1)S(1)}, u32[]{:S(2)}, u32[]{:S(2)}) collective-permute-start(bf16[8,128,128]{2,1,0:T(8,128)(2,1)S(1)} %collective-permute-done.7.refs_5_), channel_id=1, source_target_pairs={{0,16},{16,0},{1,17},{17,1},{2,18},{18,2},{3,19},{19,3},{4,20},{20... | collective-permute-start | bytes 786440 | tf_op jit(solution)/shard_map/ppermute | solution.py:30
  42.8 1.1 %gather_fusion.4 = s32[6,16]{1,0:T(8,128)} fusion(s32[8,16]{1,0:T(8,128)S(1)} %broadcast_select_fusion.1, s32[1024]{0:T(1024)S(1)} %pad_clamp_fusion), kind=kCustom, calls=%fused_computation.4 | custom fusion | bytes 792 | tf_op jit(solution)/shard_map/gather | solution.py:203
  43.9 1.1 %gather_fusion.5 = s32[6]{0:T(128)} fusion(s32[8]{0:T(128)S(1)} %fusion.1, s32[1024]{0:T(1024)S(1)} %pad_clamp_fusion), kind=kCustom, calls=%fused_computation.5 | custom fusion | bytes 72 | tf_op jit(solution)/shard_map/gather | solution.py:203
  45.1 1.1 %gather_fusion.1 = s32[2,16]{1,0:T(2,128)} fusion(s32[8,16]{1,0:T(8,128)S(1)} %broadcast_select_fusion.1, s32[1024]{0:T(1024)S(1)} %pad_clamp_fusion.2), kind=kCustom, calls=%fused_computation.1 | custom fusion | bytes 264 | tf_op jit(solution)/shard_map/gather | solution.py:207
  46.1 1.2 %gather_fusion.2 = s32[2]{0:T(128)} fusion(s32[8]{0:T(128)S(1)} %fusion.1, s32[1024]{0:T(1024)S(1)} %pad_clamp_fusion.2), kind=kCustom, calls=%fused_computation.2 | custom fusion | bytes 24 | tf_op jit(solution)/shard_map/gather | solution.py:207
  47.4 0.8 %dynamic_slice.10 = s32[16,2]{0,1:T(2,128)S(1)} dynamic-slice(s32[64,8]{0,1:T(8,128)} %param.11, s32[]{:T(128)S(6)} %select_n.158, s32[]{:T(128)S(6)} %select_n.169), dynamic_slice_sizes={16,2} | dynamic-slice | bytes 260 | tf_op jit(solution)/shard_map/dynamic_slice | solution.py:146
  48.1 0.7 %copy.22.keep_ref = s32[16,2]{1,0:T(8,128)} copy(s32[16,2]{0,1:T(2,128)S(1)} %dynamic_slice.10) | data formatting | bytes 256
  48.9 0.6 %copy-done.4 = bf16[8,128,128]{2,1,0:T(8,128)(2,1)} copy-done((bf16[8,128,128]{2,1,0:T(8,128)(2,1)}, bf16[8,128,128]{2,1,0:T(8,128)(2,1)S(1)}, u32[]{:S(2)}) %copy-start.4) | copy-done | bytes 262168
  49.5 0.7 %copy-done.7 = bf16[8,128,128]{2,1,0:T(8,128)(2,1)} copy-done((bf16[8,128,128]{2,1,0:T(8,128)(2,1)}, bf16[8,128,128]{2,1,0:T(8,128)(2,1)S(1)}, u32[]{:S(2)}) %copy-start.7) | copy-done | bytes 262168
  50.3 4.1 %shard_map.82.refs_2_ = f32[2048,256]{1,0:T(8,128)} custom-call(s32[6,16]{1,0:T(8,128)} %gather_fusion.4, s32[6]{0:T(128)} %gather_fusion.5, s32[16,2]{1,0:T(8,128)} %copy.22.keep_ref, bf16[8,128,256]{2,1,0:T(8,128)(2,1)} %copy-done.1, bf16[8,128,128]{2,1,0:T(8,128)(2,1)} %copy-done.2, bf16[8,128,128]{2,1,0:T(8,128)(2,1)} %copy-done.4, ...), custom_call_target="tpu_custom_call" | custom-call | flops 805306368 | bytes 4063232 | tf_op jit(solution)/shard_map/pallas_call | solution.py:95
  54.5 0.6 copy-done.8
  55.0 0.7 %copy-done.9 = bf16[8,128,128]{2,1,0:T(8,128)(2,1)} copy-done((bf16[8,128,128]{2,1,0:T(8,128)(2,1)}, bf16[8,128,128]{2,1,0:T(8,128)(2,1)S(1)}, u32[]{:S(2)}) %copy-start.9) | copy-done | bytes 262168
  55.7 3.5 %shard_map.83 = bf16[2048,256]{1,0:T(8,128)(2,1)} custom-call(s32[2,16]{1,0:T(2,128)} %gather_fusion.1, s32[2]{0:T(128)} %gather_fusion.2, s32[16,2]{1,0:T(8,128)} %copy.22.keep_ref, bf16[8,128,256]{2,1,0:T(8,128)(2,1)} %copy-done.1, bf16[8,128,128]{2,1,0:T(8,128)(2,1)} %copy-done.8, bf16[8,128,128]{2,1,0:T(8,128)(2,1)} %copy-done.9, ...), custom_call_target="tpu_custom_call" | custom-call | flops 268435456 | bytes 3801088 | tf_op jit(solution)/shard_map/pallas_call | solution.py:95
  (55 shorter events, 1.3 us)
Async XLA Ops:
  0.0 1.5 %copy-start = (bf16[2048,128]{1,0:T(8,128)(2,1)S(1)}, bf16[2048,128]{1,0:T(8,128)(2,1)}, u32[]{:S(2)}) copy-start(bf16[2048,128]{1,0:T(8,128)(2,1)} %param.8) | copy-start | bytes 1572868
  0.0 42.7 %copy-start.11 = (s32[6]{0:T(128)S(1)}, s32[6]{0:T(128)}, u32[]{:S(2)}) copy-start(s32[6]{0:T(128)} %constant.189) | copy-start | bytes 76
  0.0 45.0 %copy-start.10 = (s32[2]{0:T(128)S(1)}, s32[2]{0:T(128)}, u32[]{:S(2)}) copy-start(s32[2]{0:T(128)} %constant.187) | copy-start | bytes 28
  2.2 46.7 %copy-start.2 = (bf16[8,128,128]{2,1,0:T(8,128)(2,1)}, bf16[8,128,128]{2,1,0:T(8,128)(2,1)S(1)}, u32[]{:S(2)}) copy-start(bf16[8,128,128]{2,1,0:T(8,128)(2,1)S(1)} %broadcast_select_fusion.refs_0_) | copy-start | bytes 786436
  2.2 17.3 %collective-permute-start = (bf16[8,128,128]{2,1,0:T(8,128)(2,1)S(1)}, bf16[8,128,128]{2,1,0:T(8,128)(2,1)S(1)}, u32[]{:S(2)}, u32[]{:S(2)}) collective-permute-start(bf16[8,128,128]{2,1,0:T(8,128)(2,1)S(1)} %broadcast_select_fusion.refs_0_), channel_id=1, source_target_pairs={{0,1},{1,2},{2,3},{3,0},{4,5},{5,6},{6,7},{7,4},{8,9},{9,10},{10,1... | collective-permute-start | bytes 786440 | tf_op jit(solution)/shard_map/ppermute | solution.py:176
  2.5 46.4 %collective-permute-start.9 = (bf16[8,128,128]{2,1,0:T(8,128)(2,1)S(1)}, bf16[8,128,128]{2,1,0:T(8,128)(2,1)S(1)}, u32[]{:S(2)}, u32[]{:S(2)}) collective-permute-start(bf16[8,128,128]{2,1,0:T(8,128)(2,1)S(1)} %broadcast_select_fusion.refs_0_), channel_id=1, source_target_pairs={{0,16},{16,0},{1,17},{17,1},{2,18},{18,2},{3,19},{19,3},{4,20},{20... | collective-permute-start | bytes 786440 | tf_op jit(solution)/shard_map/ppermute | solution.py:171
  3.8 8.0 %collective-permute-start.1 = (bf16[128,256]{1,0:T(8,128)(2,1)S(1)}, bf16[128,256]{1,0:T(8,128)(2,1)S(1)}, u32[]{:S(2)}, u32[]{:S(2)}) collective-permute-start(bf16[128,256]{1,0:T(8,128)(2,1)S(1)} %get-tuple-element.12), channel_id=1, source_target_pairs={{0,16},{16,0},{1,17},{17,1},{2,18},{18,2},{3,19},{19,3},{4,20},{20... | collective-permute-start | bytes 196616 | tf_op jit(solution)/shard_map/ppermute | solution.py:30
  11.8 5.2 %collective-permute-start.2 = (bf16[2,128,256]{2,1,0:T(8,128)(2,1)S(1)}, bf16[2,128,256]{2,1,0:T(8,128)(2,1)S(1)}, u32[]{:S(2)}, u32[]{:S(2)}) collective-permute-start(bf16[2,128,256]{2,1,0:T(8,128)(2,1)S(1)} %pad_maximum_fusion), channel_id=1, source_target_pairs={{0,4},{4,8},{8,12},{12,0},{1,5},{5,9},{9,13},{13,1},{2,6},{6,10},{... | collective-permute-start | bytes 393224 | tf_op jit(solution)/shard_map/ppermute | solution.py:30
  11.8 6.4 %collective-permute-start.3 = (bf16[2,128,256]{2,1,0:T(8,128)(2,1)S(1)}, bf16[2,128,256]{2,1,0:T(8,128)(2,1)S(1)}, u32[]{:S(2)}, u32[]{:S(2)}) collective-permute-start(bf16[2,128,256]{2,1,0:T(8,128)(2,1)S(1)} %pad_maximum_fusion), channel_id=1, source_target_pairs={{0,8},{4,12},{8,0},{12,4},{1,9},{5,13},{9,1},{13,5},{2,10},{6,14},... | collective-permute-start | bytes 393224 | tf_op jit(solution)/shard_map/ppermute | solution.py:30
  13.4 6.0 %collective-permute-start.4 = (bf16[2,128,256]{2,1,0:T(8,128)(2,1)S(1)}, bf16[2,128,256]{2,1,0:T(8,128)(2,1)S(1)}, u32[]{:S(2)}, u32[]{:S(2)}) collective-permute-start(bf16[2,128,256]{2,1,0:T(8,128)(2,1)S(1)} %pad_maximum_fusion), channel_id=1, source_target_pairs={{0,12},{4,0},{8,4},{12,8},{1,13},{5,1},{9,5},{13,9},{2,14},{6,2},{... | collective-permute-start | bytes 393224 | tf_op jit(solution)/shard_map/ppermute | solution.py:30
  19.5 29.3 %copy-start.1 = (bf16[8,128,256]{2,1,0:T(8,128)(2,1)}, bf16[8,128,256]{2,1,0:T(8,128)(2,1)S(1)}, u32[]{:S(2)}) copy-start(bf16[8,128,256]{2,1,0:T(8,128)(2,1)S(1)} %constant_dynamic-update-slice_fusion.rf_ref) | copy-start | bytes 1572868
  19.5 29.3 %copy-start.3 = (bf16[8,128,128]{2,1,0:T(8,128)(2,1)}, bf16[8,128,128]{2,1,0:T(8,128)(2,1)S(1)}, u32[]{:S(2)}) copy-start(bf16[8,128,128]{2,1,0:T(8,128)(2,1)S(1)} %collective-permute-done.refs_2_) | copy-start | bytes 786436
  19.5 21.2 %collective-permute-start.5 = (bf16[8,128,128]{2,1,0:T(8,128)(2,1)S(1)}, bf16[8,128,128]{2,1,0:T(8,128)(2,1)S(1)}, u32[]{:S(2)}, u32[]{:S(2)}) collective-permute-start(bf16[8,128,128]{2,1,0:T(8,128)(2,1)S(1)} %broadcast_select_fusion.refs_0_), channel_id=1, source_target_pairs={{0,2},{1,3},{2,0},{3,1},{4,6},{5,7},{6,4},{7,5},{8,10},{9,11},{10,... | collective-permute-start | bytes 786440 | tf_op jit(solution)/shard_map/ppermute | solution.py:176
  21.1 20.1 %collective-permute-start.7 = (bf16[8,128,128]{2,1,0:T(8,128)(2,1)S(1)}, bf16[8,128,128]{2,1,0:T(8,128)(2,1)S(1)}, u32[]{:S(2)}, u32[]{:S(2)}) collective-permute-start(bf16[8,128,128]{2,1,0:T(8,128)(2,1)S(1)} %broadcast_select_fusion.refs_0_), channel_id=1, source_target_pairs={{0,3},{1,0},{2,1},{3,2},{4,7},{5,4},{6,5},{7,6},{8,11},{9,8},{10,9... | collective-permute-start | bytes 786440 | tf_op jit(solution)/shard_map/ppermute | solution.py:176
  21.7 27.2 %collective-permute-start.10 = (bf16[8,128,128]{2,1,0:T(8,128)(2,1)S(1)}, bf16[8,128,128]{2,1,0:T(8,128)(2,1)S(1)}, u32[]{:S(2)}, u32[]{:S(2)}) collective-permute-start(bf16[8,128,128]{2,1,0:T(8,128)(2,1)S(1)} %collective-permute-done.refs_2_), channel_id=1, source_target_pairs={{0,16},{16,0},{1,17},{17,1},{2,18},{18,2},{3,19},{19,3},{4,20},{20... | collective-permute-start | bytes 786440 | tf_op jit(solution)/shard_map/ppermute | solution.py:30
  40.7 8.1 %copy-start.5 = (bf16[8,128,128]{2,1,0:T(8,128)(2,1)}, bf16[8,128,128]{2,1,0:T(8,128)(2,1)S(1)}, u32[]{:S(2)}) copy-start(bf16[8,128,128]{2,1,0:T(8,128)(2,1)S(1)} %collective-permute-done.5.refs_4_) | copy-start | bytes 786436
  40.7 13.6 %collective-permute-start.6 = (bf16[8,128,128]{2,1,0:T(8,128)(2,1)S(1)}, bf16[8,128,128]{2,1,0:T(8,128)(2,1)S(1)}, u32[]{:S(2)}, u32[]{:S(2)}) collective-permute-start(bf16[8,128,128]{2,1,0:T(8,128)(2,1)S(1)} %collective-permute-done.5.refs_4_), channel_id=1, source_target_pairs={{0,16},{16,0},{1,17},{17,1},{2,18},{18,2},{3,19},{19,3},{4,20},{20... | collective-permute-start | bytes 786440 | tf_op jit(solution)/shard_map/ppermute | solution.py:30
  41.3 7.6 %copy-start.6 = (bf16[8,128,128]{2,1,0:T(8,128)(2,1)}, bf16[8,128,128]{2,1,0:T(8,128)(2,1)S(1)}, u32[]{:S(2)}) copy-start(bf16[8,128,128]{2,1,0:T(8,128)(2,1)S(1)} %collective-permute-done.7.refs_5_) | copy-start | bytes 786436
  41.3 13.2 %collective-permute-start.8 = (bf16[8,128,128]{2,1,0:T(8,128)(2,1)S(1)}, bf16[8,128,128]{2,1,0:T(8,128)(2,1)S(1)}, u32[]{:S(2)}, u32[]{:S(2)}) collective-permute-start(bf16[8,128,128]{2,1,0:T(8,128)(2,1)S(1)} %collective-permute-done.7.refs_5_), channel_id=1, source_target_pairs={{0,16},{16,0},{1,17},{17,1},{2,18},{18,2},{3,19},{19,3},{4,20},{20... | collective-permute-start | bytes 786440 | tf_op jit(solution)/shard_map/ppermute | solution.py:30
  48.8 0.7 %copy-start.4 = (bf16[8,128,128]{2,1,0:T(8,128)(2,1)}, bf16[8,128,128]{2,1,0:T(8,128)(2,1)S(1)}, u32[]{:S(2)}) copy-start(bf16[8,128,128]{2,1,0:T(8,128)(2,1)S(1)} %collective-permute-done.9.refs_1_) | copy-start | bytes 786436
  49.5 0.7 %copy-start.7 = (bf16[8,128,128]{2,1,0:T(8,128)(2,1)}, bf16[8,128,128]{2,1,0:T(8,128)(2,1)S(1)}, u32[]{:S(2)}) copy-start(bf16[8,128,128]{2,1,0:T(8,128)(2,1)S(1)} %collective-permute-done.10.refs_3_) | copy-start | bytes 786436
  54.3 0.7 %copy-start.8 = (bf16[8,128,128]{2,1,0:T(8,128)(2,1)}, bf16[8,128,128]{2,1,0:T(8,128)(2,1)S(1)}, u32[]{:S(2)}) copy-start(bf16[8,128,128]{2,1,0:T(8,128)(2,1)S(1)} %collective-permute-done.6.refs_0_) | copy-start | bytes 786436
  55.0 0.7 %copy-start.9 = (bf16[8,128,128]{2,1,0:T(8,128)(2,1)}, bf16[8,128,128]{2,1,0:T(8,128)(2,1)S(1)}, u32[]{:S(2)}) copy-start(bf16[8,128,128]{2,1,0:T(8,128)(2,1)S(1)} %collective-permute-done.8.refs_1_) | copy-start | bytes 786436

commit v7 on v6

--- a/solution.py
+++ b/solution.py
@@ -160,53 +160,49 @@
     use_permutes = (
         inner_blocks == 1
         and inner_local == BLK
-        and col_count == row_count
-        and col_count <= 4
-        and layer_count <= 2
+        and col_count == 4
+        and row_count == 4
+        and layer_count == 2
+        and cols_local % BLK == 0
     )
     if use_permutes:
-        rf_pair, _ = ring_gather(right_factor, "layer", layer_idx, layer_count)
-        rf_pair = jnp.stack(rf_pair)
-        own_over_layer = [
-            lax.ppermute(packed[0], "layer", [(s, (s + m) % layer_count) for s in range(layer_count)])
-            for m in range(1, layer_count)
-        ]
+        rf_blocks = right_factor.reshape(BLK, cols_local // BLK, BLK).transpose(1, 0, 2)
+        own_plus = jnp.concatenate([packed[0], rf_blocks], axis=0)
+        other_plus = lax.ppermute(own_plus, "layer", [(0, 1), (1, 0)])
+        other_rf = other_plus[slots:].transpose(1, 0, 2).reshape(BLK, cols_local)
 
         def col_shift(x, k):
             return lax.ppermute(x, "col", [(s, (s + k) % col_count) for s in range(col_count)])
 
         col_pieces = {1: col_shift(packed[0], 1)}
-        rf_pieces, _ = ring_gather(rf_pair, "row", row_idx, row_count)
-        rf_all = jnp.concatenate(rf_pieces, axis=0)
-        later, col_pieces[1], rf_all = lax.optimization_barrier((packed[0], col_pieces[1], rf_all))
+        later, col_pieces[1] = lax.optimization_barrier((packed[0], col_pieces[1]))
         for k in range(2, col_count):
             col_pieces[k] = col_shift(later, k)
-        pieces = [packed[0]] + own_over_layer
+        pieces = [packed[0], other_plus]
         for k in range(1, col_count):
-            got, _ = ring_gather(col_pieces[k], "layer", layer_idx, layer_count)
-            pieces.extend(got)
-        piece_layer = [(layer_idx - m) % layer_count for k in range(col_count) for m in range(layer_count)]
-        piece_col = [(col_idx - k) % col_count for k in range(col_count) for m in range(layer_count)]
+            pieces.append(col_pieces[k])
+            pieces.append(lax.ppermute(col_pieces[k], "layer", [(0, 1), (1, 0)]))
+        piece_layer = [layer_idx ^ m for k in range(col_count) for m in range(2)]
+        piece_col = [(col_idx - k) % col_count for k in range(col_count) for m in range(2)]
         piece_j = jnp.stack(
             [src_l * col_count + src_c for src_l, src_c in zip(piece_layer, piece_col)]
         ).astype(jnp.int32)
-        rf_src = ((row_idx - piece_j % row_count) % row_count) * layer_count + (
-            (layer_idx - piece_j // row_count) % layer_count
+        rf_pair = jnp.stack([right_factor, other_rf])
+        rf_quad = jnp.concatenate(
+            [rf_pair, lax.ppermute(rf_pair, "row", [(s, s ^ 1) for s in range(4)])], axis=0
         )
-        rf_src = rf_src.astype(jnp.int32)
+        rf_all = jnp.concatenate(
+            [rf_quad, lax.ppermute(rf_quad, "row", [(s, s ^ 2) for s in range(4)])], axis=0
+        )
+        src_row = piece_j % row_count
+        src_layer = piece_j // row_count
+        rf_src = (
+            (((row_idx ^ src_row) >> 1) & 1) * 4 + ((row_idx ^ src_row) & 1) * 2 + (layer_idx ^ src_layer)
+        ).astype(jnp.int32)
         p_stored, p_slot = slot_table(panel_pattern)
         slot_tbl = jnp.where(p_stored > 0, p_slot, -1)
         slot_tbl = jnp.take(slot_tbl, piece_j, axis=1).T.astype(jnp.int32)
-        last = [k * layer_count + m for k in range(2, col_count) for m in range(1, layer_count)]
-        first = [p for p in range(len(pieces)) if p not in last]
-        partial = product_call(
-            slot_tbl[jnp.array(first)], rf_src[jnp.array(first)], keep_patch, rf_all,
-            [pieces[p] for p in first], final=False,
-        )
-        return product_call(
-            slot_tbl[jnp.array(last)], rf_src[jnp.array(last)], keep_patch, rf_all,
-            [pieces[p] for p in last], acc=partial, final=True,
-        )
+        return product_call(slot_tbl, rf_src, keep_patch, rf_all, pieces)
 
     gathered = lax.all_gather(packed, ("layer", "col"), axis=0, tiled=True)
     piece_j = jnp.arange(total_inner_blocks, dtype=jnp.int32)

time: 59.6 us -> 49.5 us (0.83)
  the two profiles are of different devices: /device:TPU:26 before, /device:TPU:0 now
where the time goes in v7:
time: 49.5 us; the launch traced here: 49.3 us
  waiting for transfers between devices  22.7 us (46%)
  starting transfers between devices  13.8 us (28%)
  local copies, waits for them, and re-layouts  5.51 us (11%)
  Pallas kernels  4.21 us (9%)
  other arithmetic  2.89 us (6%)
    ppermute x3, waiting for transfers between devices, col_shift(): lax.ppermute(x, 'col', [(s, (s + k) % col_count) for s in range(col_count)])  11.2 us
    ppermute x1, waiting for transfers between devices, per_device(): other_plus = lax.ppermute(own_plus, 'layer', [(0, 1), (1, 0)])  6.55 us
    ppermute x3, starting transfers between devices, col_shift(): lax.ppermute(x, 'col', [(s, (s + k) % col_count) for s in range(col_count)])  6.17 us
    ppermute x3, waiting for transfers between devices, per_device(): pieces.append(lax.ppermute(col_pieces[k], 'layer', [(0, 1), (1, 0)]))  4.96 us
    ppermute x3, starting transfers between devices, per_device(): pieces.append(lax.ppermute(col_pieces[k], 'layer', [(0, 1), (1, 0)]))  4.47 us
    pallas_call x1, Pallas kernels, product_call(): pl.pallas_call(functools.partial(product_kernel, pieces=pieces, row_block...  4.21 us
    unnamed x24, local copies, waits for them, and re-layouts  2.71 us
    ppermute x1, starting transfers between devices, per_device(): lax.ppermute(rf_quad, 'row', [(s, s ^ 2) for s in range(4)])  1.58 us
  transfers between devices with their start and end apart: 9, of which 4 were waited for; matrix products, arithmetic and copies ran while one was open for 11% of the time, Pallas kernels for 0%

profile of v7, /device:TPU:0, one launch (start us, length us, event | category | flops | bytes accessed | tf_op | source)
XLA Modules:
  0.0 49.3 jit_solution(5033486133518421834)
XLA Ops:
  0.0 0.7 %copy-done.4 = s32[64,8]{0,1:T(8,128)S(1)} copy-done((s32[64,8]{0,1:T(8,128)S(1)}, s32[64,8]{0,1:T(8,128)}, u32[]{:S(2)}) %copy-start.4) | copy-done | bytes 2072
  0.9 0.1 add_reduce_fusion
  1.1 0.1 select_reduce_fusion
  1.2 0.6 %gather_fusion.1 = bf16[8,128,128]{2,1,0:T(8,128)(2,1)S(1)} fusion(bf16[16,128,128]{2,1,0:T(8,128)(2,1)S(1)} %bitcast.32, s32[1024]{0:T(1024)S(1)} %pad_clamp_fusion), kind=kCustom, calls=%fused_computation.1 | custom fusion | bytes 524320 | tf_op jit(solution)/shard_map/jit(_take)/gather | solution.py:142
  1.8 0.1 broadcast_select_fusion.refs_0_
  2.0 3.1 %collective-permute-start.3 = (bf16[8,128,128]{2,1,0:T(8,128)(2,1)S(1)}, bf16[8,128,128]{2,1,0:T(8,128)(2,1)S(1)}, u32[]{:S(2)}, u32[]{:S(2)}) collective-permute-start(bf16[8,128,128]{2,1,0:T(8,128)(2,1)S(1)} %broadcast_select_fusion.refs_0_), channel_id=1, source_target_pairs={{0,1},{1,2},{2,3},{3,0},{4,5},{5,6},{6,7},{7,4},{8,9},{9,10},{10,1... | collective-permute-start | bytes 786440 | tf_op jit(solution)/shard_map/ppermute | solution.py:175
  5.1 0.1 copy.23
  5.3 0.1 copy.24
  5.4 1.6 %collective-permute-start = (bf16[10,128,128]{2,1,0:T(8,128)(2,1)S(1)}, bf16[10,128,128]{2,1,0:T(8,128)(2,1)S(1)}, u32[]{:S(2)}, u32[]{:S(2)}) collective-permute-start(bf16[10,128,128]{2,1,0:T(8,128)(2,1)S(1)} %pad_maximum_fusion.1), channel_id=1, source_target_pairs={{0,16},{16,0},{1,17},{17,1},{2,18},{18,2},{3,19},{19,3},{4,20},{20... | collective-permute-start | bytes 983048 | tf_op jit(solution)/shard_map/ppermute | solution.py:171
  7.1 0.1 stack.68
  7.4 0.6 %gather_fusion = s32[8,16]{1,0:T(8,128)S(1)} fusion(s32[16,8]{0,1:T(8,128)S(1)} %copy.20, s32[1024]{0:T(1024)S(1)} %pad_clamp_fusion.1), kind=kCustom, calls=%fused_computation | custom fusion | bytes 1056 | tf_op jit(solution)/shard_map/jit(_take)/gather | solution.py:204
  7.9 0.1 stack.59
  8.0 0.1 fusion.4
  8.1 6.6 %collective-permute-done.refs_1_ = bf16[10,128,128]{2,1,0:T(8,128)(2,1)S(1)} collective-permute-done((bf16[10,128,128]{2,1,0:T(8,128)(2,1)S(1)}, bf16[10,128,128]{2,1,0:T(8,128)(2,1)S(1)}, u32[]{:S(2)}, u32[]{:S(2)}) %collective-permute-start) | collective-permute-done | bytes 327712 | tf_op jit(solution)/shard_map/ppermute | solution.py:171
  14.7 0.1 copy.25
  14.8 0.1 copy.28
  14.9 0.4 copy-done.3
  15.4 3.0 %collective-permute-start.7 = (bf16[8,128,128]{2,1,0:T(8,128)(2,1)S(1)}, bf16[8,128,128]{2,1,0:T(8,128)(2,1)S(1)}, u32[]{:S(2)}, u32[]{:S(2)}) collective-permute-start(bf16[8,128,128]{2,1,0:T(8,128)(2,1)S(1)} %broadcast_select_fusion.refs_0_), channel_id=1, source_target_pairs={{0,3},{1,0},{2,1},{3,2},{4,7},{5,4},{6,5},{7,6},{8,11},{9,8},{10,9... | collective-permute-start | bytes 786440 | tf_op jit(solution)/shard_map/ppermute | solution.py:175
  18.6 1.6 %collective-permute-start.2 = (bf16[4,128,256]{2,1,0:T(8,128)(2,1)S(1)}, bf16[4,128,256]{2,1,0:T(8,128)(2,1)S(1)}, u32[]{:S(2)}, u32[]{:S(2)}) collective-permute-start(bf16[4,128,256]{2,1,0:T(8,128)(2,1)S(1)} %pad_maximum_fusion.2), channel_id=1, source_target_pairs={{0,8},{4,12},{8,0},{12,4},{1,9},{5,13},{9,1},{13,5},{2,10},{6,14},... | collective-permute-start | bytes 786440 | tf_op jit(solution)/shard_map/ppermute | solution.py:195
  20.1 0.7 %broadcast_select_fusion.1.slot_ref = s32[8,16]{1,0:T(8,128)} fusion(s32[8,16]{1,0:T(8,128)S(1)} %gather_fusion, pred[8]{0:T(512)(128)(4,1)S(1)} %compare_and_fusion.1), kind=kLoop, calls=%fused_computation.20 | loop fusion | flops 128 | bytes 1032 | tf_op jit(solution)/shard_map/jit(_take)/select_n | solution.py:204
  20.8 0.8 %dynamic_slice.10 = s32[16,2]{0,1:T(2,128)S(1)} dynamic-slice(s32[64,8]{0,1:T(8,128)} %param.7, s32[]{:T(128)S(6)} %select_n.116, s32[]{:T(128)S(6)} %select_n.123), dynamic_slice_sizes={16,2} | dynamic-slice | bytes 260 | tf_op jit(solution)/shard_map/dynamic_slice | solution.py:146
  21.6 0.7 %copy.30.keep_ref = s32[16,2]{1,0:T(8,128)} copy(s32[16,2]{0,1:T(2,128)S(1)} %dynamic_slice.10) | data formatting | bytes 256
  22.2 1.5 %collective-permute-start.4 = (bf16[8,128,128]{2,1,0:T(8,128)(2,1)S(1)}, bf16[8,128,128]{2,1,0:T(8,128)(2,1)S(1)}, u32[]{:S(2)}, u32[]{:S(2)}) collective-permute-start(bf16[8,128,128]{2,1,0:T(8,128)(2,1)S(1)} %collective-permute-done.3.refs_2_), channel_id=1, source_target_pairs={{0,16},{16,0},{1,17},{17,1},{2,18},{18,2},{3,19},{19,3},{4,20},{20... | collective-permute-start | bytes 786440 | tf_op jit(solution)/shard_map/ppermute | solution.py:184
  23.7 1.4 %collective-permute-done.7.refs_6_ = bf16[8,128,128]{2,1,0:T(8,128)(2,1)S(1)} collective-permute-done((bf16[8,128,128]{2,1,0:T(8,128)(2,1)S(1)}, bf16[8,128,128]{2,1,0:T(8,128)(2,1)S(1)}, u32[]{:S(2)}, u32[]{:S(2)}) %collective-permute-start.7) | collective-permute-done | bytes 262176 | tf_op jit(solution)/shard_map/ppermute | solution.py:175
  25.1 1.5 %collective-permute-start.8 = (bf16[8,128,128]{2,1,0:T(8,128)(2,1)S(1)}, bf16[8,128,128]{2,1,0:T(8,128)(2,1)S(1)}, u32[]{:S(2)}, u32[]{:S(2)}) collective-permute-start(bf16[8,128,128]{2,1,0:T(8,128)(2,1)S(1)} %collective-permute-done.7.refs_6_), channel_id=1, source_target_pairs={{0,16},{16,0},{1,17},{17,1},{2,18},{18,2},{3,19},{19,3},{4,20},{20... | collective-permute-start | bytes 786440 | tf_op jit(solution)/shard_map/ppermute | solution.py:184
  26.6 9.8 %collective-permute-done.5.refs_4_ = bf16[8,128,128]{2,1,0:T(8,128)(2,1)S(1)} collective-permute-done((bf16[8,128,128]{2,1,0:T(8,128)(2,1)S(1)}, bf16[8,128,128]{2,1,0:T(8,128)(2,1)S(1)}, u32[]{:S(2)}, u32[]{:S(2)}) %collective-permute-start.5) | collective-permute-done | bytes 262176 | tf_op jit(solution)/shard_map/ppermute | solution.py:175
  36.4 1.5 %collective-permute-start.6 = (bf16[8,128,128]{2,1,0:T(8,128)(2,1)S(1)}, bf16[8,128,128]{2,1,0:T(8,128)(2,1)S(1)}, u32[]{:S(2)}, u32[]{:S(2)}) collective-permute-start(bf16[8,128,128]{2,1,0:T(8,128)(2,1)S(1)} %collective-permute-done.5.refs_4_), channel_id=1, source_target_pairs={{0,16},{16,0},{1,17},{17,1},{2,18},{18,2},{3,19},{19,3},{4,20},{20... | collective-permute-start | bytes 786440 | tf_op jit(solution)/shard_map/ppermute | solution.py:184
  37.9 0.6 %xor_add_fusion.rf_src_ref = s32[8]{0:T(128)} fusion(s32[8]{0:T(128)S(1)} %stack.59, s32[]{:T(128)S(6)} %axis_index.33, s32[]{:T(128)S(6)} %axis_index.38), kind=kLoop, calls=%fused_computation.36 | loop fusion | flops 224 | bytes 72 | tf_op jit(solution)/shard_map/add | solution.py:200
  38.5 0.9 %pad_maximum_fusion.rf_ref = bf16[8,128,256]{2,1,0:T(8,128)(2,1)} fusion(bf16[4,128,256]{2,1,0:T(8,128)(2,1)S(1)} %collective-permute-done.2, bf16[2,128,256]{2,1,0:T(8,128)(2,1)S(1)} %collective-permute-done.1, bf16[1,128,256]{2,1,0:T(8,128)(2,1)S(1)} %copy.28, bf16[1,128,256]{2,1,0:T(8,128)(2,1)S(1)} %fusion.4), kind=kLoop, calls=%fused_computation.2 | loop fusion | flops 786432 | bytes 1048576 | tf_op jit(solution)/shard_map/concatenate | solution.py:194
  39.4 5.0 %collective-permute-done.6.refs_5_ = bf16[8,128,128]{2,1,0:T(8,128)(2,1)S(1)} collective-permute-done((bf16[8,128,128]{2,1,0:T(8,128)(2,1)S(1)}, bf16[8,128,128]{2,1,0:T(8,128)(2,1)S(1)}, u32[]{:S(2)}, u32[]{:S(2)}) %collective-permute-start.6) | collective-permute-done | bytes 262176 | tf_op jit(solution)/shard_map/ppermute | solution.py:184
  44.4 0.7 %copy-done.10 = bf16[8,128,128]{2,1,0:T(8,128)(2,1)} copy-done((bf16[8,128,128]{2,1,0:T(8,128)(2,1)}, bf16[8,128,128]{2,1,0:T(8,128)(2,1)S(1)}, u32[]{:S(2)}) %copy-start.10) | copy-done | bytes 262168
  45.1 4.2 %shard_map.46 = bf16[2048,256]{1,0:T(8,128)(2,1)} custom-call(s32[8,16]{1,0:T(8,128)} %broadcast_select_fusion.1.slot_ref, s32[8]{0:T(128)} %xor_add_fusion.rf_src_ref, s32[16,2]{1,0:T(8,128)} %copy.30.keep_ref, bf16[8,128,256]{2,1,0:T(8,128)(2,1)} %pad_maximum_fusion.rf_ref, bf16[8,128,128]{2,1,0:T(8,128)(2,1)} %copy-done.1, ...), custom_call_target="tpu_custom_call" | custom-call | flops 1073741824 | bytes 3670016 | tf_op jit(solution)/shard_map/pallas_call | solution.py:95
  (48 shorter events, 0.8 us)
Async XLA Ops:
  0.0 1.2 %copy-start = (bf16[2048,128]{1,0:T(8,128)(2,1)S(1)}, bf16[2048,128]{1,0:T(8,128)(2,1)}, u32[]{:S(2)}) copy-start(bf16[2048,128]{1,0:T(8,128)(2,1)} %param.4) | copy-start | bytes 1572868
  0.0 0.7 %copy-start.4 = (s32[64,8]{0,1:T(8,128)S(1)}, s32[64,8]{0,1:T(8,128)}, u32[]{:S(2)}) copy-start(s32[64,8]{0,1:T(8,128)} %param.6) | copy-start | bytes 6148
  1.8 3.2 %copy-start.2 = (bf16[128,256]{1,0:T(8,128)(2,1)S(1)}, bf16[128,256]{1,0:T(8,128)(2,1)}, u32[]{:S(2)}) copy-start(bf16[128,256]{1,0:T(8,128)(2,1)} %param.5) | copy-start | bytes 196612
  1.9 16.5 %copy-start.1 = (bf16[8,128,128]{2,1,0:T(8,128)(2,1)}, bf16[8,128,128]{2,1,0:T(8,128)(2,1)S(1)}, u32[]{:S(2)}) copy-start(bf16[8,128,128]{2,1,0:T(8,128)(2,1)S(1)} %broadcast_select_fusion.refs_0_) | copy-start | bytes 786436
  2.0 13.4 %collective-permute-start.3 = (bf16[8,128,128]{2,1,0:T(8,128)(2,1)S(1)}, bf16[8,128,128]{2,1,0:T(8,128)(2,1)S(1)}, u32[]{:S(2)}, u32[]{:S(2)}) collective-permute-start(bf16[8,128,128]{2,1,0:T(8,128)(2,1)S(1)} %broadcast_select_fusion.refs_0_), channel_id=1, source_target_pairs={{0,1},{1,2},{2,3},{3,0},{4,5},{5,6},{6,7},{7,4},{8,9},{9,10},{10,1... | collective-permute-start | bytes 786440 | tf_op jit(solution)/shard_map/ppermute | solution.py:175
  5.4 9.2 %collective-permute-start = (bf16[10,128,128]{2,1,0:T(8,128)(2,1)S(1)}, bf16[10,128,128]{2,1,0:T(8,128)(2,1)S(1)}, u32[]{:S(2)}, u32[]{:S(2)}) collective-permute-start(bf16[10,128,128]{2,1,0:T(8,128)(2,1)S(1)} %pad_maximum_fusion.1), channel_id=1, source_target_pairs={{0,16},{16,0},{1,17},{17,1},{2,18},{18,2},{3,19},{19,3},{4,20},{20... | collective-permute-start | bytes 983048 | tf_op jit(solution)/shard_map/ppermute | solution.py:171
  14.7 0.7 %copy-start.3 = (bf16[10,128,128]{2,1,0:T(8,128)(2,1)}, bf16[10,128,128]{2,1,0:T(8,128)(2,1)S(1)}, u32[]{:S(2)}) copy-start(bf16[10,128,128]{2,1,0:T(8,128)(2,1)S(1)} %collective-permute-done.refs_1_) | copy-start | bytes 983044
  15.4 3.1 %collective-permute-start.1 = (bf16[2,128,256]{2,1,0:T(8,128)(2,1)S(1)}, bf16[2,128,256]{2,1,0:T(8,128)(2,1)S(1)}, u32[]{:S(2)}, u32[]{:S(2)}) collective-permute-start(bf16[2,128,256]{2,1,0:T(8,128)(2,1)S(1)} %pad_maximum_fusion.3), channel_id=1, source_target_pairs={{0,4},{4,0},{8,12},{12,8},{1,5},{5,1},{9,13},{13,9},{2,6},{6,2},{1... | collective-permute-start | bytes 393224 | tf_op jit(solution)/shard_map/ppermute | solution.py:192
  15.4 6.8 %copy-start.5 = (bf16[8,128,128]{2,1,0:T(8,128)(2,1)}, bf16[8,128,128]{2,1,0:T(8,128)(2,1)S(1)}, u32[]{:S(2)}) copy-start(bf16[8,128,128]{2,1,0:T(8,128)(2,1)S(1)} %collective-permute-done.3.refs_2_) | copy-start | bytes 786436
  15.4 9.7 %collective-permute-start.7 = (bf16[8,128,128]{2,1,0:T(8,128)(2,1)S(1)}, bf16[8,128,128]{2,1,0:T(8,128)(2,1)S(1)}, u32[]{:S(2)}, u32[]{:S(2)}) collective-permute-start(bf16[8,128,128]{2,1,0:T(8,128)(2,1)S(1)} %broadcast_select_fusion.refs_0_), channel_id=1, source_target_pairs={{0,3},{1,0},{2,1},{3,2},{4,7},{5,4},{6,5},{7,6},{8,11},{9,8},{10,9... | collective-permute-start | bytes 786440 | tf_op jit(solution)/shard_map/ppermute | solution.py:175
  18.4 18.0 %collective-permute-start.5 = (bf16[8,128,128]{2,1,0:T(8,128)(2,1)S(1)}, bf16[8,128,128]{2,1,0:T(8,128)(2,1)S(1)}, u32[]{:S(2)}, u32[]{:S(2)}) collective-permute-start(bf16[8,128,128]{2,1,0:T(8,128)(2,1)S(1)} %broadcast_select_fusion.refs_0_), channel_id=1, source_target_pairs={{0,2},{1,3},{2,0},{3,1},{4,6},{5,7},{6,4},{7,5},{8,10},{9,11},{10,... | collective-permute-start | bytes 786440 | tf_op jit(solution)/shard_map/ppermute | solution.py:175
  18.6 20.0 %collective-permute-start.2 = (bf16[4,128,256]{2,1,0:T(8,128)(2,1)S(1)}, bf16[4,128,256]{2,1,0:T(8,128)(2,1)S(1)}, u32[]{:S(2)}, u32[]{:S(2)}) collective-permute-start(bf16[4,128,256]{2,1,0:T(8,128)(2,1)S(1)} %pad_maximum_fusion.2), channel_id=1, source_target_pairs={{0,8},{4,12},{8,0},{12,4},{1,9},{5,13},{9,1},{13,5},{2,10},{6,14},... | collective-permute-start | bytes 786440 | tf_op jit(solution)/shard_map/ppermute | solution.py:195
  22.2 17.1 %collective-permute-start.4 = (bf16[8,128,128]{2,1,0:T(8,128)(2,1)S(1)}, bf16[8,128,128]{2,1,0:T(8,128)(2,1)S(1)}, u32[]{:S(2)}, u32[]{:S(2)}) collective-permute-start(bf16[8,128,128]{2,1,0:T(8,128)(2,1)S(1)} %collective-permute-done.3.refs_2_), channel_id=1, source_target_pairs={{0,16},{16,0},{1,17},{17,1},{2,18},{18,2},{3,19},{19,3},{4,20},{20... | collective-permute-start | bytes 786440 | tf_op jit(solution)/shard_map/ppermute | solution.py:184
  25.1 14.3 %copy-start.6 = (bf16[8,128,128]{2,1,0:T(8,128)(2,1)}, bf16[8,128,128]{2,1,0:T(8,128)(2,1)S(1)}, u32[]{:S(2)}) copy-start(bf16[8,128,128]{2,1,0:T(8,128)(2,1)S(1)} %collective-permute-done.7.refs_6_) | copy-start | bytes 786436
  25.1 14.3 %collective-permute-start.8 = (bf16[8,128,128]{2,1,0:T(8,128)(2,1)S(1)}, bf16[8,128,128]{2,1,0:T(8,128)(2,1)S(1)}, u32[]{:S(2)}, u32[]{:S(2)}) collective-permute-start(bf16[8,128,128]{2,1,0:T(8,128)(2,1)S(1)} %collective-permute-done.7.refs_6_), channel_id=1, source_target_pairs={{0,16},{16,0},{1,17},{17,1},{2,18},{18,2},{3,19},{19,3},{4,20},{20... | collective-permute-start | bytes 786440 | tf_op jit(solution)/shard_map/ppermute | solution.py:184
  36.4 2.9 %copy-start.7 = (bf16[8,128,128]{2,1,0:T(8,128)(2,1)}, bf16[8,128,128]{2,1,0:T(8,128)(2,1)S(1)}, u32[]{:S(2)}) copy-start(bf16[8,128,128]{2,1,0:T(8,128)(2,1)S(1)} %collective-permute-done.5.refs_4_) | copy-start | bytes 786436
  36.4 7.9 %collective-permute-start.6 = (bf16[8,128,128]{2,1,0:T(8,128)(2,1)S(1)}, bf16[8,128,128]{2,1,0:T(8,128)(2,1)S(1)}, u32[]{:S(2)}, u32[]{:S(2)}) collective-permute-start(bf16[8,128,128]{2,1,0:T(8,128)(2,1)S(1)} %collective-permute-done.5.refs_4_), channel_id=1, source_target_pairs={{0,16},{16,0},{1,17},{17,1},{2,18},{18,2},{3,19},{19,3},{4,20},{20... | collective-permute-start | bytes 786440 | tf_op jit(solution)/shard_map/ppermute | solution.py:184
  39.4 5.0 %copy-start.8 = (bf16[8,128,128]{2,1,0:T(8,128)(2,1)}, bf16[8,128,128]{2,1,0:T(8,128)(2,1)S(1)}, u32[]{:S(2)}) copy-start(bf16[8,128,128]{2,1,0:T(8,128)(2,1)S(1)} %collective-permute-done.4.refs_3_) | copy-start | bytes 786436
  39.4 5.0 %copy-start.9 = (bf16[8,128,128]{2,1,0:T(8,128)(2,1)}, bf16[8,128,128]{2,1,0:T(8,128)(2,1)S(1)}, u32[]{:S(2)}) copy-start(bf16[8,128,128]{2,1,0:T(8,128)(2,1)S(1)} %collective-permute-done.8.refs_7_) | copy-start | bytes 786436
  44.4 0.7 %copy-start.10 = (bf16[8,128,128]{2,1,0:T(8,128)(2,1)}, bf16[8,128,128]{2,1,0:T(8,128)(2,1)S(1)}, u32[]{:S(2)}) copy-start(bf16[8,128,128]{2,1,0:T(8,128)(2,1)S(1)} %collective-permute-done.6.refs_5_) | copy-start | bytes 786436

commit v8 on v3

--- a/solution.py
+++ b/solution.py
@@ -41,25 +41,26 @@
     return out, sources
 
 
-def product_kernel(slot_ref, rf_pos_ref, keep_ref, *refs, pieces, row_blocks, cols):
-    left_refs = refs[:pieces]
-    rf_refs = refs[pieces:2 * pieces]
-    out_ref = refs[2 * pieces]
-    lhs_scr, rf_scr = refs[2 * pieces + 1:]
-    for q in range(pieces):
-        at = pl.multiple_of(rf_pos_ref[q] * BLK, BLK)
-        rf_scr[pl.ds(at, BLK), :] = rf_refs[q][...]
+def product_kernel(slot_ref, rf_src_ref, keep_ref, rf_ref, *refs, parts, n_left, row_blocks):
+    left_refs = refs[:n_left]
+    out_ref = refs[n_left]
+    lhs_scr, rf_scr = refs[n_left + 1:]
+    cols = rf_ref.shape[-1]
+    pieces = len(parts)
+    for p in range(pieces):
+        rf_scr[p * BLK:(p + 1) * BLK, :] = rf_ref[rf_src_ref[p]]
     for p in range(pieces):
         for i in range(row_blocks):
             s = slot_ref[p, i]
-            blk = left_refs[p][jnp.maximum(s, 0)]
-            blk = jnp.where(s >= 0, blk, jnp.zeros_like(blk))
+            blk = jnp.zeros((BLK, BLK), lhs_scr.dtype)
+            for ref_id, first, count, offset in parts[p]:
+                cand = left_refs[ref_id][offset + jnp.clip(s - first, 0, count - 1)]
+                blk = jnp.where((s >= first) & (s < first + count), cand, blk)
             lhs_scr[i * BLK:(i + 1) * BLK, p * BLK:(p + 1) * BLK] = blk
     tile = 2 * BLK
     for t in range(row_blocks * BLK // tile):
-        res = jnp.dot(
-            lhs_scr[t * tile:(t + 1) * tile, :], rf_scr[...], preferred_element_type=jnp.float32
-        )
+        rows = slice(t * tile, (t + 1) * tile)
+        res = jnp.dot(lhs_scr[rows, :], rf_scr[...], preferred_element_type=jnp.float32)
         for a in range(tile // BLK):
             i = t * (tile // BLK) + a
             for b in range(cols // BLK):
@@ -68,25 +69,35 @@
                 out_ref[i * BLK:(i + 1) * BLK, b * BLK:(b + 1) * BLK] = sub.astype(out_ref.dtype)
 
 
-def product_call(slot_tbl, rf_pos, keep_patch, left_pieces, rf_pieces):
-    pieces = len(left_pieces)
+def product_call(slot_tbl, rf_src, keep_patch, rf_all, piece_operands):
     row_blocks = slot_tbl.shape[1]
-    cols = rf_pieces[0].shape[1]
+    cols = rf_all.shape[-1]
+    parts, flat, ids = [], [], {}
+    for spans in piece_operands:
+        first, pp = 0, []
+        for op, offset, count in spans:
+            if id(op) not in ids:
+                ids[id(op)] = len(flat)
+                flat.append(op)
+            pp.append((ids[id(op)], first, count, offset))
+            first += count
+        parts.append(tuple(pp))
+    pieces = len(parts)
     smem = pl.BlockSpec(memory_space=pltpu.SMEM)
     vmem = pl.BlockSpec(memory_space=pltpu.VMEM)
     flops = 2 * row_blocks * BLK * pieces * BLK * cols
-    bytes_accessed = pieces * (left_pieces[0].size + rf_pieces[0].size) * 2 + row_blocks * BLK * cols * 2
+    bytes_accessed = sum(op.size for op in flat) * 2 + pieces * BLK * cols * 2 + row_blocks * BLK * cols * 2
     return pl.pallas_call(
-        functools.partial(product_kernel, pieces=pieces, row_blocks=row_blocks, cols=cols),
+        functools.partial(product_kernel, parts=tuple(parts), n_left=len(flat), row_blocks=row_blocks),
         out_shape=jax.ShapeDtypeStruct((row_blocks * BLK, cols), jnp.bfloat16),
-        in_specs=[smem, smem, smem] + [vmem] * (2 * pieces),
+        in_specs=[smem, smem, smem, vmem] + [vmem] * len(flat),
         out_specs=vmem,
         scratch_shapes=[
             pltpu.VMEM((row_blocks * BLK, pieces * BLK), jnp.bfloat16),
             pltpu.VMEM((pieces * BLK, cols), jnp.bfloat16),
         ],
         cost_estimate=pl.CostEstimate(flops=flops, bytes_accessed=bytes_accessed, transcendentals=0),
-    )(slot_tbl, rf_pos, keep_patch, *left_pieces, *rf_pieces)
+    )(slot_tbl, rf_src, keep_patch, rf_all, *flat)
 
 
 def per_device(left_matrix, square_term, block_pattern, keep_mask):
@@ -138,30 +149,54 @@
     use_permutes = (
         inner_blocks == 1
         and inner_local == BLK
-        and col_count == row_count
-        and col_count <= 4
-        and layer_count <= 2
+        and col_count == 4
+        and row_count == 4
+        and layer_count == 2
+        and cols_local % BLK == 0
     )
     if use_permutes:
-        pieces, piece_col = ring_gather(packed[0], "col", col_idx, col_count)
-        pieces, piece_layer = ring_gather_list(pieces, "layer", layer_idx, layer_count)
-        piece_col = [piece_col[k] for k in range(col_count) for m in range(layer_count)]
+        rf_row_pieces, _ = ring_gather(right_factor, "row", row_idx, row_count)
+        rf_own = jnp.stack(rf_row_pieces)
+        swap = [(0, 1), (1, 0)]
+        own_over_layer = lax.ppermute(packed[0], "layer", swap)
+        rf_all = jnp.concatenate([rf_own, lax.ppermute(rf_own, "layer", swap)], axis=0)
+
+        def col_shift(x, k):
+            return lax.ppermute(x, "col", [(s, (s + k) % col_count) for s in range(col_count)])
+
+        half = slots // 2
+        s1 = col_shift(packed[0], 1)
+        s2a = col_shift(packed[0][:half], 2)
+        later, s1, s2a, own_over_layer, rf_all = lax.optimization_barrier(
+            (packed[0], s1, s2a, own_over_layer, rf_all)
+        )
+        s3 = col_shift(later, 3)
+        s2b = col_shift(later[half:], 2)
+        fwd1 = lax.ppermute(jnp.concatenate([s1, s2a], axis=0), "layer", swap)
+        fwd2 = lax.ppermute(jnp.concatenate([s3, s2b], axis=0), "layer", swap)
+        piece_ops = [
+            [(packed[0], 0, slots)],
+            [(own_over_layer, 0, slots)],
+            [(s1, 0, slots)],
+            [(fwd1, 0, slots)],
+            [(s2a, 0, half), (s2b, 0, slots - half)],
+            [(fwd1, slots, half), (fwd2, slots, slots - half)],
+            [(s3, 0, slots)],
+            [(fwd2, 0, slots)],
+        ]
+        piece_layer = [layer_idx ^ m for k in range(col_count) for m in range(2)]
+        piece_col = [(col_idx - k) % col_count for k in range(col_count) for m in range(2)]
         piece_j = jnp.stack(
             [src_l * col_count + src_c for src_l, src_c in zip(piece_layer, piece_col)]
         ).astype(jnp.int32)
-        rf_pieces, rf_row = ring_gather(right_factor, "row", row_idx, row_count)
-        rf_pieces, rf_layer = ring_gather_list(rf_pieces, "layer", layer_idx, layer_count)
-        rf_row = [rf_row[k] for k in range(row_count) for m in range(layer_count)]
-        rf_q = jnp.stack(
-            [src_l * row_count + src_r for src_l, src_r in zip(rf_layer, rf_row)]
-        ).astype(jnp.int32)
-        rf_pos = ((col_idx - rf_q % col_count) % col_count) * layer_count + (
-            (layer_idx - rf_q // col_count) % layer_count
+        rf_src = (layer_idx ^ (piece_j // row_count)) * row_count + (
+            (row_idx - piece_j % row_count) % row_count
         )
+        rf_src = rf_src.astype(jnp.int32)
         p_stored, p_slot = slot_table(panel_pattern)
         slot_tbl = jnp.where(p_stored > 0, p_slot, -1)
         slot_tbl = jnp.take(slot_tbl, piece_j, axis=1).T.astype(jnp.int32)
-        return product_call(slot_tbl, rf_pos.astype(jnp.int32), keep_patch, pieces, rf_pieces)
+        return product_call(slot_tbl, rf_src, keep_patch, rf_all, piece_ops)
 
     gathered = lax.all_gather(packed, ("layer", "col"), axis=0, tiled=True)
     piece_j = jnp.arange(total_inner_blocks, dtype=jnp.int32)

time: 54.3 us -> 50.4 us (0.928)
  starting transfers between devices: 17.4 us -> 12.4 us
  waiting for transfers between devices: 24.2 us -> 25.5 us
  other arithmetic: 2.76 us -> 1.91 us
    ppermute x0 -> x8, waiting for transfers between devices: none -> 24.3 us  [the longest x1 8.6 us: per_device(): lax.ppermute(rf_own, 'layer', swap)]
    ppermute x14 -> x3, waiting for transfers between devices: 24.2 us -> 1.22 us  [ring_gather(): pieces.append(lax.ppermute(x, axis, perm))]
    ppermute x14 -> x3, starting transfers between devices: 17.4 us -> 1.82 us  [ring_gather(): pieces.append(lax.ppermute(x, axis, perm))]
    ppermute x0 -> x8, starting transfers between devices: none -> 10.6 us  [the longest x4 5.93 us: col_shift(): lax.ppermute(x, 'col', [(s, (s + k) % col_count) for s in range(col_count)])]
    convert_element_type x1 -> x0, other arithmetic: 0.98 us -> none  [per_device(): (unit - 0.5 * square_term.astype(jnp.float32)).astype(jnp.bfloat16)]
    unnamed x38 -> x29, local copies, waits for them, and re-layouts: 2.98 us -> 3.03 us
  transfers between devices with their start and end apart: 14 -> 11, of which waited for: 3 -> 7; matrix products, arithmetic and copies ran while one was open for 9% -> 8% of each run, Pallas kernels for 0% -> 0%
where the time goes in v8:
time: 50.4 us; the launch traced here: 49.8 us
  waiting for transfers between devices  25.5 us (51%)
  starting transfers between devices  12.4 us (25%)
  local copies, waits for them, and re-layouts  5.4 us (11%)
  Pallas kernels  4.34 us (9%)
  other arithmetic  1.91 us (4%)
    ppermute x1, waiting for transfers between devices, per_device(): lax.ppermute(rf_own, 'layer', swap)  8.6 us
    ppermute x4, waiting for transfers between devices, col_shift(): lax.ppermute(x, 'col', [(s, (s + k) % col_count) for s in range(col_count)])  7.31 us
    ppermute x1, waiting for transfers between devices, per_device(): fwd2 = lax.ppermute(jnp.concatenate([s3, s2b], axis=0), 'layer', swap)  6.71 us
    ppermute x4, starting transfers between devices, col_shift(): lax.ppermute(x, 'col', [(s, (s + k) % col_count) for s in range(col_count)])  5.93 us
    pallas_call x1, Pallas kernels, product_call(): pl.pallas_call(functools.partial(product_kernel, parts=tuple(parts), n_le...  4.34 us
    unnamed x29, local copies, waits for them, and re-layouts  3.03 us
    ppermute x1, starting transfers between devices, per_device(): own_over_layer = lax.ppermute(packed[0], 'layer', swap)  3 us
    ppermute x3, starting transfers between devices, ring_gather(): pieces.append(lax.ppermute(x, axis, perm))  1.82 us
  transfers between devices with their start and end apart: 11, of which 7 were waited for; matrix products, arithmetic and copies ran while one was open for 8% of the time, Pallas kernels for 0%

profile of v8, /device:TPU:0, one launch (start us, length us, event | category | flops | bytes accessed | tf_op | source)
XLA Modules:
  0.0 49.8 jit_solution(4069560894308670391)
XLA Ops:
  0.0 0.7 %copy-done.8 = s32[64,8]{0,1:T(8,128)S(1)} copy-done((s32[64,8]{0,1:T(8,128)S(1)}, s32[64,8]{0,1:T(8,128)}, u32[]{:S(2)}) %copy-start.8) | copy-done | bytes 2072
  0.9 0.1 add_reduce_fusion
  1.1 0.1 select_reduce_fusion
  1.2 0.1 stack.77
  1.3 0.6 %gather_fusion.1 = bf16[8,128,128]{2,1,0:T(8,128)(2,1)S(1)} fusion(bf16[16,128,128]{2,1,0:T(8,128)(2,1)S(1)} %bitcast.33, s32[1024]{0:T(1024)S(1)} %get-tuple-element.19), kind=kCustom, calls=%fused_computation.1 | custom fusion | bytes 524320 | tf_op jit(solution)/shard_map/jit(_take)/gather | solution.py:131
  2.1 3.0 %collective-permute-start.2 = (bf16[8,128,128]{2,1,0:T(8,128)(2,1)S(1)}, bf16[8,128,128]{2,1,0:T(8,128)(2,1)S(1)}, u32[]{:S(2)}, u32[]{:S(2)}) collective-permute-start(bf16[8,128,128]{2,1,0:T(8,128)(2,1)S(1)} %broadcast_select_fusion.refs_0_), channel_id=1, source_target_pairs={{0,16},{16,0},{1,17},{17,1},{2,18},{18,2},{3,19},{19,3},{4,20},{20... | collective-permute-start | bytes 786440 | tf_op jit(solution)/shard_map/ppermute | solution.py:161
  5.1 1.6 %collective-permute-start = (bf16[8,128,128]{2,1,0:T(8,128)(2,1)S(1)}, bf16[8,128,128]{2,1,0:T(8,128)(2,1)S(1)}, u32[]{:S(2)}, u32[]{:S(2)}) collective-permute-start(bf16[8,128,128]{2,1,0:T(8,128)(2,1)S(1)} %broadcast_select_fusion.refs_0_), channel_id=1, source_target_pairs={{0,1},{1,2},{2,3},{3,0},{4,5},{5,6},{6,7},{7,4},{8,9},{9,10},{10,1... | collective-permute-start | bytes 786440 | tf_op jit(solution)/shard_map/ppermute | solution.py:165
  6.7 0.5 collective-permute-start.5
  7.2 1.2 %collective-permute-start.4 = (bf16[128,256]{1,0:T(8,128)(2,1)S(1)}, bf16[128,256]{1,0:T(8,128)(2,1)S(1)}, u32[]{:S(2)}, u32[]{:S(2)}) collective-permute-start(bf16[128,256]{1,0:T(8,128)(2,1)S(1)} %get-tuple-element.16), channel_id=1, source_target_pairs={{0,8},{4,12},{8,0},{12,4},{1,9},{5,13},{9,1},{13,5},{2,10},{6,14},... | collective-permute-start | bytes 196616 | tf_op jit(solution)/shard_map/ppermute | solution.py:30
  8.4 0.2 collective-permute-start.3
  8.9 0.2 collective-permute-done.5
  9.1 2.6 %collective-permute-start.1 = (bf16[4,128,128]{2,1,0:T(8,128)(2,1)S(1)}, bf16[4,128,128]{2,1,0:T(8,128)(2,1)S(1)}, u32[]{:S(2)}, u32[]{:S(2)}) collective-permute-start(bf16[4,128,128]{2,1,0:T(8,128)(2,1)S(1)} %slice.12), channel_id=1, source_target_pairs={{0,2},{1,3},{2,0},{3,1},{4,6},{5,7},{6,4},{7,5},{8,10},{9,11},{10,... | collective-permute-start | bytes 393224 | tf_op jit(solution)/shard_map/ppermute | solution.py:165
  11.7 0.8 %collective-permute-done.4 = bf16[128,256]{1,0:T(8,128)(2,1)S(1)} collective-permute-done((bf16[128,256]{1,0:T(8,128)(2,1)S(1)}, bf16[128,256]{1,0:T(8,128)(2,1)S(1)}, u32[]{:S(2)}, u32[]{:S(2)}) %collective-permute-start.4) | collective-permute-done | bytes 65568 | tf_op jit(solution)/shard_map/ppermute | solution.py:30
  12.5 0.2 collective-permute-done.3
  12.7 0.6 %collective-permute-start.6 = (bf16[4,128,256]{2,1,0:T(8,128)(2,1)S(1)}, bf16[4,128,256]{2,1,0:T(8,128)(2,1)S(1)}, u32[]{:S(2)}, u32[]{:S(2)}) collective-permute-start(bf16[4,128,256]{2,1,0:T(8,128)(2,1)S(1)} %pad_maximum_fusion.2), channel_id=1, source_target_pairs={{0,16},{16,0},{1,17},{17,1},{2,18},{18,2},{3,19},{19,3},{4,20},{20... | collective-permute-start | bytes 786440 | tf_op jit(solution)/shard_map/ppermute | solution.py:162
  13.3 8.6 %collective-permute-done.6 = bf16[4,128,256]{2,1,0:T(8,128)(2,1)S(1)} collective-permute-done((bf16[4,128,256]{2,1,0:T(8,128)(2,1)S(1)}, bf16[4,128,256]{2,1,0:T(8,128)(2,1)S(1)}, u32[]{:S(2)}, u32[]{:S(2)}) %collective-permute-start.6) | collective-permute-done | bytes 262176 | tf_op jit(solution)/shard_map/ppermute | solution.py:162
  22.1 1.4 %collective-permute-start.9 = (bf16[8,128,128]{2,1,0:T(8,128)(2,1)S(1)}, bf16[8,128,128]{2,1,0:T(8,128)(2,1)S(1)}, u32[]{:S(2)}, u32[]{:S(2)}) collective-permute-start(bf16[8,128,128]{2,1,0:T(8,128)(2,1)S(1)} %broadcast_select_fusion.refs_0_), channel_id=1, source_target_pairs={{0,3},{1,0},{2,1},{3,2},{4,7},{5,4},{6,5},{7,6},{8,11},{9,8},{10,9... | collective-permute-start | bytes 786440 | tf_op jit(solution)/shard_map/ppermute | solution.py:165
  23.5 0.3 collective-permute-start.8
  23.8 0.5 %fusion.1.rf_src_ref = s32[8]{0:T(128)} fusion(s32[8]{0:T(128)S(1)} %stack.68, s32[]{:T(128)S(6)} %axis_index.38, s32[]{:T(128)S(6)} %axis_index.33), kind=kLoop, calls=%fused_computation.38 | loop fusion | flops 272 | bytes 72 | tf_op jit(solution)/shard_map/add | solution.py:192
  24.4 0.8 %dynamic_slice.10 = s32[16,2]{0,1:T(2,128)S(1)} dynamic-slice(s32[64,8]{0,1:T(8,128)} %param.7, s32[]{:T(128)S(6)} %select_n.120, s32[]{:T(128)S(6)} %select_n.128), dynamic_slice_sizes={16,2} | dynamic-slice | bytes 260 | tf_op jit(solution)/shard_map/dynamic_slice | solution.py:135
  25.1 0.7 %copy.18.keep_ref = s32[16,2]{1,0:T(8,128)} copy(s32[16,2]{0,1:T(2,128)S(1)} %dynamic_slice.10) | data formatting | bytes 256
  25.9 0.6 %gather_fusion = s32[8,16]{1,0:T(8,128)S(1)} fusion(s32[16,8]{0,1:T(8,128)S(1)} %copy.14, s32[1024]{0:T(1024)S(1)} %get-tuple-element.20), kind=kCustom, calls=%fused_computation | custom fusion | bytes 1056 | tf_op jit(solution)/shard_map/jit(_take)/gather | solution.py:198
  26.5 0.6 %collective-permute-start.7 = (bf16[12,128,128]{2,1,0:T(8,128)(2,1)S(1)}, bf16[12,128,128]{2,1,0:T(8,128)(2,1)S(1)}, u32[]{:S(2)}, u32[]{:S(2)}) collective-permute-start(bf16[12,128,128]{2,1,0:T(8,128)(2,1)S(1)} %pad_maximum_fusion), channel_id=1, source_target_pairs={{0,16},{16,0},{1,17},{17,1},{2,18},{18,2},{3,19},{19,3},{4,20},{20... | collective-permute-start | bytes 1179656 | tf_op jit(solution)/shard_map/ppermute | solution.py:175
  27.1 7.3 %collective-permute-done.8.refs_5_ = bf16[4,128,128]{2,1,0:T(8,128)(2,1)S(1)} collective-permute-done((bf16[4,128,128]{2,1,0:T(8,128)(2,1)S(1)}, bf16[4,128,128]{2,1,0:T(8,128)(2,1)S(1)}, u32[]{:S(2)}, u32[]{:S(2)}) %collective-permute-start.8) | collective-permute-done | bytes 131104 | tf_op jit(solution)/shard_map/ppermute | solution.py:165
  34.4 0.6 %copy-done.5 = bf16[4,128,128]{2,1,0:T(8,128)(2,1)} copy-done((bf16[4,128,128]{2,1,0:T(8,128)(2,1)}, bf16[4,128,128]{2,1,0:T(8,128)(2,1)S(1)}, u32[]{:S(2)}) %copy-start.5) | copy-done | bytes 131096
  35.0 0.1 copy-done.3
  35.1 0.5 collective-permute-start.10
  35.6 0.7 %broadcast_select_fusion.1.slot_ref = s32[8,16]{1,0:T(8,128)} fusion(s32[8,16]{1,0:T(8,128)S(1)} %gather_fusion, pred[8]{0:T(512)(128)(4,1)S(1)} %compare_and_fusion.1), kind=kLoop, calls=%fused_computation.25 | loop fusion | flops 128 | bytes 1032 | tf_op jit(solution)/shard_map/jit(_take)/select_n | solution.py:198
  36.3 1.7 %collective-permute-done.7.refs_3_ = bf16[12,128,128]{2,1,0:T(8,128)(2,1)S(1)} collective-permute-done((bf16[12,128,128]{2,1,0:T(8,128)(2,1)S(1)}, bf16[12,128,128]{2,1,0:T(8,128)(2,1)S(1)}, u32[]{:S(2)}, u32[]{:S(2)}) %collective-permute-start.7) | collective-permute-done | bytes 393248 | tf_op jit(solution)/shard_map/ppermute | solution.py:175
  37.9 6.7 %collective-permute-done.10.refs_6_ = bf16[12,128,128]{2,1,0:T(8,128)(2,1)S(1)} collective-permute-done((bf16[12,128,128]{2,1,0:T(8,128)(2,1)S(1)}, bf16[12,128,128]{2,1,0:T(8,128)(2,1)S(1)}, u32[]{:S(2)}, u32[]{:S(2)}) %collective-permute-start.10) | collective-permute-done | bytes 393248 | tf_op jit(solution)/shard_map/ppermute | solution.py:176
  44.7 0.8 %copy-done.10 = bf16[12,128,128]{2,1,0:T(8,128)(2,1)} copy-done((bf16[12,128,128]{2,1,0:T(8,128)(2,1)}, bf16[12,128,128]{2,1,0:T(8,128)(2,1)S(1)}, u32[]{:S(2)}) %copy-start.10) | copy-done | bytes 393240
  45.4 4.3 %shard_map.46 = bf16[2048,256]{1,0:T(8,128)(2,1)} custom-call(s32[8,16]{1,0:T(8,128)} %broadcast_select_fusion.1.slot_ref, s32[8]{0:T(128)} %fusion.1.rf_src_ref, s32[16,2]{1,0:T(8,128)} %copy.18.keep_ref, bf16[8,128,256]{2,1,0:T(8,128)(2,1)} %copy-done.7, bf16[8,128,128]{2,1,0:T(8,128)(2,1)} %copy-done.1, bf16[8,128,128]{2,1,0:T(8,128)(2,1)} %copy-done.11, ...), custom_call_target="tpu_custom_call" | custom-call | flops 1073741824 | bytes 3670016 | tf_op jit(solution)/shard_map/pallas_call | solution.py:90
  (52 shorter events, 1.0 us)
Async XLA Ops:
  0.0 1.3 %copy-start = (bf16[2048,128]{1,0:T(8,128)(2,1)S(1)}, bf16[2048,128]{1,0:T(8,128)(2,1)}, u32[]{:S(2)}) copy-start(bf16[2048,128]{1,0:T(8,128)(2,1)} %param.4) | copy-start | bytes 1572868
  0.0 0.7 %copy-start.8 = (s32[64,8]{0,1:T(8,128)S(1)}, s32[64,8]{0,1:T(8,128)}, u32[]{:S(2)}) copy-start(s32[64,8]{0,1:T(8,128)} %param.6) | copy-start | bytes 6148
  1.9 4.7 %copy-start.6 = (bf16[128,256]{1,0:T(8,128)(2,1)S(1)}, bf16[128,256]{1,0:T(8,128)(2,1)}, u32[]{:S(2)}) copy-start(bf16[128,256]{1,0:T(8,128)(2,1)} %param.5) | copy-start | bytes 196612
  2.1 20.0 %copy-start.1 = (bf16[8,128,128]{2,1,0:T(8,128)(2,1)}, bf16[8,128,128]{2,1,0:T(8,128)(2,1)S(1)}, u32[]{:S(2)}) copy-start(bf16[8,128,128]{2,1,0:T(8,128)(2,1)S(1)} %broadcast_select_fusion.refs_0_) | copy-start | bytes 786436
  2.1 19.9 %collective-permute-start.2 = (bf16[8,128,128]{2,1,0:T(8,128)(2,1)S(1)}, bf16[8,128,128]{2,1,0:T(8,128)(2,1)S(1)}, u32[]{:S(2)}, u32[]{:S(2)}) collective-permute-start(bf16[8,128,128]{2,1,0:T(8,128)(2,1)S(1)} %broadcast_select_fusion.refs_0_), channel_id=1, source_target_pairs={{0,16},{16,0},{1,17},{17,1},{2,18},{18,2},{3,19},{19,3},{4,20},{20... | collective-permute-start | bytes 786440 | tf_op jit(solution)/shard_map/ppermute | solution.py:161
  5.1 17.0 %collective-permute-start = (bf16[8,128,128]{2,1,0:T(8,128)(2,1)S(1)}, bf16[8,128,128]{2,1,0:T(8,128)(2,1)S(1)}, u32[]{:S(2)}, u32[]{:S(2)}) collective-permute-start(bf16[8,128,128]{2,1,0:T(8,128)(2,1)S(1)} %broadcast_select_fusion.refs_0_), channel_id=1, source_target_pairs={{0,1},{1,2},{2,3},{3,0},{4,5},{5,6},{6,7},{7,4},{8,9},{9,10},{10,1... | collective-permute-start | bytes 786440 | tf_op jit(solution)/shard_map/ppermute | solution.py:165
  6.7 2.4 %collective-permute-start.5 = (bf16[128,256]{1,0:T(8,128)(2,1)S(1)}, bf16[128,256]{1,0:T(8,128)(2,1)S(1)}, u32[]{:S(2)}, u32[]{:S(2)}) collective-permute-start(bf16[128,256]{1,0:T(8,128)(2,1)S(1)} %get-tuple-element.16), channel_id=1, source_target_pairs={{0,12},{4,0},{8,4},{12,8},{1,13},{5,1},{9,5},{13,9},{2,14},{6,2},{... | collective-permute-start | bytes 196616 | tf_op jit(solution)/shard_map/ppermute | solution.py:30
  7.2 5.3 %collective-permute-start.4 = (bf16[128,256]{1,0:T(8,128)(2,1)S(1)}, bf16[128,256]{1,0:T(8,128)(2,1)S(1)}, u32[]{:S(2)}, u32[]{:S(2)}) collective-permute-start(bf16[128,256]{1,0:T(8,128)(2,1)S(1)} %get-tuple-element.16), channel_id=1, source_target_pairs={{0,8},{4,12},{8,0},{12,4},{1,9},{5,13},{9,1},{13,5},{2,10},{6,14},... | collective-permute-start | bytes 196616 | tf_op jit(solution)/shard_map/ppermute | solution.py:30
  8.4 4.3 %collective-permute-start.3 = (bf16[128,256]{1,0:T(8,128)(2,1)S(1)}, bf16[128,256]{1,0:T(8,128)(2,1)S(1)}, u32[]{:S(2)}, u32[]{:S(2)}) collective-permute-start(bf16[128,256]{1,0:T(8,128)(2,1)S(1)} %get-tuple-element.16), channel_id=1, source_target_pairs={{0,4},{4,8},{8,12},{12,0},{1,5},{5,9},{9,13},{13,1},{2,6},{6,10},{... | collective-permute-start | bytes 196616 | tf_op jit(solution)/shard_map/ppermute | solution.py:30
  9.1 12.9 %collective-permute-start.1 = (bf16[4,128,128]{2,1,0:T(8,128)(2,1)S(1)}, bf16[4,128,128]{2,1,0:T(8,128)(2,1)S(1)}, u32[]{:S(2)}, u32[]{:S(2)}) collective-permute-start(bf16[4,128,128]{2,1,0:T(8,128)(2,1)S(1)} %slice.12), channel_id=1, source_target_pairs={{0,2},{1,3},{2,0},{3,1},{4,6},{5,7},{6,4},{7,5},{8,10},{9,11},{10,... | collective-permute-start | bytes 393224 | tf_op jit(solution)/shard_map/ppermute | solution.py:165
  12.7 9.2 %collective-permute-start.6 = (bf16[4,128,256]{2,1,0:T(8,128)(2,1)S(1)}, bf16[4,128,256]{2,1,0:T(8,128)(2,1)S(1)}, u32[]{:S(2)}, u32[]{:S(2)}) collective-permute-start(bf16[4,128,256]{2,1,0:T(8,128)(2,1)S(1)} %pad_maximum_fusion.2), channel_id=1, source_target_pairs={{0,16},{16,0},{1,17},{17,1},{2,18},{18,2},{3,19},{19,3},{4,20},{20... | collective-permute-start | bytes 786440 | tf_op jit(solution)/shard_map/ppermute | solution.py:162
  22.0 22.7 %copy-start.7 = (bf16[8,128,256]{2,1,0:T(8,128)(2,1)}, bf16[8,128,256]{2,1,0:T(8,128)(2,1)S(1)}, u32[]{:S(2)}) copy-start(bf16[8,128,256]{2,1,0:T(8,128)(2,1)S(1)} %constant_dynamic-update-slice_fusion.rf_ref) | copy-start | bytes 1572868
  22.0 4.4 %copy-start.4 = (bf16[4,128,128]{2,1,0:T(8,128)(2,1)}, bf16[4,128,128]{2,1,0:T(8,128)(2,1)S(1)}, u32[]{:S(2)}) copy-start(bf16[4,128,128]{2,1,0:T(8,128)(2,1)S(1)} %collective-permute-done.1.refs_4_) | copy-start | bytes 393220
  22.0 4.5 %copy-start.11 = (bf16[8,128,128]{2,1,0:T(8,128)(2,1)}, bf16[8,128,128]{2,1,0:T(8,128)(2,1)S(1)}, u32[]{:S(2)}) copy-start(bf16[8,128,128]{2,1,0:T(8,128)(2,1)S(1)} %collective-permute-done.2.refs_1_) | copy-start | bytes 786436
  22.0 4.5 %copy-start.2 = (bf16[8,128,128]{2,1,0:T(8,128)(2,1)}, bf16[8,128,128]{2,1,0:T(8,128)(2,1)S(1)}, u32[]{:S(2)}) copy-start(bf16[8,128,128]{2,1,0:T(8,128)(2,1)S(1)} %collective-permute-done.refs_2_) | copy-start | bytes 786436
  22.1 12.3 %collective-permute-start.9 = (bf16[8,128,128]{2,1,0:T(8,128)(2,1)S(1)}, bf16[8,128,128]{2,1,0:T(8,128)(2,1)S(1)}, u32[]{:S(2)}, u32[]{:S(2)}) collective-permute-start(bf16[8,128,128]{2,1,0:T(8,128)(2,1)S(1)} %broadcast_select_fusion.refs_0_), channel_id=1, source_target_pairs={{0,3},{1,0},{2,1},{3,2},{4,7},{5,4},{6,5},{7,6},{8,11},{9,8},{10,9... | collective-permute-start | bytes 786440 | tf_op jit(solution)/shard_map/ppermute | solution.py:165
  23.5 10.9 %collective-permute-start.8 = (bf16[4,128,128]{2,1,0:T(8,128)(2,1)S(1)}, bf16[4,128,128]{2,1,0:T(8,128)(2,1)S(1)}, u32[]{:S(2)}, u32[]{:S(2)}) collective-permute-start(bf16[4,128,128]{2,1,0:T(8,128)(2,1)S(1)} %slice.7), channel_id=1, source_target_pairs={{0,2},{1,3},{2,0},{3,1},{4,6},{5,7},{6,4},{7,5},{8,10},{9,11},{10,... | collective-permute-start | bytes 393224 | tf_op jit(solution)/shard_map/ppermute | solution.py:165
  26.5 11.4 %collective-permute-start.7 = (bf16[12,128,128]{2,1,0:T(8,128)(2,1)S(1)}, bf16[12,128,128]{2,1,0:T(8,128)(2,1)S(1)}, u32[]{:S(2)}, u32[]{:S(2)}) collective-permute-start(bf16[12,128,128]{2,1,0:T(8,128)(2,1)S(1)} %pad_maximum_fusion), channel_id=1, source_target_pairs={{0,16},{16,0},{1,17},{17,1},{2,18},{18,2},{3,19},{19,3},{4,20},{20... | collective-permute-start | bytes 1179656 | tf_op jit(solution)/shard_map/ppermute | solution.py:175
  34.4 0.7 %copy-start.5 = (bf16[4,128,128]{2,1,0:T(8,128)(2,1)}, bf16[4,128,128]{2,1,0:T(8,128)(2,1)S(1)}, u32[]{:S(2)}) copy-start(bf16[4,128,128]{2,1,0:T(8,128)(2,1)S(1)} %collective-permute-done.8.refs_5_) | copy-start | bytes 393220
  34.4 0.8 %copy-start.3 = (bf16[8,128,128]{2,1,0:T(8,128)(2,1)}, bf16[8,128,128]{2,1,0:T(8,128)(2,1)S(1)}, u32[]{:S(2)}) copy-start(bf16[8,128,128]{2,1,0:T(8,128)(2,1)S(1)} %collective-permute-done.9.refs_7_) | copy-start | bytes 786436
  35.1 9.5 %collective-permute-start.10 = (bf16[12,128,128]{2,1,0:T(8,128)(2,1)S(1)}, bf16[12,128,128]{2,1,0:T(8,128)(2,1)S(1)}, u32[]{:S(2)}, u32[]{:S(2)}) collective-permute-start(bf16[12,128,128]{2,1,0:T(8,128)(2,1)S(1)} %pad_maximum_fusion.1), channel_id=1, source_target_pairs={{0,16},{16,0},{1,17},{17,1},{2,18},{18,2},{3,19},{19,3},{4,20},{20... | collective-permute-start | bytes 1179656 | tf_op jit(solution)/shard_map/ppermute | solution.py:176
  37.9 6.7 %copy-start.9 = (bf16[12,128,128]{2,1,0:T(8,128)(2,1)}, bf16[12,128,128]{2,1,0:T(8,128)(2,1)S(1)}, u32[]{:S(2)}) copy-start(bf16[12,128,128]{2,1,0:T(8,128)(2,1)S(1)} %collective-permute-done.7.refs_3_) | copy-start | bytes 1179652
  44.7 0.8 %copy-start.10 = (bf16[12,128,128]{2,1,0:T(8,128)(2,1)}, bf16[12,128,128]{2,1,0:T(8,128)(2,1)S(1)}, u32[]{:S(2)}) copy-start(bf16[12,128,128]{2,1,0:T(8,128)(2,1)S(1)} %collective-permute-done.10.refs_6_) | copy-start | bytes 1179652

commit v9 on v8

--- a/solution.py
+++ b/solution.py
@@ -155,11 +155,20 @@
         and cols_local % BLK == 0
     )
     if use_permutes:
-        rf_row_pieces, _ = ring_gather(right_factor, "row", row_idx, row_count)
-        rf_own = jnp.stack(rf_row_pieces)
         swap = [(0, 1), (1, 0)]
         own_over_layer = lax.ppermute(packed[0], "layer", swap)
-        rf_all = jnp.concatenate([rf_own, lax.ppermute(rf_own, "layer", swap)], axis=0)
+        rf_pair = jnp.stack([right_factor, lax.ppermute(right_factor, "layer", swap)])
+
+        piece_layer = [layer_idx ^ m for k in range(col_count) for m in range(2)]
+        piece_col = [(col_idx - k) % col_count for k in range(col_count) for m in range(2)]
+        piece_j = jnp.stack(
+            [src_l * col_count + src_c for src_l, src_c in zip(piece_layer, piece_col)]
+        ).astype(jnp.int32)
+        rf_src = ((row_idx - piece_j % row_count) % row_count) * 2 + (layer_idx ^ (piece_j // row_count))
+        rf_src = rf_src.astype(jnp.int32)
+        p_stored, p_slot = slot_table(panel_pattern)
+        slot_tbl = jnp.where(p_stored > 0, p_slot, -1)
+        slot_tbl = jnp.take(slot_tbl, piece_j, axis=1).T.astype(jnp.int32)
 
         def col_shift(x, k):
             return lax.ppermute(x, "col", [(s, (s + k) % col_count) for s in range(col_count)])
@@ -167,12 +176,15 @@
         half = slots // 2
         s1 = col_shift(packed[0], 1)
         s2a = col_shift(packed[0][:half], 2)
-        later, s1, s2a, own_over_layer, rf_all = lax.optimization_barrier(
-            (packed[0], s1, s2a, own_over_layer, rf_all)
+        later, s1, s2a, own_over_layer, slot_tbl, rf_src, keep_patch = lax.optimization_barrier(
+            (packed[0], s1, s2a, own_over_layer, slot_tbl, rf_src, keep_patch)
         )
         s3 = col_shift(later, 3)
         s2b = col_shift(later[half:], 2)
         fwd1 = lax.ppermute(jnp.concatenate([s1, s2a], axis=0), "layer", swap)
+        rf_pair, fwd1 = lax.optimization_barrier((rf_pair, fwd1))
+        rf_pieces, _ = ring_gather(rf_pair, "row", row_idx, row_count)
+        rf_all = jnp.concatenate(rf_pieces, axis=0)
         fwd2 = lax.ppermute(jnp.concatenate([s3, s2b], axis=0), "layer", swap)
         piece_ops = [
             [(packed[0], 0, slots)],
@@ -184,18 +196,6 @@
             [(s3, 0, slots)],
             [(fwd2, 0, slots)],
         ]
-        piece_layer = [layer_idx ^ m for k in range(col_count) for m in range(2)]
-        piece_col = [(col_idx - k) % col_count for k in range(col_count) for m in range(2)]
-        piece_j = jnp.stack(
-            [src_l * col_count + src_c for src_l, src_c in zip(piece_layer, piece_col)]
-        ).astype(jnp.int32)
-        rf_src = (layer_idx ^ (piece_j // row_count)) * row_count + (
-            (row_idx - piece_j % row_count) % row_count
-        )
-        rf_src = rf_src.astype(jnp.int32)
-        p_stored, p_slot = slot_table(panel_pattern)
-        slot_tbl = jnp.where(p_stored > 0, p_slot, -1)
-        slot_tbl = jnp.take(slot_tbl, piece_j, axis=1).T.astype(jnp.int32)
         return product_call(slot_tbl, rf_src, keep_patch, rf_all, piece_ops)
 
     gathered = lax.all_gather(packed, ("layer", "col"), axis=0, tiled=True)

time: 50.4 us -> 48.5 us (0.962)
  waiting for transfers between devices: 25.5 us -> 22 us
  starting transfers between devices: 12.4 us -> 13.4 us
  other arithmetic: 1.91 us -> 2.8 us
    ppermute x1, waiting for transfers between devices: 8.6 us -> 0.01 us  [per_device(): lax.ppermute(right_factor, 'layer', swap)]
    ppermute x4, waiting for transfers between devices: 7.31 us -> 15.1 us  [col_shift(): lax.ppermute(x, 'col', [(s, (s + k) % col_count) for s in range(col_count)])]
    ppermute x1, waiting for transfers between devices: 6.71 us -> 0.01 us  [per_device(): fwd2 = lax.ppermute(jnp.concatenate([s3, s2b], axis=0), 'layer', swap)]
    ppermute x3, waiting for transfers between devices: 1.22 us -> 6.91 us  [ring_gather(): pieces.append(lax.ppermute(x, axis, perm))]
    ppermute x1, waiting for transfers between devices: 1.67 us -> 0.01 us  [per_device(): fwd1 = lax.ppermute(jnp.concatenate([s1, s2a], axis=0), 'layer', swap)]
    ppermute x1, starting transfers between devices: 0.57 us -> 1.56 us  [per_device(): fwd1 = lax.ppermute(jnp.concatenate([s1, s2a], axis=0), 'layer', swap)]
    concatenate x0 -> x1, other arithmetic: none -> 0.86 us  [per_device(): rf_all = jnp.concatenate(rf_pieces, axis=0)]
    unnamed x29 -> x23, local copies, waits for them, and re-layouts: 3.03 us -> 2.3 us
  transfers between devices with their start and end apart: 11 -> 11, of which waited for: 7 -> 5; matrix products, arithmetic and copies ran while one was open for 8% -> 10% of each run, Pallas kernels for 0% -> 0%
where the time goes in v9:
time: 48.5 us; the launch traced here: 48.1 us
  waiting for transfers between devices  22 us (45%)
  starting transfers between devices  13.4 us (28%)
  local copies, waits for them, and re-layouts  5.33 us (11%)
  Pallas kernels  4.35 us (9%)
  other arithmetic  2.8 us (6%)
    ppermute x4, waiting for transfers between devices, col_shift(): lax.ppermute(x, 'col', [(s, (s + k) % col_count) for s in range(col_count)])  15.1 us
    ppermute x3, waiting for transfers between devices, ring_gather(): pieces.append(lax.ppermute(x, axis, perm))  6.91 us
    ppermute x4, starting transfers between devices, col_shift(): lax.ppermute(x, 'col', [(s, (s + k) % col_count) for s in range(col_count)])  5.92 us
    pallas_call x1, Pallas kernels, product_call(): pl.pallas_call(functools.partial(product_kernel, parts=tuple(parts), n_le...  4.35 us
    ppermute x1, starting transfers between devices, per_device(): own_over_layer = lax.ppermute(packed[0], 'layer', swap)  3 us
    unnamed x23, local copies, waits for them, and re-layouts  2.3 us
    ppermute x3, starting transfers between devices, ring_gather(): pieces.append(lax.ppermute(x, axis, perm))  1.81 us
    ppermute x1, starting transfers between devices, per_device(): fwd1 = lax.ppermute(jnp.concatenate([s1, s2a], axis=0), 'layer', swap)  1.56 us
  transfers between devices with their start and end apart: 11, of which 5 were waited for; matrix products, arithmetic and copies ran while one was open for 10% of the time, Pallas kernels for 0%

profile of v9, /device:TPU:0, one launch (start us, length us, event | category | flops | bytes accessed | tf_op | source)
XLA Modules:
  0.0 48.1 jit_solution(14913081543881634091)
XLA Ops:
  0.0 0.7 %copy-done.7 = s32[64,8]{0,1:T(8,128)S(1)} copy-done((s32[64,8]{0,1:T(8,128)S(1)}, s32[64,8]{0,1:T(8,128)}, u32[]{:S(2)}) %copy-start.7) | copy-done | bytes 2072
  0.8 0.1 copy.13
  0.9 0.1 add_reduce_fusion
  1.1 0.1 select_reduce_fusion
  1.2 0.6 %gather_fusion = bf16[8,128,128]{2,1,0:T(8,128)(2,1)S(1)} fusion(bf16[16,128,128]{2,1,0:T(8,128)(2,1)S(1)} %bitcast.28, s32[1024]{0:T(1024)S(1)} %pad_clamp_fusion.1), kind=kCustom, calls=%fused_computation | custom fusion | bytes 524320 | tf_op jit(solution)/shard_map/jit(_take)/gather | solution.py:131
  1.8 0.1 broadcast_select_fusion.refs_0_
  1.9 3.0 %collective-permute-start.2 = (bf16[8,128,128]{2,1,0:T(8,128)(2,1)S(1)}, bf16[8,128,128]{2,1,0:T(8,128)(2,1)S(1)}, u32[]{:S(2)}, u32[]{:S(2)}) collective-permute-start(bf16[8,128,128]{2,1,0:T(8,128)(2,1)S(1)} %broadcast_select_fusion.refs_0_), channel_id=1, source_target_pairs={{0,16},{16,0},{1,17},{17,1},{2,18},{18,2},{3,19},{19,3},{4,20},{20... | collective-permute-start | bytes 786440 | tf_op jit(solution)/shard_map/ppermute | solution.py:159
  4.9 1.6 %collective-permute-start = (bf16[8,128,128]{2,1,0:T(8,128)(2,1)S(1)}, bf16[8,128,128]{2,1,0:T(8,128)(2,1)S(1)}, u32[]{:S(2)}, u32[]{:S(2)}) collective-permute-start(bf16[8,128,128]{2,1,0:T(8,128)(2,1)S(1)} %broadcast_select_fusion.refs_0_), channel_id=1, source_target_pairs={{0,1},{1,2},{2,3},{3,0},{4,5},{5,6},{6,7},{7,4},{8,9},{9,10},{10,1... | collective-permute-start | bytes 786440 | tf_op jit(solution)/shard_map/ppermute | solution.py:174
  6.5 2.7 %collective-permute-start.1 = (bf16[4,128,128]{2,1,0:T(8,128)(2,1)S(1)}, bf16[4,128,128]{2,1,0:T(8,128)(2,1)S(1)}, u32[]{:S(2)}, u32[]{:S(2)}) collective-permute-start(bf16[4,128,128]{2,1,0:T(8,128)(2,1)S(1)} %slice.12), channel_id=1, source_target_pairs={{0,2},{1,3},{2,0},{3,1},{4,6},{5,7},{6,4},{7,5},{8,10},{9,11},{10,... | collective-permute-start | bytes 393224 | tf_op jit(solution)/shard_map/ppermute | solution.py:174
  9.3 0.1 stack.62
  9.4 0.1 stack.71
  9.7 0.6 %gather_fusion.1 = s32[8,16]{1,0:T(8,128)S(1)} fusion(s32[16,8]{0,1:T(8,128)S(1)} %copy.15, s32[1024]{0:T(1024)S(1)} %pad_clamp_fusion), kind=kCustom, calls=%fused_computation.1 | custom fusion | bytes 1056 | tf_op jit(solution)/shard_map/jit(_take)/gather | solution.py:171
  10.2 0.7 %broadcast_select_fusion.1.slot_ref = s32[8,16]{1,0:T(8,128)} fusion(s32[8,16]{1,0:T(8,128)S(1)} %gather_fusion.1, pred[8]{0:T(512)(128)(4,1)S(1)} %compare_and_fusion), kind=kLoop, calls=%fused_computation.21 | loop fusion | flops 128 | bytes 1032 | tf_op jit(solution)/shard_map/jit(_take)/select_n | solution.py:171
  10.9 0.5 %fusion.3.rf_src_ref = s32[8]{0:T(128)} fusion(s32[8]{0:T(128)S(1)} %stack.62, s32[]{:T(128)S(6)} %axis_index.36, s32[]{:T(128)S(6)} %axis_index.33), kind=kLoop, calls=%fused_computation.36 | loop fusion | flops 272 | bytes 72 | tf_op jit(solution)/shard_map/add | solution.py:167
  11.4 0.8 %dynamic_slice.11 = s32[16,2]{0,1:T(2,128)S(1)} dynamic-slice(s32[64,8]{0,1:T(8,128)} %param.7, s32[]{:T(128)S(6)} %select_n.115, s32[]{:T(128)S(6)} %select_n.133), dynamic_slice_sizes={16,2} | dynamic-slice | bytes 260 | tf_op jit(solution)/shard_map/dynamic_slice | solution.py:135
  12.1 0.7 %copy.18.keep_ref = s32[16,2]{1,0:T(8,128)} copy(s32[16,2]{0,1:T(2,128)S(1)} %dynamic_slice.11) | data formatting | bytes 256 | tf_op jit(solution)/shard_map/optimization_barrier | solution.py:179
  12.8 7.4 %collective-permute-done.1.refs_4_ = bf16[4,128,128]{2,1,0:T(8,128)(2,1)S(1)} collective-permute-done((bf16[4,128,128]{2,1,0:T(8,128)(2,1)S(1)}, bf16[4,128,128]{2,1,0:T(8,128)(2,1)S(1)}, u32[]{:S(2)}, u32[]{:S(2)}) %collective-permute-start.1) | collective-permute-done | bytes 131104 | tf_op jit(solution)/shard_map/ppermute | solution.py:174
  20.2 1.7 %collective-permute-start.9 = (bf16[8,128,128]{2,1,0:T(8,128)(2,1)S(1)}, bf16[8,128,128]{2,1,0:T(8,128)(2,1)S(1)}, u32[]{:S(2)}, u32[]{:S(2)}) collective-permute-start(bf16[8,128,128]{2,1,0:T(8,128)(2,1)S(1)} %broadcast_select_fusion.refs_0_), channel_id=1, source_target_pairs={{0,3},{1,0},{2,1},{3,2},{4,7},{5,4},{6,5},{7,6},{8,11},{9,8},{10,9... | collective-permute-start | bytes 786440 | tf_op jit(solution)/shard_map/ppermute | solution.py:174
  21.9 0.1 subtract_convert_fusion
  22.0 0.6 %collective-permute-start.3 = (bf16[128,256]{1,0:T(8,128)(2,1)S(1)}, bf16[128,256]{1,0:T(8,128)(2,1)S(1)}, u32[]{:S(2)}, u32[]{:S(2)}) collective-permute-start(bf16[128,256]{1,0:T(8,128)(2,1)S(1)} %subtract_convert_fusion), channel_id=1, source_target_pairs={{0,16},{16,0},{1,17},{17,1},{2,18},{18,2},{3,19},{19,3},{4,20},{20... | collective-permute-start | bytes 196616 | tf_op jit(solution)/shard_map/ppermute | solution.py:160
  22.7 1.6 %collective-permute-start.4 = (bf16[12,128,128]{2,1,0:T(8,128)(2,1)S(1)}, bf16[12,128,128]{2,1,0:T(8,128)(2,1)S(1)}, u32[]{:S(2)}, u32[]{:S(2)}) collective-permute-start(bf16[12,128,128]{2,1,0:T(8,128)(2,1)S(1)} %pad_maximum_fusion.1), channel_id=1, source_target_pairs={{0,16},{16,0},{1,17},{17,1},{2,18},{18,2},{3,19},{19,3},{4,20},{20... | collective-permute-start | bytes 1179656 | tf_op jit(solution)/shard_map/ppermute | solution.py:184
  24.2 7.7 %collective-permute-done.8.refs_5_ = bf16[4,128,128]{2,1,0:T(8,128)(2,1)S(1)} collective-permute-done((bf16[4,128,128]{2,1,0:T(8,128)(2,1)S(1)}, bf16[4,128,128]{2,1,0:T(8,128)(2,1)S(1)}, u32[]{:S(2)}, u32[]{:S(2)}) %collective-permute-start.8) | collective-permute-done | bytes 131104 | tf_op jit(solution)/shard_map/ppermute | solution.py:174
  32.0 0.6 %copy-done.6 = bf16[4,128,128]{2,1,0:T(8,128)(2,1)} copy-done((bf16[4,128,128]{2,1,0:T(8,128)(2,1)}, bf16[4,128,128]{2,1,0:T(8,128)(2,1)S(1)}, u32[]{:S(2)}) %copy-start.6) | copy-done | bytes 131096
  32.6 0.1 copy-done.3
  32.7 0.5 %collective-permute-start.10 = (bf16[12,128,128]{2,1,0:T(8,128)(2,1)S(1)}, bf16[12,128,128]{2,1,0:T(8,128)(2,1)S(1)}, u32[]{:S(2)}, u32[]{:S(2)}) collective-permute-start(bf16[12,128,128]{2,1,0:T(8,128)(2,1)S(1)} %pad_maximum_fusion.2), channel_id=1, source_target_pairs={{0,16},{16,0},{1,17},{17,1},{2,18},{18,2},{3,19},{19,3},{4,20},{20... | collective-permute-start | bytes 1179656 | tf_op jit(solution)/shard_map/ppermute | solution.py:188
  33.4 1.6 %collective-permute-start.6 = (bf16[2,128,256]{2,1,0:T(8,128)(2,1)S(1)}, bf16[2,128,256]{2,1,0:T(8,128)(2,1)S(1)}, u32[]{:S(2)}, u32[]{:S(2)}) collective-permute-start(bf16[2,128,256]{2,1,0:T(8,128)(2,1)S(1)} %pad_maximum_fusion.3), channel_id=1, source_target_pairs={{0,8},{4,12},{8,0},{12,4},{1,9},{5,13},{9,1},{13,5},{2,10},{6,14},... | collective-permute-start | bytes 393224 | tf_op jit(solution)/shard_map/ppermute | solution.py:30
  35.0 0.2 collective-permute-start.5
  35.2 1.1 %collective-permute-done.7 = bf16[2,128,256]{2,1,0:T(8,128)(2,1)S(1)} collective-permute-done((bf16[2,128,256]{2,1,0:T(8,128)(2,1)S(1)}, bf16[2,128,256]{2,1,0:T(8,128)(2,1)S(1)}, u32[]{:S(2)}, u32[]{:S(2)}) %collective-permute-start.7) | collective-permute-done | bytes 131104 | tf_op jit(solution)/shard_map/ppermute | solution.py:30
  36.2 5.8 %collective-permute-done.6 = bf16[2,128,256]{2,1,0:T(8,128)(2,1)S(1)} collective-permute-done((bf16[2,128,256]{2,1,0:T(8,128)(2,1)S(1)}, bf16[2,128,256]{2,1,0:T(8,128)(2,1)S(1)}, u32[]{:S(2)}, u32[]{:S(2)}) %collective-permute-start.6) | collective-permute-done | bytes 131104 | tf_op jit(solution)/shard_map/ppermute | solution.py:30
  42.1 0.9 %pad_maximum_fusion.rf_ref = bf16[8,128,256]{2,1,0:T(8,128)(2,1)} fusion(bf16[2,128,256]{2,1,0:T(8,128)(2,1)S(1)} %collective-permute-done.7, bf16[2,128,256]{2,1,0:T(8,128)(2,1)S(1)} %collective-permute-done.6, bf16[2,128,256]{2,1,0:T(8,128)(2,1)S(1)} %collective-permute-done.5, bf16[2,128,256]{2,1,0:T(8,128)(2,1)S(1)} %pad_maximum_fusion.3), kind=kLoop, calls=%fused_computation.2 | loop fusion | flops 786432 | bytes 1048576 | tf_op jit(solution)/shard_map/concatenate | solution.py:187
  43.0 0.8 %copy-done.9 = bf16[12,128,128]{2,1,0:T(8,128)(2,1)} copy-done((bf16[12,128,128]{2,1,0:T(8,128)(2,1)}, bf16[12,128,128]{2,1,0:T(8,128)(2,1)S(1)}, u32[]{:S(2)}) %copy-start.9) | copy-done | bytes 393240
  43.7 4.3 %shard_map.46 = bf16[2048,256]{1,0:T(8,128)(2,1)} custom-call(s32[8,16]{1,0:T(8,128)} %broadcast_select_fusion.1.slot_ref, s32[8]{0:T(128)} %fusion.3.rf_src_ref, s32[16,2]{1,0:T(8,128)} %copy.18.keep_ref, bf16[8,128,256]{2,1,0:T(8,128)(2,1)} %pad_maximum_fusion.rf_ref, bf16[8,128,128]{2,1,0:T(8,128)(2,1)} %copy-done.1, bf16[8,128,128]{2,1,0:T(8,128)(2,1)} %copy-done.10, ...), custom_call_target="tpu_custom_call" | custom-call | flops 1073741824 | bytes 3670016 | tf_op jit(solution)/shard_map/pallas_call | solution.py:90
  (49 shorter events, 0.8 us)
Async XLA Ops:
  0.0 1.2 %copy-start = (bf16[2048,128]{1,0:T(8,128)(2,1)S(1)}, bf16[2048,128]{1,0:T(8,128)(2,1)}, u32[]{:S(2)}) copy-start(bf16[2048,128]{1,0:T(8,128)(2,1)} %param.4) | copy-start | bytes 1572868
  0.0 0.7 %copy-start.7 = (s32[64,8]{0,1:T(8,128)S(1)}, s32[64,8]{0,1:T(8,128)}, u32[]{:S(2)}) copy-start(s32[64,8]{0,1:T(8,128)} %param.6) | copy-start | bytes 6148
  1.9 18.3 %copy-start.1 = (bf16[8,128,128]{2,1,0:T(8,128)(2,1)}, bf16[8,128,128]{2,1,0:T(8,128)(2,1)S(1)}, u32[]{:S(2)}) copy-start(bf16[8,128,128]{2,1,0:T(8,128)(2,1)S(1)} %broadcast_select_fusion.refs_0_) | copy-start | bytes 786436
  1.9 18.3 %collective-permute-start.2 = (bf16[8,128,128]{2,1,0:T(8,128)(2,1)S(1)}, bf16[8,128,128]{2,1,0:T(8,128)(2,1)S(1)}, u32[]{:S(2)}, u32[]{:S(2)}) collective-permute-start(bf16[8,128,128]{2,1,0:T(8,128)(2,1)S(1)} %broadcast_select_fusion.refs_0_), channel_id=1, source_target_pairs={{0,16},{16,0},{1,17},{17,1},{2,18},{18,2},{3,19},{19,3},{4,20},{20... | collective-permute-start | bytes 786440 | tf_op jit(solution)/shard_map/ppermute | solution.py:159
  4.9 15.3 %collective-permute-start = (bf16[8,128,128]{2,1,0:T(8,128)(2,1)S(1)}, bf16[8,128,128]{2,1,0:T(8,128)(2,1)S(1)}, u32[]{:S(2)}, u32[]{:S(2)}) collective-permute-start(bf16[8,128,128]{2,1,0:T(8,128)(2,1)S(1)} %broadcast_select_fusion.refs_0_), channel_id=1, source_target_pairs={{0,1},{1,2},{2,3},{3,0},{4,5},{5,6},{6,7},{7,4},{8,9},{9,10},{10,1... | collective-permute-start | bytes 786440 | tf_op jit(solution)/shard_map/ppermute | solution.py:174
  6.5 13.7 %collective-permute-start.1 = (bf16[4,128,128]{2,1,0:T(8,128)(2,1)S(1)}, bf16[4,128,128]{2,1,0:T(8,128)(2,1)S(1)}, u32[]{:S(2)}, u32[]{:S(2)}) collective-permute-start(bf16[4,128,128]{2,1,0:T(8,128)(2,1)S(1)} %slice.12), channel_id=1, source_target_pairs={{0,2},{1,3},{2,0},{3,1},{4,6},{5,7},{6,4},{7,5},{8,10},{9,11},{10,... | collective-permute-start | bytes 393224 | tf_op jit(solution)/shard_map/ppermute | solution.py:174
  12.8 9.1 %copy-start.4 = (bf16[128,256]{1,0:T(8,128)(2,1)S(1)}, bf16[128,256]{1,0:T(8,128)(2,1)}, u32[]{:S(2)}) copy-start(bf16[128,256]{1,0:T(8,128)(2,1)} %param.5) | copy-start | bytes 196612
  20.2 2.4 %copy-start.5 = (bf16[4,128,128]{2,1,0:T(8,128)(2,1)}, bf16[4,128,128]{2,1,0:T(8,128)(2,1)S(1)}, u32[]{:S(2)}) copy-start(bf16[4,128,128]{2,1,0:T(8,128)(2,1)S(1)} %collective-permute-done.1.refs_4_) | copy-start | bytes 393220
  20.2 2.5 %copy-start.10 = (bf16[8,128,128]{2,1,0:T(8,128)(2,1)}, bf16[8,128,128]{2,1,0:T(8,128)(2,1)S(1)}, u32[]{:S(2)}) copy-start(bf16[8,128,128]{2,1,0:T(8,128)(2,1)S(1)} %collective-permute-done.2.refs_1_) | copy-start | bytes 786436
  20.2 2.5 %copy-start.2 = (bf16[8,128,128]{2,1,0:T(8,128)(2,1)}, bf16[8,128,128]{2,1,0:T(8,128)(2,1)S(1)}, u32[]{:S(2)}) copy-start(bf16[8,128,128]{2,1,0:T(8,128)(2,1)S(1)} %collective-permute-done.refs_2_) | copy-start | bytes 786436
  20.2 11.7 %collective-permute-start.9 = (bf16[8,128,128]{2,1,0:T(8,128)(2,1)S(1)}, bf16[8,128,128]{2,1,0:T(8,128)(2,1)S(1)}, u32[]{:S(2)}, u32[]{:S(2)}) collective-permute-start(bf16[8,128,128]{2,1,0:T(8,128)(2,1)S(1)} %broadcast_select_fusion.refs_0_), channel_id=1, source_target_pairs={{0,3},{1,0},{2,1},{3,2},{4,7},{5,4},{6,5},{7,6},{8,11},{9,8},{10,9... | collective-permute-start | bytes 786440 | tf_op jit(solution)/shard_map/ppermute | solution.py:174
  21.9 10.0 %collective-permute-start.8 = (bf16[4,128,128]{2,1,0:T(8,128)(2,1)S(1)}, bf16[4,128,128]{2,1,0:T(8,128)(2,1)S(1)}, u32[]{:S(2)}, u32[]{:S(2)}) collective-permute-start(bf16[4,128,128]{2,1,0:T(8,128)(2,1)S(1)} %slice.7), channel_id=1, source_target_pairs={{0,2},{1,3},{2,0},{3,1},{4,6},{5,7},{6,4},{7,5},{8,10},{9,11},{10,... | collective-permute-start | bytes 393224 | tf_op jit(solution)/shard_map/ppermute | solution.py:174
  22.0 11.3 %collective-permute-start.3 = (bf16[128,256]{1,0:T(8,128)(2,1)S(1)}, bf16[128,256]{1,0:T(8,128)(2,1)S(1)}, u32[]{:S(2)}, u32[]{:S(2)}) collective-permute-start(bf16[128,256]{1,0:T(8,128)(2,1)S(1)} %subtract_convert_fusion), channel_id=1, source_target_pairs={{0,16},{16,0},{1,17},{17,1},{2,18},{18,2},{3,19},{19,3},{4,20},{20... | collective-permute-start | bytes 196616 | tf_op jit(solution)/shard_map/ppermute | solution.py:160
  22.7 10.7 %collective-permute-start.4 = (bf16[12,128,128]{2,1,0:T(8,128)(2,1)S(1)}, bf16[12,128,128]{2,1,0:T(8,128)(2,1)S(1)}, u32[]{:S(2)}, u32[]{:S(2)}) collective-permute-start(bf16[12,128,128]{2,1,0:T(8,128)(2,1)S(1)} %pad_maximum_fusion.1), channel_id=1, source_target_pairs={{0,16},{16,0},{1,17},{17,1},{2,18},{18,2},{3,19},{19,3},{4,20},{20... | collective-permute-start | bytes 1179656 | tf_op jit(solution)/shard_map/ppermute | solution.py:184
  31.9 0.6 %copy-start.6 = (bf16[4,128,128]{2,1,0:T(8,128)(2,1)}, bf16[4,128,128]{2,1,0:T(8,128)(2,1)S(1)}, u32[]{:S(2)}) copy-start(bf16[4,128,128]{2,1,0:T(8,128)(2,1)S(1)} %collective-permute-done.8.refs_5_) | copy-start | bytes 393220
  31.9 0.7 %copy-start.3 = (bf16[8,128,128]{2,1,0:T(8,128)(2,1)}, bf16[8,128,128]{2,1,0:T(8,128)(2,1)S(1)}, u32[]{:S(2)}) copy-start(bf16[8,128,128]{2,1,0:T(8,128)(2,1)S(1)} %collective-permute-done.9.refs_7_) | copy-start | bytes 786436
  32.7 10.3 %collective-permute-start.10 = (bf16[12,128,128]{2,1,0:T(8,128)(2,1)S(1)}, bf16[12,128,128]{2,1,0:T(8,128)(2,1)S(1)}, u32[]{:S(2)}, u32[]{:S(2)}) collective-permute-start(bf16[12,128,128]{2,1,0:T(8,128)(2,1)S(1)} %pad_maximum_fusion.2), channel_id=1, source_target_pairs={{0,16},{16,0},{1,17},{17,1},{2,18},{18,2},{3,19},{19,3},{4,20},{20... | collective-permute-start | bytes 1179656 | tf_op jit(solution)/shard_map/ppermute | solution.py:188
  33.4 9.6 %copy-start.8 = (bf16[12,128,128]{2,1,0:T(8,128)(2,1)}, bf16[12,128,128]{2,1,0:T(8,128)(2,1)S(1)}, u32[]{:S(2)}) copy-start(bf16[12,128,128]{2,1,0:T(8,128)(2,1)S(1)} %collective-permute-done.4.refs_3_) | copy-start | bytes 1179652
  33.4 2.9 %collective-permute-start.7 = (bf16[2,128,256]{2,1,0:T(8,128)(2,1)S(1)}, bf16[2,128,256]{2,1,0:T(8,128)(2,1)S(1)}, u32[]{:S(2)}, u32[]{:S(2)}) collective-permute-start(bf16[2,128,256]{2,1,0:T(8,128)(2,1)S(1)} %pad_maximum_fusion.3), channel_id=1, source_target_pairs={{0,12},{4,0},{8,4},{12,8},{1,13},{5,1},{9,5},{13,9},{2,14},{6,2},{... | collective-permute-start | bytes 393224 | tf_op jit(solution)/shard_map/ppermute | solution.py:30
  33.4 8.6 %collective-permute-start.6 = (bf16[2,128,256]{2,1,0:T(8,128)(2,1)S(1)}, bf16[2,128,256]{2,1,0:T(8,128)(2,1)S(1)}, u32[]{:S(2)}, u32[]{:S(2)}) collective-permute-start(bf16[2,128,256]{2,1,0:T(8,128)(2,1)S(1)} %pad_maximum_fusion.3), channel_id=1, source_target_pairs={{0,8},{4,12},{8,0},{12,4},{1,9},{5,13},{9,1},{13,5},{2,10},{6,14},... | collective-permute-start | bytes 393224 | tf_op jit(solution)/shard_map/ppermute | solution.py:30
  35.0 7.1 %collective-permute-start.5 = (bf16[2,128,256]{2,1,0:T(8,128)(2,1)S(1)}, bf16[2,128,256]{2,1,0:T(8,128)(2,1)S(1)}, u32[]{:S(2)}, u32[]{:S(2)}) collective-permute-start(bf16[2,128,256]{2,1,0:T(8,128)(2,1)S(1)} %pad_maximum_fusion.3), channel_id=1, source_target_pairs={{0,4},{4,8},{8,12},{12,0},{1,5},{5,9},{9,13},{13,1},{2,6},{6,10},{... | collective-permute-start | bytes 393224 | tf_op jit(solution)/shard_map/ppermute | solution.py:30
  43.0 0.8 %copy-start.9 = (bf16[12,128,128]{2,1,0:T(8,128)(2,1)}, bf16[12,128,128]{2,1,0:T(8,128)(2,1)S(1)}, u32[]{:S(2)}) copy-start(bf16[12,128,128]{2,1,0:T(8,128)(2,1)S(1)} %collective-permute-done.10.refs_6_) | copy-start | bytes 1179652

commit v10 on v5

--- a/solution.py
+++ b/solution.py
@@ -159,7 +159,23 @@
             return lax.ppermute(x, "col", [(s, (s + k) % col_count) for s in range(col_count)])
 
         col_pieces = {1: col_shift(packed[0], 1)}
-        later, col_pieces[1] = lax.optimization_barrier((packed[0], col_pieces[1]))
+        piece_layer = [(layer_idx - m) % layer_count for k in range(col_count) for m in range(layer_count)]
+        piece_src_col = [(col_idx - k) % col_count for k in range(col_count) for m in range(layer_count)]
+        piece_j = jnp.stack(
+            [src_l * col_count + src_c for src_l, src_c in zip(piece_layer, piece_src_col)]
+        ).astype(jnp.int32)
+        rf_row = [(row_idx - k) % row_count for k in range(row_count) for m in range(layer_count)]
+        rf_layer = [(layer_idx - m) % layer_count for k in range(row_count) for m in range(layer_count)]
+        rf_q = jnp.stack([src_l * row_count + src_r for src_l, src_r in zip(rf_layer, rf_row)])
+        rf_pos = ((col_idx - rf_q % col_count) % col_count) * layer_count + (
+            (layer_idx - rf_q // col_count) % layer_count
+        )
+        p_stored, p_slot = slot_table(panel_pattern)
+        slot_tbl = jnp.where(p_stored > 0, p_slot, -1).astype(jnp.int32)
+        slot_tbl = jnp.take(slot_tbl, piece_j, axis=1).T
+        later, col_pieces[1], slot_tbl, rf_pos, keep_patch, own_over_layer = lax.optimization_barrier(
+            (packed[0], col_pieces[1], slot_tbl, rf_pos.astype(jnp.int32), keep_patch, own_over_layer)
+        )
         for k in range(2, col_count):
             col_pieces[k] = col_shift(later, k)
         piece_col = [(col_idx - k) % col_count for k in range(col_count)]
@@ -167,24 +183,8 @@
         for k in range(1, col_count):
             got, _ = ring_gather(col_pieces[k], "layer", layer_idx, layer_count)
             pieces.extend(got)
-        piece_layer = [(layer_idx - m) % layer_count for k in range(col_count) for m in range(layer_count)]
-        piece_col = [piece_col[k] for k in range(col_count) for m in range(layer_count)]
-        piece_j = jnp.stack(
-            [src_l * col_count + src_c for src_l, src_c in zip(piece_layer, piece_col)]
-        ).astype(jnp.int32)
-        rf_pieces, rf_row = ring_gather(rf_pair, "row", row_idx, row_count)
-        rf_layer = [(layer_idx - m) % layer_count for k in range(row_count) for m in range(layer_count)]
-        rf_row = [rf_row[k] for k in range(row_count) for m in range(layer_count)]
-        rf_q = jnp.stack(
-            [src_l * row_count + src_r for src_l, src_r in zip(rf_layer, rf_row)]
-        ).astype(jnp.int32)
-        rf_pos = ((col_idx - rf_q % col_count) % col_count) * layer_count + (
-            (layer_idx - rf_q // col_count) % layer_count
-        )
-        p_stored, p_slot = slot_table(panel_pattern)
-        slot_tbl = jnp.where(p_stored > 0, p_slot, -1)
-        slot_tbl = jnp.take(slot_tbl, piece_j, axis=1).T.astype(jnp.int32)
-        return product_call(slot_tbl, rf_pos.astype(jnp.int32), keep_patch, pieces, rf_pieces)
+        rf_pieces, _ = ring_gather(rf_pair, "row", row_idx, row_count)
+        return product_call(slot_tbl, rf_pos, keep_patch, pieces, rf_pieces)
 
     gathered = lax.all_gather(packed, ("layer", "col"), axis=0, tiled=True)
     piece_j = jnp.arange(total_inner_blocks, dtype=jnp.int32)

time: 45.1 us -> 44.8 us (level)
  starting transfers between devices: 12.8 us -> 11.3 us
  waiting for transfers between devices: 20.3 us -> 21.5 us
    ppermute x1, starting transfers between devices: 1.49 us -> 3 us  [per_device(): lax.ppermute(packed[0], 'layer', [(s, (s + m) % layer_count) for s in ran...]
    ppermute x3, starting transfers between devices: 4.82 us -> 3.32 us  [col_shift(): lax.ppermute(x, 'col', [(s, (s + k) % col_count) for s in range(col_count)])]
    ppermute x7, starting transfers between devices: 6.44 us -> 4.97 us  [ring_gather(): pieces.append(lax.ppermute(x, axis, perm))]
    ppermute x1, waiting for transfers between devices: 0.01 us -> 0.89 us  [per_device(): lax.ppermute(packed[0], 'layer', [(s, (s + m) % layer_count) for s in ran...]
    unnamed x32 -> x31, local copies, waits for them, and re-layouts: 3.1 us -> 2.31 us
    optimization_barrier x0 -> x1, local copies, waits for them, and re-layouts: none -> 0.68 us  [per_device(): lax.optimization_barrier((packed[0], col_pieces[1], slot_tbl, rf_pos.asty...]
    ppermute x3, waiting for transfers between devices: 15.3 us -> 15.8 us  [col_shift(): lax.ppermute(x, 'col', [(s, (s + k) % col_count) for s in range(col_count)])]
  transfers between devices with their start and end apart: 11 -> 11, of which waited for: 5 -> 6; matrix products, arithmetic and copies ran while one was open for 9% -> 9% of each run, Pallas kernels for 0% -> 0%
where the time goes in v10:
time: 44.8 us; the launch traced here: 44.6 us
  waiting for transfers between devices  21.5 us (48%)
  starting transfers between devices  11.3 us (25%)
  local copies, waits for them, and re-layouts  5.4 us (12%)
  Pallas kernels  4.19 us (9%)
  other arithmetic  1.98 us (4%)
    ppermute x3, waiting for transfers between devices, col_shift(): lax.ppermute(x, 'col', [(s, (s + k) % col_count) for s in range(col_count)])  15.8 us
    ppermute x7, starting transfers between devices, ring_gather(): pieces.append(lax.ppermute(x, axis, perm))  4.97 us
    ppermute x7, waiting for transfers between devices, ring_gather(): pieces.append(lax.ppermute(x, axis, perm))  4.85 us
    pallas_call x1, Pallas kernels, product_call(): pl.pallas_call(functools.partial(product_kernel, pieces=pieces, rf_groups...  4.19 us
    ppermute x3, starting transfers between devices, col_shift(): lax.ppermute(x, 'col', [(s, (s + k) % col_count) for s in range(col_count)])  3.32 us
    ppermute x1, starting transfers between devices, per_device(): lax.ppermute(packed[0], 'layer', [(s, (s + m) % layer_count) for s in ran...  3 us
    unnamed x31, local copies, waits for them, and re-layouts  2.31 us
  transfers between devices with their start and end apart: 11, of which 6 were waited for; matrix products, arithmetic and copies ran while one was open for 9% of the time, Pallas kernels for 0%

profile of v10, /device:TPU:0, one launch (start us, length us, event | category | flops | bytes accessed | tf_op | source)
XLA Modules:
  0.0 44.6 jit_solution(3064524031376395415)
XLA Ops:
  0.0 0.7 %copy-done.4 = s32[64,8]{0,1:T(8,128)S(1)} copy-done((s32[64,8]{0,1:T(8,128)S(1)}, s32[64,8]{0,1:T(8,128)}, u32[]{:S(2)}) %copy-start.4) | copy-done | bytes 2072
  0.9 0.1 add_reduce_fusion
  1.1 0.1 select_reduce_fusion
  1.2 0.6 %gather_fusion = bf16[8,128,128]{2,1,0:T(8,128)(2,1)S(1)} fusion(bf16[16,128,128]{2,1,0:T(8,128)(2,1)S(1)} %bitcast.36, s32[1024]{0:T(1024)S(1)} %pad_clamp_fusion.1), kind=kCustom, calls=%fused_computation | custom fusion | bytes 524320 | tf_op jit(solution)/shard_map/jit(_take)/gather | solution.py:126
  1.8 0.1 broadcast_select_fusion.refs_0_
  2.0 3.0 %collective-permute-start.1 = (bf16[8,128,128]{2,1,0:T(8,128)(2,1)S(1)}, bf16[8,128,128]{2,1,0:T(8,128)(2,1)S(1)}, u32[]{:S(2)}, u32[]{:S(2)}) collective-permute-start(bf16[8,128,128]{2,1,0:T(8,128)(2,1)S(1)} %broadcast_select_fusion.refs_0_), channel_id=1, source_target_pairs={{0,16},{16,0},{1,17},{17,1},{2,18},{18,2},{3,19},{19,3},{4,20},{20... | collective-permute-start | bytes 786440 | tf_op jit(solution)/shard_map/ppermute | solution.py:155
  5.0 1.6 %collective-permute-start = (bf16[8,128,128]{2,1,0:T(8,128)(2,1)S(1)}, bf16[8,128,128]{2,1,0:T(8,128)(2,1)S(1)}, u32[]{:S(2)}, u32[]{:S(2)}) collective-permute-start(bf16[8,128,128]{2,1,0:T(8,128)(2,1)S(1)} %broadcast_select_fusion.refs_0_), channel_id=1, source_target_pairs={{0,1},{1,2},{2,3},{3,0},{4,5},{5,6},{6,7},{7,4},{8,9},{9,10},{10,1... | collective-permute-start | bytes 786440 | tf_op jit(solution)/shard_map/ppermute | solution.py:159
  6.5 0.1 subtract_convert_fusion
  6.6 0.6 %collective-permute-start.7 = (bf16[128,256]{1,0:T(8,128)(2,1)S(1)}, bf16[128,256]{1,0:T(8,128)(2,1)S(1)}, u32[]{:S(2)}, u32[]{:S(2)}) collective-permute-start(bf16[128,256]{1,0:T(8,128)(2,1)S(1)} %subtract_convert_fusion), channel_id=1, source_target_pairs={{0,16},{16,0},{1,17},{17,1},{2,18},{18,2},{3,19},{19,3},{4,20},{20... | collective-permute-start | bytes 196616 | tf_op jit(solution)/shard_map/ppermute | solution.py:30
  7.3 0.1 stack.107
  7.4 0.6 %fusion.1.rf_pos_ref = s32[8]{0:T(128)} fusion(s32[8]{0:T(128)S(1)} %stack.107, s32[]{:T(128)S(6)} %axis_index.36, s32[]{:T(128)S(6)} %axis_index.38), kind=kLoop, calls=%fused_computation.34 | loop fusion | flops 360 | bytes 72 | tf_op jit(solution)/shard_map/add | solution.py:170
  8.1 0.1 stack.98
  8.3 0.8 %dynamic_slice.11 = s32[16,2]{0,1:T(2,128)S(1)} dynamic-slice(s32[64,8]{0,1:T(8,128)} %param.7, s32[]{:T(128)S(6)} %select_n.179, s32[]{:T(128)S(6)} %select_n.204), dynamic_slice_sizes={16,2} | dynamic-slice | bytes 260 | tf_op jit(solution)/shard_map/dynamic_slice | solution.py:130
  9.1 0.7 %copy.18.keep_ref = s32[16,2]{1,0:T(8,128)} copy(s32[16,2]{0,1:T(2,128)S(1)} %dynamic_slice.11) | data formatting | bytes 256 | tf_op jit(solution)/shard_map/optimization_barrier | solution.py:176
  9.9 0.6 %gather_fusion.1 = s32[8,16]{1,0:T(8,128)S(1)} fusion(s32[16,8]{0,1:T(8,128)S(1)} %copy.15, s32[1024]{0:T(1024)S(1)} %pad_clamp_fusion), kind=kCustom, calls=%fused_computation.1 | custom fusion | bytes 1056 | tf_op jit(solution)/shard_map/jit(_take)/gather | solution.py:175
  10.4 0.7 %broadcast_select_fusion.1.slot_ref = s32[8,16]{1,0:T(8,128)} fusion(s32[8,16]{1,0:T(8,128)S(1)} %gather_fusion.1, pred[8]{0:T(512)(128)(4,1)S(1)} %compare_and_fusion), kind=kLoop, calls=%fused_computation.21 | loop fusion | flops 128 | bytes 1032 | tf_op jit(solution)/shard_map/jit(_take)/select_n | solution.py:175
  11.1 0.9 %collective-permute-done.1.refs_1_ = bf16[8,128,128]{2,1,0:T(8,128)(2,1)S(1)} collective-permute-done((bf16[8,128,128]{2,1,0:T(8,128)(2,1)S(1)}, bf16[8,128,128]{2,1,0:T(8,128)(2,1)S(1)}, u32[]{:S(2)}, u32[]{:S(2)}) %collective-permute-start.1) | collective-permute-done | bytes 262176 | tf_op jit(solution)/shard_map/ppermute | solution.py:155
  12.0 2.6 %collective-permute-done.refs_2_ = bf16[8,128,128]{2,1,0:T(8,128)(2,1)S(1)} collective-permute-done((bf16[8,128,128]{2,1,0:T(8,128)(2,1)S(1)}, bf16[8,128,128]{2,1,0:T(8,128)(2,1)S(1)}, u32[]{:S(2)}, u32[]{:S(2)}) %collective-permute-start) | collective-permute-done | bytes 262176 | tf_op jit(solution)/shard_map/ppermute | solution.py:159
  14.6 1.7 %collective-permute-start.5 = (bf16[8,128,128]{2,1,0:T(8,128)(2,1)S(1)}, bf16[8,128,128]{2,1,0:T(8,128)(2,1)S(1)}, u32[]{:S(2)}, u32[]{:S(2)}) collective-permute-start(bf16[8,128,128]{2,1,0:T(8,128)(2,1)S(1)} %broadcast_select_fusion.refs_0_), channel_id=1, source_target_pairs={{0,3},{1,0},{2,1},{3,2},{4,7},{5,4},{6,5},{7,6},{8,11},{9,8},{10,9... | collective-permute-start | bytes 786440 | tf_op jit(solution)/shard_map/ppermute | solution.py:159
  16.5 1.1 %collective-permute-start.2 = (bf16[8,128,128]{2,1,0:T(8,128)(2,1)S(1)}, bf16[8,128,128]{2,1,0:T(8,128)(2,1)S(1)}, u32[]{:S(2)}, u32[]{:S(2)}) collective-permute-start(bf16[8,128,128]{2,1,0:T(8,128)(2,1)S(1)} %collective-permute-done.refs_2_), channel_id=1, source_target_pairs={{0,16},{16,0},{1,17},{17,1},{2,18},{18,2},{3,19},{19,3},{4,20},{20... | collective-permute-start | bytes 786440 | tf_op jit(solution)/shard_map/ppermute | solution.py:30
  17.6 5.5 %collective-permute-done.5.refs_6_ = bf16[8,128,128]{2,1,0:T(8,128)(2,1)S(1)} collective-permute-done((bf16[8,128,128]{2,1,0:T(8,128)(2,1)S(1)}, bf16[8,128,128]{2,1,0:T(8,128)(2,1)S(1)}, u32[]{:S(2)}, u32[]{:S(2)}) %collective-permute-start.5) | collective-permute-done | bytes 262176 | tf_op jit(solution)/shard_map/ppermute | solution.py:159
  23.1 1.0 %collective-permute-start.6 = (bf16[8,128,128]{2,1,0:T(8,128)(2,1)S(1)}, bf16[8,128,128]{2,1,0:T(8,128)(2,1)S(1)}, u32[]{:S(2)}, u32[]{:S(2)}) collective-permute-start(bf16[8,128,128]{2,1,0:T(8,128)(2,1)S(1)} %collective-permute-done.5.refs_6_), channel_id=1, source_target_pairs={{0,16},{16,0},{1,17},{17,1},{2,18},{18,2},{3,19},{19,3},{4,20},{20... | collective-permute-start | bytes 786440 | tf_op jit(solution)/shard_map/ppermute | solution.py:30
  24.1 7.7 %collective-permute-done.3.refs_4_ = bf16[8,128,128]{2,1,0:T(8,128)(2,1)S(1)} collective-permute-done((bf16[8,128,128]{2,1,0:T(8,128)(2,1)S(1)}, bf16[8,128,128]{2,1,0:T(8,128)(2,1)S(1)}, u32[]{:S(2)}, u32[]{:S(2)}) %collective-permute-start.3) | collective-permute-done | bytes 262176 | tf_op jit(solution)/shard_map/ppermute | solution.py:159
  31.8 0.7 %collective-permute-start.4 = (bf16[8,128,128]{2,1,0:T(8,128)(2,1)S(1)}, bf16[8,128,128]{2,1,0:T(8,128)(2,1)S(1)}, u32[]{:S(2)}, u32[]{:S(2)}) collective-permute-start(bf16[8,128,128]{2,1,0:T(8,128)(2,1)S(1)} %collective-permute-done.3.refs_4_), channel_id=1, source_target_pairs={{0,16},{16,0},{1,17},{17,1},{2,18},{18,2},{3,19},{19,3},{4,20},{20... | collective-permute-start | bytes 786440 | tf_op jit(solution)/shard_map/ppermute | solution.py:30
  32.5 1.5 %collective-permute-start.9 = (bf16[2,128,256]{2,1,0:T(8,128)(2,1)S(1)}, bf16[2,128,256]{2,1,0:T(8,128)(2,1)S(1)}, u32[]{:S(2)}, u32[]{:S(2)}) collective-permute-start(bf16[2,128,256]{2,1,0:T(8,128)(2,1)S(1)} %pad_maximum_fusion.refs_8_), channel_id=1, source_target_pairs={{0,8},{4,12},{8,0},{12,4},{1,9},{5,13},{9,1},{13,5},{2,10},{6,14},... | collective-permute-start | bytes 393224 | tf_op jit(solution)/shard_map/ppermute | solution.py:30
  34.0 3.9 %collective-permute-done.9.refs_10_ = bf16[2,128,256]{2,1,0:T(8,128)(2,1)S(1)} collective-permute-done((bf16[2,128,256]{2,1,0:T(8,128)(2,1)S(1)}, bf16[2,128,256]{2,1,0:T(8,128)(2,1)S(1)}, u32[]{:S(2)}, u32[]{:S(2)}) %collective-permute-start.9) | collective-permute-done | bytes 131104 | tf_op jit(solution)/shard_map/ppermute | solution.py:30
  37.9 0.9 %collective-permute-done.8.refs_9_ = bf16[2,128,256]{2,1,0:T(8,128)(2,1)S(1)} collective-permute-done((bf16[2,128,256]{2,1,0:T(8,128)(2,1)S(1)}, bf16[2,128,256]{2,1,0:T(8,128)(2,1)S(1)}, u32[]{:S(2)}, u32[]{:S(2)}) %collective-permute-start.8) | collective-permute-done | bytes 131104 | tf_op jit(solution)/shard_map/ppermute | solution.py:30
  39.0 0.5 %copy-done.14 = bf16[2,128,256]{2,1,0:T(8,128)(2,1)} copy-done((bf16[2,128,256]{2,1,0:T(8,128)(2,1)}, bf16[2,128,256]{2,1,0:T(8,128)(2,1)S(1)}, u32[]{:S(2)}) %copy-start.14) | copy-done | bytes 131096
  39.5 0.1 copy-done.9
  39.6 0.1 copy-done.10
  39.7 0.7 %copy-done.11 = bf16[8,128,128]{2,1,0:T(8,128)(2,1)} copy-done((bf16[8,128,128]{2,1,0:T(8,128)(2,1)}, bf16[8,128,128]{2,1,0:T(8,128)(2,1)S(1)}, u32[]{:S(2)}) %copy-start.11) | copy-done | bytes 262168
  40.4 4.2 %shard_map.46 = bf16[2048,256]{1,0:T(8,128)(2,1)} custom-call(s32[8,16]{1,0:T(8,128)} %broadcast_select_fusion.1.slot_ref, s32[8]{0:T(128)} %fusion.1.rf_pos_ref, s32[16,2]{1,0:T(8,128)} %copy.18.keep_ref, bf16[8,128,128]{2,1,0:T(8,128)(2,1)} %copy-done.1, bf16[8,128,128]{2,1,0:T(8,128)(2,1)} %copy-done.5, bf16[8,128,128]{2,1,0:T(8,128)(2,1)} %copy-done.6, ...), custom_call_target="tpu_custom_call" | custom-call | flops 1073741824 | bytes 3670016 | tf_op jit(solution)/shard_map/pallas_call | solution.py:83
  (53 shorter events, 0.8 us)
Async XLA Ops:
  0.0 1.2 %copy-start = (bf16[2048,128]{1,0:T(8,128)(2,1)S(1)}, bf16[2048,128]{1,0:T(8,128)(2,1)}, u32[]{:S(2)}) copy-start(bf16[2048,128]{1,0:T(8,128)(2,1)} %param.4) | copy-start | bytes 1572868
  0.0 0.7 %copy-start.4 = (s32[64,8]{0,1:T(8,128)S(1)}, s32[64,8]{0,1:T(8,128)}, u32[]{:S(2)}) copy-start(s32[64,8]{0,1:T(8,128)} %param.6) | copy-start | bytes 6148
  1.8 4.7 %copy-start.2 = (bf16[128,256]{1,0:T(8,128)(2,1)S(1)}, bf16[128,256]{1,0:T(8,128)(2,1)}, u32[]{:S(2)}) copy-start(bf16[128,256]{1,0:T(8,128)(2,1)} %param.5) | copy-start | bytes 196612
  1.9 14.4 %copy-start.1 = (bf16[8,128,128]{2,1,0:T(8,128)(2,1)}, bf16[8,128,128]{2,1,0:T(8,128)(2,1)S(1)}, u32[]{:S(2)}) copy-start(bf16[8,128,128]{2,1,0:T(8,128)(2,1)S(1)} %broadcast_select_fusion.refs_0_) | copy-start | bytes 786436
  2.0 10.0 %collective-permute-start.1 = (bf16[8,128,128]{2,1,0:T(8,128)(2,1)S(1)}, bf16[8,128,128]{2,1,0:T(8,128)(2,1)S(1)}, u32[]{:S(2)}, u32[]{:S(2)}) collective-permute-start(bf16[8,128,128]{2,1,0:T(8,128)(2,1)S(1)} %broadcast_select_fusion.refs_0_), channel_id=1, source_target_pairs={{0,16},{16,0},{1,17},{17,1},{2,18},{18,2},{3,19},{19,3},{4,20},{20... | collective-permute-start | bytes 786440 | tf_op jit(solution)/shard_map/ppermute | solution.py:155
  5.0 9.6 %collective-permute-start = (bf16[8,128,128]{2,1,0:T(8,128)(2,1)S(1)}, bf16[8,128,128]{2,1,0:T(8,128)(2,1)S(1)}, u32[]{:S(2)}, u32[]{:S(2)}) collective-permute-start(bf16[8,128,128]{2,1,0:T(8,128)(2,1)S(1)} %broadcast_select_fusion.refs_0_), channel_id=1, source_target_pairs={{0,1},{1,2},{2,3},{3,0},{4,5},{5,6},{6,7},{7,4},{8,9},{9,10},{10,1... | collective-permute-start | bytes 786440 | tf_op jit(solution)/shard_map/ppermute | solution.py:159
  6.6 9.8 %collective-permute-start.7 = (bf16[128,256]{1,0:T(8,128)(2,1)S(1)}, bf16[128,256]{1,0:T(8,128)(2,1)S(1)}, u32[]{:S(2)}, u32[]{:S(2)}) collective-permute-start(bf16[128,256]{1,0:T(8,128)(2,1)S(1)} %subtract_convert_fusion), channel_id=1, source_target_pairs={{0,16},{16,0},{1,17},{17,1},{2,18},{18,2},{3,19},{19,3},{4,20},{20... | collective-permute-start | bytes 196616 | tf_op jit(solution)/shard_map/ppermute | solution.py:30
  12.0 26.9 %copy-start.5 = (bf16[8,128,128]{2,1,0:T(8,128)(2,1)}, bf16[8,128,128]{2,1,0:T(8,128)(2,1)S(1)}, u32[]{:S(2)}) copy-start(bf16[8,128,128]{2,1,0:T(8,128)(2,1)S(1)} %collective-permute-done.1.refs_1_) | copy-start | bytes 786436
  14.6 24.3 %copy-start.6 = (bf16[8,128,128]{2,1,0:T(8,128)(2,1)}, bf16[8,128,128]{2,1,0:T(8,128)(2,1)S(1)}, u32[]{:S(2)}) copy-start(bf16[8,128,128]{2,1,0:T(8,128)(2,1)S(1)} %collective-permute-done.refs_2_) | copy-start | bytes 786436
  14.6 8.5 %collective-permute-start.5 = (bf16[8,128,128]{2,1,0:T(8,128)(2,1)S(1)}, bf16[8,128,128]{2,1,0:T(8,128)(2,1)S(1)}, u32[]{:S(2)}, u32[]{:S(2)}) collective-permute-start(bf16[8,128,128]{2,1,0:T(8,128)(2,1)S(1)} %broadcast_select_fusion.refs_0_), channel_id=1, source_target_pairs={{0,3},{1,0},{2,1},{3,2},{4,7},{5,4},{6,5},{7,6},{8,11},{9,8},{10,9... | collective-permute-start | bytes 786440 | tf_op jit(solution)/shard_map/ppermute | solution.py:159
  16.3 15.5 %collective-permute-start.3 = (bf16[8,128,128]{2,1,0:T(8,128)(2,1)S(1)}, bf16[8,128,128]{2,1,0:T(8,128)(2,1)S(1)}, u32[]{:S(2)}, u32[]{:S(2)}) collective-permute-start(bf16[8,128,128]{2,1,0:T(8,128)(2,1)S(1)} %broadcast_select_fusion.refs_0_), channel_id=1, source_target_pairs={{0,2},{1,3},{2,0},{3,1},{4,6},{5,7},{6,4},{7,5},{8,10},{9,11},{10,... | collective-permute-start | bytes 786440 | tf_op jit(solution)/shard_map/ppermute | solution.py:159
  16.5 22.5 %copy-start.3 = (bf16[2,128,256]{2,1,0:T(8,128)(2,1)}, bf16[2,128,256]{2,1,0:T(8,128)(2,1)S(1)}, u32[]{:S(2)}) copy-start(bf16[2,128,256]{2,1,0:T(8,128)(2,1)S(1)} %pad_maximum_fusion.refs_8_) | copy-start | bytes 393220
  16.5 17.5 %collective-permute-start.10 = (bf16[2,128,256]{2,1,0:T(8,128)(2,1)S(1)}, bf16[2,128,256]{2,1,0:T(8,128)(2,1)S(1)}, u32[]{:S(2)}, u32[]{:S(2)}) collective-permute-start(bf16[2,128,256]{2,1,0:T(8,128)(2,1)S(1)} %pad_maximum_fusion.refs_8_), channel_id=1, source_target_pairs={{0,12},{4,0},{8,4},{12,8},{1,13},{5,1},{9,5},{13,9},{2,14},{6,2},{... | collective-permute-start | bytes 393224 | tf_op jit(solution)/shard_map/ppermute | solution.py:30
  16.5 22.3 %collective-permute-start.2 = (bf16[8,128,128]{2,1,0:T(8,128)(2,1)S(1)}, bf16[8,128,128]{2,1,0:T(8,128)(2,1)S(1)}, u32[]{:S(2)}, u32[]{:S(2)}) collective-permute-start(bf16[8,128,128]{2,1,0:T(8,128)(2,1)S(1)} %collective-permute-done.refs_2_), channel_id=1, source_target_pairs={{0,16},{16,0},{1,17},{17,1},{2,18},{18,2},{3,19},{19,3},{4,20},{20... | collective-permute-start | bytes 786440 | tf_op jit(solution)/shard_map/ppermute | solution.py:30
  23.1 15.8 %copy-start.7 = (bf16[8,128,128]{2,1,0:T(8,128)(2,1)}, bf16[8,128,128]{2,1,0:T(8,128)(2,1)S(1)}, u32[]{:S(2)}) copy-start(bf16[8,128,128]{2,1,0:T(8,128)(2,1)S(1)} %collective-permute-done.5.refs_6_) | copy-start | bytes 786436
  23.1 15.8 %collective-permute-start.6 = (bf16[8,128,128]{2,1,0:T(8,128)(2,1)S(1)}, bf16[8,128,128]{2,1,0:T(8,128)(2,1)S(1)}, u32[]{:S(2)}, u32[]{:S(2)}) collective-permute-start(bf16[8,128,128]{2,1,0:T(8,128)(2,1)S(1)} %collective-permute-done.5.refs_6_), channel_id=1, source_target_pairs={{0,16},{16,0},{1,17},{17,1},{2,18},{18,2},{3,19},{19,3},{4,20},{20... | collective-permute-start | bytes 786440 | tf_op jit(solution)/shard_map/ppermute | solution.py:30
  31.8 7.1 %copy-start.8 = (bf16[8,128,128]{2,1,0:T(8,128)(2,1)}, bf16[8,128,128]{2,1,0:T(8,128)(2,1)S(1)}, u32[]{:S(2)}) copy-start(bf16[8,128,128]{2,1,0:T(8,128)(2,1)S(1)} %collective-permute-done.3.refs_4_) | copy-start | bytes 786436
  31.8 7.0 %collective-permute-start.4 = (bf16[8,128,128]{2,1,0:T(8,128)(2,1)S(1)}, bf16[8,128,128]{2,1,0:T(8,128)(2,1)S(1)}, u32[]{:S(2)}, u32[]{:S(2)}) collective-permute-start(bf16[8,128,128]{2,1,0:T(8,128)(2,1)S(1)} %collective-permute-done.3.refs_4_), channel_id=1, source_target_pairs={{0,16},{16,0},{1,17},{17,1},{2,18},{18,2},{3,19},{19,3},{4,20},{20... | collective-permute-start | bytes 786440 | tf_op jit(solution)/shard_map/ppermute | solution.py:30
  32.5 5.4 %collective-permute-start.9 = (bf16[2,128,256]{2,1,0:T(8,128)(2,1)S(1)}, bf16[2,128,256]{2,1,0:T(8,128)(2,1)S(1)}, u32[]{:S(2)}, u32[]{:S(2)}) collective-permute-start(bf16[2,128,256]{2,1,0:T(8,128)(2,1)S(1)} %pad_maximum_fusion.refs_8_), channel_id=1, source_target_pairs={{0,8},{4,12},{8,0},{12,4},{1,9},{5,13},{9,1},{13,5},{2,10},{6,14},... | collective-permute-start | bytes 393224 | tf_op jit(solution)/shard_map/ppermute | solution.py:30
  34.0 4.9 %copy-start.12 = (bf16[2,128,256]{2,1,0:T(8,128)(2,1)}, bf16[2,128,256]{2,1,0:T(8,128)(2,1)S(1)}, u32[]{:S(2)}) copy-start(bf16[2,128,256]{2,1,0:T(8,128)(2,1)S(1)} %collective-permute-done.10.refs_11_) | copy-start | bytes 393220
  34.0 4.8 %collective-permute-start.8 = (bf16[2,128,256]{2,1,0:T(8,128)(2,1)S(1)}, bf16[2,128,256]{2,1,0:T(8,128)(2,1)S(1)}, u32[]{:S(2)}, u32[]{:S(2)}) collective-permute-start(bf16[2,128,256]{2,1,0:T(8,128)(2,1)S(1)} %pad_maximum_fusion.refs_8_), channel_id=1, source_target_pairs={{0,4},{4,8},{8,12},{12,0},{1,5},{5,9},{9,13},{13,1},{2,6},{6,10},{... | collective-permute-start | bytes 393224 | tf_op jit(solution)/shard_map/ppermute | solution.py:30
  37.9 1.0 %copy-start.13 = (bf16[2,128,256]{2,1,0:T(8,128)(2,1)}, bf16[2,128,256]{2,1,0:T(8,128)(2,1)S(1)}, u32[]{:S(2)}) copy-start(bf16[2,128,256]{2,1,0:T(8,128)(2,1)S(1)} %collective-permute-done.9.refs_10_) | copy-start | bytes 393220
  38.9 0.7 %copy-start.14 = (bf16[2,128,256]{2,1,0:T(8,128)(2,1)}, bf16[2,128,256]{2,1,0:T(8,128)(2,1)S(1)}, u32[]{:S(2)}) copy-start(bf16[2,128,256]{2,1,0:T(8,128)(2,1)S(1)} %collective-permute-done.8.refs_9_) | copy-start | bytes 393220
  38.9 0.8 %copy-start.9 = (bf16[8,128,128]{2,1,0:T(8,128)(2,1)}, bf16[8,128,128]{2,1,0:T(8,128)(2,1)S(1)}, u32[]{:S(2)}) copy-start(bf16[8,128,128]{2,1,0:T(8,128)(2,1)S(1)} %collective-permute-done.2.refs_3_) | copy-start | bytes 786436
  38.9 0.8 %copy-start.10 = (bf16[8,128,128]{2,1,0:T(8,128)(2,1)}, bf16[8,128,128]{2,1,0:T(8,128)(2,1)S(1)}, u32[]{:S(2)}) copy-start(bf16[8,128,128]{2,1,0:T(8,128)(2,1)S(1)} %collective-permute-done.6.refs_7_) | copy-start | bytes 786436
  39.7 0.7 %copy-start.11 = (bf16[8,128,128]{2,1,0:T(8,128)(2,1)}, bf16[8,128,128]{2,1,0:T(8,128)(2,1)S(1)}, u32[]{:S(2)}) copy-start(bf16[8,128,128]{2,1,0:T(8,128)(2,1)S(1)} %collective-permute-done.4.refs_5_) | copy-start | bytes 786436

commit v11 on v10

--- a/solution.py
+++ b/solution.py
@@ -56,7 +56,7 @@
             blk = left_refs[p][jnp.maximum(s, 0)]
             blk = jnp.where(s >= 0, blk, jnp.zeros_like(blk))
             lhs_scr[i * BLK:(i + 1) * BLK, p * BLK:(p + 1) * BLK] = blk
-    tile = 2 * BLK
+    tile = 4 * BLK
     for t in range(row_blocks * BLK // tile):
         res = jnp.dot(
             lhs_scr[t * tile:(t + 1) * tile, :], rf_scr[...], preferred_element_type=jnp.float32

time: 44.8 us -> 44.7 us (level)
  no operation moved by 1% of the time
where the time goes in v11:
time: 44.7 us; the launch traced here: 44.5 us
  waiting for transfers between devices  21.5 us (48%)
  starting transfers between devices  11.3 us (25%)
  local copies, waits for them, and re-layouts  5.4 us (12%)
  Pallas kernels  4.11 us (9%)
  other arithmetic  1.98 us (4%)
    ppermute x3, waiting for transfers between devices, col_shift(): lax.ppermute(x, 'col', [(s, (s + k) % col_count) for s in range(col_count)])  15.8 us
    ppermute x7, starting transfers between devices, ring_gather(): pieces.append(lax.ppermute(x, axis, perm))  4.97 us
    ppermute x7, waiting for transfers between devices, ring_gather(): pieces.append(lax.ppermute(x, axis, perm))  4.85 us
    pallas_call x1, Pallas kernels, product_call(): pl.pallas_call(functools.partial(product_kernel, pieces=pieces, rf_groups...  4.11 us
    ppermute x3, starting transfers between devices, col_shift(): lax.ppermute(x, 'col', [(s, (s + k) % col_count) for s in range(col_count)])  3.32 us
    ppermute x1, starting transfers between devices, per_device(): lax.ppermute(packed[0], 'layer', [(s, (s + m) % layer_count) for s in ran...  3 us
    unnamed x31, local copies, waits for them, and re-layouts  2.31 us
  transfers between devices with their start and end apart: 11, of which 6 were waited for; matrix products, arithmetic and copies ran while one was open for 9% of the time, Pallas kernels for 0%

profile of v11, /device:TPU:0, one launch (start us, length us, event | category | flops | bytes accessed | tf_op | source)
XLA Modules:
  0.0 44.5 jit_solution(13066674911134152439)
XLA Ops:
  0.0 0.7 %copy-done.4 = s32[64,8]{0,1:T(8,128)S(1)} copy-done((s32[64,8]{0,1:T(8,128)S(1)}, s32[64,8]{0,1:T(8,128)}, u32[]{:S(2)}) %copy-start.4) | copy-done | bytes 2072
  0.8 0.1 copy.13
  0.9 0.1 add_reduce_fusion
  1.1 0.1 select_reduce_fusion
  1.2 0.6 %gather_fusion = bf16[8,128,128]{2,1,0:T(8,128)(2,1)S(1)} fusion(bf16[16,128,128]{2,1,0:T(8,128)(2,1)S(1)} %bitcast.36, s32[1024]{0:T(1024)S(1)} %pad_clamp_fusion.1), kind=kCustom, calls=%fused_computation | custom fusion | bytes 524320 | tf_op jit(solution)/shard_map/jit(_take)/gather | solution.py:126
  1.8 0.1 broadcast_select_fusion.refs_0_
  2.0 3.0 %collective-permute-start.1 = (bf16[8,128,128]{2,1,0:T(8,128)(2,1)S(1)}, bf16[8,128,128]{2,1,0:T(8,128)(2,1)S(1)}, u32[]{:S(2)}, u32[]{:S(2)}) collective-permute-start(bf16[8,128,128]{2,1,0:T(8,128)(2,1)S(1)} %broadcast_select_fusion.refs_0_), channel_id=1, source_target_pairs={{0,16},{16,0},{1,17},{17,1},{2,18},{18,2},{3,19},{19,3},{4,20},{20... | collective-permute-start | bytes 786440 | tf_op jit(solution)/shard_map/ppermute | solution.py:155
  5.0 1.6 %collective-permute-start = (bf16[8,128,128]{2,1,0:T(8,128)(2,1)S(1)}, bf16[8,128,128]{2,1,0:T(8,128)(2,1)S(1)}, u32[]{:S(2)}, u32[]{:S(2)}) collective-permute-start(bf16[8,128,128]{2,1,0:T(8,128)(2,1)S(1)} %broadcast_select_fusion.refs_0_), channel_id=1, source_target_pairs={{0,1},{1,2},{2,3},{3,0},{4,5},{5,6},{6,7},{7,4},{8,9},{9,10},{10,1... | collective-permute-start | bytes 786440 | tf_op jit(solution)/shard_map/ppermute | solution.py:159
  6.5 0.1 subtract_convert_fusion
  6.6 0.6 %collective-permute-start.7 = (bf16[128,256]{1,0:T(8,128)(2,1)S(1)}, bf16[128,256]{1,0:T(8,128)(2,1)S(1)}, u32[]{:S(2)}, u32[]{:S(2)}) collective-permute-start(bf16[128,256]{1,0:T(8,128)(2,1)S(1)} %subtract_convert_fusion), channel_id=1, source_target_pairs={{0,16},{16,0},{1,17},{17,1},{2,18},{18,2},{3,19},{19,3},{4,20},{20... | collective-permute-start | bytes 196616 | tf_op jit(solution)/shard_map/ppermute | solution.py:30
  7.4 0.6 %fusion.1.rf_pos_ref = s32[8]{0:T(128)} fusion(s32[8]{0:T(128)S(1)} %stack.107, s32[]{:T(128)S(6)} %axis_index.36, s32[]{:T(128)S(6)} %axis_index.38), kind=kLoop, calls=%fused_computation.34 | loop fusion | flops 360 | bytes 72 | tf_op jit(solution)/shard_map/add | solution.py:170
  8.1 0.1 stack.98
  8.3 0.8 %dynamic_slice.11 = s32[16,2]{0,1:T(2,128)S(1)} dynamic-slice(s32[64,8]{0,1:T(8,128)} %param.7, s32[]{:T(128)S(6)} %select_n.179, s32[]{:T(128)S(6)} %select_n.204), dynamic_slice_sizes={16,2} | dynamic-slice | bytes 260 | tf_op jit(solution)/shard_map/dynamic_slice | solution.py:130
  9.1 0.7 %copy.18.keep_ref = s32[16,2]{1,0:T(8,128)} copy(s32[16,2]{0,1:T(2,128)S(1)} %dynamic_slice.11) | data formatting | bytes 256 | tf_op jit(solution)/shard_map/optimization_barrier | solution.py:176
  9.9 0.6 %gather_fusion.1 = s32[8,16]{1,0:T(8,128)S(1)} fusion(s32[16,8]{0,1:T(8,128)S(1)} %copy.15, s32[1024]{0:T(1024)S(1)} %pad_clamp_fusion), kind=kCustom, calls=%fused_computation.1 | custom fusion | bytes 1056 | tf_op jit(solution)/shard_map/jit(_take)/gather | solution.py:175
  10.4 0.7 %broadcast_select_fusion.1.slot_ref = s32[8,16]{1,0:T(8,128)} fusion(s32[8,16]{1,0:T(8,128)S(1)} %gather_fusion.1, pred[8]{0:T(512)(128)(4,1)S(1)} %compare_and_fusion), kind=kLoop, calls=%fused_computation.21 | loop fusion | flops 128 | bytes 1032 | tf_op jit(solution)/shard_map/jit(_take)/select_n | solution.py:175
  11.1 0.9 %collective-permute-done.1.refs_1_ = bf16[8,128,128]{2,1,0:T(8,128)(2,1)S(1)} collective-permute-done((bf16[8,128,128]{2,1,0:T(8,128)(2,1)S(1)}, bf16[8,128,128]{2,1,0:T(8,128)(2,1)S(1)}, u32[]{:S(2)}, u32[]{:S(2)}) %collective-permute-start.1) | collective-permute-done | bytes 262176 | tf_op jit(solution)/shard_map/ppermute | solution.py:155
  12.0 2.6 %collective-permute-done.refs_2_ = bf16[8,128,128]{2,1,0:T(8,128)(2,1)S(1)} collective-permute-done((bf16[8,128,128]{2,1,0:T(8,128)(2,1)S(1)}, bf16[8,128,128]{2,1,0:T(8,128)(2,1)S(1)}, u32[]{:S(2)}, u32[]{:S(2)}) %collective-permute-start) | collective-permute-done | bytes 262176 | tf_op jit(solution)/shard_map/ppermute | solution.py:159
  14.6 1.7 %collective-permute-start.5 = (bf16[8,128,128]{2,1,0:T(8,128)(2,1)S(1)}, bf16[8,128,128]{2,1,0:T(8,128)(2,1)S(1)}, u32[]{:S(2)}, u32[]{:S(2)}) collective-permute-start(bf16[8,128,128]{2,1,0:T(8,128)(2,1)S(1)} %broadcast_select_fusion.refs_0_), channel_id=1, source_target_pairs={{0,3},{1,0},{2,1},{3,2},{4,7},{5,4},{6,5},{7,6},{8,11},{9,8},{10,9... | collective-permute-start | bytes 786440 | tf_op jit(solution)/shard_map/ppermute | solution.py:159
  16.5 1.1 %collective-permute-start.2 = (bf16[8,128,128]{2,1,0:T(8,128)(2,1)S(1)}, bf16[8,128,128]{2,1,0:T(8,128)(2,1)S(1)}, u32[]{:S(2)}, u32[]{:S(2)}) collective-permute-start(bf16[8,128,128]{2,1,0:T(8,128)(2,1)S(1)} %collective-permute-done.refs_2_), channel_id=1, source_target_pairs={{0,16},{16,0},{1,17},{17,1},{2,18},{18,2},{3,19},{19,3},{4,20},{20... | collective-permute-start | bytes 786440 | tf_op jit(solution)/shard_map/ppermute | solution.py:30
  17.6 5.5 %collective-permute-done.5.refs_6_ = bf16[8,128,128]{2,1,0:T(8,128)(2,1)S(1)} collective-permute-done((bf16[8,128,128]{2,1,0:T(8,128)(2,1)S(1)}, bf16[8,128,128]{2,1,0:T(8,128)(2,1)S(1)}, u32[]{:S(2)}, u32[]{:S(2)}) %collective-permute-start.5) | collective-permute-done | bytes 262176 | tf_op jit(solution)/shard_map/ppermute | solution.py:159
  23.1 1.0 %collective-permute-start.6 = (bf16[8,128,128]{2,1,0:T(8,128)(2,1)S(1)}, bf16[8,128,128]{2,1,0:T(8,128)(2,1)S(1)}, u32[]{:S(2)}, u32[]{:S(2)}) collective-permute-start(bf16[8,128,128]{2,1,0:T(8,128)(2,1)S(1)} %collective-permute-done.5.refs_6_), channel_id=1, source_target_pairs={{0,16},{16,0},{1,17},{17,1},{2,18},{18,2},{3,19},{19,3},{4,20},{20... | collective-permute-start | bytes 786440 | tf_op jit(solution)/shard_map/ppermute | solution.py:30
  24.1 7.7 %collective-permute-done.3.refs_4_ = bf16[8,128,128]{2,1,0:T(8,128)(2,1)S(1)} collective-permute-done((bf16[8,128,128]{2,1,0:T(8,128)(2,1)S(1)}, bf16[8,128,128]{2,1,0:T(8,128)(2,1)S(1)}, u32[]{:S(2)}, u32[]{:S(2)}) %collective-permute-start.3) | collective-permute-done | bytes 262176 | tf_op jit(solution)/shard_map/ppermute | solution.py:159
  31.8 0.7 %collective-permute-start.4 = (bf16[8,128,128]{2,1,0:T(8,128)(2,1)S(1)}, bf16[8,128,128]{2,1,0:T(8,128)(2,1)S(1)}, u32[]{:S(2)}, u32[]{:S(2)}) collective-permute-start(bf16[8,128,128]{2,1,0:T(8,128)(2,1)S(1)} %collective-permute-done.3.refs_4_), channel_id=1, source_target_pairs={{0,16},{16,0},{1,17},{17,1},{2,18},{18,2},{3,19},{19,3},{4,20},{20... | collective-permute-start | bytes 786440 | tf_op jit(solution)/shard_map/ppermute | solution.py:30
  32.5 1.5 %collective-permute-start.9 = (bf16[2,128,256]{2,1,0:T(8,128)(2,1)S(1)}, bf16[2,128,256]{2,1,0:T(8,128)(2,1)S(1)}, u32[]{:S(2)}, u32[]{:S(2)}) collective-permute-start(bf16[2,128,256]{2,1,0:T(8,128)(2,1)S(1)} %pad_maximum_fusion.refs_8_), channel_id=1, source_target_pairs={{0,8},{4,12},{8,0},{12,4},{1,9},{5,13},{9,1},{13,5},{2,10},{6,14},... | collective-permute-start | bytes 393224 | tf_op jit(solution)/shard_map/ppermute | solution.py:30
  34.0 3.9 %collective-permute-done.9.refs_10_ = bf16[2,128,256]{2,1,0:T(8,128)(2,1)S(1)} collective-permute-done((bf16[2,128,256]{2,1,0:T(8,128)(2,1)S(1)}, bf16[2,128,256]{2,1,0:T(8,128)(2,1)S(1)}, u32[]{:S(2)}, u32[]{:S(2)}) %collective-permute-start.9) | collective-permute-done | bytes 131104 | tf_op jit(solution)/shard_map/ppermute | solution.py:30
  37.9 0.9 %collective-permute-done.8.refs_9_ = bf16[2,128,256]{2,1,0:T(8,128)(2,1)S(1)} collective-permute-done((bf16[2,128,256]{2,1,0:T(8,128)(2,1)S(1)}, bf16[2,128,256]{2,1,0:T(8,128)(2,1)S(1)}, u32[]{:S(2)}, u32[]{:S(2)}) %collective-permute-start.8) | collective-permute-done | bytes 131104 | tf_op jit(solution)/shard_map/ppermute | solution.py:30
  39.0 0.5 %copy-done.14 = bf16[2,128,256]{2,1,0:T(8,128)(2,1)} copy-done((bf16[2,128,256]{2,1,0:T(8,128)(2,1)}, bf16[2,128,256]{2,1,0:T(8,128)(2,1)S(1)}, u32[]{:S(2)}) %copy-start.14) | copy-done | bytes 131096
  39.5 0.1 copy-done.9
  39.6 0.1 copy-done.10
  39.7 0.7 %copy-done.11 = bf16[8,128,128]{2,1,0:T(8,128)(2,1)} copy-done((bf16[8,128,128]{2,1,0:T(8,128)(2,1)}, bf16[8,128,128]{2,1,0:T(8,128)(2,1)S(1)}, u32[]{:S(2)}) %copy-start.11) | copy-done | bytes 262168
  40.4 4.1 %shard_map.46 = bf16[2048,256]{1,0:T(8,128)(2,1)} custom-call(s32[8,16]{1,0:T(8,128)} %broadcast_select_fusion.1.slot_ref, s32[8]{0:T(128)} %fusion.1.rf_pos_ref, s32[16,2]{1,0:T(8,128)} %copy.18.keep_ref, bf16[8,128,128]{2,1,0:T(8,128)(2,1)} %copy-done.1, bf16[8,128,128]{2,1,0:T(8,128)(2,1)} %copy-done.5, bf16[8,128,128]{2,1,0:T(8,128)(2,1)} %copy-done.6, ...), custom_call_target="tpu_custom_call" | custom-call | flops 1073741824 | bytes 3670016 | tf_op jit(solution)/shard_map/pallas_call | solution.py:83
  (53 shorter events, 0.8 us)
Async XLA Ops:
  0.0 1.2 %copy-start = (bf16[2048,128]{1,0:T(8,128)(2,1)S(1)}, bf16[2048,128]{1,0:T(8,128)(2,1)}, u32[]{:S(2)}) copy-start(bf16[2048,128]{1,0:T(8,128)(2,1)} %param.4) | copy-start | bytes 1572868
  0.0 0.7 %copy-start.4 = (s32[64,8]{0,1:T(8,128)S(1)}, s32[64,8]{0,1:T(8,128)}, u32[]{:S(2)}) copy-start(s32[64,8]{0,1:T(8,128)} %param.6) | copy-start | bytes 6148
  1.8 4.7 %copy-start.2 = (bf16[128,256]{1,0:T(8,128)(2,1)S(1)}, bf16[128,256]{1,0:T(8,128)(2,1)}, u32[]{:S(2)}) copy-start(bf16[128,256]{1,0:T(8,128)(2,1)} %param.5) | copy-start | bytes 196612
  1.9 14.4 %copy-start.1 = (bf16[8,128,128]{2,1,0:T(8,128)(2,1)}, bf16[8,128,128]{2,1,0:T(8,128)(2,1)S(1)}, u32[]{:S(2)}) copy-start(bf16[8,128,128]{2,1,0:T(8,128)(2,1)S(1)} %broadcast_select_fusion.refs_0_) | copy-start | bytes 786436
  2.0 10.0 %collective-permute-start.1 = (bf16[8,128,128]{2,1,0:T(8,128)(2,1)S(1)}, bf16[8,128,128]{2,1,0:T(8,128)(2,1)S(1)}, u32[]{:S(2)}, u32[]{:S(2)}) collective-permute-start(bf16[8,128,128]{2,1,0:T(8,128)(2,1)S(1)} %broadcast_select_fusion.refs_0_), channel_id=1, source_target_pairs={{0,16},{16,0},{1,17},{17,1},{2,18},{18,2},{3,19},{19,3},{4,20},{20... | collective-permute-start | bytes 786440 | tf_op jit(solution)/shard_map/ppermute | solution.py:155
  5.0 9.6 %collective-permute-start = (bf16[8,128,128]{2,1,0:T(8,128)(2,1)S(1)}, bf16[8,128,128]{2,1,0:T(8,128)(2,1)S(1)}, u32[]{:S(2)}, u32[]{:S(2)}) collective-permute-start(bf16[8,128,128]{2,1,0:T(8,128)(2,1)S(1)} %broadcast_select_fusion.refs_0_), channel_id=1, source_target_pairs={{0,1},{1,2},{2,3},{3,0},{4,5},{5,6},{6,7},{7,4},{8,9},{9,10},{10,1... | collective-permute-start | bytes 786440 | tf_op jit(solution)/shard_map/ppermute | solution.py:159
  6.6 9.8 %collective-permute-start.7 = (bf16[128,256]{1,0:T(8,128)(2,1)S(1)}, bf16[128,256]{1,0:T(8,128)(2,1)S(1)}, u32[]{:S(2)}, u32[]{:S(2)}) collective-permute-start(bf16[128,256]{1,0:T(8,128)(2,1)S(1)} %subtract_convert_fusion), channel_id=1, source_target_pairs={{0,16},{16,0},{1,17},{17,1},{2,18},{18,2},{3,19},{19,3},{4,20},{20... | collective-permute-start | bytes 196616 | tf_op jit(solution)/shard_map/ppermute | solution.py:30
  12.0 26.9 %copy-start.5 = (bf16[8,128,128]{2,1,0:T(8,128)(2,1)}, bf16[8,128,128]{2,1,0:T(8,128)(2,1)S(1)}, u32[]{:S(2)}) copy-start(bf16[8,128,128]{2,1,0:T(8,128)(2,1)S(1)} %collective-permute-done.1.refs_1_) | copy-start | bytes 786436
  14.6 24.3 %copy-start.6 = (bf16[8,128,128]{2,1,0:T(8,128)(2,1)}, bf16[8,128,128]{2,1,0:T(8,128)(2,1)S(1)}, u32[]{:S(2)}) copy-start(bf16[8,128,128]{2,1,0:T(8,128)(2,1)S(1)} %collective-permute-done.refs_2_) | copy-start | bytes 786436
  14.6 8.5 %collective-permute-start.5 = (bf16[8,128,128]{2,1,0:T(8,128)(2,1)S(1)}, bf16[8,128,128]{2,1,0:T(8,128)(2,1)S(1)}, u32[]{:S(2)}, u32[]{:S(2)}) collective-permute-start(bf16[8,128,128]{2,1,0:T(8,128)(2,1)S(1)} %broadcast_select_fusion.refs_0_), channel_id=1, source_target_pairs={{0,3},{1,0},{2,1},{3,2},{4,7},{5,4},{6,5},{7,6},{8,11},{9,8},{10,9... | collective-permute-start | bytes 786440 | tf_op jit(solution)/shard_map/ppermute | solution.py:159
  16.3 15.5 %collective-permute-start.3 = (bf16[8,128,128]{2,1,0:T(8,128)(2,1)S(1)}, bf16[8,128,128]{2,1,0:T(8,128)(2,1)S(1)}, u32[]{:S(2)}, u32[]{:S(2)}) collective-permute-start(bf16[8,128,128]{2,1,0:T(8,128)(2,1)S(1)} %broadcast_select_fusion.refs_0_), channel_id=1, source_target_pairs={{0,2},{1,3},{2,0},{3,1},{4,6},{5,7},{6,4},{7,5},{8,10},{9,11},{10,... | collective-permute-start | bytes 786440 | tf_op jit(solution)/shard_map/ppermute | solution.py:159
  16.5 22.5 %copy-start.3 = (bf16[2,128,256]{2,1,0:T(8,128)(2,1)}, bf16[2,128,256]{2,1,0:T(8,128)(2,1)S(1)}, u32[]{:S(2)}) copy-start(bf16[2,128,256]{2,1,0:T(8,128)(2,1)S(1)} %pad_maximum_fusion.refs_8_) | copy-start | bytes 393220
  16.5 17.5 %collective-permute-start.10 = (bf16[2,128,256]{2,1,0:T(8,128)(2,1)S(1)}, bf16[2,128,256]{2,1,0:T(8,128)(2,1)S(1)}, u32[]{:S(2)}, u32[]{:S(2)}) collective-permute-start(bf16[2,128,256]{2,1,0:T(8,128)(2,1)S(1)} %pad_maximum_fusion.refs_8_), channel_id=1, source_target_pairs={{0,12},{4,0},{8,4},{12,8},{1,13},{5,1},{9,5},{13,9},{2,14},{6,2},{... | collective-permute-start | bytes 393224 | tf_op jit(solution)/shard_map/ppermute | solution.py:30
  16.5 22.3 %collective-permute-start.2 = (bf16[8,128,128]{2,1,0:T(8,128)(2,1)S(1)}, bf16[8,128,128]{2,1,0:T(8,128)(2,1)S(1)}, u32[]{:S(2)}, u32[]{:S(2)}) collective-permute-start(bf16[8,128,128]{2,1,0:T(8,128)(2,1)S(1)} %collective-permute-done.refs_2_), channel_id=1, source_target_pairs={{0,16},{16,0},{1,17},{17,1},{2,18},{18,2},{3,19},{19,3},{4,20},{20... | collective-permute-start | bytes 786440 | tf_op jit(solution)/shard_map/ppermute | solution.py:30
  23.1 15.8 %copy-start.7 = (bf16[8,128,128]{2,1,0:T(8,128)(2,1)}, bf16[8,128,128]{2,1,0:T(8,128)(2,1)S(1)}, u32[]{:S(2)}) copy-start(bf16[8,128,128]{2,1,0:T(8,128)(2,1)S(1)} %collective-permute-done.5.refs_6_) | copy-start | bytes 786436
  23.1 15.8 %collective-permute-start.6 = (bf16[8,128,128]{2,1,0:T(8,128)(2,1)S(1)}, bf16[8,128,128]{2,1,0:T(8,128)(2,1)S(1)}, u32[]{:S(2)}, u32[]{:S(2)}) collective-permute-start(bf16[8,128,128]{2,1,0:T(8,128)(2,1)S(1)} %collective-permute-done.5.refs_6_), channel_id=1, source_target_pairs={{0,16},{16,0},{1,17},{17,1},{2,18},{18,2},{3,19},{19,3},{4,20},{20... | collective-permute-start | bytes 786440 | tf_op jit(solution)/shard_map/ppermute | solution.py:30
  31.8 7.1 %copy-start.8 = (bf16[8,128,128]{2,1,0:T(8,128)(2,1)}, bf16[8,128,128]{2,1,0:T(8,128)(2,1)S(1)}, u32[]{:S(2)}) copy-start(bf16[8,128,128]{2,1,0:T(8,128)(2,1)S(1)} %collective-permute-done.3.refs_4_) | copy-start | bytes 786436
  31.8 7.0 %collective-permute-start.4 = (bf16[8,128,128]{2,1,0:T(8,128)(2,1)S(1)}, bf16[8,128,128]{2,1,0:T(8,128)(2,1)S(1)}, u32[]{:S(2)}, u32[]{:S(2)}) collective-permute-start(bf16[8,128,128]{2,1,0:T(8,128)(2,1)S(1)} %collective-permute-done.3.refs_4_), channel_id=1, source_target_pairs={{0,16},{16,0},{1,17},{17,1},{2,18},{18,2},{3,19},{19,3},{4,20},{20... | collective-permute-start | bytes 786440 | tf_op jit(solution)/shard_map/ppermute | solution.py:30
  32.5 5.4 %collective-permute-start.9 = (bf16[2,128,256]{2,1,0:T(8,128)(2,1)S(1)}, bf16[2,128,256]{2,1,0:T(8,128)(2,1)S(1)}, u32[]{:S(2)}, u32[]{:S(2)}) collective-permute-start(bf16[2,128,256]{2,1,0:T(8,128)(2,1)S(1)} %pad_maximum_fusion.refs_8_), channel_id=1, source_target_pairs={{0,8},{4,12},{8,0},{12,4},{1,9},{5,13},{9,1},{13,5},{2,10},{6,14},... | collective-permute-start | bytes 393224 | tf_op jit(solution)/shard_map/ppermute | solution.py:30
  34.0 4.9 %copy-start.12 = (bf16[2,128,256]{2,1,0:T(8,128)(2,1)}, bf16[2,128,256]{2,1,0:T(8,128)(2,1)S(1)}, u32[]{:S(2)}) copy-start(bf16[2,128,256]{2,1,0:T(8,128)(2,1)S(1)} %collective-permute-done.10.refs_11_) | copy-start | bytes 393220
  34.0 4.8 %collective-permute-start.8 = (bf16[2,128,256]{2,1,0:T(8,128)(2,1)S(1)}, bf16[2,128,256]{2,1,0:T(8,128)(2,1)S(1)}, u32[]{:S(2)}, u32[]{:S(2)}) collective-permute-start(bf16[2,128,256]{2,1,0:T(8,128)(2,1)S(1)} %pad_maximum_fusion.refs_8_), channel_id=1, source_target_pairs={{0,4},{4,8},{8,12},{12,0},{1,5},{5,9},{9,13},{13,1},{2,6},{6,10},{... | collective-permute-start | bytes 393224 | tf_op jit(solution)/shard_map/ppermute | solution.py:30
  37.9 1.0 %copy-start.13 = (bf16[2,128,256]{2,1,0:T(8,128)(2,1)}, bf16[2,128,256]{2,1,0:T(8,128)(2,1)S(1)}, u32[]{:S(2)}) copy-start(bf16[2,128,256]{2,1,0:T(8,128)(2,1)S(1)} %collective-permute-done.9.refs_10_) | copy-start | bytes 393220
  38.9 0.7 %copy-start.14 = (bf16[2,128,256]{2,1,0:T(8,128)(2,1)}, bf16[2,128,256]{2,1,0:T(8,128)(2,1)S(1)}, u32[]{:S(2)}) copy-start(bf16[2,128,256]{2,1,0:T(8,128)(2,1)S(1)} %collective-permute-done.8.refs_9_) | copy-start | bytes 393220
  38.9 0.8 %copy-start.9 = (bf16[8,128,128]{2,1,0:T(8,128)(2,1)}, bf16[8,128,128]{2,1,0:T(8,128)(2,1)S(1)}, u32[]{:S(2)}) copy-start(bf16[8,128,128]{2,1,0:T(8,128)(2,1)S(1)} %collective-permute-done.2.refs_3_) | copy-start | bytes 786436
  38.9 0.8 %copy-start.10 = (bf16[8,128,128]{2,1,0:T(8,128)(2,1)}, bf16[8,128,128]{2,1,0:T(8,128)(2,1)S(1)}, u32[]{:S(2)}) copy-start(bf16[8,128,128]{2,1,0:T(8,128)(2,1)S(1)} %collective-permute-done.6.refs_7_) | copy-start | bytes 786436
  39.7 0.7 %copy-start.11 = (bf16[8,128,128]{2,1,0:T(8,128)(2,1)}, bf16[8,128,128]{2,1,0:T(8,128)(2,1)S(1)}, u32[]{:S(2)}) copy-start(bf16[8,128,128]{2,1,0:T(8,128)(2,1)S(1)} %collective-permute-done.4.refs_5_) | copy-start | bytes 786436

commit v12 on v11

--- a/solution.py
+++ b/solution.py
@@ -45,15 +45,19 @@
     left_refs = refs[:pieces]
     rf_refs = refs[pieces:pieces + rf_groups]
     out_ref = refs[pieces + rf_groups]
-    lhs_scr, rf_scr = refs[pieces + rf_groups + 1:]
+    lhs_scr, rf_scr, left_buf, sems = refs[pieces + rf_groups + 1:]
     per_group = pieces // rf_groups
+    copies = [pltpu.make_async_copy(left_refs[p], left_buf.at[p], sems.at[p]) for p in range(pieces)]
+    for c in copies:
+        c.start()
     for q in range(pieces):
         at = pl.multiple_of(rf_pos_ref[q] * BLK, BLK)
         rf_scr[pl.ds(at, BLK), :] = rf_refs[q // per_group][q % per_group]
     for p in range(pieces):
+        copies[p].wait()
         for i in range(row_blocks):
             s = slot_ref[p, i]
-            blk = left_refs[p][jnp.maximum(s, 0)]
+            blk = left_buf[p, jnp.maximum(s, 0)]
             blk = jnp.where(s >= 0, blk, jnp.zeros_like(blk))
             lhs_scr[i * BLK:(i + 1) * BLK, p * BLK:(p + 1) * BLK] = blk
     tile = 4 * BLK
@@ -85,11 +89,13 @@
             product_kernel, pieces=pieces, rf_groups=rf_groups, row_blocks=row_blocks, cols=cols
         ),
         out_shape=jax.ShapeDtypeStruct((row_blocks * BLK, cols), jnp.bfloat16),
-        in_specs=[smem, smem, smem] + [vmem] * (pieces + rf_groups),
+        in_specs=[smem, smem, smem] + [pl.BlockSpec(memory_space=pl.ANY)] * pieces + [vmem] * rf_groups,
         out_specs=vmem,
         scratch_shapes=[
             pltpu.VMEM((row_blocks * BLK, pieces * BLK), jnp.bfloat16),
             pltpu.VMEM((pieces * BLK, cols), jnp.bfloat16),
+            pltpu.VMEM((pieces,) + left_pieces[0].shape, left_pieces[0].dtype),
+            pltpu.SemaphoreType.DMA((pieces,)),
         ],
         cost_estimate=pl.CostEstimate(flops=flops, bytes_accessed=bytes_accessed, transcendentals=0),
     )(slot_tbl, rf_pos, keep_patch, *left_pieces, *rf_pieces)

time: 44.7 us -> 46.1 us (1.031)
  Pallas kernels: 4.11 us -> 5.52 us
    pallas_call x1, Pallas kernels: 4.11 us -> 5.52 us  [product_call(): pl.pallas_call(functools.partial(product_kernel, pieces=pieces, rf_groups...]
where the time goes in v12:
time: 46.1 us; the launch traced here: 45.9 us
  waiting for transfers between devices  21.5 us (47%)
  starting transfers between devices  11.3 us (25%)
  Pallas kernels  5.52 us (12%)
  local copies, waits for them, and re-layouts  5.4 us (12%)
  other arithmetic  1.98 us (4%)
    ppermute x3, waiting for transfers between devices, col_shift(): lax.ppermute(x, 'col', [(s, (s + k) % col_count) for s in range(col_count)])  15.8 us
    pallas_call x1, Pallas kernels, product_call(): pl.pallas_call(functools.partial(product_kernel, pieces=pieces, rf_groups...  5.52 us
    ppermute x7, starting transfers between devices, ring_gather(): pieces.append(lax.ppermute(x, axis, perm))  4.97 us
    ppermute x7, waiting for transfers between devices, ring_gather(): pieces.append(lax.ppermute(x, axis, perm))  4.85 us
    ppermute x3, starting transfers between devices, col_shift(): lax.ppermute(x, 'col', [(s, (s + k) % col_count) for s in range(col_count)])  3.32 us
    ppermute x1, starting transfers between devices, per_device(): lax.ppermute(packed[0], 'layer', [(s, (s + m) % layer_count) for s in ran...  3 us
    unnamed x31, local copies, waits for them, and re-layouts  2.31 us
  transfers between devices with their start and end apart: 11, of which 6 were waited for; matrix products, arithmetic and copies ran while one was open for 9% of the time, Pallas kernels for 0%

profile of v12, /device:TPU:0, one launch (start us, length us, event | category | flops | bytes accessed | tf_op | source)
XLA Modules:
  0.0 45.9 jit_solution(5016436427431003501)
XLA Ops:
  0.0 0.7 %copy-done.4 = s32[64,8]{0,1:T(8,128)S(1)} copy-done((s32[64,8]{0,1:T(8,128)S(1)}, s32[64,8]{0,1:T(8,128)}, u32[]{:S(2)}) %copy-start.4) | copy-done | bytes 2072
  0.8 0.1 copy.13
  0.9 0.1 add_reduce_fusion
  1.1 0.1 select_reduce_fusion
  1.2 0.6 %gather_fusion = bf16[8,128,128]{2,1,0:T(8,128)(2,1)S(1)} fusion(bf16[16,128,128]{2,1,0:T(8,128)(2,1)S(1)} %bitcast.36, s32[1024]{0:T(1024)S(1)} %pad_clamp_fusion.1), kind=kCustom, calls=%fused_computation | custom fusion | bytes 524320 | tf_op jit(solution)/shard_map/jit(_take)/gather | solution.py:132
  1.8 0.1 broadcast_select_fusion.refs_0_
  2.0 3.0 %collective-permute-start.1 = (bf16[8,128,128]{2,1,0:T(8,128)(2,1)S(1)}, bf16[8,128,128]{2,1,0:T(8,128)(2,1)S(1)}, u32[]{:S(2)}, u32[]{:S(2)}) collective-permute-start(bf16[8,128,128]{2,1,0:T(8,128)(2,1)S(1)} %broadcast_select_fusion.refs_0_), channel_id=1, source_target_pairs={{0,16},{16,0},{1,17},{17,1},{2,18},{18,2},{3,19},{19,3},{4,20},{20... | collective-permute-start | bytes 786440 | tf_op jit(solution)/shard_map/ppermute | solution.py:161
  5.0 1.6 %collective-permute-start = (bf16[8,128,128]{2,1,0:T(8,128)(2,1)S(1)}, bf16[8,128,128]{2,1,0:T(8,128)(2,1)S(1)}, u32[]{:S(2)}, u32[]{:S(2)}) collective-permute-start(bf16[8,128,128]{2,1,0:T(8,128)(2,1)S(1)} %broadcast_select_fusion.refs_0_), channel_id=1, source_target_pairs={{0,1},{1,2},{2,3},{3,0},{4,5},{5,6},{6,7},{7,4},{8,9},{9,10},{10,1... | collective-permute-start | bytes 786440 | tf_op jit(solution)/shard_map/ppermute | solution.py:165
  6.5 0.1 subtract_convert_fusion
  6.6 0.6 %collective-permute-start.7 = (bf16[128,256]{1,0:T(8,128)(2,1)S(1)}, bf16[128,256]{1,0:T(8,128)(2,1)S(1)}, u32[]{:S(2)}, u32[]{:S(2)}) collective-permute-start(bf16[128,256]{1,0:T(8,128)(2,1)S(1)} %subtract_convert_fusion), channel_id=1, source_target_pairs={{0,16},{16,0},{1,17},{17,1},{2,18},{18,2},{3,19},{19,3},{4,20},{20... | collective-permute-start | bytes 196616 | tf_op jit(solution)/shard_map/ppermute | solution.py:30
  7.4 0.6 %fusion.1.rf_pos_ref = s32[8]{0:T(128)} fusion(s32[8]{0:T(128)S(1)} %stack.107, s32[]{:T(128)S(6)} %axis_index.36, s32[]{:T(128)S(6)} %axis_index.38), kind=kLoop, calls=%fused_computation.34 | loop fusion | flops 360 | bytes 72 | tf_op jit(solution)/shard_map/add | solution.py:176
  8.1 0.1 stack.98
  8.3 0.8 %dynamic_slice.11 = s32[16,2]{0,1:T(2,128)S(1)} dynamic-slice(s32[64,8]{0,1:T(8,128)} %param.7, s32[]{:T(128)S(6)} %select_n.179, s32[]{:T(128)S(6)} %select_n.204), dynamic_slice_sizes={16,2} | dynamic-slice | bytes 260 | tf_op jit(solution)/shard_map/dynamic_slice | solution.py:136
  9.1 0.7 %copy.18.keep_ref = s32[16,2]{1,0:T(8,128)} copy(s32[16,2]{0,1:T(2,128)S(1)} %dynamic_slice.11) | data formatting | bytes 256 | tf_op jit(solution)/shard_map/optimization_barrier | solution.py:182
  9.9 0.6 %gather_fusion.1 = s32[8,16]{1,0:T(8,128)S(1)} fusion(s32[16,8]{0,1:T(8,128)S(1)} %copy.15, s32[1024]{0:T(1024)S(1)} %pad_clamp_fusion), kind=kCustom, calls=%fused_computation.1 | custom fusion | bytes 1056 | tf_op jit(solution)/shard_map/jit(_take)/gather | solution.py:181
  10.4 0.7 %broadcast_select_fusion.1.slot_ref = s32[8,16]{1,0:T(8,128)} fusion(s32[8,16]{1,0:T(8,128)S(1)} %gather_fusion.1, pred[8]{0:T(512)(128)(4,1)S(1)} %compare_and_fusion), kind=kLoop, calls=%fused_computation.21 | loop fusion | flops 128 | bytes 1032 | tf_op jit(solution)/shard_map/jit(_take)/select_n | solution.py:181
  11.1 0.9 %collective-permute-done.1.refs_1_ = bf16[8,128,128]{2,1,0:T(8,128)(2,1)S(1)} collective-permute-done((bf16[8,128,128]{2,1,0:T(8,128)(2,1)S(1)}, bf16[8,128,128]{2,1,0:T(8,128)(2,1)S(1)}, u32[]{:S(2)}, u32[]{:S(2)}) %collective-permute-start.1) | collective-permute-done | bytes 262176 | tf_op jit(solution)/shard_map/ppermute | solution.py:161
  12.0 2.6 %collective-permute-done.refs_2_ = bf16[8,128,128]{2,1,0:T(8,128)(2,1)S(1)} collective-permute-done((bf16[8,128,128]{2,1,0:T(8,128)(2,1)S(1)}, bf16[8,128,128]{2,1,0:T(8,128)(2,1)S(1)}, u32[]{:S(2)}, u32[]{:S(2)}) %collective-permute-start) | collective-permute-done | bytes 262176 | tf_op jit(solution)/shard_map/ppermute | solution.py:165
  14.6 1.7 %collective-permute-start.5 = (bf16[8,128,128]{2,1,0:T(8,128)(2,1)S(1)}, bf16[8,128,128]{2,1,0:T(8,128)(2,1)S(1)}, u32[]{:S(2)}, u32[]{:S(2)}) collective-permute-start(bf16[8,128,128]{2,1,0:T(8,128)(2,1)S(1)} %broadcast_select_fusion.refs_0_), channel_id=1, source_target_pairs={{0,3},{1,0},{2,1},{3,2},{4,7},{5,4},{6,5},{7,6},{8,11},{9,8},{10,9... | collective-permute-start | bytes 786440 | tf_op jit(solution)/shard_map/ppermute | solution.py:165
  16.5 1.1 %collective-permute-start.2 = (bf16[8,128,128]{2,1,0:T(8,128)(2,1)S(1)}, bf16[8,128,128]{2,1,0:T(8,128)(2,1)S(1)}, u32[]{:S(2)}, u32[]{:S(2)}) collective-permute-start(bf16[8,128,128]{2,1,0:T(8,128)(2,1)S(1)} %collective-permute-done.refs_2_), channel_id=1, source_target_pairs={{0,16},{16,0},{1,17},{17,1},{2,18},{18,2},{3,19},{19,3},{4,20},{20... | collective-permute-start | bytes 786440 | tf_op jit(solution)/shard_map/ppermute | solution.py:30
  17.6 5.5 %collective-permute-done.5.refs_6_ = bf16[8,128,128]{2,1,0:T(8,128)(2,1)S(1)} collective-permute-done((bf16[8,128,128]{2,1,0:T(8,128)(2,1)S(1)}, bf16[8,128,128]{2,1,0:T(8,128)(2,1)S(1)}, u32[]{:S(2)}, u32[]{:S(2)}) %collective-permute-start.5) | collective-permute-done | bytes 262176 | tf_op jit(solution)/shard_map/ppermute | solution.py:165
  23.1 1.0 %collective-permute-start.6 = (bf16[8,128,128]{2,1,0:T(8,128)(2,1)S(1)}, bf16[8,128,128]{2,1,0:T(8,128)(2,1)S(1)}, u32[]{:S(2)}, u32[]{:S(2)}) collective-permute-start(bf16[8,128,128]{2,1,0:T(8,128)(2,1)S(1)} %collective-permute-done.5.refs_6_), channel_id=1, source_target_pairs={{0,16},{16,0},{1,17},{17,1},{2,18},{18,2},{3,19},{19,3},{4,20},{20... | collective-permute-start | bytes 786440 | tf_op jit(solution)/shard_map/ppermute | solution.py:30
  24.1 7.7 %collective-permute-done.3.refs_4_ = bf16[8,128,128]{2,1,0:T(8,128)(2,1)S(1)} collective-permute-done((bf16[8,128,128]{2,1,0:T(8,128)(2,1)S(1)}, bf16[8,128,128]{2,1,0:T(8,128)(2,1)S(1)}, u32[]{:S(2)}, u32[]{:S(2)}) %collective-permute-start.3) | collective-permute-done | bytes 262176 | tf_op jit(solution)/shard_map/ppermute | solution.py:165
  31.8 0.7 %collective-permute-start.4 = (bf16[8,128,128]{2,1,0:T(8,128)(2,1)S(1)}, bf16[8,128,128]{2,1,0:T(8,128)(2,1)S(1)}, u32[]{:S(2)}, u32[]{:S(2)}) collective-permute-start(bf16[8,128,128]{2,1,0:T(8,128)(2,1)S(1)} %collective-permute-done.3.refs_4_), channel_id=1, source_target_pairs={{0,16},{16,0},{1,17},{17,1},{2,18},{18,2},{3,19},{19,3},{4,20},{20... | collective-permute-start | bytes 786440 | tf_op jit(solution)/shard_map/ppermute | solution.py:30
  32.5 1.5 %collective-permute-start.9 = (bf16[2,128,256]{2,1,0:T(8,128)(2,1)S(1)}, bf16[2,128,256]{2,1,0:T(8,128)(2,1)S(1)}, u32[]{:S(2)}, u32[]{:S(2)}) collective-permute-start(bf16[2,128,256]{2,1,0:T(8,128)(2,1)S(1)} %pad_maximum_fusion.refs_8_), channel_id=1, source_target_pairs={{0,8},{4,12},{8,0},{12,4},{1,9},{5,13},{9,1},{13,5},{2,10},{6,14},... | collective-permute-start | bytes 393224 | tf_op jit(solution)/shard_map/ppermute | solution.py:30
  34.0 3.9 %collective-permute-done.9.refs_10_ = bf16[2,128,256]{2,1,0:T(8,128)(2,1)S(1)} collective-permute-done((bf16[2,128,256]{2,1,0:T(8,128)(2,1)S(1)}, bf16[2,128,256]{2,1,0:T(8,128)(2,1)S(1)}, u32[]{:S(2)}, u32[]{:S(2)}) %collective-permute-start.9) | collective-permute-done | bytes 131104 | tf_op jit(solution)/shard_map/ppermute | solution.py:30
  37.9 0.9 %collective-permute-done.8.refs_9_ = bf16[2,128,256]{2,1,0:T(8,128)(2,1)S(1)} collective-permute-done((bf16[2,128,256]{2,1,0:T(8,128)(2,1)S(1)}, bf16[2,128,256]{2,1,0:T(8,128)(2,1)S(1)}, u32[]{:S(2)}, u32[]{:S(2)}) %collective-permute-start.8) | collective-permute-done | bytes 131104 | tf_op jit(solution)/shard_map/ppermute | solution.py:30
  39.0 0.5 %copy-done.14 = bf16[2,128,256]{2,1,0:T(8,128)(2,1)} copy-done((bf16[2,128,256]{2,1,0:T(8,128)(2,1)}, bf16[2,128,256]{2,1,0:T(8,128)(2,1)S(1)}, u32[]{:S(2)}) %copy-start.14) | copy-done | bytes 131096
  39.5 0.1 copy-done.9
  39.6 0.1 copy-done.10
  39.7 0.7 %copy-done.11 = bf16[8,128,128]{2,1,0:T(8,128)(2,1)} copy-done((bf16[8,128,128]{2,1,0:T(8,128)(2,1)}, bf16[8,128,128]{2,1,0:T(8,128)(2,1)S(1)}, u32[]{:S(2)}) %copy-start.11) | copy-done | bytes 262168
  40.4 5.5 %shard_map.46 = bf16[2048,256]{1,0:T(8,128)(2,1)} custom-call(s32[8,16]{1,0:T(8,128)} %broadcast_select_fusion.1.slot_ref, s32[8]{0:T(128)} %fusion.1.rf_pos_ref, s32[16,2]{1,0:T(8,128)} %copy.18.keep_ref, bf16[8,128,128]{2,1,0:T(8,128)(2,1)} %copy-done.1, bf16[8,128,128]{2,1,0:T(8,128)(2,1)} %copy-done.5, bf16[8,128,128]{2,1,0:T(8,128)(2,1)} %copy-done.6, ...), custom_call_target="tpu_custom_call" | custom-call | flops 1073741824 | bytes 3670016 | tf_op jit(solution)/shard_map/pallas_call | solution.py:87
  (53 shorter events, 0.8 us)
Async XLA Ops:
  0.0 1.2 %copy-start = (bf16[2048,128]{1,0:T(8,128)(2,1)S(1)}, bf16[2048,128]{1,0:T(8,128)(2,1)}, u32[]{:S(2)}) copy-start(bf16[2048,128]{1,0:T(8,128)(2,1)} %param.4) | copy-start | bytes 1572868
  0.0 0.7 %copy-start.4 = (s32[64,8]{0,1:T(8,128)S(1)}, s32[64,8]{0,1:T(8,128)}, u32[]{:S(2)}) copy-start(s32[64,8]{0,1:T(8,128)} %param.6) | copy-start | bytes 6148
  1.8 4.7 %copy-start.2 = (bf16[128,256]{1,0:T(8,128)(2,1)S(1)}, bf16[128,256]{1,0:T(8,128)(2,1)}, u32[]{:S(2)}) copy-start(bf16[128,256]{1,0:T(8,128)(2,1)} %param.5) | copy-start | bytes 196612
  1.9 14.4 %copy-start.1 = (bf16[8,128,128]{2,1,0:T(8,128)(2,1)}, bf16[8,128,128]{2,1,0:T(8,128)(2,1)S(1)}, u32[]{:S(2)}) copy-start(bf16[8,128,128]{2,1,0:T(8,128)(2,1)S(1)} %broadcast_select_fusion.refs_0_) | copy-start | bytes 786436
  2.0 10.0 %collective-permute-start.1 = (bf16[8,128,128]{2,1,0:T(8,128)(2,1)S(1)}, bf16[8,128,128]{2,1,0:T(8,128)(2,1)S(1)}, u32[]{:S(2)}, u32[]{:S(2)}) collective-permute-start(bf16[8,128,128]{2,1,0:T(8,128)(2,1)S(1)} %broadcast_select_fusion.refs_0_), channel_id=1, source_target_pairs={{0,16},{16,0},{1,17},{17,1},{2,18},{18,2},{3,19},{19,3},{4,20},{20... | collective-permute-start | bytes 786440 | tf_op jit(solution)/shard_map/ppermute | solution.py:161
  5.0 9.6 %collective-permute-start = (bf16[8,128,128]{2,1,0:T(8,128)(2,1)S(1)}, bf16[8,128,128]{2,1,0:T(8,128)(2,1)S(1)}, u32[]{:S(2)}, u32[]{:S(2)}) collective-permute-start(bf16[8,128,128]{2,1,0:T(8,128)(2,1)S(1)} %broadcast_select_fusion.refs_0_), channel_id=1, source_target_pairs={{0,1},{1,2},{2,3},{3,0},{4,5},{5,6},{6,7},{7,4},{8,9},{9,10},{10,1... | collective-permute-start | bytes 786440 | tf_op jit(solution)/shard_map/ppermute | solution.py:165
  6.6 9.8 %collective-permute-start.7 = (bf16[128,256]{1,0:T(8,128)(2,1)S(1)}, bf16[128,256]{1,0:T(8,128)(2,1)S(1)}, u32[]{:S(2)}, u32[]{:S(2)}) collective-permute-start(bf16[128,256]{1,0:T(8,128)(2,1)S(1)} %subtract_convert_fusion), channel_id=1, source_target_pairs={{0,16},{16,0},{1,17},{17,1},{2,18},{18,2},{3,19},{19,3},{4,20},{20... | collective-permute-start | bytes 196616 | tf_op jit(solution)/shard_map/ppermute | solution.py:30
  12.0 26.9 %copy-start.5 = (bf16[8,128,128]{2,1,0:T(8,128)(2,1)}, bf16[8,128,128]{2,1,0:T(8,128)(2,1)S(1)}, u32[]{:S(2)}) copy-start(bf16[8,128,128]{2,1,0:T(8,128)(2,1)S(1)} %collective-permute-done.1.refs_1_) | copy-start | bytes 786436
  14.6 24.3 %copy-start.6 = (bf16[8,128,128]{2,1,0:T(8,128)(2,1)}, bf16[8,128,128]{2,1,0:T(8,128)(2,1)S(1)}, u32[]{:S(2)}) copy-start(bf16[8,128,128]{2,1,0:T(8,128)(2,1)S(1)} %collective-permute-done.refs_2_) | copy-start | bytes 786436
  14.6 8.5 %collective-permute-start.5 = (bf16[8,128,128]{2,1,0:T(8,128)(2,1)S(1)}, bf16[8,128,128]{2,1,0:T(8,128)(2,1)S(1)}, u32[]{:S(2)}, u32[]{:S(2)}) collective-permute-start(bf16[8,128,128]{2,1,0:T(8,128)(2,1)S(1)} %broadcast_select_fusion.refs_0_), channel_id=1, source_target_pairs={{0,3},{1,0},{2,1},{3,2},{4,7},{5,4},{6,5},{7,6},{8,11},{9,8},{10,9... | collective-permute-start | bytes 786440 | tf_op jit(solution)/shard_map/ppermute | solution.py:165
  16.3 15.5 %collective-permute-start.3 = (bf16[8,128,128]{2,1,0:T(8,128)(2,1)S(1)}, bf16[8,128,128]{2,1,0:T(8,128)(2,1)S(1)}, u32[]{:S(2)}, u32[]{:S(2)}) collective-permute-start(bf16[8,128,128]{2,1,0:T(8,128)(2,1)S(1)} %broadcast_select_fusion.refs_0_), channel_id=1, source_target_pairs={{0,2},{1,3},{2,0},{3,1},{4,6},{5,7},{6,4},{7,5},{8,10},{9,11},{10,... | collective-permute-start | bytes 786440 | tf_op jit(solution)/shard_map/ppermute | solution.py:165
  16.5 22.5 %copy-start.3 = (bf16[2,128,256]{2,1,0:T(8,128)(2,1)}, bf16[2,128,256]{2,1,0:T(8,128)(2,1)S(1)}, u32[]{:S(2)}) copy-start(bf16[2,128,256]{2,1,0:T(8,128)(2,1)S(1)} %pad_maximum_fusion.refs_8_) | copy-start | bytes 393220
  16.5 17.5 %collective-permute-start.10 = (bf16[2,128,256]{2,1,0:T(8,128)(2,1)S(1)}, bf16[2,128,256]{2,1,0:T(8,128)(2,1)S(1)}, u32[]{:S(2)}, u32[]{:S(2)}) collective-permute-start(bf16[2,128,256]{2,1,0:T(8,128)(2,1)S(1)} %pad_maximum_fusion.refs_8_), channel_id=1, source_target_pairs={{0,12},{4,0},{8,4},{12,8},{1,13},{5,1},{9,5},{13,9},{2,14},{6,2},{... | collective-permute-start | bytes 393224 | tf_op jit(solution)/shard_map/ppermute | solution.py:30
  16.5 22.3 %collective-permute-start.2 = (bf16[8,128,128]{2,1,0:T(8,128)(2,1)S(1)}, bf16[8,128,128]{2,1,0:T(8,128)(2,1)S(1)}, u32[]{:S(2)}, u32[]{:S(2)}) collective-permute-start(bf16[8,128,128]{2,1,0:T(8,128)(2,1)S(1)} %collective-permute-done.refs_2_), channel_id=1, source_target_pairs={{0,16},{16,0},{1,17},{17,1},{2,18},{18,2},{3,19},{19,3},{4,20},{20... | collective-permute-start | bytes 786440 | tf_op jit(solution)/shard_map/ppermute | solution.py:30
  23.1 15.8 %copy-start.7 = (bf16[8,128,128]{2,1,0:T(8,128)(2,1)}, bf16[8,128,128]{2,1,0:T(8,128)(2,1)S(1)}, u32[]{:S(2)}) copy-start(bf16[8,128,128]{2,1,0:T(8,128)(2,1)S(1)} %collective-permute-done.5.refs_6_) | copy-start | bytes 786436
  23.1 15.8 %collective-permute-start.6 = (bf16[8,128,128]{2,1,0:T(8,128)(2,1)S(1)}, bf16[8,128,128]{2,1,0:T(8,128)(2,1)S(1)}, u32[]{:S(2)}, u32[]{:S(2)}) collective-permute-start(bf16[8,128,128]{2,1,0:T(8,128)(2,1)S(1)} %collective-permute-done.5.refs_6_), channel_id=1, source_target_pairs={{0,16},{16,0},{1,17},{17,1},{2,18},{18,2},{3,19},{19,3},{4,20},{20... | collective-permute-start | bytes 786440 | tf_op jit(solution)/shard_map/ppermute | solution.py:30
  31.8 7.1 %copy-start.8 = (bf16[8,128,128]{2,1,0:T(8,128)(2,1)}, bf16[8,128,128]{2,1,0:T(8,128)(2,1)S(1)}, u32[]{:S(2)}) copy-start(bf16[8,128,128]{2,1,0:T(8,128)(2,1)S(1)} %collective-permute-done.3.refs_4_) | copy-start | bytes 786436
  31.8 7.0 %collective-permute-start.4 = (bf16[8,128,128]{2,1,0:T(8,128)(2,1)S(1)}, bf16[8,128,128]{2,1,0:T(8,128)(2,1)S(1)}, u32[]{:S(2)}, u32[]{:S(2)}) collective-permute-start(bf16[8,128,128]{2,1,0:T(8,128)(2,1)S(1)} %collective-permute-done.3.refs_4_), channel_id=1, source_target_pairs={{0,16},{16,0},{1,17},{17,1},{2,18},{18,2},{3,19},{19,3},{4,20},{20... | collective-permute-start | bytes 786440 | tf_op jit(solution)/shard_map/ppermute | solution.py:30
  32.5 5.4 %collective-permute-start.9 = (bf16[2,128,256]{2,1,0:T(8,128)(2,1)S(1)}, bf16[2,128,256]{2,1,0:T(8,128)(2,1)S(1)}, u32[]{:S(2)}, u32[]{:S(2)}) collective-permute-start(bf16[2,128,256]{2,1,0:T(8,128)(2,1)S(1)} %pad_maximum_fusion.refs_8_), channel_id=1, source_target_pairs={{0,8},{4,12},{8,0},{12,4},{1,9},{5,13},{9,1},{13,5},{2,10},{6,14},... | collective-permute-start | bytes 393224 | tf_op jit(solution)/shard_map/ppermute | solution.py:30
  34.0 4.9 %copy-start.12 = (bf16[2,128,256]{2,1,0:T(8,128)(2,1)}, bf16[2,128,256]{2,1,0:T(8,128)(2,1)S(1)}, u32[]{:S(2)}) copy-start(bf16[2,128,256]{2,1,0:T(8,128)(2,1)S(1)} %collective-permute-done.10.refs_11_) | copy-start | bytes 393220
  34.0 4.8 %collective-permute-start.8 = (bf16[2,128,256]{2,1,0:T(8,128)(2,1)S(1)}, bf16[2,128,256]{2,1,0:T(8,128)(2,1)S(1)}, u32[]{:S(2)}, u32[]{:S(2)}) collective-permute-start(bf16[2,128,256]{2,1,0:T(8,128)(2,1)S(1)} %pad_maximum_fusion.refs_8_), channel_id=1, source_target_pairs={{0,4},{4,8},{8,12},{12,0},{1,5},{5,9},{9,13},{13,1},{2,6},{6,10},{... | collective-permute-start | bytes 393224 | tf_op jit(solution)/shard_map/ppermute | solution.py:30
  37.9 1.0 %copy-start.13 = (bf16[2,128,256]{2,1,0:T(8,128)(2,1)}, bf16[2,128,256]{2,1,0:T(8,128)(2,1)S(1)}, u32[]{:S(2)}) copy-start(bf16[2,128,256]{2,1,0:T(8,128)(2,1)S(1)} %collective-permute-done.9.refs_10_) | copy-start | bytes 393220
  38.9 0.7 %copy-start.14 = (bf16[2,128,256]{2,1,0:T(8,128)(2,1)}, bf16[2,128,256]{2,1,0:T(8,128)(2,1)S(1)}, u32[]{:S(2)}) copy-start(bf16[2,128,256]{2,1,0:T(8,128)(2,1)S(1)} %collective-permute-done.8.refs_9_) | copy-start | bytes 393220
  38.9 0.8 %copy-start.9 = (bf16[8,128,128]{2,1,0:T(8,128)(2,1)}, bf16[8,128,128]{2,1,0:T(8,128)(2,1)S(1)}, u32[]{:S(2)}) copy-start(bf16[8,128,128]{2,1,0:T(8,128)(2,1)S(1)} %collective-permute-done.2.refs_3_) | copy-start | bytes 786436
  38.9 0.8 %copy-start.10 = (bf16[8,128,128]{2,1,0:T(8,128)(2,1)}, bf16[8,128,128]{2,1,0:T(8,128)(2,1)S(1)}, u32[]{:S(2)}) copy-start(bf16[8,128,128]{2,1,0:T(8,128)(2,1)S(1)} %collective-permute-done.6.refs_7_) | copy-start | bytes 786436
  39.7 0.7 %copy-start.11 = (bf16[8,128,128]{2,1,0:T(8,128)(2,1)}, bf16[8,128,128]{2,1,0:T(8,128)(2,1)S(1)}, u32[]{:S(2)}) copy-start(bf16[8,128,128]{2,1,0:T(8,128)(2,1)S(1)} %collective-permute-done.4.refs_5_) | copy-start | bytes 786436

commit v13 on v11

--- a/solution.py
+++ b/solution.py
@@ -53,7 +53,7 @@
     for p in range(pieces):
         for i in range(row_blocks):
             s = slot_ref[p, i]
-            blk = left_refs[p][jnp.maximum(s, 0)]
+            blk = left_refs[p][jnp.clip(s, 0, left_refs[p].shape[0] - 1)]
             blk = jnp.where(s >= 0, blk, jnp.zeros_like(blk))
             lhs_scr[i * BLK:(i + 1) * BLK, p * BLK:(p + 1) * BLK] = blk
     tile = 4 * BLK

time: 44.7 us -> 44.8 us (level)
  no operation moved by 1% of the time
where the time goes in v13:
time: 44.8 us; the launch traced here: 44.6 us
  waiting for transfers between devices  21.5 us (48%)
  starting transfers between devices  11.3 us (25%)
  local copies, waits for them, and re-layouts  5.4 us (12%)
  Pallas kernels  4.14 us (9%)
  other arithmetic  1.98 us (4%)
    ppermute x3, waiting for transfers between devices, col_shift(): lax.ppermute(x, 'col', [(s, (s + k) % col_count) for s in range(col_count)])  15.8 us
    ppermute x7, starting transfers between devices, ring_gather(): pieces.append(lax.ppermute(x, axis, perm))  4.97 us
    ppermute x7, waiting for transfers between devices, ring_gather(): pieces.append(lax.ppermute(x, axis, perm))  4.85 us
    pallas_call x1, Pallas kernels, product_call(): pl.pallas_call(functools.partial(product_kernel, pieces=pieces, rf_groups...  4.14 us
    ppermute x3, starting transfers between devices, col_shift(): lax.ppermute(x, 'col', [(s, (s + k) % col_count) for s in range(col_count)])  3.32 us
    ppermute x1, starting transfers between devices, per_device(): lax.ppermute(packed[0], 'layer', [(s, (s + m) % layer_count) for s in ran...  3 us
    unnamed x31, local copies, waits for them, and re-layouts  2.31 us
  transfers between devices with their start and end apart: 11, of which 6 were waited for; matrix products, arithmetic and copies ran while one was open for 9% of the time, Pallas kernels for 0%

profile of v13, /device:TPU:0, one launch (start us, length us, event | category | flops | bytes accessed | tf_op | source)
XLA Modules:
  0.0 44.6 jit_solution(6479996234912196198)
XLA Ops:
  0.0 0.7 %copy-done.4 = s32[64,8]{0,1:T(8,128)S(1)} copy-done((s32[64,8]{0,1:T(8,128)S(1)}, s32[64,8]{0,1:T(8,128)}, u32[]{:S(2)}) %copy-start.4) | copy-done | bytes 2072
  0.9 0.1 add_reduce_fusion
  1.1 0.1 select_reduce_fusion
  1.2 0.6 %gather_fusion = bf16[8,128,128]{2,1,0:T(8,128)(2,1)S(1)} fusion(bf16[16,128,128]{2,1,0:T(8,128)(2,1)S(1)} %bitcast.36, s32[1024]{0:T(1024)S(1)} %pad_clamp_fusion.1), kind=kCustom, calls=%fused_computation | custom fusion | bytes 524320 | tf_op jit(solution)/shard_map/jit(_take)/gather | solution.py:126
  1.8 0.1 broadcast_select_fusion.refs_0_
  2.0 3.0 %collective-permute-start.1 = (bf16[8,128,128]{2,1,0:T(8,128)(2,1)S(1)}, bf16[8,128,128]{2,1,0:T(8,128)(2,1)S(1)}, u32[]{:S(2)}, u32[]{:S(2)}) collective-permute-start(bf16[8,128,128]{2,1,0:T(8,128)(2,1)S(1)} %broadcast_select_fusion.refs_0_), channel_id=1, source_target_pairs={{0,16},{16,0},{1,17},{17,1},{2,18},{18,2},{3,19},{19,3},{4,20},{20... | collective-permute-start | bytes 786440 | tf_op jit(solution)/shard_map/ppermute | solution.py:155
  5.0 1.6 %collective-permute-start = (bf16[8,128,128]{2,1,0:T(8,128)(2,1)S(1)}, bf16[8,128,128]{2,1,0:T(8,128)(2,1)S(1)}, u32[]{:S(2)}, u32[]{:S(2)}) collective-permute-start(bf16[8,128,128]{2,1,0:T(8,128)(2,1)S(1)} %broadcast_select_fusion.refs_0_), channel_id=1, source_target_pairs={{0,1},{1,2},{2,3},{3,0},{4,5},{5,6},{6,7},{7,4},{8,9},{9,10},{10,1... | collective-permute-start | bytes 786440 | tf_op jit(solution)/shard_map/ppermute | solution.py:159
  6.5 0.1 subtract_convert_fusion
  6.6 0.6 %collective-permute-start.7 = (bf16[128,256]{1,0:T(8,128)(2,1)S(1)}, bf16[128,256]{1,0:T(8,128)(2,1)S(1)}, u32[]{:S(2)}, u32[]{:S(2)}) collective-permute-start(bf16[128,256]{1,0:T(8,128)(2,1)S(1)} %subtract_convert_fusion), channel_id=1, source_target_pairs={{0,16},{16,0},{1,17},{17,1},{2,18},{18,2},{3,19},{19,3},{4,20},{20... | collective-permute-start | bytes 196616 | tf_op jit(solution)/shard_map/ppermute | solution.py:30
  7.3 0.1 stack.107
  7.4 0.6 %fusion.1.rf_pos_ref = s32[8]{0:T(128)} fusion(s32[8]{0:T(128)S(1)} %stack.107, s32[]{:T(128)S(6)} %axis_index.36, s32[]{:T(128)S(6)} %axis_index.38), kind=kLoop, calls=%fused_computation.34 | loop fusion | flops 360 | bytes 72 | tf_op jit(solution)/shard_map/add | solution.py:170
  8.1 0.1 stack.98
  8.3 0.8 %dynamic_slice.11 = s32[16,2]{0,1:T(2,128)S(1)} dynamic-slice(s32[64,8]{0,1:T(8,128)} %param.7, s32[]{:T(128)S(6)} %select_n.179, s32[]{:T(128)S(6)} %select_n.204), dynamic_slice_sizes={16,2} | dynamic-slice | bytes 260 | tf_op jit(solution)/shard_map/dynamic_slice | solution.py:130
  9.1 0.7 %copy.18.keep_ref = s32[16,2]{1,0:T(8,128)} copy(s32[16,2]{0,1:T(2,128)S(1)} %dynamic_slice.11) | data formatting | bytes 256 | tf_op jit(solution)/shard_map/optimization_barrier | solution.py:176
  9.9 0.6 %gather_fusion.1 = s32[8,16]{1,0:T(8,128)S(1)} fusion(s32[16,8]{0,1:T(8,128)S(1)} %copy.15, s32[1024]{0:T(1024)S(1)} %pad_clamp_fusion), kind=kCustom, calls=%fused_computation.1 | custom fusion | bytes 1056 | tf_op jit(solution)/shard_map/jit(_take)/gather | solution.py:175
  10.4 0.7 %broadcast_select_fusion.1.slot_ref = s32[8,16]{1,0:T(8,128)} fusion(s32[8,16]{1,0:T(8,128)S(1)} %gather_fusion.1, pred[8]{0:T(512)(128)(4,1)S(1)} %compare_and_fusion), kind=kLoop, calls=%fused_computation.21 | loop fusion | flops 128 | bytes 1032 | tf_op jit(solution)/shard_map/jit(_take)/select_n | solution.py:175
  11.1 0.9 %collective-permute-done.1.refs_1_ = bf16[8,128,128]{2,1,0:T(8,128)(2,1)S(1)} collective-permute-done((bf16[8,128,128]{2,1,0:T(8,128)(2,1)S(1)}, bf16[8,128,128]{2,1,0:T(8,128)(2,1)S(1)}, u32[]{:S(2)}, u32[]{:S(2)}) %collective-permute-start.1) | collective-permute-done | bytes 262176 | tf_op jit(solution)/shard_map/ppermute | solution.py:155
  12.0 2.6 %collective-permute-done.refs_2_ = bf16[8,128,128]{2,1,0:T(8,128)(2,1)S(1)} collective-permute-done((bf16[8,128,128]{2,1,0:T(8,128)(2,1)S(1)}, bf16[8,128,128]{2,1,0:T(8,128)(2,1)S(1)}, u32[]{:S(2)}, u32[]{:S(2)}) %collective-permute-start) | collective-permute-done | bytes 262176 | tf_op jit(solution)/shard_map/ppermute | solution.py:159
  14.6 1.7 %collective-permute-start.5 = (bf16[8,128,128]{2,1,0:T(8,128)(2,1)S(1)}, bf16[8,128,128]{2,1,0:T(8,128)(2,1)S(1)}, u32[]{:S(2)}, u32[]{:S(2)}) collective-permute-start(bf16[8,128,128]{2,1,0:T(8,128)(2,1)S(1)} %broadcast_select_fusion.refs_0_), channel_id=1, source_target_pairs={{0,3},{1,0},{2,1},{3,2},{4,7},{5,4},{6,5},{7,6},{8,11},{9,8},{10,9... | collective-permute-start | bytes 786440 | tf_op jit(solution)/shard_map/ppermute | solution.py:159
  16.5 1.1 %collective-permute-start.2 = (bf16[8,128,128]{2,1,0:T(8,128)(2,1)S(1)}, bf16[8,128,128]{2,1,0:T(8,128)(2,1)S(1)}, u32[]{:S(2)}, u32[]{:S(2)}) collective-permute-start(bf16[8,128,128]{2,1,0:T(8,128)(2,1)S(1)} %collective-permute-done.refs_2_), channel_id=1, source_target_pairs={{0,16},{16,0},{1,17},{17,1},{2,18},{18,2},{3,19},{19,3},{4,20},{20... | collective-permute-start | bytes 786440 | tf_op jit(solution)/shard_map/ppermute | solution.py:30
  17.6 5.5 %collective-permute-done.5.refs_6_ = bf16[8,128,128]{2,1,0:T(8,128)(2,1)S(1)} collective-permute-done((bf16[8,128,128]{2,1,0:T(8,128)(2,1)S(1)}, bf16[8,128,128]{2,1,0:T(8,128)(2,1)S(1)}, u32[]{:S(2)}, u32[]{:S(2)}) %collective-permute-start.5) | collective-permute-done | bytes 262176 | tf_op jit(solution)/shard_map/ppermute | solution.py:159
  23.1 1.0 %collective-permute-start.6 = (bf16[8,128,128]{2,1,0:T(8,128)(2,1)S(1)}, bf16[8,128,128]{2,1,0:T(8,128)(2,1)S(1)}, u32[]{:S(2)}, u32[]{:S(2)}) collective-permute-start(bf16[8,128,128]{2,1,0:T(8,128)(2,1)S(1)} %collective-permute-done.5.refs_6_), channel_id=1, source_target_pairs={{0,16},{16,0},{1,17},{17,1},{2,18},{18,2},{3,19},{19,3},{4,20},{20... | collective-permute-start | bytes 786440 | tf_op jit(solution)/shard_map/ppermute | solution.py:30
  24.1 7.7 %collective-permute-done.3.refs_4_ = bf16[8,128,128]{2,1,0:T(8,128)(2,1)S(1)} collective-permute-done((bf16[8,128,128]{2,1,0:T(8,128)(2,1)S(1)}, bf16[8,128,128]{2,1,0:T(8,128)(2,1)S(1)}, u32[]{:S(2)}, u32[]{:S(2)}) %collective-permute-start.3) | collective-permute-done | bytes 262176 | tf_op jit(solution)/shard_map/ppermute | solution.py:159
  31.8 0.7 %collective-permute-start.4 = (bf16[8,128,128]{2,1,0:T(8,128)(2,1)S(1)}, bf16[8,128,128]{2,1,0:T(8,128)(2,1)S(1)}, u32[]{:S(2)}, u32[]{:S(2)}) collective-permute-start(bf16[8,128,128]{2,1,0:T(8,128)(2,1)S(1)} %collective-permute-done.3.refs_4_), channel_id=1, source_target_pairs={{0,16},{16,0},{1,17},{17,1},{2,18},{18,2},{3,19},{19,3},{4,20},{20... | collective-permute-start | bytes 786440 | tf_op jit(solution)/shard_map/ppermute | solution.py:30
  32.5 1.5 %collective-permute-start.9 = (bf16[2,128,256]{2,1,0:T(8,128)(2,1)S(1)}, bf16[2,128,256]{2,1,0:T(8,128)(2,1)S(1)}, u32[]{:S(2)}, u32[]{:S(2)}) collective-permute-start(bf16[2,128,256]{2,1,0:T(8,128)(2,1)S(1)} %pad_maximum_fusion.refs_8_), channel_id=1, source_target_pairs={{0,8},{4,12},{8,0},{12,4},{1,9},{5,13},{9,1},{13,5},{2,10},{6,14},... | collective-permute-start | bytes 393224 | tf_op jit(solution)/shard_map/ppermute | solution.py:30
  34.0 3.9 %collective-permute-done.9.refs_10_ = bf16[2,128,256]{2,1,0:T(8,128)(2,1)S(1)} collective-permute-done((bf16[2,128,256]{2,1,0:T(8,128)(2,1)S(1)}, bf16[2,128,256]{2,1,0:T(8,128)(2,1)S(1)}, u32[]{:S(2)}, u32[]{:S(2)}) %collective-permute-start.9) | collective-permute-done | bytes 131104 | tf_op jit(solution)/shard_map/ppermute | solution.py:30
  37.9 0.9 %collective-permute-done.8.refs_9_ = bf16[2,128,256]{2,1,0:T(8,128)(2,1)S(1)} collective-permute-done((bf16[2,128,256]{2,1,0:T(8,128)(2,1)S(1)}, bf16[2,128,256]{2,1,0:T(8,128)(2,1)S(1)}, u32[]{:S(2)}, u32[]{:S(2)}) %collective-permute-start.8) | collective-permute-done | bytes 131104 | tf_op jit(solution)/shard_map/ppermute | solution.py:30
  39.0 0.5 %copy-done.14 = bf16[2,128,256]{2,1,0:T(8,128)(2,1)} copy-done((bf16[2,128,256]{2,1,0:T(8,128)(2,1)}, bf16[2,128,256]{2,1,0:T(8,128)(2,1)S(1)}, u32[]{:S(2)}) %copy-start.14) | copy-done | bytes 131096
  39.5 0.1 copy-done.9
  39.6 0.1 copy-done.10
  39.7 0.7 %copy-done.11 = bf16[8,128,128]{2,1,0:T(8,128)(2,1)} copy-done((bf16[8,128,128]{2,1,0:T(8,128)(2,1)}, bf16[8,128,128]{2,1,0:T(8,128)(2,1)S(1)}, u32[]{:S(2)}) %copy-start.11) | copy-done | bytes 262168
  40.4 4.1 %shard_map.46 = bf16[2048,256]{1,0:T(8,128)(2,1)} custom-call(s32[8,16]{1,0:T(8,128)} %broadcast_select_fusion.1.slot_ref, s32[8]{0:T(128)} %fusion.1.rf_pos_ref, s32[16,2]{1,0:T(8,128)} %copy.18.keep_ref, bf16[8,128,128]{2,1,0:T(8,128)(2,1)} %copy-done.1, bf16[8,128,128]{2,1,0:T(8,128)(2,1)} %copy-done.5, bf16[8,128,128]{2,1,0:T(8,128)(2,1)} %copy-done.6, ...), custom_call_target="tpu_custom_call" | custom-call | flops 1073741824 | bytes 3670016 | tf_op jit(solution)/shard_map/pallas_call | solution.py:83
  (53 shorter events, 0.8 us)
Async XLA Ops:
  0.0 1.2 %copy-start = (bf16[2048,128]{1,0:T(8,128)(2,1)S(1)}, bf16[2048,128]{1,0:T(8,128)(2,1)}, u32[]{:S(2)}) copy-start(bf16[2048,128]{1,0:T(8,128)(2,1)} %param.4) | copy-start | bytes 1572868
  0.0 0.7 %copy-start.4 = (s32[64,8]{0,1:T(8,128)S(1)}, s32[64,8]{0,1:T(8,128)}, u32[]{:S(2)}) copy-start(s32[64,8]{0,1:T(8,128)} %param.6) | copy-start | bytes 6148
  1.8 4.7 %copy-start.2 = (bf16[128,256]{1,0:T(8,128)(2,1)S(1)}, bf16[128,256]{1,0:T(8,128)(2,1)}, u32[]{:S(2)}) copy-start(bf16[128,256]{1,0:T(8,128)(2,1)} %param.5) | copy-start | bytes 196612
  1.9 14.4 %copy-start.1 = (bf16[8,128,128]{2,1,0:T(8,128)(2,1)}, bf16[8,128,128]{2,1,0:T(8,128)(2,1)S(1)}, u32[]{:S(2)}) copy-start(bf16[8,128,128]{2,1,0:T(8,128)(2,1)S(1)} %broadcast_select_fusion.refs_0_) | copy-start | bytes 786436
  2.0 10.0 %collective-permute-start.1 = (bf16[8,128,128]{2,1,0:T(8,128)(2,1)S(1)}, bf16[8,128,128]{2,1,0:T(8,128)(2,1)S(1)}, u32[]{:S(2)}, u32[]{:S(2)}) collective-permute-start(bf16[8,128,128]{2,1,0:T(8,128)(2,1)S(1)} %broadcast_select_fusion.refs_0_), channel_id=1, source_target_pairs={{0,16},{16,0},{1,17},{17,1},{2,18},{18,2},{3,19},{19,3},{4,20},{20... | collective-permute-start | bytes 786440 | tf_op jit(solution)/shard_map/ppermute | solution.py:155
  5.0 9.6 %collective-permute-start = (bf16[8,128,128]{2,1,0:T(8,128)(2,1)S(1)}, bf16[8,128,128]{2,1,0:T(8,128)(2,1)S(1)}, u32[]{:S(2)}, u32[]{:S(2)}) collective-permute-start(bf16[8,128,128]{2,1,0:T(8,128)(2,1)S(1)} %broadcast_select_fusion.refs_0_), channel_id=1, source_target_pairs={{0,1},{1,2},{2,3},{3,0},{4,5},{5,6},{6,7},{7,4},{8,9},{9,10},{10,1... | collective-permute-start | bytes 786440 | tf_op jit(solution)/shard_map/ppermute | solution.py:159
  6.6 9.8 %collective-permute-start.7 = (bf16[128,256]{1,0:T(8,128)(2,1)S(1)}, bf16[128,256]{1,0:T(8,128)(2,1)S(1)}, u32[]{:S(2)}, u32[]{:S(2)}) collective-permute-start(bf16[128,256]{1,0:T(8,128)(2,1)S(1)} %subtract_convert_fusion), channel_id=1, source_target_pairs={{0,16},{16,0},{1,17},{17,1},{2,18},{18,2},{3,19},{19,3},{4,20},{20... | collective-permute-start | bytes 196616 | tf_op jit(solution)/shard_map/ppermute | solution.py:30
  12.0 26.9 %copy-start.5 = (bf16[8,128,128]{2,1,0:T(8,128)(2,1)}, bf16[8,128,128]{2,1,0:T(8,128)(2,1)S(1)}, u32[]{:S(2)}) copy-start(bf16[8,128,128]{2,1,0:T(8,128)(2,1)S(1)} %collective-permute-done.1.refs_1_) | copy-start | bytes 786436
  14.6 24.3 %copy-start.6 = (bf16[8,128,128]{2,1,0:T(8,128)(2,1)}, bf16[8,128,128]{2,1,0:T(8,128)(2,1)S(1)}, u32[]{:S(2)}) copy-start(bf16[8,128,128]{2,1,0:T(8,128)(2,1)S(1)} %collective-permute-done.refs_2_) | copy-start | bytes 786436
  14.6 8.5 %collective-permute-start.5 = (bf16[8,128,128]{2,1,0:T(8,128)(2,1)S(1)}, bf16[8,128,128]{2,1,0:T(8,128)(2,1)S(1)}, u32[]{:S(2)}, u32[]{:S(2)}) collective-permute-start(bf16[8,128,128]{2,1,0:T(8,128)(2,1)S(1)} %broadcast_select_fusion.refs_0_), channel_id=1, source_target_pairs={{0,3},{1,0},{2,1},{3,2},{4,7},{5,4},{6,5},{7,6},{8,11},{9,8},{10,9... | collective-permute-start | bytes 786440 | tf_op jit(solution)/shard_map/ppermute | solution.py:159
  16.3 15.5 %collective-permute-start.3 = (bf16[8,128,128]{2,1,0:T(8,128)(2,1)S(1)}, bf16[8,128,128]{2,1,0:T(8,128)(2,1)S(1)}, u32[]{:S(2)}, u32[]{:S(2)}) collective-permute-start(bf16[8,128,128]{2,1,0:T(8,128)(2,1)S(1)} %broadcast_select_fusion.refs_0_), channel_id=1, source_target_pairs={{0,2},{1,3},{2,0},{3,1},{4,6},{5,7},{6,4},{7,5},{8,10},{9,11},{10,... | collective-permute-start | bytes 786440 | tf_op jit(solution)/shard_map/ppermute | solution.py:159
  16.5 22.5 %copy-start.3 = (bf16[2,128,256]{2,1,0:T(8,128)(2,1)}, bf16[2,128,256]{2,1,0:T(8,128)(2,1)S(1)}, u32[]{:S(2)}) copy-start(bf16[2,128,256]{2,1,0:T(8,128)(2,1)S(1)} %pad_maximum_fusion.refs_8_) | copy-start | bytes 393220
  16.5 17.5 %collective-permute-start.10 = (bf16[2,128,256]{2,1,0:T(8,128)(2,1)S(1)}, bf16[2,128,256]{2,1,0:T(8,128)(2,1)S(1)}, u32[]{:S(2)}, u32[]{:S(2)}) collective-permute-start(bf16[2,128,256]{2,1,0:T(8,128)(2,1)S(1)} %pad_maximum_fusion.refs_8_), channel_id=1, source_target_pairs={{0,12},{4,0},{8,4},{12,8},{1,13},{5,1},{9,5},{13,9},{2,14},{6,2},{... | collective-permute-start | bytes 393224 | tf_op jit(solution)/shard_map/ppermute | solution.py:30
  16.5 22.3 %collective-permute-start.2 = (bf16[8,128,128]{2,1,0:T(8,128)(2,1)S(1)}, bf16[8,128,128]{2,1,0:T(8,128)(2,1)S(1)}, u32[]{:S(2)}, u32[]{:S(2)}) collective-permute-start(bf16[8,128,128]{2,1,0:T(8,128)(2,1)S(1)} %collective-permute-done.refs_2_), channel_id=1, source_target_pairs={{0,16},{16,0},{1,17},{17,1},{2,18},{18,2},{3,19},{19,3},{4,20},{20... | collective-permute-start | bytes 786440 | tf_op jit(solution)/shard_map/ppermute | solution.py:30
  23.1 15.8 %copy-start.7 = (bf16[8,128,128]{2,1,0:T(8,128)(2,1)}, bf16[8,128,128]{2,1,0:T(8,128)(2,1)S(1)}, u32[]{:S(2)}) copy-start(bf16[8,128,128]{2,1,0:T(8,128)(2,1)S(1)} %collective-permute-done.5.refs_6_) | copy-start | bytes 786436
  23.1 15.8 %collective-permute-start.6 = (bf16[8,128,128]{2,1,0:T(8,128)(2,1)S(1)}, bf16[8,128,128]{2,1,0:T(8,128)(2,1)S(1)}, u32[]{:S(2)}, u32[]{:S(2)}) collective-permute-start(bf16[8,128,128]{2,1,0:T(8,128)(2,1)S(1)} %collective-permute-done.5.refs_6_), channel_id=1, source_target_pairs={{0,16},{16,0},{1,17},{17,1},{2,18},{18,2},{3,19},{19,3},{4,20},{20... | collective-permute-start | bytes 786440 | tf_op jit(solution)/shard_map/ppermute | solution.py:30
  31.8 7.1 %copy-start.8 = (bf16[8,128,128]{2,1,0:T(8,128)(2,1)}, bf16[8,128,128]{2,1,0:T(8,128)(2,1)S(1)}, u32[]{:S(2)}) copy-start(bf16[8,128,128]{2,1,0:T(8,128)(2,1)S(1)} %collective-permute-done.3.refs_4_) | copy-start | bytes 786436
  31.8 7.0 %collective-permute-start.4 = (bf16[8,128,128]{2,1,0:T(8,128)(2,1)S(1)}, bf16[8,128,128]{2,1,0:T(8,128)(2,1)S(1)}, u32[]{:S(2)}, u32[]{:S(2)}) collective-permute-start(bf16[8,128,128]{2,1,0:T(8,128)(2,1)S(1)} %collective-permute-done.3.refs_4_), channel_id=1, source_target_pairs={{0,16},{16,0},{1,17},{17,1},{2,18},{18,2},{3,19},{19,3},{4,20},{20... | collective-permute-start | bytes 786440 | tf_op jit(solution)/shard_map/ppermute | solution.py:30
  32.5 5.4 %collective-permute-start.9 = (bf16[2,128,256]{2,1,0:T(8,128)(2,1)S(1)}, bf16[2,128,256]{2,1,0:T(8,128)(2,1)S(1)}, u32[]{:S(2)}, u32[]{:S(2)}) collective-permute-start(bf16[2,128,256]{2,1,0:T(8,128)(2,1)S(1)} %pad_maximum_fusion.refs_8_), channel_id=1, source_target_pairs={{0,8},{4,12},{8,0},{12,4},{1,9},{5,13},{9,1},{13,5},{2,10},{6,14},... | collective-permute-start | bytes 393224 | tf_op jit(solution)/shard_map/ppermute | solution.py:30
  34.0 4.9 %copy-start.12 = (bf16[2,128,256]{2,1,0:T(8,128)(2,1)}, bf16[2,128,256]{2,1,0:T(8,128)(2,1)S(1)}, u32[]{:S(2)}) copy-start(bf16[2,128,256]{2,1,0:T(8,128)(2,1)S(1)} %collective-permute-done.10.refs_11_) | copy-start | bytes 393220
  34.0 4.8 %collective-permute-start.8 = (bf16[2,128,256]{2,1,0:T(8,128)(2,1)S(1)}, bf16[2,128,256]{2,1,0:T(8,128)(2,1)S(1)}, u32[]{:S(2)}, u32[]{:S(2)}) collective-permute-start(bf16[2,128,256]{2,1,0:T(8,128)(2,1)S(1)} %pad_maximum_fusion.refs_8_), channel_id=1, source_target_pairs={{0,4},{4,8},{8,12},{12,0},{1,5},{5,9},{9,13},{13,1},{2,6},{6,10},{... | collective-permute-start | bytes 393224 | tf_op jit(solution)/shard_map/ppermute | solution.py:30
  37.9 1.0 %copy-start.13 = (bf16[2,128,256]{2,1,0:T(8,128)(2,1)}, bf16[2,128,256]{2,1,0:T(8,128)(2,1)S(1)}, u32[]{:S(2)}) copy-start(bf16[2,128,256]{2,1,0:T(8,128)(2,1)S(1)} %collective-permute-done.9.refs_10_) | copy-start | bytes 393220
  38.9 0.7 %copy-start.14 = (bf16[2,128,256]{2,1,0:T(8,128)(2,1)}, bf16[2,128,256]{2,1,0:T(8,128)(2,1)S(1)}, u32[]{:S(2)}) copy-start(bf16[2,128,256]{2,1,0:T(8,128)(2,1)S(1)} %collective-permute-done.8.refs_9_) | copy-start | bytes 393220
  38.9 0.8 %copy-start.9 = (bf16[8,128,128]{2,1,0:T(8,128)(2,1)}, bf16[8,128,128]{2,1,0:T(8,128)(2,1)S(1)}, u32[]{:S(2)}) copy-start(bf16[8,128,128]{2,1,0:T(8,128)(2,1)S(1)} %collective-permute-done.2.refs_3_) | copy-start | bytes 786436
  38.9 0.8 %copy-start.10 = (bf16[8,128,128]{2,1,0:T(8,128)(2,1)}, bf16[8,128,128]{2,1,0:T(8,128)(2,1)S(1)}, u32[]{:S(2)}) copy-start(bf16[8,128,128]{2,1,0:T(8,128)(2,1)S(1)} %collective-permute-done.6.refs_7_) | copy-start | bytes 786436
  39.7 0.7 %copy-start.11 = (bf16[8,128,128]{2,1,0:T(8,128)(2,1)}, bf16[8,128,128]{2,1,0:T(8,128)(2,1)S(1)}, u32[]{:S(2)}) copy-start(bf16[8,128,128]{2,1,0:T(8,128)(2,1)S(1)} %collective-permute-done.4.refs_5_) | copy-start | bytes 786436

commit v14 on v13

--- a/solution.py
+++ b/solution.py
@@ -151,14 +151,15 @@
     if use_permutes:
         rf_pair, rf_layer_src = ring_gather(right_factor, "layer", layer_idx, layer_count)
         rf_pair = jnp.stack(rf_pair)
+        own_piece, rf_pair = lax.optimization_barrier((packed[0], rf_pair))
         own_over_layer = [
-            lax.ppermute(packed[0], "layer", [(s, (s + m) % layer_count) for s in range(layer_count)])
+            lax.ppermute(own_piece, "layer", [(s, (s + m) % layer_count) for s in range(layer_count)])
             for m in range(1, layer_count)
         ]
         def col_shift(x, k):
             return lax.ppermute(x, "col", [(s, (s + k) % col_count) for s in range(col_count)])
 
-        col_pieces = {1: col_shift(packed[0], 1)}
+        col_pieces = {1: col_shift(own_piece, 1)}
         piece_layer = [(layer_idx - m) % layer_count for k in range(col_count) for m in range(layer_count)]
         piece_src_col = [(col_idx - k) % col_count for k in range(col_count) for m in range(layer_count)]
         piece_j = jnp.stack(
@@ -173,8 +174,11 @@
         p_stored, p_slot = slot_table(panel_pattern)
         slot_tbl = jnp.where(p_stored > 0, p_slot, -1).astype(jnp.int32)
         slot_tbl = jnp.take(slot_tbl, piece_j, axis=1).T
-        later, col_pieces[1], slot_tbl, rf_pos, keep_patch, own_over_layer = lax.optimization_barrier(
-            (packed[0], col_pieces[1], slot_tbl, rf_pos.astype(jnp.int32), keep_patch, own_over_layer)
+        rf_pieces, _ = ring_gather(rf_pair, "row", row_idx, row_count)
+        later, col_pieces[1], slot_tbl, rf_pos, keep_patch, own_over_layer, rf_pieces = (
+            lax.optimization_barrier(
+                (own_piece, col_pieces[1], slot_tbl, rf_pos.astype(jnp.int32), keep_patch, own_over_layer, rf_pieces)
+            )
         )
         for k in range(2, col_count):
             col_pieces[k] = col_shift(later, k)
@@ -183,7 +187,6 @@
         for k in range(1, col_count):
             got, _ = ring_gather(col_pieces[k], "layer", layer_idx, layer_count)
             pieces.extend(got)
-        rf_pieces, _ = ring_gather(rf_pair, "row", row_idx, row_count)
         return product_call(slot_tbl, rf_pos, keep_patch, pieces, rf_pieces)
 
     gathered = lax.all_gather(packed, ("layer", "col"), axis=0, tiled=True)

time: 44.8 us -> 51.4 us (1.15)
  waiting for transfers between devices: 21.5 us -> 25.6 us
  starting transfers between devices: 11.3 us -> 13.3 us
  other arithmetic: 1.98 us -> 2.87 us
  local copies, waits for them, and re-layouts: 5.4 us -> 4.63 us
    ppermute x7, waiting for transfers between devices: 4.85 us -> 11.7 us  [ring_gather(): pieces.append(lax.ppermute(x, axis, perm))]
    ppermute x7, starting transfers between devices: 4.97 us -> 7.39 us  [ring_gather(): pieces.append(lax.ppermute(x, axis, perm))]
    ppermute x3, waiting for transfers between devices: 15.8 us -> 13.9 us  [col_shift(): lax.ppermute(x, 'col', [(s, (s + k) % col_count) for s in range(col_count)])]
    ppermute x1, starting transfers between devices: 3 us -> 1.26 us  [per_device(): lax.ppermute(own_piece, 'layer', [(s, (s + m) % layer_count) for s in ran...]
    ppermute x3, starting transfers between devices: 3.32 us -> 4.67 us  [col_shift(): lax.ppermute(x, 'col', [(s, (s + k) % col_count) for s in range(col_count)])]
    convert_element_type x1, other arithmetic: 0.09 us -> 0.98 us  [per_device(): (unit - 0.5 * square_term.astype(jnp.float32)).astype(jnp.bfloat16)]
    ppermute x1, waiting for transfers between devices: 0.89 us -> 0.01 us  [per_device(): lax.ppermute(own_piece, 'layer', [(s, (s + m) % layer_count) for s in ran...]
    unnamed x31, local copies, waits for them, and re-layouts: 2.31 us -> 1.53 us
  transfers between devices with their start and end apart: 11 -> 11, of which waited for: 6 -> 5; matrix products, arithmetic and copies ran while one was open for 9% -> 10% of each run, Pallas kernels for 0% -> 0%
where the time goes in v14:
time: 51.4 us; the launch traced here: 50.8 us
  waiting for transfers between devices  25.6 us (50%)
  starting transfers between devices  13.3 us (26%)
  local copies, waits for them, and re-layouts  4.63 us (9%)
  Pallas kernels  4.15 us (8%)
  other arithmetic  2.87 us (6%)
    ppermute x3, waiting for transfers between devices, col_shift(): lax.ppermute(x, 'col', [(s, (s + k) % col_count) for s in range(col_count)])  13.9 us
    ppermute x7, waiting for transfers between devices, ring_gather(): pieces.append(lax.ppermute(x, axis, perm))  11.7 us
    ppermute x7, starting transfers between devices, ring_gather(): pieces.append(lax.ppermute(x, axis, perm))  7.39 us
    ppermute x3, starting transfers between devices, col_shift(): lax.ppermute(x, 'col', [(s, (s + k) % col_count) for s in range(col_count)])  4.67 us
    pallas_call x1, Pallas kernels, product_call(): pl.pallas_call(functools.partial(product_kernel, pieces=pieces, rf_groups...  4.15 us
    unnamed x31, local copies, waits for them, and re-layouts  1.53 us
    ppermute x1, starting transfers between devices, per_device(): lax.ppermute(own_piece, 'layer', [(s, (s + m) % layer_count) for s in ran...  1.26 us
  transfers between devices with their start and end apart: 11, of which 5 were waited for; matrix products, arithmetic and copies ran while one was open for 10% of the time, Pallas kernels for 0%

profile of v14, /device:TPU:0, one launch (start us, length us, event | category | flops | bytes accessed | tf_op | source)
XLA Modules:
  0.0 50.8 jit_solution(15666667571926866333)
XLA Ops:
  0.0 1.0 %subtract_convert_fusion = bf16[128,256]{1,0:T(8,128)(2,1)S(1)} fusion(bf16[128,256]{1,0:T(8,128)(2,1)} %param.5, s32[256]{0:T(256)S(1)} %iota_add_fusion, s32[128]{0:T(128)S(1)} %iota_add_fusion.1), kind=kLoop, calls=%fused_computation.4 | loop fusion | flops 196608 | bytes 132608 | tf_op jit(solution)/shard_map/convert_element_type | solution.py:142
  1.0 3.0 %collective-permute-start = (bf16[128,256]{1,0:T(8,128)(2,1)S(1)}, bf16[128,256]{1,0:T(8,128)(2,1)S(1)}, u32[]{:S(2)}, u32[]{:S(2)}) collective-permute-start(bf16[128,256]{1,0:T(8,128)(2,1)S(1)} %subtract_convert_fusion), channel_id=1, source_target_pairs={{0,16},{16,0},{1,17},{17,1},{2,18},{18,2},{3,19},{19,3},{4,20},{20... | collective-permute-start | bytes 196616 | tf_op jit(solution)/shard_map/ppermute | solution.py:30
  4.0 0.7 %copy-done.4 = s32[64,8]{0,1:T(8,128)S(1)} copy-done((s32[64,8]{0,1:T(8,128)S(1)}, s32[64,8]{0,1:T(8,128)}, u32[]{:S(2)}) %copy-start.4) | copy-done | bytes 2072
  4.9 0.1 copy.13
  5.0 0.1 add_reduce_fusion
  5.1 0.1 select_reduce_fusion
  5.3 0.1 fusion.8
  5.4 0.1 stack.92
  5.5 0.1 stack.101
  5.8 0.6 %gather_fusion = bf16[8,128,128]{2,1,0:T(8,128)(2,1)S(1)} fusion(bf16[16,128,128]{2,1,0:T(8,128)(2,1)S(1)} %bitcast.36, s32[1024]{0:T(1024)S(1)} %pad_clamp_fusion.1), kind=kCustom, calls=%fused_computation | custom fusion | bytes 524320 | tf_op jit(solution)/shard_map/jit(_take)/gather | solution.py:126
  6.4 0.1 broadcast_select_fusion.refs_0_
  6.5 0.6 %gather_fusion.1 = s32[8,16]{1,0:T(8,128)S(1)} fusion(s32[16,8]{0,1:T(8,128)S(1)} %copy.15, s32[1024]{0:T(1024)S(1)} %pad_clamp_fusion), kind=kCustom, calls=%fused_computation.1 | custom fusion | bytes 1056 | tf_op jit(solution)/shard_map/jit(_take)/gather | solution.py:176
  7.1 1.3 %collective-permute-start.2 = (bf16[8,128,128]{2,1,0:T(8,128)(2,1)S(1)}, bf16[8,128,128]{2,1,0:T(8,128)(2,1)S(1)}, u32[]{:S(2)}, u32[]{:S(2)}) collective-permute-start(bf16[8,128,128]{2,1,0:T(8,128)(2,1)S(1)} %broadcast_select_fusion.refs_0_), channel_id=1, source_target_pairs={{0,16},{16,0},{1,17},{17,1},{2,18},{18,2},{3,19},{19,3},{4,20},{20... | collective-permute-start | bytes 786440 | tf_op jit(solution)/shard_map/ppermute | solution.py:156
  8.4 1.6 %collective-permute-start.1 = (bf16[8,128,128]{2,1,0:T(8,128)(2,1)S(1)}, bf16[8,128,128]{2,1,0:T(8,128)(2,1)S(1)}, u32[]{:S(2)}, u32[]{:S(2)}) collective-permute-start(bf16[8,128,128]{2,1,0:T(8,128)(2,1)S(1)} %broadcast_select_fusion.refs_0_), channel_id=1, source_target_pairs={{0,1},{1,2},{2,3},{3,0},{4,5},{5,6},{6,7},{7,4},{8,9},{9,10},{10,1... | collective-permute-start | bytes 786440 | tf_op jit(solution)/shard_map/ppermute | solution.py:160
  9.9 0.7 %broadcast_select_fusion.1.slot_ref = s32[8,16]{1,0:T(8,128)} fusion(s32[8,16]{1,0:T(8,128)S(1)} %gather_fusion.1, pred[8]{0:T(512)(128)(4,1)S(1)} %compare_and_fusion), kind=kLoop, calls=%fused_computation.21 | loop fusion | flops 128 | bytes 1032 | tf_op jit(solution)/shard_map/jit(_take)/select_n | solution.py:176
  10.6 0.8 %dynamic_slice.11 = s32[16,2]{0,1:T(2,128)S(1)} dynamic-slice(s32[64,8]{0,1:T(8,128)} %param.7, s32[]{:T(128)S(6)} %select_n.179, s32[]{:T(128)S(6)} %select_n.205), dynamic_slice_sizes={16,2} | dynamic-slice | bytes 260 | tf_op jit(solution)/shard_map/dynamic_slice | solution.py:130
  11.4 0.7 %copy.18.keep_ref = s32[16,2]{1,0:T(8,128)} copy(s32[16,2]{0,1:T(2,128)S(1)} %dynamic_slice.11) | data formatting | bytes 256 | tf_op jit(solution)/shard_map/optimization_barrier | solution.py:179
  12.1 1.6 %collective-permute-start.4 = (bf16[2,128,256]{2,1,0:T(8,128)(2,1)S(1)}, bf16[2,128,256]{2,1,0:T(8,128)(2,1)S(1)}, u32[]{:S(2)}, u32[]{:S(2)}) collective-permute-start(bf16[2,128,256]{2,1,0:T(8,128)(2,1)S(1)} %pad_maximum_fusion.refs_8_), channel_id=1, source_target_pairs={{0,8},{4,12},{8,0},{12,4},{1,9},{5,13},{9,1},{13,5},{2,10},{6,14},... | collective-permute-start | bytes 393224 | tf_op jit(solution)/shard_map/ppermute | solution.py:30
  13.7 0.2 collective-permute-start.3
  13.9 0.6 %fusion.1.rf_pos_ref = s32[8]{0:T(128)} fusion(s32[8]{0:T(128)S(1)} %stack.110, s32[]{:T(128)S(6)} %axis_index.36, s32[]{:T(128)S(6)} %axis_index.38), kind=kLoop, calls=%fused_computation.34 | loop fusion | flops 360 | bytes 72 | tf_op jit(solution)/shard_map/add | solution.py:171
  14.5 0.5 collective-permute-done.5.refs_11_
  15.0 5.8 %collective-permute-done.4.refs_10_ = bf16[2,128,256]{2,1,0:T(8,128)(2,1)S(1)} collective-permute-done((bf16[2,128,256]{2,1,0:T(8,128)(2,1)S(1)}, bf16[2,128,256]{2,1,0:T(8,128)(2,1)S(1)}, u32[]{:S(2)}, u32[]{:S(2)}) %collective-permute-start.4) | collective-permute-done | bytes 131104 | tf_op jit(solution)/shard_map/ppermute | solution.py:30
  20.8 2.3 %collective-permute-start.9 = (bf16[8,128,128]{2,1,0:T(8,128)(2,1)S(1)}, bf16[8,128,128]{2,1,0:T(8,128)(2,1)S(1)}, u32[]{:S(2)}, u32[]{:S(2)}) collective-permute-start(bf16[8,128,128]{2,1,0:T(8,128)(2,1)S(1)} %broadcast_select_fusion.refs_0_), channel_id=1, source_target_pairs={{0,3},{1,0},{2,1},{3,2},{4,7},{5,4},{6,5},{7,6},{8,11},{9,8},{10,9... | collective-permute-start | bytes 786440 | tf_op jit(solution)/shard_map/ppermute | solution.py:160
  23.1 0.8 %collective-permute-start.7 = (bf16[8,128,128]{2,1,0:T(8,128)(2,1)S(1)}, bf16[8,128,128]{2,1,0:T(8,128)(2,1)S(1)}, u32[]{:S(2)}, u32[]{:S(2)}) collective-permute-start(bf16[8,128,128]{2,1,0:T(8,128)(2,1)S(1)} %broadcast_select_fusion.refs_0_), channel_id=1, source_target_pairs={{0,2},{1,3},{2,0},{3,1},{4,6},{5,7},{6,4},{7,5},{8,10},{9,11},{10,... | collective-permute-start | bytes 786440 | tf_op jit(solution)/shard_map/ppermute | solution.py:160
  23.9 0.8 %collective-permute-start.6 = (bf16[8,128,128]{2,1,0:T(8,128)(2,1)S(1)}, bf16[8,128,128]{2,1,0:T(8,128)(2,1)S(1)}, u32[]{:S(2)}, u32[]{:S(2)}) collective-permute-start(bf16[8,128,128]{2,1,0:T(8,128)(2,1)S(1)} %collective-permute-done.1.refs_2_), channel_id=1, source_target_pairs={{0,16},{16,0},{1,17},{17,1},{2,18},{18,2},{3,19},{19,3},{4,20},{20... | collective-permute-start | bytes 786440 | tf_op jit(solution)/shard_map/ppermute | solution.py:30
  24.8 5.1 %collective-permute-done.9.refs_6_ = bf16[8,128,128]{2,1,0:T(8,128)(2,1)S(1)} collective-permute-done((bf16[8,128,128]{2,1,0:T(8,128)(2,1)S(1)}, bf16[8,128,128]{2,1,0:T(8,128)(2,1)S(1)}, u32[]{:S(2)}, u32[]{:S(2)}) %collective-permute-start.9) | collective-permute-done | bytes 262176 | tf_op jit(solution)/shard_map/ppermute | solution.py:160
  29.9 0.8 %collective-permute-start.10 = (bf16[8,128,128]{2,1,0:T(8,128)(2,1)S(1)}, bf16[8,128,128]{2,1,0:T(8,128)(2,1)S(1)}, u32[]{:S(2)}, u32[]{:S(2)}) collective-permute-start(bf16[8,128,128]{2,1,0:T(8,128)(2,1)S(1)} %collective-permute-done.9.refs_6_), channel_id=1, source_target_pairs={{0,16},{16,0},{1,17},{17,1},{2,18},{18,2},{3,19},{19,3},{4,20},{20... | collective-permute-start | bytes 786440 | tf_op jit(solution)/shard_map/ppermute | solution.py:30
  30.7 8.8 %collective-permute-done.7.refs_4_ = bf16[8,128,128]{2,1,0:T(8,128)(2,1)S(1)} collective-permute-done((bf16[8,128,128]{2,1,0:T(8,128)(2,1)S(1)}, bf16[8,128,128]{2,1,0:T(8,128)(2,1)S(1)}, u32[]{:S(2)}, u32[]{:S(2)}) %collective-permute-start.7) | collective-permute-done | bytes 262176 | tf_op jit(solution)/shard_map/ppermute | solution.py:160
  39.5 0.9 %collective-permute-start.8 = (bf16[8,128,128]{2,1,0:T(8,128)(2,1)S(1)}, bf16[8,128,128]{2,1,0:T(8,128)(2,1)S(1)}, u32[]{:S(2)}, u32[]{:S(2)}) collective-permute-start(bf16[8,128,128]{2,1,0:T(8,128)(2,1)S(1)} %collective-permute-done.7.refs_4_), channel_id=1, source_target_pairs={{0,16},{16,0},{1,17},{17,1},{2,18},{18,2},{3,19},{19,3},{4,20},{20... | collective-permute-start | bytes 786440 | tf_op jit(solution)/shard_map/ppermute | solution.py:30
  40.5 5.4 %collective-permute-done.8.refs_5_ = bf16[8,128,128]{2,1,0:T(8,128)(2,1)S(1)} collective-permute-done((bf16[8,128,128]{2,1,0:T(8,128)(2,1)S(1)}, bf16[8,128,128]{2,1,0:T(8,128)(2,1)S(1)}, u32[]{:S(2)}, u32[]{:S(2)}) %collective-permute-start.8) | collective-permute-done | bytes 262176 | tf_op jit(solution)/shard_map/ppermute | solution.py:30
  46.0 0.7 %copy-done.11 = bf16[8,128,128]{2,1,0:T(8,128)(2,1)} copy-done((bf16[8,128,128]{2,1,0:T(8,128)(2,1)}, bf16[8,128,128]{2,1,0:T(8,128)(2,1)S(1)}, u32[]{:S(2)}) %copy-start.11) | copy-done | bytes 262168
  46.7 4.1 %shard_map.46 = bf16[2048,256]{1,0:T(8,128)(2,1)} custom-call(s32[8,16]{1,0:T(8,128)} %broadcast_select_fusion.1.slot_ref, s32[8]{0:T(128)} %fusion.1.rf_pos_ref, s32[16,2]{1,0:T(8,128)} %copy.18.keep_ref, bf16[8,128,128]{2,1,0:T(8,128)(2,1)} %copy-done.1, bf16[8,128,128]{2,1,0:T(8,128)(2,1)} %copy-done.5, bf16[8,128,128]{2,1,0:T(8,128)(2,1)} %copy-done.6, ...), custom_call_target="tpu_custom_call" | custom-call | flops 1073741824 | bytes 3670016 | tf_op jit(solution)/shard_map/pallas_call | solution.py:83
  (53 shorter events, 0.6 us)
Async XLA Ops:
  0.0 5.8 %copy-start = (bf16[2048,128]{1,0:T(8,128)(2,1)S(1)}, bf16[2048,128]{1,0:T(8,128)(2,1)}, u32[]{:S(2)}) copy-start(bf16[2048,128]{1,0:T(8,128)(2,1)} %param.4) | copy-start | bytes 1572868
  1.0 6.1 %collective-permute-start = (bf16[128,256]{1,0:T(8,128)(2,1)S(1)}, bf16[128,256]{1,0:T(8,128)(2,1)S(1)}, u32[]{:S(2)}, u32[]{:S(2)}) collective-permute-start(bf16[128,256]{1,0:T(8,128)(2,1)S(1)} %subtract_convert_fusion), channel_id=1, source_target_pairs={{0,16},{16,0},{1,17},{17,1},{2,18},{18,2},{3,19},{19,3},{4,20},{20... | collective-permute-start | bytes 196616 | tf_op jit(solution)/shard_map/ppermute | solution.py:30
  4.0 1.3 %copy-start.2 = (bf16[128,256]{1,0:T(8,128)(2,1)S(1)}, bf16[128,256]{1,0:T(8,128)(2,1)}, u32[]{:S(2)}) copy-start(bf16[128,256]{1,0:T(8,128)(2,1)} %param.5) | copy-start | bytes 196612
  4.0 0.7 %copy-start.4 = (s32[64,8]{0,1:T(8,128)S(1)}, s32[64,8]{0,1:T(8,128)}, u32[]{:S(2)}) copy-start(s32[64,8]{0,1:T(8,128)} %param.6) | copy-start | bytes 6148
  6.5 39.4 %copy-start.1 = (bf16[8,128,128]{2,1,0:T(8,128)(2,1)}, bf16[8,128,128]{2,1,0:T(8,128)(2,1)S(1)}, u32[]{:S(2)}) copy-start(bf16[8,128,128]{2,1,0:T(8,128)(2,1)S(1)} %broadcast_select_fusion.refs_0_) | copy-start | bytes 786436
  7.1 38.8 %copy-start.3 = (bf16[2,128,256]{2,1,0:T(8,128)(2,1)}, bf16[2,128,256]{2,1,0:T(8,128)(2,1)S(1)}, u32[]{:S(2)}) copy-start(bf16[2,128,256]{2,1,0:T(8,128)(2,1)S(1)} %pad_maximum_fusion.refs_8_) | copy-start | bytes 393220
  7.1 13.7 %collective-permute-start.2 = (bf16[8,128,128]{2,1,0:T(8,128)(2,1)S(1)}, bf16[8,128,128]{2,1,0:T(8,128)(2,1)S(1)}, u32[]{:S(2)}, u32[]{:S(2)}) collective-permute-start(bf16[8,128,128]{2,1,0:T(8,128)(2,1)S(1)} %broadcast_select_fusion.refs_0_), channel_id=1, source_target_pairs={{0,16},{16,0},{1,17},{17,1},{2,18},{18,2},{3,19},{19,3},{4,20},{20... | collective-permute-start | bytes 786440 | tf_op jit(solution)/shard_map/ppermute | solution.py:156
  8.4 12.5 %collective-permute-start.1 = (bf16[8,128,128]{2,1,0:T(8,128)(2,1)S(1)}, bf16[8,128,128]{2,1,0:T(8,128)(2,1)S(1)}, u32[]{:S(2)}, u32[]{:S(2)}) collective-permute-start(bf16[8,128,128]{2,1,0:T(8,128)(2,1)S(1)} %broadcast_select_fusion.refs_0_), channel_id=1, source_target_pairs={{0,1},{1,2},{2,3},{3,0},{4,5},{5,6},{6,7},{7,4},{8,9},{9,10},{10,1... | collective-permute-start | bytes 786440 | tf_op jit(solution)/shard_map/ppermute | solution.py:160
  12.1 2.8 %collective-permute-start.5 = (bf16[2,128,256]{2,1,0:T(8,128)(2,1)S(1)}, bf16[2,128,256]{2,1,0:T(8,128)(2,1)S(1)}, u32[]{:S(2)}, u32[]{:S(2)}) collective-permute-start(bf16[2,128,256]{2,1,0:T(8,128)(2,1)S(1)} %pad_maximum_fusion.refs_8_), channel_id=1, source_target_pairs={{0,12},{4,0},{8,4},{12,8},{1,13},{5,1},{9,5},{13,9},{2,14},{6,2},{... | collective-permute-start | bytes 393224 | tf_op jit(solution)/shard_map/ppermute | solution.py:30
  12.1 8.6 %collective-permute-start.4 = (bf16[2,128,256]{2,1,0:T(8,128)(2,1)S(1)}, bf16[2,128,256]{2,1,0:T(8,128)(2,1)S(1)}, u32[]{:S(2)}, u32[]{:S(2)}) collective-permute-start(bf16[2,128,256]{2,1,0:T(8,128)(2,1)S(1)} %pad_maximum_fusion.refs_8_), channel_id=1, source_target_pairs={{0,8},{4,12},{8,0},{12,4},{1,9},{5,13},{9,1},{13,5},{2,10},{6,14},... | collective-permute-start | bytes 393224 | tf_op jit(solution)/shard_map/ppermute | solution.py:30
  13.7 7.1 %collective-permute-start.3 = (bf16[2,128,256]{2,1,0:T(8,128)(2,1)S(1)}, bf16[2,128,256]{2,1,0:T(8,128)(2,1)S(1)}, u32[]{:S(2)}, u32[]{:S(2)}) collective-permute-start(bf16[2,128,256]{2,1,0:T(8,128)(2,1)S(1)} %pad_maximum_fusion.refs_8_), channel_id=1, source_target_pairs={{0,4},{4,8},{8,12},{12,0},{1,5},{5,9},{9,13},{13,1},{2,6},{6,10},{... | collective-permute-start | bytes 393224 | tf_op jit(solution)/shard_map/ppermute | solution.py:30
  15.0 30.9 %copy-start.12 = (bf16[2,128,256]{2,1,0:T(8,128)(2,1)}, bf16[2,128,256]{2,1,0:T(8,128)(2,1)S(1)}, u32[]{:S(2)}) copy-start(bf16[2,128,256]{2,1,0:T(8,128)(2,1)S(1)} %collective-permute-done.5.refs_11_) | copy-start | bytes 393220
  20.8 25.1 %copy-start.13 = (bf16[2,128,256]{2,1,0:T(8,128)(2,1)}, bf16[2,128,256]{2,1,0:T(8,128)(2,1)S(1)}, u32[]{:S(2)}) copy-start(bf16[2,128,256]{2,1,0:T(8,128)(2,1)S(1)} %collective-permute-done.4.refs_10_) | copy-start | bytes 393220
  20.8 25.1 %copy-start.14 = (bf16[2,128,256]{2,1,0:T(8,128)(2,1)}, bf16[2,128,256]{2,1,0:T(8,128)(2,1)S(1)}, u32[]{:S(2)}) copy-start(bf16[2,128,256]{2,1,0:T(8,128)(2,1)S(1)} %collective-permute-done.3.refs_9_) | copy-start | bytes 393220
  20.8 25.1 %copy-start.5 = (bf16[8,128,128]{2,1,0:T(8,128)(2,1)}, bf16[8,128,128]{2,1,0:T(8,128)(2,1)S(1)}, u32[]{:S(2)}) copy-start(bf16[8,128,128]{2,1,0:T(8,128)(2,1)S(1)} %collective-permute-done.2.refs_1_) | copy-start | bytes 786436
  20.8 25.1 %copy-start.6 = (bf16[8,128,128]{2,1,0:T(8,128)(2,1)}, bf16[8,128,128]{2,1,0:T(8,128)(2,1)S(1)}, u32[]{:S(2)}) copy-start(bf16[8,128,128]{2,1,0:T(8,128)(2,1)S(1)} %collective-permute-done.1.refs_2_) | copy-start | bytes 786436
  20.8 9.0 %collective-permute-start.9 = (bf16[8,128,128]{2,1,0:T(8,128)(2,1)S(1)}, bf16[8,128,128]{2,1,0:T(8,128)(2,1)S(1)}, u32[]{:S(2)}, u32[]{:S(2)}) collective-permute-start(bf16[8,128,128]{2,1,0:T(8,128)(2,1)S(1)} %broadcast_select_fusion.refs_0_), channel_id=1, source_target_pairs={{0,3},{1,0},{2,1},{3,2},{4,7},{5,4},{6,5},{7,6},{8,11},{9,8},{10,9... | collective-permute-start | bytes 786440 | tf_op jit(solution)/shard_map/ppermute | solution.py:160
  23.1 16.4 %collective-permute-start.7 = (bf16[8,128,128]{2,1,0:T(8,128)(2,1)S(1)}, bf16[8,128,128]{2,1,0:T(8,128)(2,1)S(1)}, u32[]{:S(2)}, u32[]{:S(2)}) collective-permute-start(bf16[8,128,128]{2,1,0:T(8,128)(2,1)S(1)} %broadcast_select_fusion.refs_0_), channel_id=1, source_target_pairs={{0,2},{1,3},{2,0},{3,1},{4,6},{5,7},{6,4},{7,5},{8,10},{9,11},{10,... | collective-permute-start | bytes 786440 | tf_op jit(solution)/shard_map/ppermute | solution.py:160
  23.9 16.5 %collective-permute-start.6 = (bf16[8,128,128]{2,1,0:T(8,128)(2,1)S(1)}, bf16[8,128,128]{2,1,0:T(8,128)(2,1)S(1)}, u32[]{:S(2)}, u32[]{:S(2)}) collective-permute-start(bf16[8,128,128]{2,1,0:T(8,128)(2,1)S(1)} %collective-permute-done.1.refs_2_), channel_id=1, source_target_pairs={{0,16},{16,0},{1,17},{17,1},{2,18},{18,2},{3,19},{19,3},{4,20},{20... | collective-permute-start | bytes 786440 | tf_op jit(solution)/shard_map/ppermute | solution.py:30
  29.9 16.0 %copy-start.7 = (bf16[8,128,128]{2,1,0:T(8,128)(2,1)}, bf16[8,128,128]{2,1,0:T(8,128)(2,1)S(1)}, u32[]{:S(2)}) copy-start(bf16[8,128,128]{2,1,0:T(8,128)(2,1)S(1)} %collective-permute-done.9.refs_6_) | copy-start | bytes 786436
  29.9 10.6 %collective-permute-start.10 = (bf16[8,128,128]{2,1,0:T(8,128)(2,1)S(1)}, bf16[8,128,128]{2,1,0:T(8,128)(2,1)S(1)}, u32[]{:S(2)}, u32[]{:S(2)}) collective-permute-start(bf16[8,128,128]{2,1,0:T(8,128)(2,1)S(1)} %collective-permute-done.9.refs_6_), channel_id=1, source_target_pairs={{0,16},{16,0},{1,17},{17,1},{2,18},{18,2},{3,19},{19,3},{4,20},{20... | collective-permute-start | bytes 786440 | tf_op jit(solution)/shard_map/ppermute | solution.py:30
  39.5 6.4 %copy-start.8 = (bf16[8,128,128]{2,1,0:T(8,128)(2,1)}, bf16[8,128,128]{2,1,0:T(8,128)(2,1)S(1)}, u32[]{:S(2)}) copy-start(bf16[8,128,128]{2,1,0:T(8,128)(2,1)S(1)} %collective-permute-done.7.refs_4_) | copy-start | bytes 786436
  39.5 6.4 %collective-permute-start.8 = (bf16[8,128,128]{2,1,0:T(8,128)(2,1)S(1)}, bf16[8,128,128]{2,1,0:T(8,128)(2,1)S(1)}, u32[]{:S(2)}, u32[]{:S(2)}) collective-permute-start(bf16[8,128,128]{2,1,0:T(8,128)(2,1)S(1)} %collective-permute-done.7.refs_4_), channel_id=1, source_target_pairs={{0,16},{16,0},{1,17},{17,1},{2,18},{18,2},{3,19},{19,3},{4,20},{20... | collective-permute-start | bytes 786440 | tf_op jit(solution)/shard_map/ppermute | solution.py:30
  40.4 5.5 %copy-start.9 = (bf16[8,128,128]{2,1,0:T(8,128)(2,1)}, bf16[8,128,128]{2,1,0:T(8,128)(2,1)S(1)}, u32[]{:S(2)}) copy-start(bf16[8,128,128]{2,1,0:T(8,128)(2,1)S(1)} %collective-permute-done.6.refs_3_) | copy-start | bytes 786436
  40.5 5.5 %copy-start.10 = (bf16[8,128,128]{2,1,0:T(8,128)(2,1)}, bf16[8,128,128]{2,1,0:T(8,128)(2,1)S(1)}, u32[]{:S(2)}) copy-start(bf16[8,128,128]{2,1,0:T(8,128)(2,1)S(1)} %collective-permute-done.10.refs_7_) | copy-start | bytes 786436
  46.0 0.7 %copy-start.11 = (bf16[8,128,128]{2,1,0:T(8,128)(2,1)}, bf16[8,128,128]{2,1,0:T(8,128)(2,1)S(1)}, u32[]{:S(2)}) copy-start(bf16[8,128,128]{2,1,0:T(8,128)(2,1)S(1)} %collective-permute-done.8.refs_5_) | copy-start | bytes 786436

commit v15 on v13

--- a/solution.py
+++ b/solution.py
@@ -41,15 +41,14 @@
     return out, sources
 
 
-def product_kernel(slot_ref, rf_pos_ref, keep_ref, *refs, pieces, rf_groups, row_blocks, cols):
+def product_kernel(slot_ref, rf_pos_ref, keep_ref, *refs, pieces, rf_groups, rf_entries, row_blocks, cols):
     left_refs = refs[:pieces]
     rf_refs = refs[pieces:pieces + rf_groups]
     out_ref = refs[pieces + rf_groups]
     lhs_scr, rf_scr = refs[pieces + rf_groups + 1:]
-    per_group = pieces // rf_groups
-    for q in range(pieces):
+    for q, (ref_id, entry) in enumerate(rf_entries):
         at = pl.multiple_of(rf_pos_ref[q] * BLK, BLK)
-        rf_scr[pl.ds(at, BLK), :] = rf_refs[q // per_group][q % per_group]
+        rf_scr[pl.ds(at, BLK), :] = rf_refs[ref_id][entry]
     for p in range(pieces):
         for i in range(row_blocks):
             s = slot_ref[p, i]
@@ -69,7 +68,7 @@
                 out_ref[i * BLK:(i + 1) * BLK, b * BLK:(b + 1) * BLK] = sub.astype(out_ref.dtype)
 
 
-def product_call(slot_tbl, rf_pos, keep_patch, left_pieces, rf_pieces):
+def product_call(slot_tbl, rf_pos, keep_patch, left_pieces, rf_pieces, rf_entries):
     pieces = len(left_pieces)
     rf_groups = len(rf_pieces)
     row_blocks = slot_tbl.shape[1]
@@ -82,7 +81,12 @@
     )
     return pl.pallas_call(
         functools.partial(
-            product_kernel, pieces=pieces, rf_groups=rf_groups, row_blocks=row_blocks, cols=cols
+            product_kernel,
+            pieces=pieces,
+            rf_groups=rf_groups,
+            rf_entries=tuple(rf_entries),
+            row_blocks=row_blocks,
+            cols=cols,
         ),
         out_shape=jax.ShapeDtypeStruct((row_blocks * BLK, cols), jnp.bfloat16),
         in_specs=[smem, smem, smem] + [vmem] * (pieces + rf_groups),
@@ -164,8 +168,8 @@
         piece_j = jnp.stack(
             [src_l * col_count + src_c for src_l, src_c in zip(piece_layer, piece_src_col)]
         ).astype(jnp.int32)
-        rf_row = [(row_idx - k) % row_count for k in range(row_count) for m in range(layer_count)]
-        rf_layer = [(layer_idx - m) % layer_count for k in range(row_count) for m in range(layer_count)]
+        rf_row = [q // layer_count for q in range(row_count * layer_count)]
+        rf_layer = [(layer_idx - q % layer_count) % layer_count for q in range(row_count * layer_count)]
         rf_q = jnp.stack([src_l * row_count + src_r for src_l, src_r in zip(rf_layer, rf_row)])
         rf_pos = ((col_idx - rf_q % col_count) % col_count) * layer_count + (
             (layer_idx - rf_q // col_count) % layer_count
@@ -183,8 +187,11 @@
         for k in range(1, col_count):
             got, _ = ring_gather(col_pieces[k], "layer", layer_idx, layer_count)
             pieces.extend(got)
-        rf_pieces, _ = ring_gather(rf_pair, "row", row_idx, row_count)
-        return product_call(slot_tbl, rf_pos, keep_patch, pieces, rf_pieces)
+        padded = jnp.concatenate([rf_pair, jnp.zeros_like(rf_pair)], axis=0)
+        rf_gathered = lax.all_gather(padded, "row", axis=0, tiled=True)
+        rf_entries = [(0, (q // layer_count) * 2 * layer_count + q % layer_count)
+                      for q in range(row_count * layer_count)]
+        return product_call(slot_tbl, rf_pos, keep_patch, pieces, [rf_gathered], rf_entries)
 
     gathered = lax.all_gather(packed, ("layer", "col"), axis=0, tiled=True)
     piece_j = jnp.arange(total_inner_blocks, dtype=jnp.int32)

time: 44.8 us -> 61.8 us (1.38)
  between operations: 0.22 us -> 13.6 us
  starting transfers between devices: 11.3 us -> 13.6 us
  waiting for transfers between devices: 21.5 us -> 22.7 us
  local copies, waits for them, and re-layouts: 5.4 us -> 4.67 us
  other arithmetic: 1.98 us -> 2.7 us
    ppermute x7 -> x4, waiting for transfers between devices: 4.85 us -> 9.89 us  [ring_gather(): pieces.append(lax.ppermute(x, axis, perm))]
    ppermute x3, waiting for transfers between devices: 15.8 us -> 12.8 us  [col_shift(): lax.ppermute(x, 'col', [(s, (s + k) % col_count) for s in range(col_count)])]
    ppermute x3, starting transfers between devices: 3.32 us -> 5.48 us  [col_shift(): lax.ppermute(x, 'col', [(s, (s + k) % col_count) for s in range(col_count)])]
    ppermute x1, waiting for transfers between devices: 0.89 us -> 0.01 us  [per_device(): lax.ppermute(packed[0], 'layer', [(s, (s + m) % layer_count) for s in ran...]
    unnamed x31 -> x23, local copies, waits for them, and re-layouts: 2.31 us -> 1.49 us
    concatenate x0 -> x1, other arithmetic: none -> 0.79 us  [per_device(): padded = jnp.concatenate([rf_pair, jnp.zeros_like(rf_pair)], axis=0)]
    ppermute x7 -> x4, starting transfers between devices: 4.97 us -> 5.07 us  [ring_gather(): pieces.append(lax.ppermute(x, axis, perm))]
  transfers between devices with their start and end apart: 11 -> 9, of which waited for: 6 -> 4; matrix products, arithmetic and copies ran while one was open for 9% -> 8% of each run, Pallas kernels for 0% -> 0%
where the time goes in v15:
time: 61.8 us; the launch traced here: 61.6 us
  waiting for transfers between devices  22.7 us (37%)
  starting transfers between devices  13.6 us (22%)
  between operations  13.6 us (22%)
  local copies, waits for them, and re-layouts  4.67 us (8%)
  Pallas kernels  4.35 us (7%)
  other arithmetic  2.7 us (4%)
    ppermute x3, waiting for transfers between devices, col_shift(): lax.ppermute(x, 'col', [(s, (s + k) % col_count) for s in range(col_count)])  12.8 us
    ppermute x4, waiting for transfers between devices, ring_gather(): pieces.append(lax.ppermute(x, axis, perm))  9.89 us
    ppermute x3, starting transfers between devices, col_shift(): lax.ppermute(x, 'col', [(s, (s + k) % col_count) for s in range(col_count)])  5.48 us
    ppermute x4, starting transfers between devices, ring_gather(): pieces.append(lax.ppermute(x, axis, perm))  5.07 us
    pallas_call x1, Pallas kernels, product_call(): pl.pallas_call(functools.partial(product_kernel, pieces=pieces, rf_groups...  4.35 us
    ppermute x1, starting transfers between devices, per_device(): lax.ppermute(packed[0], 'layer', [(s, (s + m) % layer_count) for s in ran...  3 us
    unnamed x23, local copies, waits for them, and re-layouts  1.49 us
  transfers between devices with their start and end apart: 9, of which 4 were waited for; matrix products, arithmetic and copies ran while one was open for 8% of the time, Pallas kernels for 0%

profile of v15, /device:TPU:0, one launch (start us, length us, event | category | flops | bytes accessed | tf_op | source)
XLA Modules:
  0.0 61.6 jit_solution(8268767727617016468)
XLA Ops:
  6.5 0.7 %copy-done.10 = s32[64,8]{0,1:T(8,128)S(1)} copy-done((s32[64,8]{0,1:T(8,128)S(1)}, s32[64,8]{0,1:T(8,128)}, u32[]{:S(2)}) %copy-start.10) | copy-done | bytes 2072
  7.3 0.1 compare_bitcast_fusion
  7.4 0.1 copy.17
  7.5 0.1 add_reduce_fusion
  7.6 0.1 select_reduce_fusion
  7.8 0.6 gather_fusion
  8.4 0.1 broadcast_select_fusion.refs_0_
  8.5 3.0 %collective-permute-start.1 = (bf16[8,128,128]{2,1,0:T(8,128)(2,1)S(1)}, bf16[8,128,128]{2,1,0:T(8,128)(2,1)S(1)}, u32[]{:S(2)}, u32[]{:S(2)}) collective-permute-start(bf16[8,128,128]{2,1,0:T(8,128)(2,1)S(1)} %broadcast_select_fusion.refs_0_), channel_id=1, source_target_pairs={{0,16},{16,0},{1,17},{17,1},{2,18},{18,2},{3,19},{19,3},{4,20},{20... | collective-permute-start | bytes 786440 | tf_op jit(solution)/shard_map/ppermute | solution.py:159
  11.5 1.6 %collective-permute-start = (bf16[8,128,128]{2,1,0:T(8,128)(2,1)S(1)}, bf16[8,128,128]{2,1,0:T(8,128)(2,1)S(1)}, u32[]{:S(2)}, u32[]{:S(2)}) collective-permute-start(bf16[8,128,128]{2,1,0:T(8,128)(2,1)S(1)} %broadcast_select_fusion.refs_0_), channel_id=1, source_target_pairs={{0,1},{1,2},{2,3},{3,0},{4,5},{5,6},{6,7},{7,4},{8,9},{9,10},{10,1... | collective-permute-start | bytes 786440 | tf_op jit(solution)/shard_map/ppermute | solution.py:163
  13.1 0.1 subtract_convert_fusion
  13.2 0.6 collective-permute-start.7
  13.8 0.1 fusion.8
  14.0 0.1 pad.2.clone
  14.1 0.1 stack.104
  14.2 5.0 %collective-permute-done.7 = bf16[128,256]{1,0:T(8,128)(2,1)S(1)} collective-permute-done((bf16[128,256]{1,0:T(8,128)(2,1)S(1)}, bf16[128,256]{1,0:T(8,128)(2,1)S(1)}, u32[]{:S(2)}, u32[]{:S(2)}) %collective-permute-start.7) | collective-permute-done | bytes 65568 | tf_op jit(solution)/shard_map/ppermute | solution.py:30
  19.2 0.8 %maximum_maximum_fusion = bf16[4,128,256]{2,1,0:T(8,128)(2,1)} fusion(bf16[1,128,256]{2,1,0:T(8,128)(2,1)S(1)} %bitcast.37, bf16[1,128,256]{2,1,0:T(8,128)(2,1)S(1)} %fusion.8, bf16[4]{0:T(256)(128)(2,1)S(1)} %pad.2.clone), kind=kLoop, calls=%fused_computation.2 | loop fusion | flops 262144 | bytes 393224 | tf_op jit(solution)/shard_map/concatenate | solution.py:190
  20.0 0.5 fusion.1.rf_pos_ref
  20.6 0.1 stack.86
  20.7 0.1 stack.95
  20.8 0.8 %dynamic_slice.11 = s32[16,2]{0,1:T(2,128)S(1)} dynamic-slice(s32[64,8]{0,1:T(8,128)} %param.7, s32[]{:T(128)S(6)} %select_n.155, s32[]{:T(128)S(6)} %select_n.176), dynamic_slice_sizes={16,2} | dynamic-slice | bytes 260 | tf_op jit(solution)/shard_map/dynamic_slice | solution.py:134
  21.6 0.7 %copy.22.keep_ref = s32[16,2]{1,0:T(8,128)} copy(s32[16,2]{0,1:T(2,128)S(1)} %dynamic_slice.11) | data formatting | bytes 256 | tf_op jit(solution)/shard_map/optimization_barrier | solution.py:180
  22.4 0.6 gather_fusion.1
  22.9 0.7 %broadcast_select_fusion.1.slot_ref = s32[8,16]{1,0:T(8,128)} fusion(s32[8,16]{1,0:T(8,128)S(1)} %gather_fusion.1, pred[8]{0:T(512)(128)(4,1)S(1)} %compare_and_fusion), kind=kLoop, calls=%fused_computation.21 | loop fusion | flops 128 | bytes 1032 | tf_op jit(solution)/shard_map/jit(_take)/select_n | solution.py:179
  23.6 3.9 %collective-permute-start.5 = (bf16[8,128,128]{2,1,0:T(8,128)(2,1)S(1)}, bf16[8,128,128]{2,1,0:T(8,128)(2,1)S(1)}, u32[]{:S(2)}, u32[]{:S(2)}) collective-permute-start(bf16[8,128,128]{2,1,0:T(8,128)(2,1)S(1)} %broadcast_select_fusion.refs_0_), channel_id=1, source_target_pairs={{0,3},{1,0},{2,1},{3,2},{4,7},{5,4},{6,5},{7,6},{8,11},{9,8},{10,9... | collective-permute-start | bytes 786440 | tf_op jit(solution)/shard_map/ppermute | solution.py:163
  27.5 1.5 %collective-permute-start.2 = (bf16[8,128,128]{2,1,0:T(8,128)(2,1)S(1)}, bf16[8,128,128]{2,1,0:T(8,128)(2,1)S(1)}, u32[]{:S(2)}, u32[]{:S(2)}) collective-permute-start(bf16[8,128,128]{2,1,0:T(8,128)(2,1)S(1)} %collective-permute-done.refs_2_), channel_id=1, source_target_pairs={{0,16},{16,0},{1,17},{17,1},{2,18},{18,2},{3,19},{19,3},{4,20},{20... | collective-permute-start | bytes 786440 | tf_op jit(solution)/shard_map/ppermute | solution.py:30
  29.0 5.3 %collective-permute-done.5.refs_6_ = bf16[8,128,128]{2,1,0:T(8,128)(2,1)S(1)} collective-permute-done((bf16[8,128,128]{2,1,0:T(8,128)(2,1)S(1)}, bf16[8,128,128]{2,1,0:T(8,128)(2,1)S(1)}, u32[]{:S(2)}, u32[]{:S(2)}) %collective-permute-start.5) | collective-permute-done | bytes 262176 | tf_op jit(solution)/shard_map/ppermute | solution.py:163
  34.3 1.5 %collective-permute-start.6 = (bf16[8,128,128]{2,1,0:T(8,128)(2,1)S(1)}, bf16[8,128,128]{2,1,0:T(8,128)(2,1)S(1)}, u32[]{:S(2)}, u32[]{:S(2)}) collective-permute-start(bf16[8,128,128]{2,1,0:T(8,128)(2,1)S(1)} %collective-permute-done.5.refs_6_), channel_id=1, source_target_pairs={{0,16},{16,0},{1,17},{17,1},{2,18},{18,2},{3,19},{19,3},{4,20},{20... | collective-permute-start | bytes 786440 | tf_op jit(solution)/shard_map/ppermute | solution.py:30
  35.8 7.6 %collective-permute-done.3.refs_4_ = bf16[8,128,128]{2,1,0:T(8,128)(2,1)S(1)} collective-permute-done((bf16[8,128,128]{2,1,0:T(8,128)(2,1)S(1)}, bf16[8,128,128]{2,1,0:T(8,128)(2,1)S(1)}, u32[]{:S(2)}, u32[]{:S(2)}) %collective-permute-start.3) | collective-permute-done | bytes 262176 | tf_op jit(solution)/shard_map/ppermute | solution.py:163
  43.3 1.5 %collective-permute-start.4 = (bf16[8,128,128]{2,1,0:T(8,128)(2,1)S(1)}, bf16[8,128,128]{2,1,0:T(8,128)(2,1)S(1)}, u32[]{:S(2)}, u32[]{:S(2)}) collective-permute-start(bf16[8,128,128]{2,1,0:T(8,128)(2,1)S(1)} %collective-permute-done.3.refs_4_), channel_id=1, source_target_pairs={{0,16},{16,0},{1,17},{17,1},{2,18},{18,2},{3,19},{19,3},{4,20},{20... | collective-permute-start | bytes 786440 | tf_op jit(solution)/shard_map/ppermute | solution.py:30
  44.8 4.9 %collective-permute-done.4.refs_5_ = bf16[8,128,128]{2,1,0:T(8,128)(2,1)S(1)} collective-permute-done((bf16[8,128,128]{2,1,0:T(8,128)(2,1)S(1)}, bf16[8,128,128]{2,1,0:T(8,128)(2,1)S(1)}, u32[]{:S(2)}, u32[]{:S(2)}) %collective-permute-start.4) | collective-permute-done | bytes 262176 | tf_op jit(solution)/shard_map/ppermute | solution.py:30
  49.7 0.6 %copy-done.8 = bf16[8,128,128]{2,1,0:T(8,128)(2,1)} copy-done((bf16[8,128,128]{2,1,0:T(8,128)(2,1)}, bf16[8,128,128]{2,1,0:T(8,128)(2,1)S(1)}, u32[]{:S(2)}) %copy-start.8) | copy-done | bytes 262168
  50.4 4.4 %shard_map.46 = bf16[2048,256]{1,0:T(8,128)(2,1)} custom-call(s32[8,16]{1,0:T(8,128)} %broadcast_select_fusion.1.slot_ref, s32[8]{0:T(128)} %fusion.1.rf_pos_ref, s32[16,2]{1,0:T(8,128)} %copy.22.keep_ref, bf16[8,128,128]{2,1,0:T(8,128)(2,1)} %copy-done.1, bf16[8,128,128]{2,1,0:T(8,128)(2,1)} %copy-done.2, bf16[8,128,128]{2,1,0:T(8,128)(2,1)} %copy-done.3, ...), custom_call_target="tpu_custom_call" | custom-call | flops 1073741824 | bytes 4194304 | tf_op jit(solution)/shard_map/pallas_call | solution.py:82
  (44 shorter events, 0.4 us)
Async XLA Ops:
  6.5 1.2 %copy-start = (bf16[2048,128]{1,0:T(8,128)(2,1)S(1)}, bf16[2048,128]{1,0:T(8,128)(2,1)}, u32[]{:S(2)}) copy-start(bf16[2048,128]{1,0:T(8,128)(2,1)} %param.4) | copy-start | bytes 1572868
  6.5 43.2 %all-gather.2.cloned.1.call-start = ((), (), s32[]{:S(2)}) async-start(), calls=%async_computation | async-start | bytes 1310720 | tf_op jit(solution)/shard_map/all_gather | solution.py:191
  6.5 0.7 %copy-start.10 = (s32[64,8]{0,1:T(8,128)S(1)}, s32[64,8]{0,1:T(8,128)}, u32[]{:S(2)}) copy-start(s32[64,8]{0,1:T(8,128)} %param.6) | copy-start | bytes 6148
  8.4 4.7 %copy-start.9 = (bf16[128,256]{1,0:T(8,128)(2,1)S(1)}, bf16[128,256]{1,0:T(8,128)(2,1)}, u32[]{:S(2)}) copy-start(bf16[128,256]{1,0:T(8,128)(2,1)} %param.5) | copy-start | bytes 196612
  8.5 19.0 %copy-start.1 = (bf16[8,128,128]{2,1,0:T(8,128)(2,1)}, bf16[8,128,128]{2,1,0:T(8,128)(2,1)S(1)}, u32[]{:S(2)}) copy-start(bf16[8,128,128]{2,1,0:T(8,128)(2,1)S(1)} %broadcast_select_fusion.refs_0_) | copy-start | bytes 786436
  8.5 15.1 %collective-permute-start.1 = (bf16[8,128,128]{2,1,0:T(8,128)(2,1)S(1)}, bf16[8,128,128]{2,1,0:T(8,128)(2,1)S(1)}, u32[]{:S(2)}, u32[]{:S(2)}) collective-permute-start(bf16[8,128,128]{2,1,0:T(8,128)(2,1)S(1)} %broadcast_select_fusion.refs_0_), channel_id=1, source_target_pairs={{0,16},{16,0},{1,17},{17,1},{2,18},{18,2},{3,19},{19,3},{4,20},{20... | collective-permute-start | bytes 786440 | tf_op jit(solution)/shard_map/ppermute | solution.py:159
  11.5 12.1 %collective-permute-start = (bf16[8,128,128]{2,1,0:T(8,128)(2,1)S(1)}, bf16[8,128,128]{2,1,0:T(8,128)(2,1)S(1)}, u32[]{:S(2)}, u32[]{:S(2)}) collective-permute-start(bf16[8,128,128]{2,1,0:T(8,128)(2,1)S(1)} %broadcast_select_fusion.refs_0_), channel_id=1, source_target_pairs={{0,1},{1,2},{2,3},{3,0},{4,5},{5,6},{6,7},{7,4},{8,9},{9,10},{10,1... | collective-permute-start | bytes 786440 | tf_op jit(solution)/shard_map/ppermute | solution.py:163
  13.2 6.0 %collective-permute-start.7 = (bf16[128,256]{1,0:T(8,128)(2,1)S(1)}, bf16[128,256]{1,0:T(8,128)(2,1)S(1)}, u32[]{:S(2)}, u32[]{:S(2)}) collective-permute-start(bf16[128,256]{1,0:T(8,128)(2,1)S(1)} %subtract_convert_fusion), channel_id=1, source_target_pairs={{0,16},{16,0},{1,17},{17,1},{2,18},{18,2},{3,19},{19,3},{4,20},{20... | collective-permute-start | bytes 196616 | tf_op jit(solution)/shard_map/ppermute | solution.py:30
  23.6 26.1 %copy-start.2 = (bf16[8,128,128]{2,1,0:T(8,128)(2,1)}, bf16[8,128,128]{2,1,0:T(8,128)(2,1)S(1)}, u32[]{:S(2)}) copy-start(bf16[8,128,128]{2,1,0:T(8,128)(2,1)S(1)} %collective-permute-done.1.refs_1_) | copy-start | bytes 786436
  23.6 26.1 %copy-start.3 = (bf16[8,128,128]{2,1,0:T(8,128)(2,1)}, bf16[8,128,128]{2,1,0:T(8,128)(2,1)S(1)}, u32[]{:S(2)}) copy-start(bf16[8,128,128]{2,1,0:T(8,128)(2,1)S(1)} %collective-permute-done.refs_2_) | copy-start | bytes 786436
  23.6 10.7 %collective-permute-start.5 = (bf16[8,128,128]{2,1,0:T(8,128)(2,1)S(1)}, bf16[8,128,128]{2,1,0:T(8,128)(2,1)S(1)}, u32[]{:S(2)}, u32[]{:S(2)}) collective-permute-start(bf16[8,128,128]{2,1,0:T(8,128)(2,1)S(1)} %broadcast_select_fusion.refs_0_), channel_id=1, source_target_pairs={{0,3},{1,0},{2,1},{3,2},{4,7},{5,4},{6,5},{7,6},{8,11},{9,8},{10,9... | collective-permute-start | bytes 786440 | tf_op jit(solution)/shard_map/ppermute | solution.py:163
  27.5 15.8 %collective-permute-start.3 = (bf16[8,128,128]{2,1,0:T(8,128)(2,1)S(1)}, bf16[8,128,128]{2,1,0:T(8,128)(2,1)S(1)}, u32[]{:S(2)}, u32[]{:S(2)}) collective-permute-start(bf16[8,128,128]{2,1,0:T(8,128)(2,1)S(1)} %broadcast_select_fusion.refs_0_), channel_id=1, source_target_pairs={{0,2},{1,3},{2,0},{3,1},{4,6},{5,7},{6,4},{7,5},{8,10},{9,11},{10,... | collective-permute-start | bytes 786440 | tf_op jit(solution)/shard_map/ppermute | solution.py:163
  27.5 17.3 %collective-permute-start.2 = (bf16[8,128,128]{2,1,0:T(8,128)(2,1)S(1)}, bf16[8,128,128]{2,1,0:T(8,128)(2,1)S(1)}, u32[]{:S(2)}, u32[]{:S(2)}) collective-permute-start(bf16[8,128,128]{2,1,0:T(8,128)(2,1)S(1)} %collective-permute-done.refs_2_), channel_id=1, source_target_pairs={{0,16},{16,0},{1,17},{17,1},{2,18},{18,2},{3,19},{19,3},{4,20},{20... | collective-permute-start | bytes 786440 | tf_op jit(solution)/shard_map/ppermute | solution.py:30
  34.3 15.4 %copy-start.4 = (bf16[8,128,128]{2,1,0:T(8,128)(2,1)}, bf16[8,128,128]{2,1,0:T(8,128)(2,1)S(1)}, u32[]{:S(2)}) copy-start(bf16[8,128,128]{2,1,0:T(8,128)(2,1)S(1)} %collective-permute-done.5.refs_6_) | copy-start | bytes 786436
  34.3 10.6 %collective-permute-start.6 = (bf16[8,128,128]{2,1,0:T(8,128)(2,1)S(1)}, bf16[8,128,128]{2,1,0:T(8,128)(2,1)S(1)}, u32[]{:S(2)}, u32[]{:S(2)}) collective-permute-start(bf16[8,128,128]{2,1,0:T(8,128)(2,1)S(1)} %collective-permute-done.5.refs_6_), channel_id=1, source_target_pairs={{0,16},{16,0},{1,17},{17,1},{2,18},{18,2},{3,19},{19,3},{4,20},{20... | collective-permute-start | bytes 786440 | tf_op jit(solution)/shard_map/ppermute | solution.py:30
  43.3 6.4 %copy-start.5 = (bf16[8,128,128]{2,1,0:T(8,128)(2,1)}, bf16[8,128,128]{2,1,0:T(8,128)(2,1)S(1)}, u32[]{:S(2)}) copy-start(bf16[8,128,128]{2,1,0:T(8,128)(2,1)S(1)} %collective-permute-done.3.refs_4_) | copy-start | bytes 786436
  43.3 6.4 %collective-permute-start.4 = (bf16[8,128,128]{2,1,0:T(8,128)(2,1)S(1)}, bf16[8,128,128]{2,1,0:T(8,128)(2,1)S(1)}, u32[]{:S(2)}, u32[]{:S(2)}) collective-permute-start(bf16[8,128,128]{2,1,0:T(8,128)(2,1)S(1)} %collective-permute-done.3.refs_4_), channel_id=1, source_target_pairs={{0,16},{16,0},{1,17},{17,1},{2,18},{18,2},{3,19},{19,3},{4,20},{20... | collective-permute-start | bytes 786440 | tf_op jit(solution)/shard_map/ppermute | solution.py:30
  44.8 4.9 %copy-start.6 = (bf16[8,128,128]{2,1,0:T(8,128)(2,1)}, bf16[8,128,128]{2,1,0:T(8,128)(2,1)S(1)}, u32[]{:S(2)}) copy-start(bf16[8,128,128]{2,1,0:T(8,128)(2,1)S(1)} %collective-permute-done.2.refs_3_) | copy-start | bytes 786436
  44.8 4.9 %copy-start.7 = (bf16[8,128,128]{2,1,0:T(8,128)(2,1)}, bf16[8,128,128]{2,1,0:T(8,128)(2,1)S(1)}, u32[]{:S(2)}) copy-start(bf16[8,128,128]{2,1,0:T(8,128)(2,1)S(1)} %collective-permute-done.6.refs_7_) | copy-start | bytes 786436
  49.7 0.7 %copy-start.8 = (bf16[8,128,128]{2,1,0:T(8,128)(2,1)}, bf16[8,128,128]{2,1,0:T(8,128)(2,1)S(1)}, u32[]{:S(2)}) copy-start(bf16[8,128,128]{2,1,0:T(8,128)(2,1)S(1)} %collective-permute-done.4.refs_5_) | copy-start | bytes 786436
Sparse Core Ops, SparseCore 0:
  20.1 18.2 all-gather.1

commit v16 on v13

--- a/solution.py
+++ b/solution.py
@@ -45,17 +45,22 @@
     left_refs = refs[:pieces]
     rf_refs = refs[pieces:pieces + rf_groups]
     out_ref = refs[pieces + rf_groups]
-    lhs_scr, rf_scr = refs[pieces + rf_groups + 1:]
+    lhs_scr, rf_scr, rf_buf, sems = refs[pieces + rf_groups + 1:]
     per_group = pieces // rf_groups
-    for q in range(pieces):
-        at = pl.multiple_of(rf_pos_ref[q] * BLK, BLK)
-        rf_scr[pl.ds(at, BLK), :] = rf_refs[q // per_group][q % per_group]
+    copies = [pltpu.make_async_copy(rf_refs[g], rf_buf.at[g], sems.at[g]) for g in range(rf_groups)]
+    for c in copies:
+        c.start()
     for p in range(pieces):
         for i in range(row_blocks):
             s = slot_ref[p, i]
             blk = left_refs[p][jnp.clip(s, 0, left_refs[p].shape[0] - 1)]
             blk = jnp.where(s >= 0, blk, jnp.zeros_like(blk))
             lhs_scr[i * BLK:(i + 1) * BLK, p * BLK:(p + 1) * BLK] = blk
+    for c in copies:
+        c.wait()
+    for q in range(pieces):
+        at = pl.multiple_of(rf_pos_ref[q] * BLK, BLK)
+        rf_scr[pl.ds(at, BLK), :] = rf_buf[q // per_group, q % per_group]
     tile = 4 * BLK
     for t in range(row_blocks * BLK // tile):
         res = jnp.dot(
@@ -85,11 +90,13 @@
             product_kernel, pieces=pieces, rf_groups=rf_groups, row_blocks=row_blocks, cols=cols
         ),
         out_shape=jax.ShapeDtypeStruct((row_blocks * BLK, cols), jnp.bfloat16),
-        in_specs=[smem, smem, smem] + [vmem] * (pieces + rf_groups),
+        in_specs=[smem, smem, smem] + [vmem] * pieces + [pl.BlockSpec(memory_space=pl.ANY)] * rf_groups,
         out_specs=vmem,
         scratch_shapes=[
             pltpu.VMEM((row_blocks * BLK, pieces * BLK), jnp.bfloat16),
             pltpu.VMEM((pieces * BLK, cols), jnp.bfloat16),
+            pltpu.VMEM((rf_groups,) + rf_pieces[0].shape, rf_pieces[0].dtype),
+            pltpu.SemaphoreType.DMA((rf_groups,)),
         ],
         cost_estimate=pl.CostEstimate(flops=flops, bytes_accessed=bytes_accessed, transcendentals=0),
     )(slot_tbl, rf_pos, keep_patch, *left_pieces, *rf_pieces)

time: 44.8 us -> 45.7 us (1.020)
  Pallas kernels: 4.14 us -> 5.12 us
    pallas_call x1, Pallas kernels: 4.14 us -> 5.12 us  [product_call(): pl.pallas_call(functools.partial(product_kernel, pieces=pieces, rf_groups...]
where the time goes in v16:
time: 45.7 us; the launch traced here: 45.5 us
  waiting for transfers between devices  21.5 us (47%)
  starting transfers between devices  11.3 us (25%)
  local copies, waits for them, and re-layouts  5.4 us (12%)
  Pallas kernels  5.12 us (11%)
  other arithmetic  1.98 us (4%)
    ppermute x3, waiting for transfers between devices, col_shift(): lax.ppermute(x, 'col', [(s, (s + k) % col_count) for s in range(col_count)])  15.8 us
    pallas_call x1, Pallas kernels, product_call(): pl.pallas_call(functools.partial(product_kernel, pieces=pieces, rf_groups...  5.12 us
    ppermute x7, starting transfers between devices, ring_gather(): pieces.append(lax.ppermute(x, axis, perm))  4.97 us
    ppermute x7, waiting for transfers between devices, ring_gather(): pieces.append(lax.ppermute(x, axis, perm))  4.85 us
    ppermute x3, starting transfers between devices, col_shift(): lax.ppermute(x, 'col', [(s, (s + k) % col_count) for s in range(col_count)])  3.32 us
    ppermute x1, starting transfers between devices, per_device(): lax.ppermute(packed[0], 'layer', [(s, (s + m) % layer_count) for s in ran...  3 us
    unnamed x31, local copies, waits for them, and re-layouts  2.31 us
  transfers between devices with their start and end apart: 11, of which 6 were waited for; matrix products, arithmetic and copies ran while one was open for 9% of the time, Pallas kernels for 0%

profile of v16, /device:TPU:0, one launch (start us, length us, event | category | flops | bytes accessed | tf_op | source)
XLA Modules:
  0.0 45.5 jit_solution(3998619885500096930)
XLA Ops:
  0.0 0.7 %copy-done.4 = s32[64,8]{0,1:T(8,128)S(1)} copy-done((s32[64,8]{0,1:T(8,128)S(1)}, s32[64,8]{0,1:T(8,128)}, u32[]{:S(2)}) %copy-start.4) | copy-done | bytes 2072
  0.8 0.1 copy.13
  0.9 0.1 add_reduce_fusion
  1.1 0.1 select_reduce_fusion
  1.2 0.6 %gather_fusion = bf16[8,128,128]{2,1,0:T(8,128)(2,1)S(1)} fusion(bf16[16,128,128]{2,1,0:T(8,128)(2,1)S(1)} %bitcast.36, s32[1024]{0:T(1024)S(1)} %pad_clamp_fusion.1), kind=kCustom, calls=%fused_computation | custom fusion | bytes 524320 | tf_op jit(solution)/shard_map/jit(_take)/gather | solution.py:133
  1.8 0.1 broadcast_select_fusion.refs_0_
  2.0 3.0 %collective-permute-start.1 = (bf16[8,128,128]{2,1,0:T(8,128)(2,1)S(1)}, bf16[8,128,128]{2,1,0:T(8,128)(2,1)S(1)}, u32[]{:S(2)}, u32[]{:S(2)}) collective-permute-start(bf16[8,128,128]{2,1,0:T(8,128)(2,1)S(1)} %broadcast_select_fusion.refs_0_), channel_id=1, source_target_pairs={{0,16},{16,0},{1,17},{17,1},{2,18},{18,2},{3,19},{19,3},{4,20},{20... | collective-permute-start | bytes 786440 | tf_op jit(solution)/shard_map/ppermute | solution.py:162
  5.0 1.6 %collective-permute-start = (bf16[8,128,128]{2,1,0:T(8,128)(2,1)S(1)}, bf16[8,128,128]{2,1,0:T(8,128)(2,1)S(1)}, u32[]{:S(2)}, u32[]{:S(2)}) collective-permute-start(bf16[8,128,128]{2,1,0:T(8,128)(2,1)S(1)} %broadcast_select_fusion.refs_0_), channel_id=1, source_target_pairs={{0,1},{1,2},{2,3},{3,0},{4,5},{5,6},{6,7},{7,4},{8,9},{9,10},{10,1... | collective-permute-start | bytes 786440 | tf_op jit(solution)/shard_map/ppermute | solution.py:166
  6.5 0.1 subtract_convert_fusion
  6.6 0.6 %collective-permute-start.7 = (bf16[128,256]{1,0:T(8,128)(2,1)S(1)}, bf16[128,256]{1,0:T(8,128)(2,1)S(1)}, u32[]{:S(2)}, u32[]{:S(2)}) collective-permute-start(bf16[128,256]{1,0:T(8,128)(2,1)S(1)} %subtract_convert_fusion), channel_id=1, source_target_pairs={{0,16},{16,0},{1,17},{17,1},{2,18},{18,2},{3,19},{19,3},{4,20},{20... | collective-permute-start | bytes 196616 | tf_op jit(solution)/shard_map/ppermute | solution.py:30
  7.4 0.6 %fusion.1.rf_pos_ref = s32[8]{0:T(128)} fusion(s32[8]{0:T(128)S(1)} %stack.107, s32[]{:T(128)S(6)} %axis_index.36, s32[]{:T(128)S(6)} %axis_index.38), kind=kLoop, calls=%fused_computation.34 | loop fusion | flops 360 | bytes 72 | tf_op jit(solution)/shard_map/add | solution.py:177
  8.1 0.1 stack.98
  8.3 0.8 %dynamic_slice.11 = s32[16,2]{0,1:T(2,128)S(1)} dynamic-slice(s32[64,8]{0,1:T(8,128)} %param.7, s32[]{:T(128)S(6)} %select_n.179, s32[]{:T(128)S(6)} %select_n.204), dynamic_slice_sizes={16,2} | dynamic-slice | bytes 260 | tf_op jit(solution)/shard_map/dynamic_slice | solution.py:137
  9.1 0.7 %copy.18.keep_ref = s32[16,2]{1,0:T(8,128)} copy(s32[16,2]{0,1:T(2,128)S(1)} %dynamic_slice.11) | data formatting | bytes 256 | tf_op jit(solution)/shard_map/optimization_barrier | solution.py:183
  9.9 0.6 %gather_fusion.1 = s32[8,16]{1,0:T(8,128)S(1)} fusion(s32[16,8]{0,1:T(8,128)S(1)} %copy.15, s32[1024]{0:T(1024)S(1)} %pad_clamp_fusion), kind=kCustom, calls=%fused_computation.1 | custom fusion | bytes 1056 | tf_op jit(solution)/shard_map/jit(_take)/gather | solution.py:182
  10.4 0.7 %broadcast_select_fusion.1.slot_ref = s32[8,16]{1,0:T(8,128)} fusion(s32[8,16]{1,0:T(8,128)S(1)} %gather_fusion.1, pred[8]{0:T(512)(128)(4,1)S(1)} %compare_and_fusion), kind=kLoop, calls=%fused_computation.21 | loop fusion | flops 128 | bytes 1032 | tf_op jit(solution)/shard_map/jit(_take)/select_n | solution.py:182
  11.1 0.9 %collective-permute-done.1.refs_1_ = bf16[8,128,128]{2,1,0:T(8,128)(2,1)S(1)} collective-permute-done((bf16[8,128,128]{2,1,0:T(8,128)(2,1)S(1)}, bf16[8,128,128]{2,1,0:T(8,128)(2,1)S(1)}, u32[]{:S(2)}, u32[]{:S(2)}) %collective-permute-start.1) | collective-permute-done | bytes 262176 | tf_op jit(solution)/shard_map/ppermute | solution.py:162
  12.0 2.6 %collective-permute-done.refs_2_ = bf16[8,128,128]{2,1,0:T(8,128)(2,1)S(1)} collective-permute-done((bf16[8,128,128]{2,1,0:T(8,128)(2,1)S(1)}, bf16[8,128,128]{2,1,0:T(8,128)(2,1)S(1)}, u32[]{:S(2)}, u32[]{:S(2)}) %collective-permute-start) | collective-permute-done | bytes 262176 | tf_op jit(solution)/shard_map/ppermute | solution.py:166
  14.6 1.7 %collective-permute-start.5 = (bf16[8,128,128]{2,1,0:T(8,128)(2,1)S(1)}, bf16[8,128,128]{2,1,0:T(8,128)(2,1)S(1)}, u32[]{:S(2)}, u32[]{:S(2)}) collective-permute-start(bf16[8,128,128]{2,1,0:T(8,128)(2,1)S(1)} %broadcast_select_fusion.refs_0_), channel_id=1, source_target_pairs={{0,3},{1,0},{2,1},{3,2},{4,7},{5,4},{6,5},{7,6},{8,11},{9,8},{10,9... | collective-permute-start | bytes 786440 | tf_op jit(solution)/shard_map/ppermute | solution.py:166
  16.5 1.1 %collective-permute-start.2 = (bf16[8,128,128]{2,1,0:T(8,128)(2,1)S(1)}, bf16[8,128,128]{2,1,0:T(8,128)(2,1)S(1)}, u32[]{:S(2)}, u32[]{:S(2)}) collective-permute-start(bf16[8,128,128]{2,1,0:T(8,128)(2,1)S(1)} %collective-permute-done.refs_2_), channel_id=1, source_target_pairs={{0,16},{16,0},{1,17},{17,1},{2,18},{18,2},{3,19},{19,3},{4,20},{20... | collective-permute-start | bytes 786440 | tf_op jit(solution)/shard_map/ppermute | solution.py:30
  17.6 5.5 %collective-permute-done.5.refs_6_ = bf16[8,128,128]{2,1,0:T(8,128)(2,1)S(1)} collective-permute-done((bf16[8,128,128]{2,1,0:T(8,128)(2,1)S(1)}, bf16[8,128,128]{2,1,0:T(8,128)(2,1)S(1)}, u32[]{:S(2)}, u32[]{:S(2)}) %collective-permute-start.5) | collective-permute-done | bytes 262176 | tf_op jit(solution)/shard_map/ppermute | solution.py:166
  23.1 1.0 %collective-permute-start.6 = (bf16[8,128,128]{2,1,0:T(8,128)(2,1)S(1)}, bf16[8,128,128]{2,1,0:T(8,128)(2,1)S(1)}, u32[]{:S(2)}, u32[]{:S(2)}) collective-permute-start(bf16[8,128,128]{2,1,0:T(8,128)(2,1)S(1)} %collective-permute-done.5.refs_6_), channel_id=1, source_target_pairs={{0,16},{16,0},{1,17},{17,1},{2,18},{18,2},{3,19},{19,3},{4,20},{20... | collective-permute-start | bytes 786440 | tf_op jit(solution)/shard_map/ppermute | solution.py:30
  24.1 7.7 %collective-permute-done.3.refs_4_ = bf16[8,128,128]{2,1,0:T(8,128)(2,1)S(1)} collective-permute-done((bf16[8,128,128]{2,1,0:T(8,128)(2,1)S(1)}, bf16[8,128,128]{2,1,0:T(8,128)(2,1)S(1)}, u32[]{:S(2)}, u32[]{:S(2)}) %collective-permute-start.3) | collective-permute-done | bytes 262176 | tf_op jit(solution)/shard_map/ppermute | solution.py:166
  31.8 0.7 %collective-permute-start.4 = (bf16[8,128,128]{2,1,0:T(8,128)(2,1)S(1)}, bf16[8,128,128]{2,1,0:T(8,128)(2,1)S(1)}, u32[]{:S(2)}, u32[]{:S(2)}) collective-permute-start(bf16[8,128,128]{2,1,0:T(8,128)(2,1)S(1)} %collective-permute-done.3.refs_4_), channel_id=1, source_target_pairs={{0,16},{16,0},{1,17},{17,1},{2,18},{18,2},{3,19},{19,3},{4,20},{20... | collective-permute-start | bytes 786440 | tf_op jit(solution)/shard_map/ppermute | solution.py:30
  32.5 1.5 %collective-permute-start.9 = (bf16[2,128,256]{2,1,0:T(8,128)(2,1)S(1)}, bf16[2,128,256]{2,1,0:T(8,128)(2,1)S(1)}, u32[]{:S(2)}, u32[]{:S(2)}) collective-permute-start(bf16[2,128,256]{2,1,0:T(8,128)(2,1)S(1)} %pad_maximum_fusion.refs_8_), channel_id=1, source_target_pairs={{0,8},{4,12},{8,0},{12,4},{1,9},{5,13},{9,1},{13,5},{2,10},{6,14},... | collective-permute-start | bytes 393224 | tf_op jit(solution)/shard_map/ppermute | solution.py:30
  34.0 3.9 %collective-permute-done.9.refs_10_ = bf16[2,128,256]{2,1,0:T(8,128)(2,1)S(1)} collective-permute-done((bf16[2,128,256]{2,1,0:T(8,128)(2,1)S(1)}, bf16[2,128,256]{2,1,0:T(8,128)(2,1)S(1)}, u32[]{:S(2)}, u32[]{:S(2)}) %collective-permute-start.9) | collective-permute-done | bytes 131104 | tf_op jit(solution)/shard_map/ppermute | solution.py:30
  37.9 0.9 %collective-permute-done.8.refs_9_ = bf16[2,128,256]{2,1,0:T(8,128)(2,1)S(1)} collective-permute-done((bf16[2,128,256]{2,1,0:T(8,128)(2,1)S(1)}, bf16[2,128,256]{2,1,0:T(8,128)(2,1)S(1)}, u32[]{:S(2)}, u32[]{:S(2)}) %collective-permute-start.8) | collective-permute-done | bytes 131104 | tf_op jit(solution)/shard_map/ppermute | solution.py:30
  39.0 0.5 %copy-done.14 = bf16[2,128,256]{2,1,0:T(8,128)(2,1)} copy-done((bf16[2,128,256]{2,1,0:T(8,128)(2,1)}, bf16[2,128,256]{2,1,0:T(8,128)(2,1)S(1)}, u32[]{:S(2)}) %copy-start.14) | copy-done | bytes 131096
  39.5 0.1 copy-done.9
  39.6 0.1 copy-done.10
  39.7 0.7 %copy-done.11 = bf16[8,128,128]{2,1,0:T(8,128)(2,1)} copy-done((bf16[8,128,128]{2,1,0:T(8,128)(2,1)}, bf16[8,128,128]{2,1,0:T(8,128)(2,1)S(1)}, u32[]{:S(2)}) %copy-start.11) | copy-done | bytes 262168
  40.4 5.1 %shard_map.46 = bf16[2048,256]{1,0:T(8,128)(2,1)} custom-call(s32[8,16]{1,0:T(8,128)} %broadcast_select_fusion.1.slot_ref, s32[8]{0:T(128)} %fusion.1.rf_pos_ref, s32[16,2]{1,0:T(8,128)} %copy.18.keep_ref, bf16[8,128,128]{2,1,0:T(8,128)(2,1)} %copy-done.1, bf16[8,128,128]{2,1,0:T(8,128)(2,1)} %copy-done.5, bf16[8,128,128]{2,1,0:T(8,128)(2,1)} %copy-done.6, ...), custom_call_target="tpu_custom_call" | custom-call | flops 1073741824 | bytes 3670016 | tf_op jit(solution)/shard_map/pallas_call | solution.py:88
  (53 shorter events, 0.8 us)
Async XLA Ops:
  0.0 1.2 %copy-start = (bf16[2048,128]{1,0:T(8,128)(2,1)S(1)}, bf16[2048,128]{1,0:T(8,128)(2,1)}, u32[]{:S(2)}) copy-start(bf16[2048,128]{1,0:T(8,128)(2,1)} %param.4) | copy-start | bytes 1572868
  0.0 0.7 %copy-start.4 = (s32[64,8]{0,1:T(8,128)S(1)}, s32[64,8]{0,1:T(8,128)}, u32[]{:S(2)}) copy-start(s32[64,8]{0,1:T(8,128)} %param.6) | copy-start | bytes 6148
  1.8 4.7 %copy-start.2 = (bf16[128,256]{1,0:T(8,128)(2,1)S(1)}, bf16[128,256]{1,0:T(8,128)(2,1)}, u32[]{:S(2)}) copy-start(bf16[128,256]{1,0:T(8,128)(2,1)} %param.5) | copy-start | bytes 196612
  1.9 14.4 %copy-start.1 = (bf16[8,128,128]{2,1,0:T(8,128)(2,1)}, bf16[8,128,128]{2,1,0:T(8,128)(2,1)S(1)}, u32[]{:S(2)}) copy-start(bf16[8,128,128]{2,1,0:T(8,128)(2,1)S(1)} %broadcast_select_fusion.refs_0_) | copy-start | bytes 786436
  2.0 10.0 %collective-permute-start.1 = (bf16[8,128,128]{2,1,0:T(8,128)(2,1)S(1)}, bf16[8,128,128]{2,1,0:T(8,128)(2,1)S(1)}, u32[]{:S(2)}, u32[]{:S(2)}) collective-permute-start(bf16[8,128,128]{2,1,0:T(8,128)(2,1)S(1)} %broadcast_select_fusion.refs_0_), channel_id=1, source_target_pairs={{0,16},{16,0},{1,17},{17,1},{2,18},{18,2},{3,19},{19,3},{4,20},{20... | collective-permute-start | bytes 786440 | tf_op jit(solution)/shard_map/ppermute | solution.py:162
  5.0 9.6 %collective-permute-start = (bf16[8,128,128]{2,1,0:T(8,128)(2,1)S(1)}, bf16[8,128,128]{2,1,0:T(8,128)(2,1)S(1)}, u32[]{:S(2)}, u32[]{:S(2)}) collective-permute-start(bf16[8,128,128]{2,1,0:T(8,128)(2,1)S(1)} %broadcast_select_fusion.refs_0_), channel_id=1, source_target_pairs={{0,1},{1,2},{2,3},{3,0},{4,5},{5,6},{6,7},{7,4},{8,9},{9,10},{10,1... | collective-permute-start | bytes 786440 | tf_op jit(solution)/shard_map/ppermute | solution.py:166
  6.6 9.8 %collective-permute-start.7 = (bf16[128,256]{1,0:T(8,128)(2,1)S(1)}, bf16[128,256]{1,0:T(8,128)(2,1)S(1)}, u32[]{:S(2)}, u32[]{:S(2)}) collective-permute-start(bf16[128,256]{1,0:T(8,128)(2,1)S(1)} %subtract_convert_fusion), channel_id=1, source_target_pairs={{0,16},{16,0},{1,17},{17,1},{2,18},{18,2},{3,19},{19,3},{4,20},{20... | collective-permute-start | bytes 196616 | tf_op jit(solution)/shard_map/ppermute | solution.py:30
  12.0 26.9 %copy-start.5 = (bf16[8,128,128]{2,1,0:T(8,128)(2,1)}, bf16[8,128,128]{2,1,0:T(8,128)(2,1)S(1)}, u32[]{:S(2)}) copy-start(bf16[8,128,128]{2,1,0:T(8,128)(2,1)S(1)} %collective-permute-done.1.refs_1_) | copy-start | bytes 786436
  14.6 24.3 %copy-start.6 = (bf16[8,128,128]{2,1,0:T(8,128)(2,1)}, bf16[8,128,128]{2,1,0:T(8,128)(2,1)S(1)}, u32[]{:S(2)}) copy-start(bf16[8,128,128]{2,1,0:T(8,128)(2,1)S(1)} %collective-permute-done.refs_2_) | copy-start | bytes 786436
  14.6 8.5 %collective-permute-start.5 = (bf16[8,128,128]{2,1,0:T(8,128)(2,1)S(1)}, bf16[8,128,128]{2,1,0:T(8,128)(2,1)S(1)}, u32[]{:S(2)}, u32[]{:S(2)}) collective-permute-start(bf16[8,128,128]{2,1,0:T(8,128)(2,1)S(1)} %broadcast_select_fusion.refs_0_), channel_id=1, source_target_pairs={{0,3},{1,0},{2,1},{3,2},{4,7},{5,4},{6,5},{7,6},{8,11},{9,8},{10,9... | collective-permute-start | bytes 786440 | tf_op jit(solution)/shard_map/ppermute | solution.py:166
  16.3 15.5 %collective-permute-start.3 = (bf16[8,128,128]{2,1,0:T(8,128)(2,1)S(1)}, bf16[8,128,128]{2,1,0:T(8,128)(2,1)S(1)}, u32[]{:S(2)}, u32[]{:S(2)}) collective-permute-start(bf16[8,128,128]{2,1,0:T(8,128)(2,1)S(1)} %broadcast_select_fusion.refs_0_), channel_id=1, source_target_pairs={{0,2},{1,3},{2,0},{3,1},{4,6},{5,7},{6,4},{7,5},{8,10},{9,11},{10,... | collective-permute-start | bytes 786440 | tf_op jit(solution)/shard_map/ppermute | solution.py:166
  16.5 22.5 %copy-start.3 = (bf16[2,128,256]{2,1,0:T(8,128)(2,1)}, bf16[2,128,256]{2,1,0:T(8,128)(2,1)S(1)}, u32[]{:S(2)}) copy-start(bf16[2,128,256]{2,1,0:T(8,128)(2,1)S(1)} %pad_maximum_fusion.refs_8_) | copy-start | bytes 393220
  16.5 17.5 %collective-permute-start.10 = (bf16[2,128,256]{2,1,0:T(8,128)(2,1)S(1)}, bf16[2,128,256]{2,1,0:T(8,128)(2,1)S(1)}, u32[]{:S(2)}, u32[]{:S(2)}) collective-permute-start(bf16[2,128,256]{2,1,0:T(8,128)(2,1)S(1)} %pad_maximum_fusion.refs_8_), channel_id=1, source_target_pairs={{0,12},{4,0},{8,4},{12,8},{1,13},{5,1},{9,5},{13,9},{2,14},{6,2},{... | collective-permute-start | bytes 393224 | tf_op jit(solution)/shard_map/ppermute | solution.py:30
  16.5 22.3 %collective-permute-start.2 = (bf16[8,128,128]{2,1,0:T(8,128)(2,1)S(1)}, bf16[8,128,128]{2,1,0:T(8,128)(2,1)S(1)}, u32[]{:S(2)}, u32[]{:S(2)}) collective-permute-start(bf16[8,128,128]{2,1,0:T(8,128)(2,1)S(1)} %collective-permute-done.refs_2_), channel_id=1, source_target_pairs={{0,16},{16,0},{1,17},{17,1},{2,18},{18,2},{3,19},{19,3},{4,20},{20... | collective-permute-start | bytes 786440 | tf_op jit(solution)/shard_map/ppermute | solution.py:30
  23.1 15.8 %copy-start.7 = (bf16[8,128,128]{2,1,0:T(8,128)(2,1)}, bf16[8,128,128]{2,1,0:T(8,128)(2,1)S(1)}, u32[]{:S(2)}) copy-start(bf16[8,128,128]{2,1,0:T(8,128)(2,1)S(1)} %collective-permute-done.5.refs_6_) | copy-start | bytes 786436
  23.1 15.8 %collective-permute-start.6 = (bf16[8,128,128]{2,1,0:T(8,128)(2,1)S(1)}, bf16[8,128,128]{2,1,0:T(8,128)(2,1)S(1)}, u32[]{:S(2)}, u32[]{:S(2)}) collective-permute-start(bf16[8,128,128]{2,1,0:T(8,128)(2,1)S(1)} %collective-permute-done.5.refs_6_), channel_id=1, source_target_pairs={{0,16},{16,0},{1,17},{17,1},{2,18},{18,2},{3,19},{19,3},{4,20},{20... | collective-permute-start | bytes 786440 | tf_op jit(solution)/shard_map/ppermute | solution.py:30
  31.8 7.1 %copy-start.8 = (bf16[8,128,128]{2,1,0:T(8,128)(2,1)}, bf16[8,128,128]{2,1,0:T(8,128)(2,1)S(1)}, u32[]{:S(2)}) copy-start(bf16[8,128,128]{2,1,0:T(8,128)(2,1)S(1)} %collective-permute-done.3.refs_4_) | copy-start | bytes 786436
  31.8 7.0 %collective-permute-start.4 = (bf16[8,128,128]{2,1,0:T(8,128)(2,1)S(1)}, bf16[8,128,128]{2,1,0:T(8,128)(2,1)S(1)}, u32[]{:S(2)}, u32[]{:S(2)}) collective-permute-start(bf16[8,128,128]{2,1,0:T(8,128)(2,1)S(1)} %collective-permute-done.3.refs_4_), channel_id=1, source_target_pairs={{0,16},{16,0},{1,17},{17,1},{2,18},{18,2},{3,19},{19,3},{4,20},{20... | collective-permute-start | bytes 786440 | tf_op jit(solution)/shard_map/ppermute | solution.py:30
  32.5 5.4 %collective-permute-start.9 = (bf16[2,128,256]{2,1,0:T(8,128)(2,1)S(1)}, bf16[2,128,256]{2,1,0:T(8,128)(2,1)S(1)}, u32[]{:S(2)}, u32[]{:S(2)}) collective-permute-start(bf16[2,128,256]{2,1,0:T(8,128)(2,1)S(1)} %pad_maximum_fusion.refs_8_), channel_id=1, source_target_pairs={{0,8},{4,12},{8,0},{12,4},{1,9},{5,13},{9,1},{13,5},{2,10},{6,14},... | collective-permute-start | bytes 393224 | tf_op jit(solution)/shard_map/ppermute | solution.py:30
  34.0 4.9 %copy-start.12 = (bf16[2,128,256]{2,1,0:T(8,128)(2,1)}, bf16[2,128,256]{2,1,0:T(8,128)(2,1)S(1)}, u32[]{:S(2)}) copy-start(bf16[2,128,256]{2,1,0:T(8,128)(2,1)S(1)} %collective-permute-done.10.refs_11_) | copy-start | bytes 393220
  34.0 4.8 %collective-permute-start.8 = (bf16[2,128,256]{2,1,0:T(8,128)(2,1)S(1)}, bf16[2,128,256]{2,1,0:T(8,128)(2,1)S(1)}, u32[]{:S(2)}, u32[]{:S(2)}) collective-permute-start(bf16[2,128,256]{2,1,0:T(8,128)(2,1)S(1)} %pad_maximum_fusion.refs_8_), channel_id=1, source_target_pairs={{0,4},{4,8},{8,12},{12,0},{1,5},{5,9},{9,13},{13,1},{2,6},{6,10},{... | collective-permute-start | bytes 393224 | tf_op jit(solution)/shard_map/ppermute | solution.py:30
  37.9 1.0 %copy-start.13 = (bf16[2,128,256]{2,1,0:T(8,128)(2,1)}, bf16[2,128,256]{2,1,0:T(8,128)(2,1)S(1)}, u32[]{:S(2)}) copy-start(bf16[2,128,256]{2,1,0:T(8,128)(2,1)S(1)} %collective-permute-done.9.refs_10_) | copy-start | bytes 393220
  38.9 0.7 %copy-start.14 = (bf16[2,128,256]{2,1,0:T(8,128)(2,1)}, bf16[2,128,256]{2,1,0:T(8,128)(2,1)S(1)}, u32[]{:S(2)}) copy-start(bf16[2,128,256]{2,1,0:T(8,128)(2,1)S(1)} %collective-permute-done.8.refs_9_) | copy-start | bytes 393220
  38.9 0.8 %copy-start.9 = (bf16[8,128,128]{2,1,0:T(8,128)(2,1)}, bf16[8,128,128]{2,1,0:T(8,128)(2,1)S(1)}, u32[]{:S(2)}) copy-start(bf16[8,128,128]{2,1,0:T(8,128)(2,1)S(1)} %collective-permute-done.2.refs_3_) | copy-start | bytes 786436
  38.9 0.8 %copy-start.10 = (bf16[8,128,128]{2,1,0:T(8,128)(2,1)}, bf16[8,128,128]{2,1,0:T(8,128)(2,1)S(1)}, u32[]{:S(2)}) copy-start(bf16[8,128,128]{2,1,0:T(8,128)(2,1)S(1)} %collective-permute-done.6.refs_7_) | copy-start | bytes 786436
  39.7 0.7 %copy-start.11 = (bf16[8,128,128]{2,1,0:T(8,128)(2,1)}, bf16[8,128,128]{2,1,0:T(8,128)(2,1)S(1)}, u32[]{:S(2)}) copy-start(bf16[8,128,128]{2,1,0:T(8,128)(2,1)S(1)} %collective-permute-done.4.refs_5_) | copy-start | bytes 786436

commit v17 on v13

--- a/solution.py
+++ b/solution.py
@@ -56,7 +56,7 @@
             blk = left_refs[p][jnp.clip(s, 0, left_refs[p].shape[0] - 1)]
             blk = jnp.where(s >= 0, blk, jnp.zeros_like(blk))
             lhs_scr[i * BLK:(i + 1) * BLK, p * BLK:(p + 1) * BLK] = blk
-    tile = 4 * BLK
+    tile = 8 * BLK
     for t in range(row_blocks * BLK // tile):
         res = jnp.dot(
             lhs_scr[t * tile:(t + 1) * tile, :], rf_scr[...], preferred_element_type=jnp.float32

time: 44.8 us -> 44.7 us (level)
  no operation moved by 1% of the time
where the time goes in v17:
time: 44.7 us; the launch traced here: 44.5 us
  waiting for transfers between devices  21.5 us (48%)
  starting transfers between devices  11.3 us (25%)
  local copies, waits for them, and re-layouts  5.4 us (12%)
  Pallas kernels  4.07 us (9%)
  other arithmetic  1.98 us (4%)
    ppermute x3, waiting for transfers between devices, col_shift(): lax.ppermute(x, 'col', [(s, (s + k) % col_count) for s in range(col_count)])  15.8 us
    ppermute x7, starting transfers between devices, ring_gather(): pieces.append(lax.ppermute(x, axis, perm))  4.97 us
    ppermute x7, waiting for transfers between devices, ring_gather(): pieces.append(lax.ppermute(x, axis, perm))  4.85 us
    pallas_call x1, Pallas kernels, product_call(): pl.pallas_call(functools.partial(product_kernel, pieces=pieces, rf_groups...  4.07 us
    ppermute x3, starting transfers between devices, col_shift(): lax.ppermute(x, 'col', [(s, (s + k) % col_count) for s in range(col_count)])  3.32 us
    ppermute x1, starting transfers between devices, per_device(): lax.ppermute(packed[0], 'layer', [(s, (s + m) % layer_count) for s in ran...  3 us
    unnamed x31, local copies, waits for them, and re-layouts  2.31 us
  transfers between devices with their start and end apart: 11, of which 6 were waited for; matrix products, arithmetic and copies ran while one was open for 9% of the time, Pallas kernels for 0%

profile of v17, /device:TPU:0, one launch (start us, length us, event | category | flops | bytes accessed | tf_op | source)
XLA Modules:
  0.0 44.5 jit_solution(6451776996825283677)
XLA Ops:
  0.0 0.7 %copy-done.4 = s32[64,8]{0,1:T(8,128)S(1)} copy-done((s32[64,8]{0,1:T(8,128)S(1)}, s32[64,8]{0,1:T(8,128)}, u32[]{:S(2)}) %copy-start.4) | copy-done | bytes 2072
  0.8 0.1 copy.13
  0.9 0.1 add_reduce_fusion
  1.1 0.1 select_reduce_fusion
  1.2 0.6 %gather_fusion = bf16[8,128,128]{2,1,0:T(8,128)(2,1)S(1)} fusion(bf16[16,128,128]{2,1,0:T(8,128)(2,1)S(1)} %bitcast.36, s32[1024]{0:T(1024)S(1)} %pad_clamp_fusion.1), kind=kCustom, calls=%fused_computation | custom fusion | bytes 524320 | tf_op jit(solution)/shard_map/jit(_take)/gather | solution.py:126
  1.8 0.1 broadcast_select_fusion.refs_0_
  2.0 3.0 %collective-permute-start.1 = (bf16[8,128,128]{2,1,0:T(8,128)(2,1)S(1)}, bf16[8,128,128]{2,1,0:T(8,128)(2,1)S(1)}, u32[]{:S(2)}, u32[]{:S(2)}) collective-permute-start(bf16[8,128,128]{2,1,0:T(8,128)(2,1)S(1)} %broadcast_select_fusion.refs_0_), channel_id=1, source_target_pairs={{0,16},{16,0},{1,17},{17,1},{2,18},{18,2},{3,19},{19,3},{4,20},{20... | collective-permute-start | bytes 786440 | tf_op jit(solution)/shard_map/ppermute | solution.py:155
  5.0 1.6 %collective-permute-start = (bf16[8,128,128]{2,1,0:T(8,128)(2,1)S(1)}, bf16[8,128,128]{2,1,0:T(8,128)(2,1)S(1)}, u32[]{:S(2)}, u32[]{:S(2)}) collective-permute-start(bf16[8,128,128]{2,1,0:T(8,128)(2,1)S(1)} %broadcast_select_fusion.refs_0_), channel_id=1, source_target_pairs={{0,1},{1,2},{2,3},{3,0},{4,5},{5,6},{6,7},{7,4},{8,9},{9,10},{10,1... | collective-permute-start | bytes 786440 | tf_op jit(solution)/shard_map/ppermute | solution.py:159
  6.5 0.1 subtract_convert_fusion
  6.6 0.6 %collective-permute-start.7 = (bf16[128,256]{1,0:T(8,128)(2,1)S(1)}, bf16[128,256]{1,0:T(8,128)(2,1)S(1)}, u32[]{:S(2)}, u32[]{:S(2)}) collective-permute-start(bf16[128,256]{1,0:T(8,128)(2,1)S(1)} %subtract_convert_fusion), channel_id=1, source_target_pairs={{0,16},{16,0},{1,17},{17,1},{2,18},{18,2},{3,19},{19,3},{4,20},{20... | collective-permute-start | bytes 196616 | tf_op jit(solution)/shard_map/ppermute | solution.py:30
  7.4 0.6 %fusion.1.rf_pos_ref = s32[8]{0:T(128)} fusion(s32[8]{0:T(128)S(1)} %stack.107, s32[]{:T(128)S(6)} %axis_index.36, s32[]{:T(128)S(6)} %axis_index.38), kind=kLoop, calls=%fused_computation.34 | loop fusion | flops 360 | bytes 72 | tf_op jit(solution)/shard_map/add | solution.py:170
  8.1 0.1 stack.98
  8.3 0.8 %dynamic_slice.11 = s32[16,2]{0,1:T(2,128)S(1)} dynamic-slice(s32[64,8]{0,1:T(8,128)} %param.7, s32[]{:T(128)S(6)} %select_n.179, s32[]{:T(128)S(6)} %select_n.204), dynamic_slice_sizes={16,2} | dynamic-slice | bytes 260 | tf_op jit(solution)/shard_map/dynamic_slice | solution.py:130
  9.1 0.7 %copy.18.keep_ref = s32[16,2]{1,0:T(8,128)} copy(s32[16,2]{0,1:T(2,128)S(1)} %dynamic_slice.11) | data formatting | bytes 256 | tf_op jit(solution)/shard_map/optimization_barrier | solution.py:176
  9.9 0.6 %gather_fusion.1 = s32[8,16]{1,0:T(8,128)S(1)} fusion(s32[16,8]{0,1:T(8,128)S(1)} %copy.15, s32[1024]{0:T(1024)S(1)} %pad_clamp_fusion), kind=kCustom, calls=%fused_computation.1 | custom fusion | bytes 1056 | tf_op jit(solution)/shard_map/jit(_take)/gather | solution.py:175
  10.4 0.7 %broadcast_select_fusion.1.slot_ref = s32[8,16]{1,0:T(8,128)} fusion(s32[8,16]{1,0:T(8,128)S(1)} %gather_fusion.1, pred[8]{0:T(512)(128)(4,1)S(1)} %compare_and_fusion), kind=kLoop, calls=%fused_computation.21 | loop fusion | flops 128 | bytes 1032 | tf_op jit(solution)/shard_map/jit(_take)/select_n | solution.py:175
  11.1 0.9 %collective-permute-done.1.refs_1_ = bf16[8,128,128]{2,1,0:T(8,128)(2,1)S(1)} collective-permute-done((bf16[8,128,128]{2,1,0:T(8,128)(2,1)S(1)}, bf16[8,128,128]{2,1,0:T(8,128)(2,1)S(1)}, u32[]{:S(2)}, u32[]{:S(2)}) %collective-permute-start.1) | collective-permute-done | bytes 262176 | tf_op jit(solution)/shard_map/ppermute | solution.py:155
  12.0 2.6 %collective-permute-done.refs_2_ = bf16[8,128,128]{2,1,0:T(8,128)(2,1)S(1)} collective-permute-done((bf16[8,128,128]{2,1,0:T(8,128)(2,1)S(1)}, bf16[8,128,128]{2,1,0:T(8,128)(2,1)S(1)}, u32[]{:S(2)}, u32[]{:S(2)}) %collective-permute-start) | collective-permute-done | bytes 262176 | tf_op jit(solution)/shard_map/ppermute | solution.py:159
  14.6 1.7 %collective-permute-start.5 = (bf16[8,128,128]{2,1,0:T(8,128)(2,1)S(1)}, bf16[8,128,128]{2,1,0:T(8,128)(2,1)S(1)}, u32[]{:S(2)}, u32[]{:S(2)}) collective-permute-start(bf16[8,128,128]{2,1,0:T(8,128)(2,1)S(1)} %broadcast_select_fusion.refs_0_), channel_id=1, source_target_pairs={{0,3},{1,0},{2,1},{3,2},{4,7},{5,4},{6,5},{7,6},{8,11},{9,8},{10,9... | collective-permute-start | bytes 786440 | tf_op jit(solution)/shard_map/ppermute | solution.py:159
  16.5 1.1 %collective-permute-start.2 = (bf16[8,128,128]{2,1,0:T(8,128)(2,1)S(1)}, bf16[8,128,128]{2,1,0:T(8,128)(2,1)S(1)}, u32[]{:S(2)}, u32[]{:S(2)}) collective-permute-start(bf16[8,128,128]{2,1,0:T(8,128)(2,1)S(1)} %collective-permute-done.refs_2_), channel_id=1, source_target_pairs={{0,16},{16,0},{1,17},{17,1},{2,18},{18,2},{3,19},{19,3},{4,20},{20... | collective-permute-start | bytes 786440 | tf_op jit(solution)/shard_map/ppermute | solution.py:30
  17.6 5.5 %collective-permute-done.5.refs_6_ = bf16[8,128,128]{2,1,0:T(8,128)(2,1)S(1)} collective-permute-done((bf16[8,128,128]{2,1,0:T(8,128)(2,1)S(1)}, bf16[8,128,128]{2,1,0:T(8,128)(2,1)S(1)}, u32[]{:S(2)}, u32[]{:S(2)}) %collective-permute-start.5) | collective-permute-done | bytes 262176 | tf_op jit(solution)/shard_map/ppermute | solution.py:159
  23.1 1.0 %collective-permute-start.6 = (bf16[8,128,128]{2,1,0:T(8,128)(2,1)S(1)}, bf16[8,128,128]{2,1,0:T(8,128)(2,1)S(1)}, u32[]{:S(2)}, u32[]{:S(2)}) collective-permute-start(bf16[8,128,128]{2,1,0:T(8,128)(2,1)S(1)} %collective-permute-done.5.refs_6_), channel_id=1, source_target_pairs={{0,16},{16,0},{1,17},{17,1},{2,18},{18,2},{3,19},{19,3},{4,20},{20... | collective-permute-start | bytes 786440 | tf_op jit(solution)/shard_map/ppermute | solution.py:30
  24.1 7.7 %collective-permute-done.3.refs_4_ = bf16[8,128,128]{2,1,0:T(8,128)(2,1)S(1)} collective-permute-done((bf16[8,128,128]{2,1,0:T(8,128)(2,1)S(1)}, bf16[8,128,128]{2,1,0:T(8,128)(2,1)S(1)}, u32[]{:S(2)}, u32[]{:S(2)}) %collective-permute-start.3) | collective-permute-done | bytes 262176 | tf_op jit(solution)/shard_map/ppermute | solution.py:159
  31.8 0.7 %collective-permute-start.4 = (bf16[8,128,128]{2,1,0:T(8,128)(2,1)S(1)}, bf16[8,128,128]{2,1,0:T(8,128)(2,1)S(1)}, u32[]{:S(2)}, u32[]{:S(2)}) collective-permute-start(bf16[8,128,128]{2,1,0:T(8,128)(2,1)S(1)} %collective-permute-done.3.refs_4_), channel_id=1, source_target_pairs={{0,16},{16,0},{1,17},{17,1},{2,18},{18,2},{3,19},{19,3},{4,20},{20... | collective-permute-start | bytes 786440 | tf_op jit(solution)/shard_map/ppermute | solution.py:30
  32.5 1.5 %collective-permute-start.9 = (bf16[2,128,256]{2,1,0:T(8,128)(2,1)S(1)}, bf16[2,128,256]{2,1,0:T(8,128)(2,1)S(1)}, u32[]{:S(2)}, u32[]{:S(2)}) collective-permute-start(bf16[2,128,256]{2,1,0:T(8,128)(2,1)S(1)} %pad_maximum_fusion.refs_8_), channel_id=1, source_target_pairs={{0,8},{4,12},{8,0},{12,4},{1,9},{5,13},{9,1},{13,5},{2,10},{6,14},... | collective-permute-start | bytes 393224 | tf_op jit(solution)/shard_map/ppermute | solution.py:30
  34.0 3.9 %collective-permute-done.9.refs_10_ = bf16[2,128,256]{2,1,0:T(8,128)(2,1)S(1)} collective-permute-done((bf16[2,128,256]{2,1,0:T(8,128)(2,1)S(1)}, bf16[2,128,256]{2,1,0:T(8,128)(2,1)S(1)}, u32[]{:S(2)}, u32[]{:S(2)}) %collective-permute-start.9) | collective-permute-done | bytes 131104 | tf_op jit(solution)/shard_map/ppermute | solution.py:30
  37.9 0.9 %collective-permute-done.8.refs_9_ = bf16[2,128,256]{2,1,0:T(8,128)(2,1)S(1)} collective-permute-done((bf16[2,128,256]{2,1,0:T(8,128)(2,1)S(1)}, bf16[2,128,256]{2,1,0:T(8,128)(2,1)S(1)}, u32[]{:S(2)}, u32[]{:S(2)}) %collective-permute-start.8) | collective-permute-done | bytes 131104 | tf_op jit(solution)/shard_map/ppermute | solution.py:30
  39.0 0.5 %copy-done.14 = bf16[2,128,256]{2,1,0:T(8,128)(2,1)} copy-done((bf16[2,128,256]{2,1,0:T(8,128)(2,1)}, bf16[2,128,256]{2,1,0:T(8,128)(2,1)S(1)}, u32[]{:S(2)}) %copy-start.14) | copy-done | bytes 131096
  39.5 0.1 copy-done.9
  39.6 0.1 copy-done.10
  39.7 0.7 %copy-done.11 = bf16[8,128,128]{2,1,0:T(8,128)(2,1)} copy-done((bf16[8,128,128]{2,1,0:T(8,128)(2,1)}, bf16[8,128,128]{2,1,0:T(8,128)(2,1)S(1)}, u32[]{:S(2)}) %copy-start.11) | copy-done | bytes 262168
  40.4 4.1 %shard_map.46 = bf16[2048,256]{1,0:T(8,128)(2,1)} custom-call(s32[8,16]{1,0:T(8,128)} %broadcast_select_fusion.1.slot_ref, s32[8]{0:T(128)} %fusion.1.rf_pos_ref, s32[16,2]{1,0:T(8,128)} %copy.18.keep_ref, bf16[8,128,128]{2,1,0:T(8,128)(2,1)} %copy-done.1, bf16[8,128,128]{2,1,0:T(8,128)(2,1)} %copy-done.5, bf16[8,128,128]{2,1,0:T(8,128)(2,1)} %copy-done.6, ...), custom_call_target="tpu_custom_call" | custom-call | flops 1073741824 | bytes 3670016 | tf_op jit(solution)/shard_map/pallas_call | solution.py:83
  (53 shorter events, 0.8 us)
Async XLA Ops:
  0.0 1.2 %copy-start = (bf16[2048,128]{1,0:T(8,128)(2,1)S(1)}, bf16[2048,128]{1,0:T(8,128)(2,1)}, u32[]{:S(2)}) copy-start(bf16[2048,128]{1,0:T(8,128)(2,1)} %param.4) | copy-start | bytes 1572868
  0.0 0.7 %copy-start.4 = (s32[64,8]{0,1:T(8,128)S(1)}, s32[64,8]{0,1:T(8,128)}, u32[]{:S(2)}) copy-start(s32[64,8]{0,1:T(8,128)} %param.6) | copy-start | bytes 6148
  1.8 4.7 %copy-start.2 = (bf16[128,256]{1,0:T(8,128)(2,1)S(1)}, bf16[128,256]{1,0:T(8,128)(2,1)}, u32[]{:S(2)}) copy-start(bf16[128,256]{1,0:T(8,128)(2,1)} %param.5) | copy-start | bytes 196612
  1.9 14.4 %copy-start.1 = (bf16[8,128,128]{2,1,0:T(8,128)(2,1)}, bf16[8,128,128]{2,1,0:T(8,128)(2,1)S(1)}, u32[]{:S(2)}) copy-start(bf16[8,128,128]{2,1,0:T(8,128)(2,1)S(1)} %broadcast_select_fusion.refs_0_) | copy-start | bytes 786436
  2.0 10.0 %collective-permute-start.1 = (bf16[8,128,128]{2,1,0:T(8,128)(2,1)S(1)}, bf16[8,128,128]{2,1,0:T(8,128)(2,1)S(1)}, u32[]{:S(2)}, u32[]{:S(2)}) collective-permute-start(bf16[8,128,128]{2,1,0:T(8,128)(2,1)S(1)} %broadcast_select_fusion.refs_0_), channel_id=1, source_target_pairs={{0,16},{16,0},{1,17},{17,1},{2,18},{18,2},{3,19},{19,3},{4,20},{20... | collective-permute-start | bytes 786440 | tf_op jit(solution)/shard_map/ppermute | solution.py:155
  5.0 9.6 %collective-permute-start = (bf16[8,128,128]{2,1,0:T(8,128)(2,1)S(1)}, bf16[8,128,128]{2,1,0:T(8,128)(2,1)S(1)}, u32[]{:S(2)}, u32[]{:S(2)}) collective-permute-start(bf16[8,128,128]{2,1,0:T(8,128)(2,1)S(1)} %broadcast_select_fusion.refs_0_), channel_id=1, source_target_pairs={{0,1},{1,2},{2,3},{3,0},{4,5},{5,6},{6,7},{7,4},{8,9},{9,10},{10,1... | collective-permute-start | bytes 786440 | tf_op jit(solution)/shard_map/ppermute | solution.py:159
  6.6 9.8 %collective-permute-start.7 = (bf16[128,256]{1,0:T(8,128)(2,1)S(1)}, bf16[128,256]{1,0:T(8,128)(2,1)S(1)}, u32[]{:S(2)}, u32[]{:S(2)}) collective-permute-start(bf16[128,256]{1,0:T(8,128)(2,1)S(1)} %subtract_convert_fusion), channel_id=1, source_target_pairs={{0,16},{16,0},{1,17},{17,1},{2,18},{18,2},{3,19},{19,3},{4,20},{20... | collective-permute-start | bytes 196616 | tf_op jit(solution)/shard_map/ppermute | solution.py:30
  12.0 26.9 %copy-start.5 = (bf16[8,128,128]{2,1,0:T(8,128)(2,1)}, bf16[8,128,128]{2,1,0:T(8,128)(2,1)S(1)}, u32[]{:S(2)}) copy-start(bf16[8,128,128]{2,1,0:T(8,128)(2,1)S(1)} %collective-permute-done.1.refs_1_) | copy-start | bytes 786436
  14.6 24.3 %copy-start.6 = (bf16[8,128,128]{2,1,0:T(8,128)(2,1)}, bf16[8,128,128]{2,1,0:T(8,128)(2,1)S(1)}, u32[]{:S(2)}) copy-start(bf16[8,128,128]{2,1,0:T(8,128)(2,1)S(1)} %collective-permute-done.refs_2_) | copy-start | bytes 786436
  14.6 8.5 %collective-permute-start.5 = (bf16[8,128,128]{2,1,0:T(8,128)(2,1)S(1)}, bf16[8,128,128]{2,1,0:T(8,128)(2,1)S(1)}, u32[]{:S(2)}, u32[]{:S(2)}) collective-permute-start(bf16[8,128,128]{2,1,0:T(8,128)(2,1)S(1)} %broadcast_select_fusion.refs_0_), channel_id=1, source_target_pairs={{0,3},{1,0},{2,1},{3,2},{4,7},{5,4},{6,5},{7,6},{8,11},{9,8},{10,9... | collective-permute-start | bytes 786440 | tf_op jit(solution)/shard_map/ppermute | solution.py:159
  16.3 15.5 %collective-permute-start.3 = (bf16[8,128,128]{2,1,0:T(8,128)(2,1)S(1)}, bf16[8,128,128]{2,1,0:T(8,128)(2,1)S(1)}, u32[]{:S(2)}, u32[]{:S(2)}) collective-permute-start(bf16[8,128,128]{2,1,0:T(8,128)(2,1)S(1)} %broadcast_select_fusion.refs_0_), channel_id=1, source_target_pairs={{0,2},{1,3},{2,0},{3,1},{4,6},{5,7},{6,4},{7,5},{8,10},{9,11},{10,... | collective-permute-start | bytes 786440 | tf_op jit(solution)/shard_map/ppermute | solution.py:159
  16.5 22.5 %copy-start.3 = (bf16[2,128,256]{2,1,0:T(8,128)(2,1)}, bf16[2,128,256]{2,1,0:T(8,128)(2,1)S(1)}, u32[]{:S(2)}) copy-start(bf16[2,128,256]{2,1,0:T(8,128)(2,1)S(1)} %pad_maximum_fusion.refs_8_) | copy-start | bytes 393220
  16.5 17.5 %collective-permute-start.10 = (bf16[2,128,256]{2,1,0:T(8,128)(2,1)S(1)}, bf16[2,128,256]{2,1,0:T(8,128)(2,1)S(1)}, u32[]{:S(2)}, u32[]{:S(2)}) collective-permute-start(bf16[2,128,256]{2,1,0:T(8,128)(2,1)S(1)} %pad_maximum_fusion.refs_8_), channel_id=1, source_target_pairs={{0,12},{4,0},{8,4},{12,8},{1,13},{5,1},{9,5},{13,9},{2,14},{6,2},{... | collective-permute-start | bytes 393224 | tf_op jit(solution)/shard_map/ppermute | solution.py:30
  16.5 22.3 %collective-permute-start.2 = (bf16[8,128,128]{2,1,0:T(8,128)(2,1)S(1)}, bf16[8,128,128]{2,1,0:T(8,128)(2,1)S(1)}, u32[]{:S(2)}, u32[]{:S(2)}) collective-permute-start(bf16[8,128,128]{2,1,0:T(8,128)(2,1)S(1)} %collective-permute-done.refs_2_), channel_id=1, source_target_pairs={{0,16},{16,0},{1,17},{17,1},{2,18},{18,2},{3,19},{19,3},{4,20},{20... | collective-permute-start | bytes 786440 | tf_op jit(solution)/shard_map/ppermute | solution.py:30
  23.1 15.8 %copy-start.7 = (bf16[8,128,128]{2,1,0:T(8,128)(2,1)}, bf16[8,128,128]{2,1,0:T(8,128)(2,1)S(1)}, u32[]{:S(2)}) copy-start(bf16[8,128,128]{2,1,0:T(8,128)(2,1)S(1)} %collective-permute-done.5.refs_6_) | copy-start | bytes 786436
  23.1 15.8 %collective-permute-start.6 = (bf16[8,128,128]{2,1,0:T(8,128)(2,1)S(1)}, bf16[8,128,128]{2,1,0:T(8,128)(2,1)S(1)}, u32[]{:S(2)}, u32[]{:S(2)}) collective-permute-start(bf16[8,128,128]{2,1,0:T(8,128)(2,1)S(1)} %collective-permute-done.5.refs_6_), channel_id=1, source_target_pairs={{0,16},{16,0},{1,17},{17,1},{2,18},{18,2},{3,19},{19,3},{4,20},{20... | collective-permute-start | bytes 786440 | tf_op jit(solution)/shard_map/ppermute | solution.py:30
  31.8 7.1 %copy-start.8 = (bf16[8,128,128]{2,1,0:T(8,128)(2,1)}, bf16[8,128,128]{2,1,0:T(8,128)(2,1)S(1)}, u32[]{:S(2)}) copy-start(bf16[8,128,128]{2,1,0:T(8,128)(2,1)S(1)} %collective-permute-done.3.refs_4_) | copy-start | bytes 786436
  31.8 7.0 %collective-permute-start.4 = (bf16[8,128,128]{2,1,0:T(8,128)(2,1)S(1)}, bf16[8,128,128]{2,1,0:T(8,128)(2,1)S(1)}, u32[]{:S(2)}, u32[]{:S(2)}) collective-permute-start(bf16[8,128,128]{2,1,0:T(8,128)(2,1)S(1)} %collective-permute-done.3.refs_4_), channel_id=1, source_target_pairs={{0,16},{16,0},{1,17},{17,1},{2,18},{18,2},{3,19},{19,3},{4,20},{20... | collective-permute-start | bytes 786440 | tf_op jit(solution)/shard_map/ppermute | solution.py:30
  32.5 5.4 %collective-permute-start.9 = (bf16[2,128,256]{2,1,0:T(8,128)(2,1)S(1)}, bf16[2,128,256]{2,1,0:T(8,128)(2,1)S(1)}, u32[]{:S(2)}, u32[]{:S(2)}) collective-permute-start(bf16[2,128,256]{2,1,0:T(8,128)(2,1)S(1)} %pad_maximum_fusion.refs_8_), channel_id=1, source_target_pairs={{0,8},{4,12},{8,0},{12,4},{1,9},{5,13},{9,1},{13,5},{2,10},{6,14},... | collective-permute-start | bytes 393224 | tf_op jit(solution)/shard_map/ppermute | solution.py:30
  34.0 4.9 %copy-start.12 = (bf16[2,128,256]{2,1,0:T(8,128)(2,1)}, bf16[2,128,256]{2,1,0:T(8,128)(2,1)S(1)}, u32[]{:S(2)}) copy-start(bf16[2,128,256]{2,1,0:T(8,128)(2,1)S(1)} %collective-permute-done.10.refs_11_) | copy-start | bytes 393220
  34.0 4.8 %collective-permute-start.8 = (bf16[2,128,256]{2,1,0:T(8,128)(2,1)S(1)}, bf16[2,128,256]{2,1,0:T(8,128)(2,1)S(1)}, u32[]{:S(2)}, u32[]{:S(2)}) collective-permute-start(bf16[2,128,256]{2,1,0:T(8,128)(2,1)S(1)} %pad_maximum_fusion.refs_8_), channel_id=1, source_target_pairs={{0,4},{4,8},{8,12},{12,0},{1,5},{5,9},{9,13},{13,1},{2,6},{6,10},{... | collective-permute-start | bytes 393224 | tf_op jit(solution)/shard_map/ppermute | solution.py:30
  37.9 1.0 %copy-start.13 = (bf16[2,128,256]{2,1,0:T(8,128)(2,1)}, bf16[2,128,256]{2,1,0:T(8,128)(2,1)S(1)}, u32[]{:S(2)}) copy-start(bf16[2,128,256]{2,1,0:T(8,128)(2,1)S(1)} %collective-permute-done.9.refs_10_) | copy-start | bytes 393220
  38.9 0.7 %copy-start.14 = (bf16[2,128,256]{2,1,0:T(8,128)(2,1)}, bf16[2,128,256]{2,1,0:T(8,128)(2,1)S(1)}, u32[]{:S(2)}) copy-start(bf16[2,128,256]{2,1,0:T(8,128)(2,1)S(1)} %collective-permute-done.8.refs_9_) | copy-start | bytes 393220
  38.9 0.8 %copy-start.9 = (bf16[8,128,128]{2,1,0:T(8,128)(2,1)}, bf16[8,128,128]{2,1,0:T(8,128)(2,1)S(1)}, u32[]{:S(2)}) copy-start(bf16[8,128,128]{2,1,0:T(8,128)(2,1)S(1)} %collective-permute-done.2.refs_3_) | copy-start | bytes 786436
  38.9 0.8 %copy-start.10 = (bf16[8,128,128]{2,1,0:T(8,128)(2,1)}, bf16[8,128,128]{2,1,0:T(8,128)(2,1)S(1)}, u32[]{:S(2)}) copy-start(bf16[8,128,128]{2,1,0:T(8,128)(2,1)S(1)} %collective-permute-done.6.refs_7_) | copy-start | bytes 786436
  39.7 0.7 %copy-start.11 = (bf16[8,128,128]{2,1,0:T(8,128)(2,1)}, bf16[8,128,128]{2,1,0:T(8,128)(2,1)S(1)}, u32[]{:S(2)}) copy-start(bf16[8,128,128]{2,1,0:T(8,128)(2,1)S(1)} %collective-permute-done.4.refs_5_) | copy-start | bytes 786436
